TPU v7x, 128 devices: a whole 4x4x4 slice. The times are simulated.
128 devices in a mesh: pipe: 8 (over z, core), ctx: 16 (over y, x).
Axes of the slice: x: 4, y: 4, z: 4, core: 2. Of those that a mesh axis runs over, the one named last changes fastest.
Arguments:
- grad_in: bfloat16 [8, 4096, 8192], P('pipe', 'ctx'), may hold values from -6 to 6
- query: bfloat16 [8, 4096, 512], P('pipe', 'ctx'), may hold values from -8 to 8
- keyval: bfloat16 [8, 4096, 256], P('pipe', 'ctx'), may hold values from -8 to 8
- w_qkv: bfloat16 [8, 8192, 768], P('pipe', 'ctx'), may hold values from -0.0625 to 0.0625
- w_out: bfloat16 [8, 8192, 512], P('pipe', 'ctx'), may hold values from -0.25 to 0.25
- doc_lengths: int32 [8, 8], P('pipe'), may hold values from 1 to 2048, 4096 in all within a row
- order: int32 [8, 32], P('pipe'), may hold values from 0 to 31, as said below
Outputs:
- passed_grad: bfloat16 [8, 4096, 8192], P('pipe', 'ctx')
Inputs may be any that keep to these rules, and one draw needn't show every extreme that they name: Each row of order is a permutation of 0 to 31; entry d * 2 + k (device d's stored slot k, k < 2) names one of the sequence blocks e * 2 to e * 2 + 1 of device e = (d + k * 8) mod 16. `doc_lengths`: each row sums to 4096 and its largest entry is 2048.
All inputs are finite; a program needn't handle non-finite values.
Results may differ from a plain program's by a relative error of at most 0.015.
Values may be sent and summed in bfloat16 or wider, within the bound.
No kernel may reach another device: no remote copies, remote signals or barrier semaphores. Data moves between devices by JAX's collectives and lax.ppermute only.
A program may use at most 128 MiB of HBM per device.

v0:
```python
import math

import jax
import jax.numpy as jnp
from jax import lax
from jax.sharding import PartitionSpec as P

BLOCK = 128


ROPE_BASE = 500000.0
MASKED = -1e30


def passed_along(value, axis, steps):
    count = lax.axis_size(axis)
    pairs = [(source, (source + steps) % count) for source in range(count)]
    return lax.ppermute(value, axis, pairs)


def passed_along_2(value, axis, by):
    size = lax.axis_size(axis)
    pairs = [(i, i + by) for i in range(size) if 0 <= i + by < size]
    return lax.ppermute(value, axis, pairs)


def rope_tables(positions, head_dim):
    half_width = head_dim // 2
    inv_freq = ROPE_BASE ** (-(jnp.arange(half_width, dtype=jnp.float32) * 2.0 / head_dim))
    angles = positions.astype(jnp.float32)[:, None] * inv_freq[None, :]
    angles = jnp.concatenate([angles, angles], axis=1)
    return (jnp.cos(angles), jnp.sin(angles))


def unrotate(gradient, positions):
    cosine, sine_table = rope_tables(positions, gradient.shape[1])
    half_width = gradient.shape[1] // 2
    turned = jnp.concatenate([-gradient[:, half_width:], gradient[:, :half_width]], axis=1)
    return gradient * cosine - turned * sine_table


def doc_ids(positions, lengths):
    doc_ends = jnp.cumsum(lengths)[:-1]
    return jnp.sum((positions[:, None] >= doc_ends[None, :]).astype(jnp.int32), axis=1)


def seq_to_stored(rows, block_order, device, ctx_size, per_device):
    width = rows.shape[1]
    first_block = device * per_device
    blocks = rows.reshape(per_device, BLOCK, width)
    pieces = []
    for slot_k in range(per_device):
        offset = slot_k * ctx_size // per_device
        slot_at = (device - offset) % ctx_size * per_device + slot_k
        local_index = block_order[slot_at] - first_block
        chosen = lax.dynamic_index_in_dim(blocks, local_index, 0, keepdims=False)
        if slot_k > 0:
            chosen = passed_along(chosen, "ctx", -offset)
        pieces.append(chosen)
    return jnp.concatenate(pieces, axis=0)


def stored_to_seq(rows, block_order, device, ctx_size, per_device):
    width = rows.shape[1]
    first_block = device * per_device
    blocks = rows.reshape(per_device, BLOCK, width)
    pieces = []
    local_ids = []
    for slot_k in range(per_device):
        offset = slot_k * ctx_size // per_device
        piece = blocks[slot_k]
        if slot_k > 0:
            piece = passed_along(piece, "ctx", offset)
        pieces.append(piece)
        sender_slot = (device - offset) % ctx_size * per_device + slot_k
        local_ids.append(block_order[sender_slot] - first_block)
    stacked = jnp.stack(pieces)
    index_list = jnp.stack(local_ids)
    choose = (jnp.arange(per_device, dtype=jnp.int32)[:, None] == index_list[None, :]).astype(
        rows.dtype
    )
    placed = jnp.einsum("pk,kbw->pbw", choose, stacked, preferred_element_type=jnp.float32)
    return placed.astype(rows.dtype).reshape(-1, width)


def contract_rows(left_rows, right_rows):
    return lax.dot_general(
        left_rows, right_rows, (((0,), (0,)), ((), ())), preferred_element_type=jnp.float32
    )


def contract_cols(left_rows, right_rows):
    return lax.dot_general(
        left_rows, right_rows, (((1,), (1,)), ((), ())), preferred_element_type=jnp.float32
    )


def block_scores(query_rows, key_rows, query_pos, query_doc, key_pos, key_doc, score_scale):
    scores = contract_cols(query_rows, key_rows) * score_scale
    visible = (query_doc[:, None] == key_doc[None, :]) & (key_pos[None, :] <= query_pos[:, None])
    return (scores, visible)


def body(grad_in, query, keyval, w_qkv, w_out, doc_lengths, order):
    section_grad_in = grad_in[0]
    stored_query = query[0]
    stored_keyval = keyval[0]
    in_weight = w_qkv[0]
    out_weight = w_out[0]
    lengths = doc_lengths[0]
    block_order = order[0]
    ctx_size = lax.axis_size("ctx")
    device = lax.axis_index("ctx")
    local_rows = section_grad_in.shape[0]
    head_dim = stored_keyval.shape[1] // 2
    group = stored_query.shape[1] // head_dim
    per_device = local_rows // BLOCK
    block_count = block_order.shape[0]
    seq_len = local_rows * ctx_size
    first_row = device * local_rows
    score_scale = 1.0 / math.sqrt(head_dim)
    key_block = math.gcd(seq_len, 512)
    key_steps = seq_len // key_block
    within = jnp.arange(BLOCK, dtype=jnp.int32)
    out_grad = jnp.dot(
        section_grad_in,
        lax.all_gather(out_weight, "ctx", axis=0, tiled=True),
        preferred_element_type=jnp.float32,
    ).astype(jnp.bfloat16)
    local_out_grad = seq_to_stored(out_grad, block_order, device, ctx_size, per_device)
    query_positions = (block_order[:, None] * BLOCK + within[None, :]).reshape(-1)
    gathered = lax.all_gather(stored_keyval, "ctx", axis=0, tiled=True)
    slot_ids = jnp.arange(block_count, dtype=jnp.int32)
    inverse = jnp.sum(
        jnp.where(block_order[None, :] == slot_ids[:, None], slot_ids[None, :], 0), axis=1
    )
    all_keyval = gathered.reshape(block_count, BLOCK, 2 * head_dim)[inverse].reshape(
        seq_len, 2 * head_dim
    )
    key_positions = jnp.arange(seq_len, dtype=jnp.int32)
    key_docs = doc_ids(key_positions, lengths)
    query_pos = lax.dynamic_slice_in_dim(query_positions, first_row, local_rows)
    query_doc = doc_ids(query_pos, lengths)
    flat_rows = local_rows * group
    flat_query = stored_query.reshape(flat_rows, head_dim)
    flat_grad = local_out_grad.reshape(flat_rows, head_dim)
    flat_pos = jnp.repeat(query_pos, group)
    flat_doc = jnp.repeat(query_doc, group)
    key_blocks = (
        all_keyval.reshape(key_steps, key_block, 2 * head_dim),
        key_positions.reshape(key_steps, key_block),
        key_docs.reshape(key_steps, key_block),
    )

    def running_total(carried, current):
        row_top, row_total, weighted = carried
        pair_rows, key_pos, key_doc = current
        scores, visible = block_scores(
            flat_query, pair_rows[:, :head_dim], flat_pos, flat_doc, key_pos, key_doc, score_scale
        )
        new_top = jnp.maximum(row_top, jnp.max(jnp.where(visible, scores, MASKED), axis=1))
        rescale = jnp.exp(row_top - new_top)
        weights = jnp.where(visible, jnp.exp(scores - new_top[:, None]), 0.0)
        row_total = row_total * rescale + jnp.sum(weights, axis=1)
        value_wide = pair_rows[:, head_dim:].astype(jnp.float32)
        weighted = weighted * rescale[:, None] + jnp.dot(
            weights, value_wide, precision=lax.Precision.HIGHEST
        )
        return ((new_top, row_total, weighted), None)

    start_top = jnp.full((flat_rows,), MASKED, jnp.float32)
    start_carry = (
        start_top,
        jnp.zeros((flat_rows,), jnp.float32),
        jnp.zeros((flat_rows, head_dim), jnp.float32),
    )
    (row_top, row_total, weighted), unused = lax.scan(running_total, start_carry, key_blocks)
    log_total = row_top + jnp.log(row_total)
    attn_out = weighted / row_total[:, None]
    row_delta = jnp.sum(flat_grad.astype(jnp.float32) * attn_out, axis=1)

    def grad_step(summed, current):
        pair_rows, key_pos, key_doc = current
        scores, visible = block_scores(
            flat_query, pair_rows[:, :head_dim], flat_pos, flat_doc, key_pos, key_doc, score_scale
        )
        attn_prob = jnp.where(visible, jnp.exp(scores - log_total[:, None]), 0.0)
        prob_grad = contract_cols(flat_grad, pair_rows[:, head_dim:])
        score_grad = (score_scale * attn_prob * (prob_grad - row_delta[:, None])).astype(
            jnp.bfloat16
        )
        summed = summed + jnp.dot(
            score_grad, pair_rows[:, :head_dim], preferred_element_type=jnp.float32
        )
        key_term = contract_rows(score_grad, flat_query)
        value_term = contract_rows(attn_prob.astype(jnp.bfloat16), flat_grad)
        return (summed, jnp.concatenate([key_term, value_term], axis=1))

    query_grad_rot, key_terms = lax.scan(
        grad_step, jnp.zeros((flat_rows, head_dim), jnp.float32), key_blocks
    )
    own_positions = first_row + jnp.arange(local_rows, dtype=jnp.int32)
    keyval_grad = lax.psum_scatter(
        key_terms.reshape(seq_len, 2 * head_dim).astype(jnp.bfloat16),
        "ctx",
        scatter_dimension=0,
        tiled=True,
    ).astype(jnp.float32)
    query_grad = (
        unrotate(query_grad_rot, flat_pos)
        .reshape(local_rows, group * head_dim)
        .astype(jnp.bfloat16)
    )
    query_grad = stored_to_seq(query_grad, block_order, device, ctx_size, per_device)
    key_grad = unrotate(keyval_grad[:, :head_dim], own_positions).astype(jnp.bfloat16)
    value_grad = keyval_grad[:, head_dim:].astype(jnp.bfloat16)
    qkv_grad = jnp.concatenate([query_grad, key_grad, value_grad], axis=1)
    projected = contract_cols(qkv_grad, lax.all_gather(in_weight, "ctx", axis=0, tiled=True))
    section_grad = (section_grad_in.astype(jnp.float32) + projected).astype(jnp.bfloat16)
    passed = passed_along_2(section_grad, "pipe", -1)
    return passed[None]


def solution(mesh):
    return jax.shard_map(
        body,
        mesh=mesh,
        in_specs=(
            P("pipe", "ctx", None),
            P("pipe", "ctx", None),
            P("pipe", "ctx", None),
            P("pipe", "ctx", None),
            P("pipe", "ctx", None),
            P("pipe", None),
            P("pipe", None),
        ),
        out_specs=P("pipe", "ctx", None),
        check_vma=False,
    )
```

profile of v0, /device:TPU:1, one launch (start us, length us, event | category | flops | bytes accessed | tf_op | source)
XLA Modules:
  0.0 424.1 jit_solution(3476864368131219313)
XLA Ops:
  8.1 1.3 constant_dynamic-slice_fusion.5
  10.7 0.8 reduce-window.4
  11.6 1.1 reshape_squeeze.3
  14.5 42.2 %all-gather.7.cloned.1.call-done = bf16[1,4096,256]{2,1,0:T(8,128)(2,1)} async-done(((bf16[1,256,256]{2,1,0:T(8,128)(2,1)}), bf16[1,4096,256]{2,1,0:T(8,128)(2,1)}) %all-gather.7.cloned.1.call-update) | async-done | bytes 2097168 | tf_op jit(solution)/shard_map/all_gather | solution.py:132
  56.7 3.6 gather_fusion
  60.3 51.0 %while.28 = (s32[]{:T(128)}, f32[1024]{0:T(1024)S(1)}, f32[1024]{0:T(1024)S(1)}, f32[1024,128]{1,0:T(8,128)}, s32[8,512]{1,0:T(8,128)S(1)}, /*index=5*/s32[8,512...) while((s32[]{:T(128)}, f32[1024]{0:T(1024)S(1)}, ...), condition=%wide.region_7.8_spmd.clone, body=%wide.region_4.7_spmd.clone.sunk | while | flops 949883904 | bytes 12720321 | solution.py:177
  60.3 1.0 dynamic-slice_bitcast_fusion.6
  63.4 2.4 convolution_add_fusion.4
  65.9 0.8 copy-done.1
  66.7 1.0 dynamic-slice_bitcast_fusion.6
  69.8 2.4 convolution_add_fusion.4
  73.1 1.0 dynamic-slice_bitcast_fusion.6
  76.2 2.4 convolution_add_fusion.4
  79.5 1.0 dynamic-slice_bitcast_fusion.6
  82.6 2.4 convolution_add_fusion.4
  85.8 1.0 dynamic-slice_bitcast_fusion.6
  88.9 2.4 convolution_add_fusion.4
  92.2 1.1 dynamic-slice_bitcast_fusion.6
  95.3 2.4 convolution_add_fusion.4
  98.6 1.0 dynamic-slice_bitcast_fusion.6
  101.7 2.4 convolution_add_fusion.4
  104.9 1.0 dynamic-slice_bitcast_fusion.6
  108.0 2.4 convolution_add_fusion.4
  111.3 18.4 %all-gather.9.cloned.1.call-done = bf16[1,8192,512]{2,1,0:T(8,128)(2,1)} async-done(((bf16[1,512,512]{2,1,0:T(8,128)(2,1)}), bf16[1,8192,512]{2,1,0:T(8,128)(2,1)}) %all-gather.9.cloned.1.call-update) | async-done | bytes 8388624 | tf_op jit(solution)/shard_map/all_gather | solution.py:127
  129.7 7.0 %fusion.43 = bf16[256,512]{1,0:T(8,128)(2,1)S(1)} fusion(bf16[1,8192,512]{2,1,0:T(8,128)(2,1)} %all-gather.9.cloned.1.call-done, bf16[1,256,8192]{2,1,0:T(8,128)(2,1)} %param.11), kind=kOutput, calls=%fused_computation.55 | convolution fusion | flops 2147614720 | bytes 12845056 | tf_op jit(solution)/shard_map/dot_general | solution.py:125
  136.7 2.8 collective-permute-start
  139.5 3.2 collective-permute-done
  143.3 41.0 %while.29 = (s32[]{:T(128)}, f32[1024,128]{1,0:T(8,128)S(1)}, bf16[8,512,256]{2,1,0:T(8,128)(2,1)}, s32[8,512]{1,0:T(8,128)S(1)}, s32[8,512]{1,0:T(8,128)S(1)}, ...) while((s32[]{:T(128)}, f32[1024,128]{1,0:T(8,128)S(1)}, ...), condition=%wide.region_10.11_spmd.clone, body=%wide.region_9.10_spmd.clone.sunk | while | flops 677642240 | bytes 14342807 | solution.py:199
  143.3 1.0 dynamic-slice_bitcast_fusion.7
  148.4 1.0 dynamic-slice_bitcast_fusion.7
  153.5 1.0 dynamic-slice_bitcast_fusion.7
  158.7 1.0 dynamic-slice_bitcast_fusion.7
  163.8 1.0 dynamic-slice_bitcast_fusion.7
  168.9 1.0 dynamic-slice_bitcast_fusion.7
  174.0 1.0 dynamic-slice_bitcast_fusion.7
  179.2 1.0 dynamic-slice_bitcast_fusion.7
  185.6 2.4 fusion.49
  188.1 2.9 collective-permute-start.1
  191.2 2.4 collective-permute-done.1
  194.6 63.0 %reduce-scatter.2.cloned.1.call-done = bf16[256,256]{1,0:T(8,128)(2,1)} async-done(((bf16[4096,256]{1,0:T(8,128)(2,1)}), bf16[256,256]{1,0:T(8,128)(2,1)}) %reduce-scatter.2.cloned.1.call-update) | async-done | bytes 131088 | tf_op jit(solution)/shard_map/reduce_scatter | solution.py:203
  257.6 0.9 convert_element_type.75
  258.5 0.9 slice.79
  259.4 0.8 slice.80
  260.9 89.8 %all-gather.11.cloned.1.call-done = bf16[1,8192,768]{2,1,0:T(8,128)(2,1)} async-done(((bf16[1,512,768]{2,1,0:T(8,128)(2,1)}), bf16[1,8192,768]{2,1,0:T(8,128)(2,1)}) %all-gather.11.cloned.1.call-update) | async-done | bytes 12582928 | tf_op jit(solution)/shard_map/all_gather | solution.py:218
  350.7 14.8 %fusion.37 = bf16[256,8192]{1,0:T(8,128)(2,1)} fusion(bf16[1,8192,768]{2,1,0:T(8,128)(2,1)} %all-gather.11.cloned.1.call-done, bf16[1,256,8192]{2,1,0:T(8,128)(2,1)} %param.11, bf16[256,128]{1,0:T(8,128)(2,1)S(1)} %slice.80, bf16[256,128]{1,0:T(8,128)(2,1)S(1)} %fusion.57, bf16[256,512]{1,0:T(8,128)(2,1)S(1)} %bitcast.123), kind=kOutput, calls=%fused_computation.50 | convolution fusion | flops 3228696576 | bytes 21364736 | tf_op jit(solution)/shard_map/dot_general | solution.py:93
  365.5 2.6 collective-permute-start.2
  368.1 47.5 %collective-permute-done.2 = bf16[256,8192]{1,0:T(8,128)(2,1)S(1)} collective-permute-done((bf16[256,8192]{1,0:T(8,128)(2,1)}, bf16[256,8192]{1,0:T(8,128)(2,1)S(1)}, u32[]{:S(2)}, u32[]{:S(2)}) %collective-permute-start.2) | collective-permute-done | bytes 4194336 | tf_op jit(solution)/shard_map/ppermute | solution.py:24
  415.6 2.0 copy.44
  (262 shorter events, 61.7 us)
Async XLA Ops:
  6.5 50.2 %all-gather.7.cloned.1.call-start = ((), (), s32[]{:S(2)}) async-start(), calls=%async_computation.2 | async-start | bytes 2228224 | tf_op jit(solution)/shard_map/all_gather | solution.py:132
  7.3 122.5 %all-gather.9.cloned.1.call-start = ((), (), s32[]{:S(2)}) async-start(), calls=%async_computation.3 | async-start | bytes 8912896 | tf_op jit(solution)/shard_map/all_gather | solution.py:127
  8.0 249.6 %reduce-scatter.2.cloned.1.call-start = ((), (), s32[]{:S(2)}) async-start(), calls=%async_computation.1 | async-start | bytes 2228224 | tf_op jit(solution)/shard_map/reduce_scatter | solution.py:203
  62.4 1.0 copy-start
  65.9 0.8 copy-start.1
  68.8 1.1 copy-start
  72.3 0.8 copy-start.1
  75.1 1.1 copy-start
  78.6 0.8 copy-start.1
  81.5 1.0 copy-start
  85.0 0.8 copy-start.1
  87.9 1.0 copy-start
  91.3 0.8 copy-start.1
  94.3 1.0 copy-start
  97.8 0.8 copy-start.1
  100.6 1.0 copy-start
  104.1 0.8 copy-start.1
  107.0 1.0 copy-start
  110.5 0.8 copy-start.1
  111.3 31.6 %copy-start.2 = (f32[1024,128]{1,0:T(8,128)S(1)}, f32[1024,128]{1,0:T(8,128)}, u32[]{:S(2)}) copy-start(f32[1024,128]{1,0:T(8,128)} %get-tuple-element.124) | copy-start | bytes 1572868
  136.7 5.9 %collective-permute-start = (bf16[128,512]{1,0:T(8,128)(2,1)S(1)}, bf16[128,512]{1,0:T(8,128)(2,1)S(1)}, u32[]{:S(2)}, u32[]{:S(2)}) collective-permute-start(bf16[128,512]{1,0:T(8,128)(2,1)S(1)} %get-tuple-element.270), channel_id=1, source_target_pairs={{0,8},{1,9},{2,10},{3,11},{4,12},{5,13},{6,14},{7,15},{8,0},{9,1},... | collective-permute-start | bytes 393224 | tf_op jit(solution)/shard_map/ppermute | solution.py:18
  184.3 166.3 %all-gather.11.cloned.1.call-start = ((), (), s32[]{:S(2)}) async-start(), calls=%async_computation.4 | async-start | bytes 13369344 | tf_op jit(solution)/shard_map/all_gather | solution.py:218
  188.1 5.6 %collective-permute-start.1 = (bf16[128,512]{1,0:T(8,128)(2,1)S(1)}, bf16[128,512]{1,0:T(8,128)(2,1)S(1)}, u32[]{:S(2)}, u32[]{:S(2)}) collective-permute-start(bf16[128,512]{1,0:T(8,128)(2,1)S(1)} %slice.59), channel_id=1, source_target_pairs={{0,8},{1,9},{2,10},{3,11},{4,12},{5,13},{6,14},{7,15},{8,0},{9,1},... | collective-permute-start | bytes 393224 | tf_op jit(solution)/shard_map/ppermute | solution.py:18
  365.5 50.1 %collective-permute-start.2 = (bf16[256,8192]{1,0:T(8,128)(2,1)}, bf16[256,8192]{1,0:T(8,128)(2,1)S(1)}, u32[]{:S(2)}, u32[]{:S(2)}) collective-permute-start(bf16[256,8192]{1,0:T(8,128)(2,1)} %fusion.37), channel_id=1, source_target_pairs={{16,0},{32,16},{48,32},{64,48},{80,64},{96,80},{112,96},{17,1},{33... | collective-permute-start | bytes 12582920 | tf_op jit(solution)/shard_map/ppermute | solution.py:24
Sparse Core Ops, SparseCore 0:
  9.5 47.1 all-gather.6
  58.8 70.8 all-gather.8
  184.4 73.1 reduce-scatter.1
  259.8 90.8 all-gather.10
where the time goes:
time: 425 us; the launch traced here: 424 us
  waiting for transfers between devices  269 us (63%)
  matrix products  68.8 us (16%)
  local copies, waits for them, and re-layouts  49.3 us (12%)
  between operations  14.6 us (3%)
  other arithmetic  13 us (3%)
  starting transfers between devices  8.38 us (2%)
    all_gather x1, waiting for transfers between devices, body(): lax.all_gather(in_weight, 'ctx', axis=0, tiled=True)  89.8 us
    reduce_scatter x1, waiting for transfers between devices, body(): lax.psum_scatter(key_terms.reshape(seq_len, 2 * head_dim).astype(jnp.bflo...  63 us
    ppermute x1, waiting for transfers between devices, passed_along_2(): return lax.ppermute(value, axis, pairs)  47.5 us
    all_gather x1, waiting for transfers between devices, body(): gathered = lax.all_gather(stored_keyval, 'ctx', axis=0, tiled=True)  42.2 us
    dot_general x25, matrix products, contract_cols(): lax.dot_general(left_rows, right_rows, (((1,), (1,)), ((), ())), preferre...  29.2 us
    dot_general x8, matrix products, running_total(): jnp.dot(weights, value_wide, precision=lax.Precision.HIGHEST)  19.4 us
    all_gather x1, waiting for transfers between devices, body(): lax.all_gather(out_weight, 'ctx', axis=0, tiled=True)  18.4 us
    squeeze x16, local copies, waits for them, and re-layouts, body(): lax.scan(running_total, start_carry, key_blocks)  15.7 us
  transfers between devices with their start and end apart: 7, of which 7 were waited for; matrix products, arithmetic and copies ran while one was open for 13% of the time, Pallas kernels for 0%

commit v1 on v0

--- a/solution.py
+++ b/solution.py
@@ -22,6 +22,18 @@
     size = lax.axis_size(axis)
     pairs = [(i, i + by) for i in range(size) if 0 <= i + by < size]
     return lax.ppermute(value, axis, pairs)
+
+
+def gathered_rows(value, axis):
+    count = lax.axis_size(axis)
+    spread = jnp.broadcast_to(value[None], (count,) + value.shape)
+    return lax.all_to_all(spread, axis, 0, 0, tiled=False).reshape((-1,) + value.shape[1:])
+
+
+def summed_rows(value, axis):
+    count = lax.axis_size(axis)
+    pieces = lax.all_to_all(value.reshape((count, -1) + value.shape[1:]), axis, 0, 0, tiled=False)
+    return jnp.sum(pieces.astype(jnp.float32), axis=0)
 
 
 def rope_tables(positions, head_dim):
@@ -122,6 +134,8 @@
     key_block = math.gcd(seq_len, 512)
     key_steps = seq_len // key_block
     within = jnp.arange(BLOCK, dtype=jnp.int32)
+    next_grad_in = passed_along_2(section_grad_in, "pipe", -1)
+    next_weight = lax.all_gather(passed_along_2(in_weight, "pipe", -1), "ctx", axis=0, tiled=True)
     out_grad = jnp.dot(
         section_grad_in,
         lax.all_gather(out_weight, "ctx", axis=0, tiled=True),
@@ -129,7 +143,7 @@
     ).astype(jnp.bfloat16)
     local_out_grad = seq_to_stored(out_grad, block_order, device, ctx_size, per_device)
     query_positions = (block_order[:, None] * BLOCK + within[None, :]).reshape(-1)
-    gathered = lax.all_gather(stored_keyval, "ctx", axis=0, tiled=True)
+    gathered = gathered_rows(stored_keyval, "ctx")
     slot_ids = jnp.arange(block_count, dtype=jnp.int32)
     inverse = jnp.sum(
         jnp.where(block_order[None, :] == slot_ids[:, None], slot_ids[None, :], 0), axis=1
@@ -200,12 +214,9 @@
         grad_step, jnp.zeros((flat_rows, head_dim), jnp.float32), key_blocks
     )
     own_positions = first_row + jnp.arange(local_rows, dtype=jnp.int32)
-    keyval_grad = lax.psum_scatter(
-        key_terms.reshape(seq_len, 2 * head_dim).astype(jnp.bfloat16),
-        "ctx",
-        scatter_dimension=0,
-        tiled=True,
-    ).astype(jnp.float32)
+    keyval_grad = summed_rows(
+        key_terms.reshape(seq_len, 2 * head_dim).astype(jnp.bfloat16), "ctx"
+    )
     query_grad = (
         unrotate(query_grad_rot, flat_pos)
         .reshape(local_rows, group * head_dim)
@@ -215,9 +226,9 @@
     key_grad = unrotate(keyval_grad[:, :head_dim], own_positions).astype(jnp.bfloat16)
     value_grad = keyval_grad[:, head_dim:].astype(jnp.bfloat16)
     qkv_grad = jnp.concatenate([query_grad, key_grad, value_grad], axis=1)
-    projected = contract_cols(qkv_grad, lax.all_gather(in_weight, "ctx", axis=0, tiled=True))
-    section_grad = (section_grad_in.astype(jnp.float32) + projected).astype(jnp.bfloat16)
-    passed = passed_along_2(section_grad, "pipe", -1)
+    next_qkv_grad = passed_along_2(qkv_grad, "pipe", -1)
+    projected = contract_cols(next_qkv_grad, next_weight)
+    passed = (next_grad_in.astype(jnp.float32) + projected).astype(jnp.bfloat16)
     return passed[None]
 
 

time: 425 us -> 261 us (0.61)
  waiting for transfers between devices: 269 us -> 91.4 us
  starting transfers between devices: 8.38 us -> 28.2 us
  local copies, waits for them, and re-layouts: 49.3 us -> 44.7 us
    all_gather x2 -> x1, waiting for transfers between devices: 132 us -> 0.01 us  [body(): lax.all_gather(passed_along_2(in_weight, 'pipe', -1), 'ctx', axis=0, tile...]
    reduce_scatter x1 -> x0, waiting for transfers between devices: 63 us -> none  [body(): lax.psum_scatter(key_terms.reshape(seq_len, 2 * head_dim).astype(jnp.bflo...]
    ppermute x1 -> x3, waiting for transfers between devices: 47.5 us -> 66.8 us  [passed_along_2(): return lax.ppermute(value, axis, pairs)]
    all_gather x1, waiting for transfers between devices: 18.4 us -> 0.01 us  [body(): lax.all_gather(out_weight, 'ctx', axis=0, tiled=True)]
    ppermute x2, waiting for transfers between devices: 5.6 us -> 21.5 us  [passed_along(): return lax.ppermute(value, axis, pairs)]
    all_to_all x0 -> x2, starting transfers between devices: none -> 15 us  [the longest x1 7.72 us: gathered_rows(): lax.all_to_all(spread, axis, 0, 0, tiled=False)]
  transfers between devices with their start and end apart: 7 -> 9, of which waited for: 7 -> 5; matrix products, arithmetic and copies ran while one was open for 13% -> 38% of each run, Pallas kernels for 0% -> 0%
where the time goes in v1:
time: 261 us; the launch traced here: 260 us
  waiting for transfers between devices  91.4 us (35%)
  matrix products  68.4 us (26%)
  local copies, waits for them, and re-layouts  44.7 us (17%)
  starting transfers between devices  28.2 us (11%)
  between operations  15.1 us (6%)
  other arithmetic  10.4 us (4%)
    ppermute x3, waiting for transfers between devices, passed_along_2(): return lax.ppermute(value, axis, pairs)  66.8 us
    dot_general x25, matrix products, contract_cols(): lax.dot_general(left_rows, right_rows, (((1,), (1,)), ((), ())), preferre...  29.1 us
    ppermute x2, waiting for transfers between devices, passed_along(): return lax.ppermute(value, axis, pairs)  21.5 us
    dot_general x8, matrix products, running_total(): jnp.dot(weights, value_wide, precision=lax.Precision.HIGHEST)  19.2 us
    squeeze x16, local copies, waits for them, and re-layouts, body(): lax.scan(running_total, start_carry, key_blocks)  15.6 us
    while x40, local copies, waits for them, and re-layouts  9.29 us
    all_to_all x1, starting transfers between devices, gathered_rows(): lax.all_to_all(spread, axis, 0, 0, tiled=False)  7.72 us
    dot_general x16, matrix products, contract_rows(): lax.dot_general(left_rows, right_rows, (((0,), (0,)), ((), ())), preferre...  7.65 us
  transfers between devices with their start and end apart: 9, of which 5 were waited for; matrix products, arithmetic and copies ran while one was open for 38% of the time, Pallas kernels for 0%

profile of v1, /device:TPU:1, one launch (start us, length us, event | category | flops | bytes accessed | tf_op | source)
XLA Modules:
  0.0 259.7 jit_solution(5328568877455341310)
XLA Ops:
  7.3 2.5 broadcast_in_dim.80
  9.7 7.7 %all-to-all-start = ((bf16[16,256,256]{2,1,0:T(8,128)(2,1)}), bf16[16,256,256]{2,1,0:T(8,128)(2,1)S(1)}, u32[]{:S(2)}, u32[]{:S(2)}) async-start(bf16[16,256,256]{2,1,0:T(8,128)(2,1)} %broadcast_in_dim.80), calls=%async_computation | async-start | bytes 4194304 | tf_op jit(solution)/shard_map/all_to_all | solution.py:30
  17.5 2.9 %collective-permute-start = (bf16[256,8192]{1,0:T(8,128)(2,1)}, bf16[256,8192]{1,0:T(8,128)(2,1)}, u32[]{:S(2)}, u32[]{:S(2)}) collective-permute-start(bf16[256,8192]{1,0:T(8,128)(2,1)} %bitcast.130), channel_id=1, source_target_pairs={{16,0},{32,16},{48,32},{64,48},{80,64},{96,80},{112,96},{17,1},{33... | collective-permute-start | bytes 12582920 | tf_op jit(solution)/shard_map/ppermute | solution.py:24
  20.4 1.9 collective-permute-start.4
  25.2 51.9 %collective-permute-done.4 = bf16[512,768]{1,0:T(8,128)(2,1)} collective-permute-done((bf16[512,768]{1,0:T(8,128)(2,1)}, bf16[512,768]{1,0:T(8,128)(2,1)}, u32[]{:S(2)}, u32[]{:S(2)}) %collective-permute-start.4) | collective-permute-done | bytes 786464 | tf_op jit(solution)/shard_map/ppermute | solution.py:24
  77.1 2.0 gather_fusion
  79.2 50.5 %while.28 = (s32[]{:T(128)}, f32[1024]{0:T(1024)S(1)}, f32[1024]{0:T(1024)S(1)}, f32[1024,128]{1,0:T(8,128)}, s32[8,512]{1,0:T(8,128)S(1)}, /*index=5*/s32[8,512...) while((s32[]{:T(128)}, f32[1024]{0:T(1024)S(1)}, ...), condition=%wide.region_7.8_spmd.clone, body=%wide.region_4.7_spmd.clone.sunk | while | flops 949883904 | bytes 12720321 | solution.py:191
  79.2 1.0 dynamic-slice_bitcast_fusion.6
  82.3 2.4 convolution_add_fusion.4
  84.7 0.8 copy-done.1
  85.5 1.0 dynamic-slice_bitcast_fusion.6
  88.6 2.4 convolution_add_fusion.4
  91.0 0.8 copy-done.1
  91.8 1.0 dynamic-slice_bitcast_fusion.6
  94.9 2.4 convolution_add_fusion.4
  98.1 1.0 dynamic-slice_bitcast_fusion.6
  101.2 2.4 convolution_add_fusion.4
  103.6 0.8 copy-done.1
  104.4 1.0 dynamic-slice_bitcast_fusion.6
  107.5 2.4 convolution_add_fusion.4
  109.9 0.8 copy-done.1
  110.7 1.0 dynamic-slice_bitcast_fusion.6
  113.8 2.4 convolution_add_fusion.4
  116.3 0.8 copy-done.1
  117.1 1.0 dynamic-slice_bitcast_fusion.6
  120.2 2.4 convolution_add_fusion.4
  123.4 1.0 dynamic-slice_bitcast_fusion.6
  126.5 2.4 convolution_add_fusion.4
  129.7 7.0 %fusion.35 = bf16[256,512]{1,0:T(8,128)(2,1)S(1)} fusion(bf16[1,8192,512]{2,1,0:T(8,128)(2,1)} %all-gather.6.cloned.1.call-done, bf16[1,256,8192]{2,1,0:T(8,128)(2,1)} %param.11), kind=kOutput, calls=%fused_computation.53 | convolution fusion | flops 2147614720 | bytes 12845056 | tf_op jit(solution)/shard_map/dot_general | solution.py:139
  136.7 3.3 %collective-permute-start.1 = (bf16[128,512]{1,0:T(8,128)(2,1)S(1)}, bf16[128,512]{1,0:T(8,128)(2,1)S(1)}, u32[]{:S(2)}, u32[]{:S(2)}) collective-permute-start(bf16[128,512]{1,0:T(8,128)(2,1)S(1)} %get-tuple-element.272), channel_id=1, source_target_pairs={{0,8},{1,9},{2,10},{3,11},{4,12},{5,13},{6,14},{7,15},{8,0},{9,1},... | collective-permute-start | bytes 393224 | tf_op jit(solution)/shard_map/ppermute | solution.py:18
  140.0 4.6 %collective-permute-done.1 = bf16[128,512]{1,0:T(8,128)(2,1)S(1)} collective-permute-done((bf16[128,512]{1,0:T(8,128)(2,1)S(1)}, bf16[128,512]{1,0:T(8,128)(2,1)S(1)}, u32[]{:S(2)}, u32[]{:S(2)}) %collective-permute-start.1) | collective-permute-done | bytes 131104 | tf_op jit(solution)/shard_map/ppermute | solution.py:18
  145.2 40.9 %while.29 = (s32[]{:T(128)}, f32[1024,128]{1,0:T(8,128)S(1)}, bf16[8,512,256]{2,1,0:T(8,128)(2,1)}, s32[8,512]{1,0:T(8,128)S(1)}, s32[8,512]{1,0:T(8,128)S(1)}, ...) while((s32[]{:T(128)}, f32[1024,128]{1,0:T(8,128)S(1)}, ...), condition=%wide.region_10.11_spmd.clone, body=%wide.region_9.10_spmd.clone.sunk | while | flops 677642240 | bytes 14342807 | solution.py:213
  145.2 1.0 dynamic-slice_bitcast_fusion.7
  150.4 1.0 dynamic-slice_bitcast_fusion.7
  155.5 1.0 dynamic-slice_bitcast_fusion.7
  160.6 1.0 dynamic-slice_bitcast_fusion.7
  165.7 1.0 dynamic-slice_bitcast_fusion.7
  170.8 1.0 dynamic-slice_bitcast_fusion.7
  175.9 1.0 dynamic-slice_bitcast_fusion.7
  181.0 1.0 dynamic-slice_bitcast_fusion.7
  186.1 7.3 %all-to-all-start.1 = ((bf16[16,256,256]{2,1,0:T(8,128)(2,1)}), bf16[16,256,256]{2,1,0:T(8,128)(2,1)S(1)}, u32[]{:S(2)}, u32[]{:S(2)}) async-start(bf16[16,256,256]{2,1,0:T(8,128)(2,1)} %bitcast.116), calls=%async_computation.1 | async-start | bytes 4194304 | tf_op jit(solution)/shard_map/all_to_all | solution.py:35
  194.0 2.4 fusion.39
  196.5 3.1 %collective-permute-start.2 = (bf16[128,512]{1,0:T(8,128)(2,1)S(1)}, bf16[128,512]{1,0:T(8,128)(2,1)S(1)}, u32[]{:S(2)}, u32[]{:S(2)}) collective-permute-start(bf16[128,512]{1,0:T(8,128)(2,1)S(1)} %slice.59), channel_id=1, source_target_pairs={{0,8},{1,9},{2,10},{3,11},{4,12},{5,13},{6,14},{7,15},{8,0},{9,1},... | collective-permute-start | bytes 393224 | tf_op jit(solution)/shard_map/ppermute | solution.py:18
  199.9 16.9 %collective-permute-done.2 = bf16[128,512]{1,0:T(8,128)(2,1)S(1)} collective-permute-done((bf16[128,512]{1,0:T(8,128)(2,1)S(1)}, bf16[128,512]{1,0:T(8,128)(2,1)S(1)}, u32[]{:S(2)}, u32[]{:S(2)}) %collective-permute-start.2) | collective-permute-done | bytes 131104 | tf_op jit(solution)/shard_map/ppermute | solution.py:18
  217.8 2.4 all-to-all-done.1
  221.2 1.9 collective-permute-start.3
  223.2 14.9 %collective-permute-done.3 = bf16[256,768]{1,0:T(8,128)(2,1)S(1)} collective-permute-done((bf16[256,768]{1,0:T(8,128)(2,1)S(1)}, bf16[256,768]{1,0:T(8,128)(2,1)S(1)}, u32[]{:S(2)}, u32[]{:S(2)}) %collective-permute-start.3) | collective-permute-done | bytes 393248 | tf_op jit(solution)/shard_map/ppermute | solution.py:24
  238.1 14.8 %fusion.34 = bf16[1,256,8192]{2,1,0:T(8,128)(2,1)} fusion(bf16[256,8192]{1,0:T(8,128)(2,1)} %collective-permute-done, bf16[256,768]{1,0:T(8,128)(2,1)S(1)} %collective-permute-done.3, bf16[8192,768]{1,0:T(8,128)(2,1)} %all-gather.4.cloned.1.call-done), kind=kOutput, calls=%fused_computation.50 | convolution fusion | flops 3227516928 | bytes 21364736 | tf_op jit(solution)/shard_map/dot_general | solution.py:105
  (270 shorter events, 56.9 us)
Async XLA Ops:
  6.5 123.1 %all-gather.6.cloned.1.call-start = ((), (), s32[]{:S(2)}) async-start(), calls=%async_computation.3 | async-start | bytes 8912896 | tf_op jit(solution)/shard_map/all_gather | solution.py:141
  9.7 12.6 %copy-start.4 = (s32[1,32]{1,0:T(1,128)S(1)}, s32[1,32]{1,0:T(1,128)}, u32[]{:S(2)}) copy-start(s32[1,32]{1,0:T(1,128)} %param.17) | copy-start | bytes 388
  9.7 14.6 %copy-start.5 = (s32[1,8]{1,0:T(1,128)S(1)}, s32[1,8]{1,0:T(1,128)}, u32[]{:S(2)}) copy-start(s32[1,8]{1,0:T(1,128)} %param.16) | copy-start | bytes 100
  9.7 14.9 %copy-start.3 = (bf16[1,256,512]{2,1,0:T(8,128)(2,1)S(1)}, bf16[1,256,512]{2,1,0:T(8,128)(2,1)}, u32[]{:S(2)}) copy-start(bf16[1,256,512]{2,1,0:T(8,128)(2,1)} %param.12) | copy-start | bytes 786436
  9.7 67.4 %all-to-all-start = ((bf16[16,256,256]{2,1,0:T(8,128)(2,1)}), bf16[16,256,256]{2,1,0:T(8,128)(2,1)S(1)}, u32[]{:S(2)}, u32[]{:S(2)}) async-start(bf16[16,256,256]{2,1,0:T(8,128)(2,1)} %broadcast_in_dim.80), calls=%async_computation | async-start | bytes 4194304 | tf_op jit(solution)/shard_map/all_to_all | solution.py:30
  17.5 220.6 %all-gather.4.cloned.1.call-start = ((), (), s32[]{:S(2)}) async-start(), calls=%async_computation.2 | async-start | bytes 13369344 | tf_op jit(solution)/shard_map/all_gather | solution.py:138
  17.5 205.6 %collective-permute-start = (bf16[256,8192]{1,0:T(8,128)(2,1)}, bf16[256,8192]{1,0:T(8,128)(2,1)}, u32[]{:S(2)}, u32[]{:S(2)}) collective-permute-start(bf16[256,8192]{1,0:T(8,128)(2,1)} %bitcast.130), channel_id=1, source_target_pairs={{16,0},{32,16},{48,32},{64,48},{80,64},{96,80},{112,96},{17,1},{33... | collective-permute-start | bytes 12582920 | tf_op jit(solution)/shard_map/ppermute | solution.py:24
  20.4 56.7 %collective-permute-start.4 = (bf16[512,768]{1,0:T(8,128)(2,1)}, bf16[512,768]{1,0:T(8,128)(2,1)}, u32[]{:S(2)}, u32[]{:S(2)}) collective-permute-start(bf16[512,768]{1,0:T(8,128)(2,1)} %bitcast.22), channel_id=1, source_target_pairs={{16,0},{32,16},{48,32},{64,48},{80,64},{96,80},{112,96},{17,1},{33... | collective-permute-start | bytes 2359304 | tf_op jit(solution)/shard_map/ppermute | solution.py:24
  81.2 1.1 copy-start
  84.7 0.8 copy-start.1
  87.6 1.0 copy-start
  91.0 0.8 copy-start.1
  93.9 1.0 copy-start
  97.3 0.8 copy-start.1
  100.2 1.0 copy-start
  103.6 0.8 copy-start.1
  106.5 1.0 copy-start
  109.9 0.8 copy-start.1
  112.8 1.1 copy-start
  116.2 0.8 copy-start.1
  119.1 1.1 copy-start
  122.6 0.8 copy-start.1
  125.4 1.0 copy-start
  128.9 0.8 copy-start.1
  129.7 15.2 %copy-start.2 = (f32[1024,128]{1,0:T(8,128)S(1)}, f32[1024,128]{1,0:T(8,128)}, u32[]{:S(2)}) copy-start(f32[1024,128]{1,0:T(8,128)} %get-tuple-element.124) | copy-start | bytes 1572868
  136.7 7.9 %collective-permute-start.1 = (bf16[128,512]{1,0:T(8,128)(2,1)S(1)}, bf16[128,512]{1,0:T(8,128)(2,1)S(1)}, u32[]{:S(2)}, u32[]{:S(2)}) collective-permute-start(bf16[128,512]{1,0:T(8,128)(2,1)S(1)} %get-tuple-element.272), channel_id=1, source_target_pairs={{0,8},{1,9},{2,10},{3,11},{4,12},{5,13},{6,14},{7,15},{8,0},{9,1},... | collective-permute-start | bytes 393224 | tf_op jit(solution)/shard_map/ppermute | solution.py:18
  186.1 34.1 %all-to-all-start.1 = ((bf16[16,256,256]{2,1,0:T(8,128)(2,1)}), bf16[16,256,256]{2,1,0:T(8,128)(2,1)S(1)}, u32[]{:S(2)}, u32[]{:S(2)}) async-start(bf16[16,256,256]{2,1,0:T(8,128)(2,1)} %bitcast.116), calls=%async_computation.1 | async-start | bytes 4194304 | tf_op jit(solution)/shard_map/all_to_all | solution.py:35
  196.5 20.3 %collective-permute-start.2 = (bf16[128,512]{1,0:T(8,128)(2,1)S(1)}, bf16[128,512]{1,0:T(8,128)(2,1)S(1)}, u32[]{:S(2)}, u32[]{:S(2)}) collective-permute-start(bf16[128,512]{1,0:T(8,128)(2,1)S(1)} %slice.59), channel_id=1, source_target_pairs={{0,8},{1,9},{2,10},{3,11},{4,12},{5,13},{6,14},{7,15},{8,0},{9,1},... | collective-permute-start | bytes 393224 | tf_op jit(solution)/shard_map/ppermute | solution.py:18
  221.2 16.8 %collective-permute-start.3 = (bf16[256,768]{1,0:T(8,128)(2,1)S(1)}, bf16[256,768]{1,0:T(8,128)(2,1)S(1)}, u32[]{:S(2)}, u32[]{:S(2)}) collective-permute-start(bf16[256,768]{1,0:T(8,128)(2,1)S(1)} %pad_maximum_fusion.1), channel_id=1, source_target_pairs={{16,0},{32,16},{48,32},{64,48},{80,64},{96,80},{112,96},{17,1},{33... | collective-permute-start | bytes 1179656 | tf_op jit(solution)/shard_map/ppermute | solution.py:24
Sparse Core Ops, SparseCore 0:
  9.5 90.3 all-gather.5
  102.0 115.4 all-gather.3

commit v2 on v1

--- a/solution.py
+++ b/solution.py
@@ -134,8 +134,9 @@
     key_block = math.gcd(seq_len, 512)
     key_steps = seq_len // key_block
     within = jnp.arange(BLOCK, dtype=jnp.int32)
+    query_width = stored_query.shape[1]
+    next_shard = passed_along_2(in_weight, "pipe", -1)
     next_grad_in = passed_along_2(section_grad_in, "pipe", -1)
-    next_weight = lax.all_gather(passed_along_2(in_weight, "pipe", -1), "ctx", axis=0, tiled=True)
     out_grad = jnp.dot(
         section_grad_in,
         lax.all_gather(out_weight, "ctx", axis=0, tiled=True),
@@ -189,6 +190,8 @@
         jnp.zeros((flat_rows, head_dim), jnp.float32),
     )
     (row_top, row_total, weighted), unused = lax.scan(running_total, start_carry, key_blocks)
+    next_shard, weighted = lax.optimization_barrier((next_shard, weighted))
+    next_weight = lax.all_gather(next_shard, "ctx", axis=0, tiled=True)
     log_total = row_top + jnp.log(row_total)
     attn_out = weighted / row_total[:, None]
     row_delta = jnp.sum(flat_grad.astype(jnp.float32) * attn_out, axis=1)
@@ -214,21 +217,26 @@
         grad_step, jnp.zeros((flat_rows, head_dim), jnp.float32), key_blocks
     )
     own_positions = first_row + jnp.arange(local_rows, dtype=jnp.int32)
-    keyval_grad = summed_rows(
-        key_terms.reshape(seq_len, 2 * head_dim).astype(jnp.bfloat16), "ctx"
-    )
     query_grad = (
         unrotate(query_grad_rot, flat_pos)
         .reshape(local_rows, group * head_dim)
         .astype(jnp.bfloat16)
     )
     query_grad = stored_to_seq(query_grad, block_order, device, ctx_size, per_device)
+    next_query_grad = passed_along_2(query_grad, "pipe", -1)
+    partial = lax.optimization_barrier(
+        next_grad_in.astype(jnp.float32)
+        + contract_cols(next_query_grad, next_weight[:, :query_width])
+    )
+    keyval_grad = summed_rows(
+        key_terms.reshape(seq_len, 2 * head_dim).astype(jnp.bfloat16), "ctx"
+    )
     key_grad = unrotate(keyval_grad[:, :head_dim], own_positions).astype(jnp.bfloat16)
     value_grad = keyval_grad[:, head_dim:].astype(jnp.bfloat16)
-    qkv_grad = jnp.concatenate([query_grad, key_grad, value_grad], axis=1)
-    next_qkv_grad = passed_along_2(qkv_grad, "pipe", -1)
-    projected = contract_cols(next_qkv_grad, next_weight)
-    passed = (next_grad_in.astype(jnp.float32) + projected).astype(jnp.bfloat16)
+    next_keyval_grad = passed_along_2(
+        jnp.concatenate([key_grad, value_grad], axis=1), "pipe", -1
+    )
+    passed = (partial + contract_cols(next_keyval_grad, next_weight[:, query_width:])).astype(jnp.bfloat16)
     return passed[None]
 
 

time: 261 us -> 292 us (1.12); the launches traced: 260 us -> 288 us
  waiting for transfers between devices: 91.4 us -> 63 us
  matrix products: 68.4 us -> 94.7 us
  local copies, waits for them, and re-layouts: 44.7 us -> 62.9 us
  other arithmetic: 10.4 us -> 22.6 us
    ppermute x3 -> x4, waiting for transfers between devices: 66.8 us -> 0.01 us  [passed_along_2(): return lax.ppermute(value, axis, pairs)]
    all_to_all x1, waiting for transfers between devices: 0.01 us -> 30.1 us  [gathered_rows(): lax.all_to_all(spread, axis, 0, 0, tiled=False)]
    dot_general x25 -> x26, matrix products: 29.1 us -> 46.7 us  [contract_cols(): lax.dot_general(left_rows, right_rows, (((1,), (1,)), ((), ())), preferre...]
    dynamic_slice x16, local copies, waits for them, and re-layouts: 0.16 us -> 16.6 us  [body(): lax.scan(running_total, start_carry, key_blocks)]
    squeeze x16, local copies, waits for them, and re-layouts: 15.6 us -> 0.42 us  [body(): lax.scan(running_total, start_carry, key_blocks)]
    broadcast_in_dim x17, local copies, waits for them, and re-layouts: 1.5 us -> 12.4 us  [body(): flat_pos = jnp.repeat(query_pos, group)]
    broadcast_in_dim x16, local copies, waits for them, and re-layouts: 1.41 us -> 11.1 us  [body(): flat_doc = jnp.repeat(query_doc, group)]
    while x40 -> x56, local copies, waits for them, and re-layouts: 9.29 us -> 0.14 us
  transfers between devices with their start and end apart: 9 -> 10, of which waited for: 5 -> 4; matrix products, arithmetic and copies ran while one was open for 38% -> 56% of each run, Pallas kernels for 0% -> 0%
where the time goes in v2:
time: 292 us; the launch traced here: 288 us
  matrix products  94.7 us (32%)
  waiting for transfers between devices  63 us (22%)
  local copies, waits for them, and re-layouts  62.9 us (22%)
  starting transfers between devices  27.5 us (9%)
  other arithmetic  22.6 us (8%)
  between operations  15.2 us (5%)
    dot_general x26, matrix products, contract_cols(): lax.dot_general(left_rows, right_rows, (((1,), (1,)), ((), ())), preferre...  46.7 us
    all_to_all x1, waiting for transfers between devices, gathered_rows(): lax.all_to_all(spread, axis, 0, 0, tiled=False)  30.1 us
    ppermute x2, waiting for transfers between devices, passed_along(): return lax.ppermute(value, axis, pairs)  28.6 us
    dot_general x8, matrix products, running_total(): jnp.dot(weights, value_wide, precision=lax.Precision.HIGHEST)  19.3 us
    dynamic_slice x16, local copies, waits for them, and re-layouts, body(): lax.scan(running_total, start_carry, key_blocks)  16.6 us
    dot_general x16, matrix products, contract_rows(): lax.dot_general(left_rows, right_rows, (((0,), (0,)), ((), ())), preferre...  15.4 us
    ppermute x4, starting transfers between devices, passed_along_2(): return lax.ppermute(value, axis, pairs)  12.7 us
    broadcast_in_dim x17, local copies, waits for them, and re-layouts, body(): flat_pos = jnp.repeat(query_pos, group)  12.4 us
  transfers between devices with their start and end apart: 10, of which 4 were waited for; matrix products, arithmetic and copies ran while one was open for 56% of the time, Pallas kernels for 0%

profile of v2, /device:TPU:1, one launch (start us, length us, event | category | flops | bytes accessed | tf_op | source)
XLA Modules:
  0.0 287.7 jit_solution(11763000874161703508)
XLA Ops:
  7.3 2.4 broadcast_in_dim.80
  9.7 7.7 %all-to-all-start = ((bf16[16,256,256]{2,1,0:T(8,128)(2,1)}), bf16[16,256,256]{2,1,0:T(8,128)(2,1)S(1)}, u32[]{:S(2)}, u32[]{:S(2)}) async-start(bf16[16,256,256]{2,1,0:T(8,128)(2,1)} %broadcast_in_dim.80), calls=%async_computation | async-start | bytes 4194304 | tf_op jit(solution)/shard_map/all_to_all | solution.py:30
  17.5 2.9 collective-permute-start.2
  21.3 1.8 reshape_squeeze.3
  25.9 30.1 %all-to-all-done = bf16[16,256,256]{2,1,0:T(8,128)(2,1)S(1)} async-done(((bf16[16,256,256]{2,1,0:T(8,128)(2,1)}), bf16[16,256,256]{2,1,0:T(8,128)(2,1)S(1)}, u32[]{:S(2)}, u32[]{:S(2)}) %all-to-all-start) | async-done | bytes 2097184 | tf_op jit(solution)/shard_map/all_to_all | solution.py:30
  57.4 2.3 gather_fusion
  59.6 62.9 %while.28 = (s32[]{:T(128)}, f32[1024]{0:T(1024)S(1)}, f32[1024]{0:T(1024)}, f32[1024,128]{1,0:T(8,128)S(1)}, s32[8,512]{1,0:T(8,128)}, /*index=5*/s32[8,512]{1,...) while((s32[]{:T(128)}, f32[1024]{0:T(1024)S(1)}, ...), condition=%wide.region_7.8_spmd.clone, body=%wide.region_4.7_spmd.clone.sunk | while | flops 949883904 | bytes 8567013 | solution.py:192
  62.8 1.6 fusion.86
  65.1 2.4 convolution_add_fusion.4
  70.7 1.6 fusion.86
  73.0 2.4 convolution_add_fusion.4
  78.5 1.6 fusion.86
  80.8 2.4 convolution_add_fusion.4
  86.4 1.6 fusion.86
  88.7 2.4 convolution_add_fusion.4
  94.3 1.6 fusion.86
  96.6 2.4 convolution_add_fusion.4
  102.1 1.6 fusion.86
  104.4 2.4 convolution_add_fusion.4
  110.0 1.6 fusion.86
  112.3 2.4 convolution_add_fusion.4
  117.8 1.6 fusion.86
  120.1 2.4 convolution_add_fusion.4
  123.6 3.9 %collective-permute-start = (bf16[256,8192]{1,0:T(8,128)(2,1)}, bf16[256,8192]{1,0:T(8,128)(2,1)}, u32[]{:S(2)}, u32[]{:S(2)}) collective-permute-start(bf16[256,8192]{1,0:T(8,128)(2,1)} %bitcast.131), channel_id=1, source_target_pairs={{16,0},{32,16},{48,32},{64,48},{80,64},{96,80},{112,96},{17,1},{33... | collective-permute-start | bytes 12582920 | tf_op jit(solution)/shard_map/ppermute | solution.py:24
  130.4 7.8 %fusion.39 = bf16[256,512]{1,0:T(8,128)(2,1)S(1)} fusion(bf16[1,8192,512]{2,1,0:T(8,128)(2,1)} %all-gather.6.cloned.1.call-done, bf16[1,256,8192]{2,1,0:T(8,128)(2,1)} %param.11), kind=kOutput, calls=%fused_computation.58 | convolution fusion | flops 2147614720 | bytes 12845056 | tf_op jit(solution)/shard_map/dot_general | solution.py:140
  138.4 9.0 %collective-permute-done.1 = bf16[128,512]{1,0:T(8,128)(2,1)S(1)} collective-permute-done((bf16[128,512]{1,0:T(8,128)(2,1)S(1)}, bf16[128,512]{1,0:T(8,128)(2,1)S(1)}, u32[]{:S(2)}, u32[]{:S(2)}) %collective-permute-start.1) | collective-permute-done | bytes 131104 | tf_op jit(solution)/shard_map/ppermute | solution.py:18
  148.9 64.6 %while.29 = (s32[]{:T(128)}, f32[1024,128]{1,0:T(8,128)S(1)}, bf16[8,512,256]{2,1,0:T(8,128)(2,1)}, s32[8,512]{1,0:T(8,128)}, s32[8,512]{1,0:T(8,128)}, /*index=...) while((s32[]{:T(128)}, f32[1024,128]{1,0:T(8,128)S(1)}, ...), condition=%wide.region_10.11_spmd.clone, body=%wide.region_9.10_spmd.clone.sunk | while | flops 677642240 | bytes 14342307 | solution.py:216
  151.5 1.7 bitcast_select_fusion.3
  159.5 1.7 bitcast_select_fusion.3
  162.1 1.5 fusion.101
  167.6 1.7 bitcast_select_fusion.3
  170.3 1.4 fusion.101
  175.7 1.7 bitcast_select_fusion.3
  183.8 1.7 bitcast_select_fusion.3
  186.4 1.4 fusion.101
  191.9 1.7 bitcast_select_fusion.3
  199.9 1.7 bitcast_select_fusion.3
  208.0 1.7 bitcast_select_fusion.3
  213.5 3.9 %all-to-all-start.1 = ((bf16[16,256,256]{2,1,0:T(8,128)(2,1)}), bf16[16,256,256]{2,1,0:T(8,128)(2,1)S(1)}, u32[]{:S(2)}, u32[]{:S(2)}) async-start(bf16[16,256,256]{2,1,0:T(8,128)(2,1)} %bitcast.117), calls=%async_computation.1 | async-start | bytes 4194304 | tf_op jit(solution)/shard_map/all_to_all | solution.py:35
  218.1 2.4 fusion.43
  220.6 3.1 %collective-permute-start.3 = (bf16[128,512]{1,0:T(8,128)(2,1)S(1)}, bf16[128,512]{1,0:T(8,128)(2,1)S(1)}, u32[]{:S(2)}, u32[]{:S(2)}) collective-permute-start(bf16[128,512]{1,0:T(8,128)(2,1)S(1)} %slice.65), channel_id=1, source_target_pairs={{0,8},{1,9},{2,10},{3,11},{4,12},{5,13},{6,14},{7,15},{8,0},{9,1},... | collective-permute-start | bytes 393224 | tf_op jit(solution)/shard_map/ppermute | solution.py:18
  223.9 19.6 %collective-permute-done.3 = bf16[128,512]{1,0:T(8,128)(2,1)S(1)} collective-permute-done((bf16[128,512]{1,0:T(8,128)(2,1)S(1)}, bf16[128,512]{1,0:T(8,128)(2,1)S(1)}, u32[]{:S(2)}, u32[]{:S(2)}) %collective-permute-start.3) | collective-permute-done | bytes 131104 | tf_op jit(solution)/shard_map/ppermute | solution.py:18
  244.4 3.0 %collective-permute-start.4 = (bf16[256,512]{1,0:T(8,128)(2,1)S(1)}, bf16[256,512]{1,0:T(8,128)(2,1)S(1)}, u32[]{:S(2)}, u32[]{:S(2)}) collective-permute-start(bf16[256,512]{1,0:T(8,128)(2,1)S(1)} %bitcast.118), channel_id=1, source_target_pairs={{16,0},{32,16},{48,32},{64,48},{80,64},{96,80},{112,96},{17,1},{33... | collective-permute-start | bytes 786440 | tf_op jit(solution)/shard_map/ppermute | solution.py:24
  247.4 3.6 %all-to-all-done.1 = bf16[16,256,256]{2,1,0:T(8,128)(2,1)S(1)} async-done(((bf16[16,256,256]{2,1,0:T(8,128)(2,1)}), bf16[16,256,256]{2,1,0:T(8,128)(2,1)S(1)}, u32[]{:S(2)}, u32[]{:S(2)}) %all-to-all-start.1) | async-done | bytes 2097184 | tf_op jit(solution)/shard_map/all_to_all | solution.py:35
  252.0 3.0 %collective-permute-start.5 = (bf16[256,256]{1,0:T(8,128)(2,1)S(1)}, bf16[256,256]{1,0:T(8,128)(2,1)S(1)}, u32[]{:S(2)}, u32[]{:S(2)}) collective-permute-start(bf16[256,256]{1,0:T(8,128)(2,1)S(1)} %pad_maximum_fusion.5), channel_id=1, source_target_pairs={{16,0},{32,16},{48,32},{64,48},{80,64},{96,80},{112,96},{17,1},{33... | collective-permute-start | bytes 393224 | tf_op jit(solution)/shard_map/ppermute | solution.py:24
  255.0 10.2 %convert_add_fusion = f32[256,8192]{1,0:T(8,128)} fusion(bf16[256,8192]{1,0:T(8,128)(2,1)} %collective-permute-done, bf16[256,512]{1,0:T(8,128)(2,1)S(1)} %collective-permute-done.4, bf16[8192,768]{1,0:T(8,128)(2,1)} %all-gather.4.cloned.1.call-done), kind=kOutput, calls=%fused_computation.52 | convolution fusion | flops 2151677952 | bytes 21233664 | tf_op jit(solution)/shard_map/dot_general | solution.py:105
  265.2 6.9 %fusion.37 = f32[256,8192]{1,0:T(8,128)} fusion(bf16[256,256]{1,0:T(8,128)(2,1)S(1)} %collective-permute-done.5, bf16[8192,768]{1,0:T(8,128)(2,1)} %all-gather.4.cloned.1.call-done), kind=kOutput, calls=%fused_computation.54 | convolution fusion | flops 1073741824 | bytes 12713984 | tf_op jit(solution)/shard_map/dot_general | solution.py:105
  272.1 8.8 %fusion.36 = bf16[1,256,8192]{2,1,0:T(8,128)(2,1)} fusion(f32[256,8192]{1,0:T(8,128)} %convert_add_fusion, f32[256,8192]{1,0:T(8,128)} %fusion.37), kind=kLoop, calls=%fused_computation.53 | loop fusion | flops 4194304 | bytes 20971520 | tf_op jit(solution)/shard_map/broadcast_in_dim | solution.py:240
  (296 shorter events, 88.8 us)
Async XLA Ops:
  6.5 123.9 %all-gather.6.cloned.1.call-start = ((), (), s32[]{:S(2)}) async-start(), calls=%async_computation.3 | async-start | bytes 8912896 | tf_op jit(solution)/shard_map/all_gather | solution.py:142
  9.7 10.7 %copy-start.9 = (s32[1,8]{1,0:T(1,128)S(1)}, s32[1,8]{1,0:T(1,128)}, u32[]{:S(2)}) copy-start(s32[1,8]{1,0:T(1,128)} %param.16) | copy-start | bytes 100
  9.7 13.4 %copy-start.8 = (s32[1,32]{1,0:T(1,128)S(1)}, s32[1,32]{1,0:T(1,128)}, u32[]{:S(2)}) copy-start(s32[1,32]{1,0:T(1,128)} %param.17) | copy-start | bytes 388
  9.7 46.4 %all-to-all-start = ((bf16[16,256,256]{2,1,0:T(8,128)(2,1)}), bf16[16,256,256]{2,1,0:T(8,128)(2,1)S(1)}, u32[]{:S(2)}, u32[]{:S(2)}) async-start(bf16[16,256,256]{2,1,0:T(8,128)(2,1)} %broadcast_in_dim.80), calls=%async_computation | async-start | bytes 4194304 | tf_op jit(solution)/shard_map/all_to_all | solution.py:30
  17.4 237.6 %all-gather.4.cloned.1.call-start = ((), (), s32[]{:S(2)}) async-start(), calls=%async_computation.2 | async-start | bytes 13369344 | tf_op jit(solution)/shard_map/all_gather | solution.py:194
  17.5 105.1 %collective-permute-start.2 = (bf16[512,768]{1,0:T(8,128)(2,1)}, bf16[512,768]{1,0:T(8,128)(2,1)S(1)}, u32[]{:S(2)}, u32[]{:S(2)}) collective-permute-start(bf16[512,768]{1,0:T(8,128)(2,1)} %bitcast.132), channel_id=1, source_target_pairs={{16,0},{32,16},{48,32},{64,48},{80,64},{96,80},{112,96},{17,1},{33... | collective-permute-start | bytes 2359304 | tf_op jit(solution)/shard_map/ppermute | solution.py:24
  56.0 1.3 copy-start
  62.7 1.7 copy-start.3
  62.7 2.3 copy-start.4
  65.1 2.4 copy-start.5
  70.6 1.6 copy-start.3
  70.7 2.3 copy-start.4
  72.9 2.4 copy-start.5
  78.5 1.7 copy-start.3
  78.5 2.3 copy-start.4
  80.8 2.4 copy-start.5
  86.3 1.7 copy-start.3
  86.4 2.3 copy-start.4
  88.7 2.4 copy-start.5
  94.2 1.6 copy-start.3
  94.3 2.3 copy-start.4
  96.5 2.4 copy-start.5
  102.1 1.7 copy-start.3
  102.1 2.3 copy-start.4
  104.4 2.4 copy-start.5
  109.9 1.6 copy-start.3
  110.0 2.3 copy-start.4
  112.2 2.4 copy-start.5
  117.8 1.7 copy-start.3
  117.8 2.3 copy-start.4
  120.1 2.4 copy-start.5
  122.6 15.6 %copy-start.2 = (f32[1024,128]{1,0:T(8,128)}, f32[1024,128]{1,0:T(8,128)S(1)}, u32[]{:S(2)}) copy-start(f32[1024,128]{1,0:T(8,128)S(1)} %get-tuple-element.127) | copy-start | bytes 1572868
  122.6 1.0 copy-start.1
  123.6 131.3 %collective-permute-start = (bf16[256,8192]{1,0:T(8,128)(2,1)}, bf16[256,8192]{1,0:T(8,128)(2,1)}, u32[]{:S(2)}, u32[]{:S(2)}) collective-permute-start(bf16[256,8192]{1,0:T(8,128)(2,1)} %bitcast.131), channel_id=1, source_target_pairs={{16,0},{32,16},{48,32},{64,48},{80,64},{96,80},{112,96},{17,1},{33... | collective-permute-start | bytes 12582920 | tf_op jit(solution)/shard_map/ppermute | solution.py:24
  130.4 8.0 %copy-start.6 = (f32[1024]{0:T(1024)S(1)}, f32[1024]{0:T(1024)}, u32[]{:S(2)}) copy-start(f32[1024]{0:T(1024)} %get-tuple-element.125) | copy-start | bytes 12292
  138.2 9.1 %collective-permute-start.1 = (bf16[128,512]{1,0:T(8,128)(2,1)S(1)}, bf16[128,512]{1,0:T(8,128)(2,1)S(1)}, u32[]{:S(2)}, u32[]{:S(2)}) collective-permute-start(bf16[128,512]{1,0:T(8,128)(2,1)S(1)} %get-tuple-element.276), channel_id=1, source_target_pairs={{0,8},{1,9},{2,10},{3,11},{4,12},{5,13},{6,14},{7,15},{8,0},{9,1},... | collective-permute-start | bytes 393224 | tf_op jit(solution)/shard_map/ppermute | solution.py:18
  213.5 3.9 %copy-start.7 = (f32[256]{0:T(256)S(1)}, f32[256]{0:T(256)}, u32[]{:S(2)}) copy-start(f32[256]{0:T(256)} %get-tuple-element.261) | copy-start | bytes 3076
  213.5 37.4 %all-to-all-start.1 = ((bf16[16,256,256]{2,1,0:T(8,128)(2,1)}), bf16[16,256,256]{2,1,0:T(8,128)(2,1)S(1)}, u32[]{:S(2)}, u32[]{:S(2)}) async-start(bf16[16,256,256]{2,1,0:T(8,128)(2,1)} %bitcast.117), calls=%async_computation.1 | async-start | bytes 4194304 | tf_op jit(solution)/shard_map/all_to_all | solution.py:35
  220.6 22.9 %collective-permute-start.3 = (bf16[128,512]{1,0:T(8,128)(2,1)S(1)}, bf16[128,512]{1,0:T(8,128)(2,1)S(1)}, u32[]{:S(2)}, u32[]{:S(2)}) collective-permute-start(bf16[128,512]{1,0:T(8,128)(2,1)S(1)} %slice.65), channel_id=1, source_target_pairs={{0,8},{1,9},{2,10},{3,11},{4,12},{5,13},{6,14},{7,15},{8,0},{9,1},... | collective-permute-start | bytes 393224 | tf_op jit(solution)/shard_map/ppermute | solution.py:18
  244.4 10.5 %collective-permute-start.4 = (bf16[256,512]{1,0:T(8,128)(2,1)S(1)}, bf16[256,512]{1,0:T(8,128)(2,1)S(1)}, u32[]{:S(2)}, u32[]{:S(2)}) collective-permute-start(bf16[256,512]{1,0:T(8,128)(2,1)S(1)} %bitcast.118), channel_id=1, source_target_pairs={{16,0},{32,16},{48,32},{64,48},{80,64},{96,80},{112,96},{17,1},{33... | collective-permute-start | bytes 786440 | tf_op jit(solution)/shard_map/ppermute | solution.py:24
  252.0 13.2 %collective-permute-start.5 = (bf16[256,256]{1,0:T(8,128)(2,1)S(1)}, bf16[256,256]{1,0:T(8,128)(2,1)S(1)}, u32[]{:S(2)}, u32[]{:S(2)}) collective-permute-start(bf16[256,256]{1,0:T(8,128)(2,1)S(1)} %pad_maximum_fusion.5), channel_id=1, source_target_pairs={{16,0},{32,16},{48,32},{64,48},{80,64},{96,80},{112,96},{17,1},{33... | collective-permute-start | bytes 393224 | tf_op jit(solution)/shard_map/ppermute | solution.py:24
Sparse Core Ops, SparseCore 0:
  9.5 90.2 all-gather.5
  123.7 91.2 all-gather.3

commit v3 on v1

--- a/solution.py
+++ b/solution.py
@@ -141,8 +141,8 @@
         lax.all_gather(out_weight, "ctx", axis=0, tiled=True),
         preferred_element_type=jnp.float32,
     ).astype(jnp.bfloat16)
-    local_out_grad = seq_to_stored(out_grad, block_order, device, ctx_size, per_device)
-    query_positions = (block_order[:, None] * BLOCK + within[None, :]).reshape(-1)
+    local_out_grad = out_grad
+    seq_query = stored_to_seq(stored_query, block_order, device, ctx_size, per_device)
     gathered = gathered_rows(stored_keyval, "ctx")
     slot_ids = jnp.arange(block_count, dtype=jnp.int32)
     inverse = jnp.sum(
@@ -153,10 +153,10 @@
     )
     key_positions = jnp.arange(seq_len, dtype=jnp.int32)
     key_docs = doc_ids(key_positions, lengths)
-    query_pos = lax.dynamic_slice_in_dim(query_positions, first_row, local_rows)
+    query_pos = first_row + jnp.arange(local_rows, dtype=jnp.int32)
     query_doc = doc_ids(query_pos, lengths)
     flat_rows = local_rows * group
-    flat_query = stored_query.reshape(flat_rows, head_dim)
+    flat_query = seq_query.reshape(flat_rows, head_dim)
     flat_grad = local_out_grad.reshape(flat_rows, head_dim)
     flat_pos = jnp.repeat(query_pos, group)
     flat_doc = jnp.repeat(query_doc, group)
@@ -222,7 +222,6 @@
         .reshape(local_rows, group * head_dim)
         .astype(jnp.bfloat16)
     )
-    query_grad = stored_to_seq(query_grad, block_order, device, ctx_size, per_device)
     key_grad = unrotate(keyval_grad[:, :head_dim], own_positions).astype(jnp.bfloat16)
     value_grad = keyval_grad[:, head_dim:].astype(jnp.bfloat16)
     qkv_grad = jnp.concatenate([query_grad, key_grad, value_grad], axis=1)

time: 261 us -> 255 us (0.977)
  starting transfers between devices: 28.2 us -> 22.8 us
    all_to_all x1, waiting for transfers between devices: 2.39 us -> 28.1 us  [summed_rows(): lax.all_to_all(value.reshape((count, -1) + value.shape[1:]), axis, 0, 0,...]
    ppermute x3, waiting for transfers between devices: 66.8 us -> 44.7 us  [passed_along_2(): return lax.ppermute(value, axis, pairs)]
    ppermute x2 -> x1, waiting for transfers between devices: 21.5 us -> 17.8 us  [passed_along(): return lax.ppermute(value, axis, pairs)]
    ppermute x2 -> x1, starting transfers between devices: 6.44 us -> 2.95 us  [passed_along(): return lax.ppermute(value, axis, pairs)]
  transfers between devices with their start and end apart: 9 -> 8, of which waited for: 5 -> 4; matrix products, arithmetic and copies ran while one was open for 38% -> 39% of each run, Pallas kernels for 0% -> 0%
where the time goes in v3:
time: 255 us; the launch traced here: 254 us
  waiting for transfers between devices  91.3 us (36%)
  matrix products  68.4 us (27%)
  local copies, waits for them, and re-layouts  45 us (18%)
  starting transfers between devices  22.8 us (9%)
  between operations  15.1 us (6%)
  other arithmetic  10.2 us (4%)
    ppermute x3, waiting for transfers between devices, passed_along_2(): return lax.ppermute(value, axis, pairs)  44.7 us
    dot_general x25, matrix products, contract_cols(): lax.dot_general(left_rows, right_rows, (((1,), (1,)), ((), ())), preferre...  29 us
    all_to_all x1, waiting for transfers between devices, summed_rows(): lax.all_to_all(value.reshape((count, -1) + value.shape[1:]), axis, 0, 0,...  28.1 us
    dot_general x8, matrix products, running_total(): jnp.dot(weights, value_wide, precision=lax.Precision.HIGHEST)  19.2 us
    ppermute x1, waiting for transfers between devices, passed_along(): return lax.ppermute(value, axis, pairs)  17.8 us
    squeeze x16, local copies, waits for them, and re-layouts, body(): lax.scan(running_total, start_carry, key_blocks)  15.6 us
    while x40, local copies, waits for them, and re-layouts  9.27 us
    all_to_all x1, starting transfers between devices, gathered_rows(): lax.all_to_all(spread, axis, 0, 0, tiled=False)  7.72 us
  transfers between devices with their start and end apart: 8, of which 4 were waited for; matrix products, arithmetic and copies ran while one was open for 39% of the time, Pallas kernels for 0%

profile of v3, /device:TPU:1, one launch (start us, length us, event | category | flops | bytes accessed | tf_op | source)
XLA Modules:
  0.0 254.3 jit_solution(6984119153864801454)
XLA Ops:
  7.3 2.5 broadcast_in_dim.79
  9.7 7.7 %all-to-all-start = ((bf16[16,256,256]{2,1,0:T(8,128)(2,1)}), bf16[16,256,256]{2,1,0:T(8,128)(2,1)S(1)}, u32[]{:S(2)}, u32[]{:S(2)}) async-start(bf16[16,256,256]{2,1,0:T(8,128)(2,1)} %broadcast_in_dim.79), calls=%async_computation | async-start | bytes 4194304 | tf_op jit(solution)/shard_map/all_to_all | solution.py:30
  17.5 2.9 %collective-permute-start.1 = (bf16[128,512]{1,0:T(8,128)(2,1)S(1)}, bf16[128,512]{1,0:T(8,128)(2,1)S(1)}, u32[]{:S(2)}, u32[]{:S(2)}) collective-permute-start(bf16[128,512]{1,0:T(8,128)(2,1)S(1)} %get-tuple-element.268), channel_id=1, source_target_pairs={{0,8},{1,9},{2,10},{3,11},{4,12},{5,13},{6,14},{7,15},{8,0},{9,1},... | collective-permute-start | bytes 393224 | tf_op jit(solution)/shard_map/ppermute | solution.py:18
  20.5 3.4 %collective-permute-start = (bf16[256,8192]{1,0:T(8,128)(2,1)}, bf16[256,8192]{1,0:T(8,128)(2,1)}, u32[]{:S(2)}, u32[]{:S(2)}) collective-permute-start(bf16[256,8192]{1,0:T(8,128)(2,1)} %bitcast.121), channel_id=1, source_target_pairs={{16,0},{32,16},{48,32},{64,48},{80,64},{96,80},{112,96},{17,1},{33... | collective-permute-start | bytes 12582920 | tf_op jit(solution)/shard_map/ppermute | solution.py:24
  23.9 1.9 collective-permute-start.3
  28.8 17.8 %collective-permute-done.1 = bf16[128,512]{1,0:T(8,128)(2,1)S(1)} collective-permute-done((bf16[128,512]{1,0:T(8,128)(2,1)S(1)}, bf16[128,512]{1,0:T(8,128)(2,1)S(1)}, u32[]{:S(2)}, u32[]{:S(2)}) %collective-permute-start.1) | collective-permute-done | bytes 131104 | tf_op jit(solution)/shard_map/ppermute | solution.py:18
  47.7 33.0 %collective-permute-done.3 = bf16[512,768]{1,0:T(8,128)(2,1)} collective-permute-done((bf16[512,768]{1,0:T(8,128)(2,1)}, bf16[512,768]{1,0:T(8,128)(2,1)}, u32[]{:S(2)}, u32[]{:S(2)}) %collective-permute-start.3) | collective-permute-done | bytes 786464 | tf_op jit(solution)/shard_map/ppermute | solution.py:24
  80.7 2.0 gather_fusion
  82.7 50.4 %while.28 = (s32[]{:T(128)}, f32[1024]{0:T(1024)S(1)}, f32[1024]{0:T(1024)S(1)}, f32[1024,128]{1,0:T(8,128)}, s32[8,512]{1,0:T(8,128)S(1)}, /*index=5*/s32[8,512...) while((s32[]{:T(128)}, f32[1024]{0:T(1024)S(1)}, ...), condition=%wide.region_7.8_spmd.clone, body=%wide.region_4.7_spmd.clone.sunk | while | flops 949883904 | bytes 12720321 | solution.py:191
  82.7 1.0 dynamic-slice_bitcast_fusion.4
  85.8 2.4 convolution_add_fusion.4
  88.3 0.8 copy-done.1
  89.1 1.0 dynamic-slice_bitcast_fusion.4
  92.2 2.4 convolution_add_fusion.4
  94.6 0.8 copy-done.1
  95.4 1.0 dynamic-slice_bitcast_fusion.4
  98.5 2.4 convolution_add_fusion.4
  100.9 0.8 copy-done.1
  101.7 1.0 dynamic-slice_bitcast_fusion.4
  104.7 2.4 convolution_add_fusion.4
  107.2 0.8 copy-done.1
  108.0 1.0 dynamic-slice_bitcast_fusion.4
  111.0 2.4 convolution_add_fusion.4
  113.4 0.8 copy-done.1
  114.2 1.0 dynamic-slice_bitcast_fusion.4
  117.3 2.4 convolution_add_fusion.4
  119.7 0.8 copy-done.1
  120.5 1.0 dynamic-slice_bitcast_fusion.4
  123.6 2.4 convolution_add_fusion.4
  126.1 0.8 copy-done.1
  126.8 1.0 dynamic-slice_bitcast_fusion.4
  129.9 2.4 convolution_add_fusion.4
  133.2 7.0 %fusion.35 = bf16[256,512]{1,0:T(8,128)(2,1)S(1)} fusion(bf16[1,8192,512]{2,1,0:T(8,128)(2,1)} %all-gather.6.cloned.1.call-done, bf16[1,256,8192]{2,1,0:T(8,128)(2,1)} %param.11), kind=kOutput, calls=%fused_computation.53 | convolution fusion | flops 2147614720 | bytes 12845056 | tf_op jit(solution)/shard_map/dot_general | solution.py:139
  140.7 40.9 %while.29 = (s32[]{:T(128)}, f32[1024,128]{1,0:T(8,128)S(1)}, bf16[8,512,256]{2,1,0:T(8,128)(2,1)}, s32[8,512]{1,0:T(8,128)S(1)}, s32[8,512]{1,0:T(8,128)S(1)}, ...) while((s32[]{:T(128)}, f32[1024,128]{1,0:T(8,128)S(1)}, ...), condition=%wide.region_10.11_spmd.clone, body=%wide.region_9.10_spmd.clone.sunk | while | flops 677642240 | bytes 14342807 | solution.py:213
  140.8 1.0 dynamic-slice_bitcast_fusion.5
  145.9 1.0 dynamic-slice_bitcast_fusion.5
  151.0 1.0 dynamic-slice_bitcast_fusion.5
  156.1 1.0 dynamic-slice_bitcast_fusion.5
  161.2 1.0 dynamic-slice_bitcast_fusion.5
  166.3 1.0 dynamic-slice_bitcast_fusion.5
  171.4 1.0 dynamic-slice_bitcast_fusion.5
  176.5 1.0 dynamic-slice_bitcast_fusion.5
  181.6 4.9 %all-to-all-start.1 = ((bf16[16,256,256]{2,1,0:T(8,128)(2,1)}), bf16[16,256,256]{2,1,0:T(8,128)(2,1)S(1)}, u32[]{:S(2)}, u32[]{:S(2)}) async-start(bf16[16,256,256]{2,1,0:T(8,128)(2,1)} %bitcast.109), calls=%async_computation.1 | async-start | bytes 4194304 | tf_op jit(solution)/shard_map/all_to_all | solution.py:35
  187.3 2.4 fusion.39
  189.8 28.1 %all-to-all-done.1 = bf16[16,256,256]{2,1,0:T(8,128)(2,1)S(1)} async-done(((bf16[16,256,256]{2,1,0:T(8,128)(2,1)}), bf16[16,256,256]{2,1,0:T(8,128)(2,1)S(1)}, u32[]{:S(2)}, u32[]{:S(2)}) %all-to-all-start.1) | async-done | bytes 2097184 | tf_op jit(solution)/shard_map/all_to_all | solution.py:35
  219.0 1.9 collective-permute-start.2
  220.9 11.7 %collective-permute-done.2 = bf16[256,768]{1,0:T(8,128)(2,1)S(1)} collective-permute-done((bf16[256,768]{1,0:T(8,128)(2,1)S(1)}, bf16[256,768]{1,0:T(8,128)(2,1)S(1)}, u32[]{:S(2)}, u32[]{:S(2)}) %collective-permute-start.2) | collective-permute-done | bytes 393248 | tf_op jit(solution)/shard_map/ppermute | solution.py:24
  232.6 14.8 %fusion.34 = bf16[1,256,8192]{2,1,0:T(8,128)(2,1)} fusion(bf16[256,8192]{1,0:T(8,128)(2,1)} %collective-permute-done, bf16[256,768]{1,0:T(8,128)(2,1)S(1)} %collective-permute-done.2, bf16[8192,768]{1,0:T(8,128)(2,1)} %all-gather.4.cloned.1.call-done), kind=kOutput, calls=%fused_computation.50 | convolution fusion | flops 3227516928 | bytes 21364736 | tf_op jit(solution)/shard_map/dot_general | solution.py:105
  (264 shorter events, 55.4 us)
Async XLA Ops:
  6.5 126.6 %all-gather.6.cloned.1.call-start = ((), (), s32[]{:S(2)}) async-start(), calls=%async_computation.3 | async-start | bytes 8912896 | tf_op jit(solution)/shard_map/all_gather | solution.py:141
  9.7 7.8 %copy-start.3 = (bf16[1,256,512]{2,1,0:T(8,128)(2,1)S(1)}, bf16[1,256,512]{2,1,0:T(8,128)(2,1)}, u32[]{:S(2)}) copy-start(bf16[1,256,512]{2,1,0:T(8,128)(2,1)} %param.12) | copy-start | bytes 786436
  9.7 16.2 %copy-start.4 = (s32[1,32]{1,0:T(1,128)S(1)}, s32[1,32]{1,0:T(1,128)}, u32[]{:S(2)}) copy-start(s32[1,32]{1,0:T(1,128)} %param.17) | copy-start | bytes 388
  9.7 18.2 %copy-start.5 = (s32[1,8]{1,0:T(1,128)S(1)}, s32[1,8]{1,0:T(1,128)}, u32[]{:S(2)}) copy-start(s32[1,8]{1,0:T(1,128)} %param.16) | copy-start | bytes 100
  9.7 70.9 %all-to-all-start = ((bf16[16,256,256]{2,1,0:T(8,128)(2,1)}), bf16[16,256,256]{2,1,0:T(8,128)(2,1)S(1)}, u32[]{:S(2)}, u32[]{:S(2)}) async-start(bf16[16,256,256]{2,1,0:T(8,128)(2,1)} %broadcast_in_dim.79), calls=%async_computation | async-start | bytes 4194304 | tf_op jit(solution)/shard_map/all_to_all | solution.py:30
  17.4 215.2 %all-gather.4.cloned.1.call-start = ((), (), s32[]{:S(2)}) async-start(), calls=%async_computation.2 | async-start | bytes 13369344 | tf_op jit(solution)/shard_map/all_gather | solution.py:138
  17.5 29.0 %collective-permute-start.1 = (bf16[128,512]{1,0:T(8,128)(2,1)S(1)}, bf16[128,512]{1,0:T(8,128)(2,1)S(1)}, u32[]{:S(2)}, u32[]{:S(2)}) collective-permute-start(bf16[128,512]{1,0:T(8,128)(2,1)S(1)} %get-tuple-element.268), channel_id=1, source_target_pairs={{0,8},{1,9},{2,10},{3,11},{4,12},{5,13},{6,14},{7,15},{8,0},{9,1},... | collective-permute-start | bytes 393224 | tf_op jit(solution)/shard_map/ppermute | solution.py:18
  20.5 200.4 %collective-permute-start = (bf16[256,8192]{1,0:T(8,128)(2,1)}, bf16[256,8192]{1,0:T(8,128)(2,1)}, u32[]{:S(2)}, u32[]{:S(2)}) collective-permute-start(bf16[256,8192]{1,0:T(8,128)(2,1)} %bitcast.121), channel_id=1, source_target_pairs={{16,0},{32,16},{48,32},{64,48},{80,64},{96,80},{112,96},{17,1},{33... | collective-permute-start | bytes 12582920 | tf_op jit(solution)/shard_map/ppermute | solution.py:24
  23.9 56.7 %collective-permute-start.3 = (bf16[512,768]{1,0:T(8,128)(2,1)}, bf16[512,768]{1,0:T(8,128)(2,1)}, u32[]{:S(2)}, u32[]{:S(2)}) collective-permute-start(bf16[512,768]{1,0:T(8,128)(2,1)} %bitcast.122), channel_id=1, source_target_pairs={{16,0},{32,16},{48,32},{64,48},{80,64},{96,80},{112,96},{17,1},{33... | collective-permute-start | bytes 2359304 | tf_op jit(solution)/shard_map/ppermute | solution.py:24
  84.8 1.1 copy-start
  88.2 0.8 copy-start.1
  91.1 1.1 copy-start
  94.6 0.8 copy-start.1
  97.4 1.0 copy-start
  100.9 0.8 copy-start.1
  103.7 1.0 copy-start
  107.1 0.8 copy-start.1
  110.0 1.0 copy-start
  113.4 0.8 copy-start.1
  116.3 1.0 copy-start
  119.7 0.8 copy-start.1
  122.6 1.1 copy-start
  126.0 0.8 copy-start.1
  128.9 1.0 copy-start
  132.3 0.8 copy-start.1
  133.1 7.2 %copy-start.2 = (f32[1024,128]{1,0:T(8,128)S(1)}, f32[1024,128]{1,0:T(8,128)}, u32[]{:S(2)}) copy-start(f32[1024,128]{1,0:T(8,128)} %get-tuple-element.124) | copy-start | bytes 1572868
  181.6 36.3 %all-to-all-start.1 = ((bf16[16,256,256]{2,1,0:T(8,128)(2,1)}), bf16[16,256,256]{2,1,0:T(8,128)(2,1)S(1)}, u32[]{:S(2)}, u32[]{:S(2)}) async-start(bf16[16,256,256]{2,1,0:T(8,128)(2,1)} %bitcast.109), calls=%async_computation.1 | async-start | bytes 4194304 | tf_op jit(solution)/shard_map/all_to_all | solution.py:35
  219.0 13.6 %collective-permute-start.2 = (bf16[256,768]{1,0:T(8,128)(2,1)S(1)}, bf16[256,768]{1,0:T(8,128)(2,1)S(1)}, u32[]{:S(2)}, u32[]{:S(2)}) collective-permute-start(bf16[256,768]{1,0:T(8,128)(2,1)S(1)} %pad_maximum_fusion.1), channel_id=1, source_target_pairs={{16,0},{32,16},{48,32},{64,48},{80,64},{96,80},{112,96},{17,1},{33... | collective-permute-start | bytes 1179656 | tf_op jit(solution)/shard_map/ppermute | solution.py:24
Sparse Core Ops, SparseCore 0:
  9.5 91.8 all-gather.5
  103.5 110.7 all-gather.3

commit v4 on v3

--- a/solution.py
+++ b/solution.py
@@ -134,8 +134,10 @@
     key_block = math.gcd(seq_len, 512)
     key_steps = seq_len // key_block
     within = jnp.arange(BLOCK, dtype=jnp.int32)
-    next_grad_in = passed_along_2(section_grad_in, "pipe", -1)
-    next_weight = lax.all_gather(passed_along_2(in_weight, "pipe", -1), "ctx", axis=0, tiled=True)
+    query_width = stored_query.shape[1]
+    next_shard = passed_along_2(in_weight, "pipe", -1)
+    next_weight_q = lax.all_gather(next_shard[:, :query_width], "ctx", axis=0, tiled=True)
+    next_weight_kv = gathered_rows(next_shard[:, query_width:], "ctx")
     out_grad = jnp.dot(
         section_grad_in,
         lax.all_gather(out_weight, "ctx", axis=0, tiled=True),
@@ -144,6 +146,8 @@
     local_out_grad = out_grad
     seq_query = stored_to_seq(stored_query, block_order, device, ctx_size, per_device)
     gathered = gathered_rows(stored_keyval, "ctx")
+    gathered, grad_source = lax.optimization_barrier((gathered, section_grad_in))
+    next_grad_in = passed_along_2(grad_source, "pipe", -1)
     slot_ids = jnp.arange(block_count, dtype=jnp.int32)
     inverse = jnp.sum(
         jnp.where(block_order[None, :] == slot_ids[:, None], slot_ids[None, :], 0), axis=1
@@ -157,6 +161,7 @@
     query_doc = doc_ids(query_pos, lengths)
     flat_rows = local_rows * group
     flat_query = seq_query.reshape(flat_rows, head_dim)
+    next_weight_kv, local_out_grad = lax.optimization_barrier((next_weight_kv, local_out_grad))
     flat_grad = local_out_grad.reshape(flat_rows, head_dim)
     flat_pos = jnp.repeat(query_pos, group)
     flat_doc = jnp.repeat(query_doc, group)
@@ -226,7 +231,9 @@
     value_grad = keyval_grad[:, head_dim:].astype(jnp.bfloat16)
     qkv_grad = jnp.concatenate([query_grad, key_grad, value_grad], axis=1)
     next_qkv_grad = passed_along_2(qkv_grad, "pipe", -1)
-    projected = contract_cols(next_qkv_grad, next_weight)
+    projected = contract_cols(next_qkv_grad[:, :query_width], next_weight_q) + contract_cols(
+        next_qkv_grad[:, query_width:], next_weight_kv
+    )
     passed = (next_grad_in.astype(jnp.float32) + projected).astype(jnp.bfloat16)
     return passed[None]
 

time: 255 us -> 288 us (1.13)
  matrix products: 68.4 us -> 96.3 us
  starting transfers between devices: 22.8 us -> 40.5 us
  waiting for transfers between devices: 91.3 us -> 77.1 us
  local copies, waits for them, and re-layouts: 45 us -> 41.1 us
  other arithmetic: 10.2 us -> 13.3 us
    ppermute x3, waiting for transfers between devices: 44.7 us -> 5.97 us  [passed_along_2(): return lax.ppermute(value, axis, pairs)]
    all_gather x1, waiting for transfers between devices: 0.02 us -> 24.7 us  [body(): lax.all_gather(out_weight, 'ctx', axis=0, tiled=True)]
    dot_general x25 -> x26, matrix products: 29 us -> 47.7 us  [contract_cols(): lax.dot_general(left_rows, right_rows, (((1,), (1,)), ((), ())), preferre...]
    squeeze x16, local copies, waits for them, and re-layouts: 15.6 us -> 0.42 us  [body(): lax.scan(running_total, start_carry, key_blocks)]
    dynamic_slice x16, local copies, waits for them, and re-layouts: 0.16 us -> 11.9 us  [body(): lax.scan(running_total, start_carry, key_blocks)]
    while x40 -> x8, local copies, waits for them, and re-layouts: 9.27 us -> 0.02 us
    dot_general x16, matrix products: 7.66 us -> 15.3 us  [contract_rows(): lax.dot_general(left_rows, right_rows, (((0,), (0,)), ((), ())), preferre...]
    all_to_all x1 -> x2, starting transfers between devices: 7.72 us -> 15.1 us  [gathered_rows(): lax.all_to_all(spread, axis, 0, 0, tiled=False)]
  transfers between devices with their start and end apart: 8 -> 9, of which waited for: 4 -> 5; matrix products, arithmetic and copies ran while one was open for 39% -> 49% of each run, Pallas kernels for 0% -> 0%
where the time goes in v4:
time: 288 us; the launch traced here: 285 us
  matrix products  96.3 us (33%)
  waiting for transfers between devices  77.1 us (27%)
  local copies, waits for them, and re-layouts  41.1 us (14%)
  starting transfers between devices  40.5 us (14%)
  between operations  14.9 us (5%)
  other arithmetic  13.3 us (5%)
    dot_general x26, matrix products, contract_cols(): lax.dot_general(left_rows, right_rows, (((1,), (1,)), ((), ())), preferre...  47.7 us
    all_to_all x1, waiting for transfers between devices, summed_rows(): lax.all_to_all(value.reshape((count, -1) + value.shape[1:]), axis, 0, 0,...  25.7 us
    all_gather x1, waiting for transfers between devices, body(): lax.all_gather(out_weight, 'ctx', axis=0, tiled=True)  24.7 us
    dot_general x8, matrix products, running_total(): jnp.dot(weights, value_wide, precision=lax.Precision.HIGHEST)  19.3 us
    ppermute x1, waiting for transfers between devices, passed_along(): return lax.ppermute(value, axis, pairs)  15.6 us
    dot_general x16, matrix products, contract_rows(): lax.dot_general(left_rows, right_rows, (((0,), (0,)), ((), ())), preferre...  15.3 us
    all_to_all x2, starting transfers between devices, gathered_rows(): lax.all_to_all(spread, axis, 0, 0, tiled=False)  15.1 us
    ppermute x3, starting transfers between devices, passed_along_2(): return lax.ppermute(value, axis, pairs)  12.1 us
  transfers between devices with their start and end apart: 9, of which 5 were waited for; matrix products, arithmetic and copies ran while one was open for 49% of the time, Pallas kernels for 0%

profile of v4, /device:TPU:1, one launch (start us, length us, event | category | flops | bytes accessed | tf_op | source)
XLA Modules:
  0.0 284.5 jit_solution(8606299775308613908)
XLA Ops:
  7.3 2.4 broadcast_in_dim.82
  9.7 7.7 %all-to-all-start = ((bf16[16,256,256]{2,1,0:T(8,128)(2,1)}), bf16[16,256,256]{2,1,0:T(8,128)(2,1)S(1)}, u32[]{:S(2)}, u32[]{:S(2)}) async-start(bf16[16,256,256]{2,1,0:T(8,128)(2,1)} %broadcast_in_dim.82), calls=%async_computation | async-start | bytes 4194304 | tf_op jit(solution)/shard_map/all_to_all | solution.py:30
  17.5 2.9 %collective-permute-start.1 = (bf16[128,512]{1,0:T(8,128)(2,1)S(1)}, bf16[128,512]{1,0:T(8,128)(2,1)S(1)}, u32[]{:S(2)}, u32[]{:S(2)}) collective-permute-start(bf16[128,512]{1,0:T(8,128)(2,1)S(1)} %get-tuple-element.276), channel_id=1, source_target_pairs={{0,8},{1,9},{2,10},{3,11},{4,12},{5,13},{6,14},{7,15},{8,0},{9,1},... | collective-permute-start | bytes 393224 | tf_op jit(solution)/shard_map/ppermute | solution.py:18
  20.4 3.4 %collective-permute-start.2 = (bf16[512,768]{1,0:T(8,128)(2,1)}, bf16[512,768]{1,0:T(8,128)(2,1)}, u32[]{:S(2)}, u32[]{:S(2)}) collective-permute-start(bf16[512,768]{1,0:T(8,128)(2,1)} %bitcast.125), channel_id=1, source_target_pairs={{16,0},{32,16},{48,32},{64,48},{80,64},{96,80},{112,96},{17,1},{33... | collective-permute-start | bytes 2359304 | tf_op jit(solution)/shard_map/ppermute | solution.py:24
  30.9 15.6 %collective-permute-done.1 = bf16[128,512]{1,0:T(8,128)(2,1)S(1)} collective-permute-done((bf16[128,512]{1,0:T(8,128)(2,1)S(1)}, bf16[128,512]{1,0:T(8,128)(2,1)S(1)}, u32[]{:S(2)}, u32[]{:S(2)}) %collective-permute-start.1) | collective-permute-done | bytes 131104 | tf_op jit(solution)/shard_map/ppermute | solution.py:18
  49.0 1.9 slice.88
  51.9 4.4 %all-to-all-done = bf16[16,256,256]{2,1,0:T(8,128)(2,1)S(1)} async-done(((bf16[16,256,256]{2,1,0:T(8,128)(2,1)}), bf16[16,256,256]{2,1,0:T(8,128)(2,1)S(1)}, u32[]{:S(2)}, u32[]{:S(2)}) %all-to-all-start) | async-done | bytes 2097184 | tf_op jit(solution)/shard_map/all_to_all | solution.py:30
  56.3 2.7 broadcast_in_dim.90
  59.0 7.4 %all-to-all-start.1 = ((bf16[16,512,256]{2,1,0:T(8,128)(2,1)}), bf16[16,512,256]{2,1,0:T(8,128)(2,1)}, u32[]{:S(2)}, u32[]{:S(2)}) async-start(bf16[16,512,256]{2,1,0:T(8,128)(2,1)} %broadcast_in_dim.90), calls=%async_computation.1 | async-start | bytes 8388608 | tf_op jit(solution)/shard_map/all_to_all | solution.py:30
  66.4 2.4 gather_fusion
  68.8 47.5 %while.28 = (s32[]{:T(128)}, f32[1024]{0:T(1024)S(1)}, f32[1024]{0:T(1024)S(1)}, f32[1024,128]{1,0:T(8,128)S(1)}, s32[8,512]{1,0:T(8,128)}, /*index=5*/s32[8,512...) while((s32[]{:T(128)}, f32[1024]{0:T(1024)S(1)}, ...), condition=%wide.region_7.8_spmd.clone, body=%wide.region_4.7_spmd.clone.sunk | while | flops 949883904 | bytes 8525969 | solution.py:196
  70.0 1.6 fusion.87
  72.3 2.4 convolution_add_fusion.5
  75.9 1.6 fusion.87
  78.2 2.4 convolution_add_fusion.5
  81.9 1.6 fusion.87
  84.1 2.4 convolution_add_fusion.5
  87.8 1.6 fusion.87
  90.1 2.4 convolution_add_fusion.5
  93.8 1.6 fusion.87
  96.0 2.4 convolution_add_fusion.5
  99.7 1.6 fusion.87
  102.0 2.4 convolution_add_fusion.5
  105.7 1.6 fusion.87
  107.9 2.4 convolution_add_fusion.5
  111.6 1.6 fusion.87
  113.9 2.4 convolution_add_fusion.5
  116.3 4.0 %collective-permute-start = (bf16[256,8192]{1,0:T(8,128)(2,1)}, bf16[256,8192]{1,0:T(8,128)(2,1)}, u32[]{:S(2)}, u32[]{:S(2)}) collective-permute-start(bf16[256,8192]{1,0:T(8,128)(2,1)} %bitcast.124), channel_id=1, source_target_pairs={{16,0},{32,16},{48,32},{64,48},{80,64},{96,80},{112,96},{17,1},{33... | collective-permute-start | bytes 12582920 | tf_op jit(solution)/shard_map/ppermute | solution.py:24
  120.3 24.7 %all-gather.6.cloned.1.call-done = bf16[1,8192,512]{2,1,0:T(8,128)(2,1)} async-done(((bf16[1,512,512]{2,1,0:T(8,128)(2,1)}), bf16[1,8192,512]{2,1,0:T(8,128)(2,1)}) %all-gather.6.cloned.1.call-update) | async-done | bytes 8388624 | tf_op jit(solution)/shard_map/all_gather | solution.py:143
  145.0 7.7 %fusion.35 = bf16[256,512]{1,0:T(8,128)(2,1)} fusion(bf16[1,8192,512]{2,1,0:T(8,128)(2,1)} %all-gather.6.cloned.1.call-done, bf16[1,256,8192]{2,1,0:T(8,128)(2,1)} %param.11), kind=kOutput, calls=%fused_computation.54 | convolution fusion | flops 2147614720 | bytes 12845056 | tf_op jit(solution)/shard_map/dot_general | solution.py:141
  154.2 54.3 %while.29 = (s32[]{:T(128)}, f32[1024,128]{1,0:T(8,128)S(1)}, bf16[8,512,256]{2,1,0:T(8,128)(2,1)}, s32[8,512]{1,0:T(8,128)}, s32[8,512]{1,0:T(8,128)}, /*index=...) while((s32[]{:T(128)}, f32[1024,128]{1,0:T(8,128)S(1)}, ...), condition=%wide.region_10.11_spmd.clone, body=%wide.region_9.10_spmd.clone.sunk | while | flops 677642240 | bytes 14342307 | solution.py:218
  155.4 1.7 bitcast_select_fusion.3
  162.2 1.7 bitcast_select_fusion.3
  169.0 1.7 bitcast_select_fusion.3
  175.8 1.7 bitcast_select_fusion.3
  182.5 1.7 bitcast_select_fusion.3
  185.2 1.5 fusion.102
  189.4 1.7 bitcast_select_fusion.3
  192.0 1.4 fusion.102
  196.2 1.7 bitcast_select_fusion.3
  202.9 1.7 bitcast_select_fusion.3
  208.5 10.3 %all-to-all-start.2 = ((bf16[16,256,256]{2,1,0:T(8,128)(2,1)}), bf16[16,256,256]{2,1,0:T(8,128)(2,1)S(1)}, u32[]{:S(2)}, u32[]{:S(2)}) async-start(bf16[16,256,256]{2,1,0:T(8,128)(2,1)} %bitcast.112), calls=%async_computation.2 | async-start | bytes 4194304 | tf_op jit(solution)/shard_map/all_to_all | solution.py:35
  219.5 2.4 fusion.39
  222.1 25.7 %all-to-all-done.2 = bf16[16,256,256]{2,1,0:T(8,128)(2,1)S(1)} async-done(((bf16[16,256,256]{2,1,0:T(8,128)(2,1)}), bf16[16,256,256]{2,1,0:T(8,128)(2,1)S(1)}, u32[]{:S(2)}, u32[]{:S(2)}) %all-to-all-start.2) | async-done | bytes 2097184 | tf_op jit(solution)/shard_map/all_to_all | solution.py:35
  248.8 4.7 %collective-permute-start.3 = (bf16[256,768]{1,0:T(8,128)(2,1)S(1)}, bf16[256,768]{1,0:T(8,128)(2,1)S(1)}, u32[]{:S(2)}, u32[]{:S(2)}) collective-permute-start(bf16[256,768]{1,0:T(8,128)(2,1)S(1)} %pad_maximum_fusion.1), channel_id=1, source_target_pairs={{16,0},{32,16},{48,32},{64,48},{80,64},{96,80},{112,96},{17,1},{33... | collective-permute-start | bytes 1179656 | tf_op jit(solution)/shard_map/ppermute | solution.py:24
  253.6 6.0 %collective-permute-done.3 = bf16[256,768]{1,0:T(8,128)(2,1)S(1)} collective-permute-done((bf16[256,768]{1,0:T(8,128)(2,1)S(1)}, bf16[256,768]{1,0:T(8,128)(2,1)S(1)}, u32[]{:S(2)}, u32[]{:S(2)}) %collective-permute-start.3) | collective-permute-done | bytes 393248 | tf_op jit(solution)/shard_map/ppermute | solution.py:24
  259.5 6.7 %fusion.44 = f32[256,8192]{1,0:T(8,128)} fusion(bf16[8192,256]{1,0:T(8,128)(2,1)} %bitcast.18, bf16[256,768]{1,0:T(8,128)(2,1)S(1)} %collective-permute-done.3), kind=kOutput, calls=%fused_computation.66 | convolution fusion | flops 1073741824 | bytes 12713984 | tf_op jit(solution)/shard_map/dot_general | solution.py:105
  266.2 11.4 %fusion.34 = bf16[1,256,8192]{2,1,0:T(8,128)(2,1)} fusion(bf16[256,8192]{1,0:T(8,128)(2,1)} %collective-permute-done, f32[256,8192]{1,0:T(8,128)} %fusion.44, bf16[8192,512]{1,0:T(8,128)(2,1)} %all-gather.4.cloned.1.call-done, bf16[256,768]{1,0:T(8,128)(2,1)S(1)} %collective-permute-done.3), kind=kOutput, calls=%fused_computation.51 | convolution fusion | flops 2155872256 | bytes 25427968 | tf_op jit(solution)/shard_map/dot_general | solution.py:105
  (240 shorter events, 65.5 us)
Async XLA Ops:
  6.5 138.5 %all-gather.6.cloned.1.call-start = ((), (), s32[]{:S(2)}) async-start(), calls=%async_computation.4 | async-start | bytes 8912896 | tf_op jit(solution)/shard_map/all_gather | solution.py:143
  9.7 7.8 %copy-start.1 = (bf16[1,256,512]{2,1,0:T(8,128)(2,1)S(1)}, bf16[1,256,512]{2,1,0:T(8,128)(2,1)}, u32[]{:S(2)}) copy-start(bf16[1,256,512]{2,1,0:T(8,128)(2,1)} %param.12) | copy-start | bytes 786436
  9.7 14.2 %copy-start.2 = (s32[1,32]{1,0:T(1,128)S(1)}, s32[1,32]{1,0:T(1,128)}, u32[]{:S(2)}) copy-start(s32[1,32]{1,0:T(1,128)} %param.17) | copy-start | bytes 388
  9.7 16.1 %copy-start.4 = (s32[1,8]{1,0:T(1,128)S(1)}, s32[1,8]{1,0:T(1,128)}, u32[]{:S(2)}) copy-start(s32[1,8]{1,0:T(1,128)} %param.16) | copy-start | bytes 100
  9.7 46.6 %all-to-all-start = ((bf16[16,256,256]{2,1,0:T(8,128)(2,1)}), bf16[16,256,256]{2,1,0:T(8,128)(2,1)S(1)}, u32[]{:S(2)}, u32[]{:S(2)}) async-start(bf16[16,256,256]{2,1,0:T(8,128)(2,1)} %broadcast_in_dim.82), calls=%async_computation | async-start | bytes 4194304 | tf_op jit(solution)/shard_map/all_to_all | solution.py:30
  17.4 248.8 %all-gather.4.cloned.1.call-start = ((), (), s32[]{:S(2)}) async-start(), calls=%async_computation.3 | async-start | bytes 8912896 | tf_op jit(solution)/shard_map/all_gather | solution.py:139
  17.5 29.0 %collective-permute-start.1 = (bf16[128,512]{1,0:T(8,128)(2,1)S(1)}, bf16[128,512]{1,0:T(8,128)(2,1)S(1)}, u32[]{:S(2)}, u32[]{:S(2)}) collective-permute-start(bf16[128,512]{1,0:T(8,128)(2,1)S(1)} %get-tuple-element.276), channel_id=1, source_target_pairs={{0,8},{1,9},{2,10},{3,11},{4,12},{5,13},{6,14},{7,15},{8,0},{9,1},... | collective-permute-start | bytes 393224 | tf_op jit(solution)/shard_map/ppermute | solution.py:18
  20.4 28.5 %collective-permute-start.2 = (bf16[512,768]{1,0:T(8,128)(2,1)}, bf16[512,768]{1,0:T(8,128)(2,1)}, u32[]{:S(2)}, u32[]{:S(2)}) collective-permute-start(bf16[512,768]{1,0:T(8,128)(2,1)} %bitcast.125), channel_id=1, source_target_pairs={{16,0},{32,16},{48,32},{64,48},{80,64},{96,80},{112,96},{17,1},{33... | collective-permute-start | bytes 2359304 | tf_op jit(solution)/shard_map/ppermute | solution.py:24
  27.3 1.4 copy-start.3
  56.3 2.7 copy-start
  59.0 93.7 %all-to-all-start.1 = ((bf16[16,512,256]{2,1,0:T(8,128)(2,1)}), bf16[16,512,256]{2,1,0:T(8,128)(2,1)}, u32[]{:S(2)}, u32[]{:S(2)}) async-start(bf16[16,512,256]{2,1,0:T(8,128)(2,1)} %broadcast_in_dim.90), calls=%async_computation.1 | async-start | bytes 8388608 | tf_op jit(solution)/shard_map/all_to_all | solution.py:30
  116.3 149.9 %collective-permute-start = (bf16[256,8192]{1,0:T(8,128)(2,1)}, bf16[256,8192]{1,0:T(8,128)(2,1)}, u32[]{:S(2)}, u32[]{:S(2)}) collective-permute-start(bf16[256,8192]{1,0:T(8,128)(2,1)} %bitcast.124), channel_id=1, source_target_pairs={{16,0},{32,16},{48,32},{64,48},{80,64},{96,80},{112,96},{17,1},{33... | collective-permute-start | bytes 12582920 | tf_op jit(solution)/shard_map/ppermute | solution.py:24
  208.5 39.3 %all-to-all-start.2 = ((bf16[16,256,256]{2,1,0:T(8,128)(2,1)}), bf16[16,256,256]{2,1,0:T(8,128)(2,1)S(1)}, u32[]{:S(2)}, u32[]{:S(2)}) async-start(bf16[16,256,256]{2,1,0:T(8,128)(2,1)} %bitcast.112), calls=%async_computation.2 | async-start | bytes 4194304 | tf_op jit(solution)/shard_map/all_to_all | solution.py:35
  248.8 10.7 %collective-permute-start.3 = (bf16[256,768]{1,0:T(8,128)(2,1)S(1)}, bf16[256,768]{1,0:T(8,128)(2,1)S(1)}, u32[]{:S(2)}, u32[]{:S(2)}) collective-permute-start(bf16[256,768]{1,0:T(8,128)(2,1)S(1)} %pad_maximum_fusion.1), channel_id=1, source_target_pairs={{16,0},{32,16},{48,32},{64,48},{80,64},{96,80},{112,96},{17,1},{33... | collective-permute-start | bytes 1179656 | tf_op jit(solution)/shard_map/ppermute | solution.py:24
Sparse Core Ops, SparseCore 0:
  9.5 135.4 all-gather.5
  147.1 75.2 all-gather.3

commit v5 on v3

--- a/solution.py
+++ b/solution.py
@@ -134,7 +134,6 @@
     key_block = math.gcd(seq_len, 512)
     key_steps = seq_len // key_block
     within = jnp.arange(BLOCK, dtype=jnp.int32)
-    next_grad_in = passed_along_2(section_grad_in, "pipe", -1)
     next_weight = lax.all_gather(passed_along_2(in_weight, "pipe", -1), "ctx", axis=0, tiled=True)
     out_grad = jnp.dot(
         section_grad_in,
@@ -144,6 +143,8 @@
     local_out_grad = out_grad
     seq_query = stored_to_seq(stored_query, block_order, device, ctx_size, per_device)
     gathered = gathered_rows(stored_keyval, "ctx")
+    gathered, grad_source = lax.optimization_barrier((gathered, section_grad_in))
+    next_grad_in = passed_along_2(grad_source, "pipe", -1)
     slot_ids = jnp.arange(block_count, dtype=jnp.int32)
     inverse = jnp.sum(
         jnp.where(block_order[None, :] == slot_ids[:, None], slot_ids[None, :], 0), axis=1
@@ -214,18 +215,21 @@
         grad_step, jnp.zeros((flat_rows, head_dim), jnp.float32), key_blocks
     )
     own_positions = first_row + jnp.arange(local_rows, dtype=jnp.int32)
-    keyval_grad = summed_rows(
-        key_terms.reshape(seq_len, 2 * head_dim).astype(jnp.bfloat16), "ctx"
-    )
     query_grad = (
         unrotate(query_grad_rot, flat_pos)
         .reshape(local_rows, group * head_dim)
         .astype(jnp.bfloat16)
     )
+    next_query_grad = passed_along_2(query_grad, "pipe", -1)
+    keyval_grad = summed_rows(
+        key_terms.reshape(seq_len, 2 * head_dim).astype(jnp.bfloat16), "ctx"
+    )
     key_grad = unrotate(keyval_grad[:, :head_dim], own_positions).astype(jnp.bfloat16)
     value_grad = keyval_grad[:, head_dim:].astype(jnp.bfloat16)
-    qkv_grad = jnp.concatenate([query_grad, key_grad, value_grad], axis=1)
-    next_qkv_grad = passed_along_2(qkv_grad, "pipe", -1)
+    next_keyval_grad = passed_along_2(
+        jnp.concatenate([key_grad, value_grad], axis=1), "pipe", -1
+    )
+    next_qkv_grad = jnp.concatenate([next_query_grad, next_keyval_grad], axis=1)
     projected = contract_cols(next_qkv_grad, next_weight)
     passed = (next_grad_in.astype(jnp.float32) + projected).astype(jnp.bfloat16)
     return passed[None]

time: 255 us -> 247 us (0.969)
  waiting for transfers between devices: 91.3 us -> 79.2 us
  starting transfers between devices: 22.8 us -> 26.3 us
    ppermute x3 -> x4, waiting for transfers between devices: 44.7 us -> 4.21 us  [passed_along_2(): return lax.ppermute(value, axis, pairs)]
    all_to_all x1, waiting for transfers between devices: 28.1 us -> 45.9 us  [summed_rows(): lax.all_to_all(value.reshape((count, -1) + value.shape[1:]), axis, 0, 0,...]
    all_to_all x1, waiting for transfers between devices: 0.01 us -> 8.63 us  [gathered_rows(): lax.all_to_all(spread, axis, 0, 0, tiled=False)]
    ppermute x3 -> x4, starting transfers between devices: 7.26 us -> 11.6 us  [passed_along_2(): return lax.ppermute(value, axis, pairs)]
  transfers between devices with their start and end apart: 8 -> 9, of which waited for: 4 -> 4; matrix products, arithmetic and copies ran while one was open for 39% -> 41% of each run, Pallas kernels for 0% -> 0%
where the time goes in v5:
time: 247 us; the launch traced here: 246 us
  waiting for transfers between devices  79.2 us (32%)
  matrix products  68.9 us (28%)
  local copies, waits for them, and re-layouts  44.9 us (18%)
  starting transfers between devices  26.3 us (11%)
  between operations  15 us (6%)
  other arithmetic  10.2 us (4%)
    all_to_all x1, waiting for transfers between devices, summed_rows(): lax.all_to_all(value.reshape((count, -1) + value.shape[1:]), axis, 0, 0,...  45.9 us
    dot_general x25, matrix products, contract_cols(): lax.dot_general(left_rows, right_rows, (((1,), (1,)), ((), ())), preferre...  29 us
    ppermute x1, waiting for transfers between devices, passed_along(): return lax.ppermute(value, axis, pairs)  19.8 us
    dot_general x8, matrix products, running_total(): jnp.dot(weights, value_wide, precision=lax.Precision.HIGHEST)  19.2 us
    squeeze x16, local copies, waits for them, and re-layouts, body(): lax.scan(running_total, start_carry, key_blocks)  15.7 us
    ppermute x4, starting transfers between devices, passed_along_2(): return lax.ppermute(value, axis, pairs)  11.6 us
    while x40, local copies, waits for them, and re-layouts  9.21 us
    all_to_all x1, waiting for transfers between devices, gathered_rows(): lax.all_to_all(spread, axis, 0, 0, tiled=False)  8.63 us
  transfers between devices with their start and end apart: 9, of which 4 were waited for; matrix products, arithmetic and copies ran while one was open for 41% of the time, Pallas kernels for 0%

profile of v5, /device:TPU:1, one launch (start us, length us, event | category | flops | bytes accessed | tf_op | source)
XLA Modules:
  0.0 246.0 jit_solution(1773569637030308710)
XLA Ops:
  7.3 2.4 broadcast_in_dim.76
  9.7 7.7 %all-to-all-start = ((bf16[16,256,256]{2,1,0:T(8,128)(2,1)}), bf16[16,256,256]{2,1,0:T(8,128)(2,1)S(1)}, u32[]{:S(2)}, u32[]{:S(2)}) async-start(bf16[16,256,256]{2,1,0:T(8,128)(2,1)} %broadcast_in_dim.76), calls=%async_computation | async-start | bytes 4194304 | tf_op jit(solution)/shard_map/all_to_all | solution.py:30
  17.5 2.9 %collective-permute-start.1 = (bf16[128,512]{1,0:T(8,128)(2,1)S(1)}, bf16[128,512]{1,0:T(8,128)(2,1)S(1)}, u32[]{:S(2)}, u32[]{:S(2)}) collective-permute-start(bf16[128,512]{1,0:T(8,128)(2,1)S(1)} %get-tuple-element.272), channel_id=1, source_target_pairs={{0,8},{1,9},{2,10},{3,11},{4,12},{5,13},{6,14},{7,15},{8,0},{9,1},... | collective-permute-start | bytes 393224 | tf_op jit(solution)/shard_map/ppermute | solution.py:18
  20.5 3.4 %collective-permute-start.4 = (bf16[512,768]{1,0:T(8,128)(2,1)}, bf16[512,768]{1,0:T(8,128)(2,1)}, u32[]{:S(2)}, u32[]{:S(2)}) collective-permute-start(bf16[512,768]{1,0:T(8,128)(2,1)} %bitcast.122), channel_id=1, source_target_pairs={{16,0},{32,16},{48,32},{64,48},{80,64},{96,80},{112,96},{17,1},{33... | collective-permute-start | bytes 2359304 | tf_op jit(solution)/shard_map/ppermute | solution.py:24
  26.7 19.8 %collective-permute-done.1 = bf16[128,512]{1,0:T(8,128)(2,1)S(1)} collective-permute-done((bf16[128,512]{1,0:T(8,128)(2,1)S(1)}, bf16[128,512]{1,0:T(8,128)(2,1)S(1)}, u32[]{:S(2)}, u32[]{:S(2)}) %collective-permute-start.1) | collective-permute-done | bytes 131104 | tf_op jit(solution)/shard_map/ppermute | solution.py:18
  47.6 8.6 %all-to-all-done = bf16[16,256,256]{2,1,0:T(8,128)(2,1)S(1)} async-done(((bf16[16,256,256]{2,1,0:T(8,128)(2,1)}), bf16[16,256,256]{2,1,0:T(8,128)(2,1)S(1)}, u32[]{:S(2)}, u32[]{:S(2)}) %all-to-all-start) | async-done | bytes 2097184 | tf_op jit(solution)/shard_map/all_to_all | solution.py:30
  56.3 2.0 gather_fusion
  58.3 50.5 %while.28 = (s32[]{:T(128)}, f32[1024]{0:T(1024)S(1)}, f32[1024]{0:T(1024)S(1)}, f32[1024,128]{1,0:T(8,128)}, s32[8,512]{1,0:T(8,128)S(1)}, /*index=5*/s32[8,512...) while((s32[]{:T(128)}, f32[1024]{0:T(1024)S(1)}, ...), condition=%wide.region_7.8_spmd.clone, body=%wide.region_4.7_spmd.clone.sunk | while | flops 949883904 | bytes 12720321 | solution.py:192
  58.3 1.0 dynamic-slice_bitcast_fusion.4
  61.4 2.4 convolution_add_fusion.4
  63.8 0.8 copy-done.1
  64.6 1.1 dynamic-slice_bitcast_fusion.4
  67.8 2.4 convolution_add_fusion.4
  70.2 0.8 copy-done.1
  71.0 1.0 dynamic-slice_bitcast_fusion.4
  74.1 2.4 convolution_add_fusion.4
  76.5 0.8 copy-done.1
  77.3 1.0 dynamic-slice_bitcast_fusion.4
  80.4 2.4 convolution_add_fusion.4
  82.8 0.8 copy-done.1
  83.6 1.0 dynamic-slice_bitcast_fusion.4
  86.7 2.4 convolution_add_fusion.4
  89.1 0.8 copy-done.1
  89.9 1.0 dynamic-slice_bitcast_fusion.4
  93.0 2.4 convolution_add_fusion.4
  95.4 0.8 copy-done.1
  96.2 1.0 dynamic-slice_bitcast_fusion.4
  99.3 2.4 convolution_add_fusion.4
  102.5 1.0 dynamic-slice_bitcast_fusion.4
  105.6 2.4 convolution_add_fusion.4
  108.8 3.9 %collective-permute-start = (bf16[256,8192]{1,0:T(8,128)(2,1)}, bf16[256,8192]{1,0:T(8,128)(2,1)}, u32[]{:S(2)}, u32[]{:S(2)}) collective-permute-start(bf16[256,8192]{1,0:T(8,128)(2,1)} %bitcast.121), channel_id=1, source_target_pairs={{16,0},{32,16},{48,32},{64,48},{80,64},{96,80},{112,96},{17,1},{33... | collective-permute-start | bytes 12582920 | tf_op jit(solution)/shard_map/ppermute | solution.py:24
  112.8 7.5 %fusion.35 = bf16[256,512]{1,0:T(8,128)(2,1)S(1)} fusion(bf16[1,8192,512]{2,1,0:T(8,128)(2,1)} %all-gather.6.cloned.1.call-done, bf16[1,256,8192]{2,1,0:T(8,128)(2,1)} %param.11), kind=kOutput, calls=%fused_computation.53 | convolution fusion | flops 2147614720 | bytes 12845056 | tf_op jit(solution)/shard_map/dot_general | solution.py:138
  120.9 40.8 %while.29 = (s32[]{:T(128)}, f32[1024,128]{1,0:T(8,128)S(1)}, bf16[8,512,256]{2,1,0:T(8,128)(2,1)}, s32[8,512]{1,0:T(8,128)S(1)}, s32[8,512]{1,0:T(8,128)S(1)}, ...) while((s32[]{:T(128)}, f32[1024,128]{1,0:T(8,128)S(1)}, ...), condition=%wide.region_10.11_spmd.clone, body=%wide.region_9.10_spmd.clone.sunk | while | flops 677642240 | bytes 14342807 | solution.py:214
  120.9 1.0 dynamic-slice_bitcast_fusion.5
  126.0 1.0 dynamic-slice_bitcast_fusion.5
  131.1 1.0 dynamic-slice_bitcast_fusion.5
  136.2 1.0 dynamic-slice_bitcast_fusion.5
  141.3 1.0 dynamic-slice_bitcast_fusion.5
  146.4 1.0 dynamic-slice_bitcast_fusion.5
  151.5 1.0 dynamic-slice_bitcast_fusion.5
  156.6 1.0 dynamic-slice_bitcast_fusion.5
  161.7 3.9 %all-to-all-start.1 = ((bf16[16,256,256]{2,1,0:T(8,128)(2,1)}), bf16[16,256,256]{2,1,0:T(8,128)(2,1)S(1)}, u32[]{:S(2)}, u32[]{:S(2)}) async-start(bf16[16,256,256]{2,1,0:T(8,128)(2,1)} %bitcast.109), calls=%async_computation.1 | async-start | bytes 4194304 | tf_op jit(solution)/shard_map/all_to_all | solution.py:35
  166.4 2.4 fusion.39
  169.0 1.9 collective-permute-start.2
  170.9 45.9 %all-to-all-done.1 = bf16[16,256,256]{2,1,0:T(8,128)(2,1)S(1)} async-done(((bf16[16,256,256]{2,1,0:T(8,128)(2,1)}), bf16[16,256,256]{2,1,0:T(8,128)(2,1)S(1)}, u32[]{:S(2)}, u32[]{:S(2)}) %all-to-all-start.1) | async-done | bytes 2097184 | tf_op jit(solution)/shard_map/all_to_all | solution.py:35
  217.8 2.4 collective-permute-start.3
  220.2 4.2 %collective-permute-done.3 = bf16[256,256]{1,0:T(8,128)(2,1)S(1)} collective-permute-done((bf16[256,256]{1,0:T(8,128)(2,1)S(1)}, bf16[256,256]{1,0:T(8,128)(2,1)S(1)}, u32[]{:S(2)}, u32[]{:S(2)}) %collective-permute-start.3) | collective-permute-done | bytes 131104 | tf_op jit(solution)/shard_map/ppermute | solution.py:24
  224.4 14.8 %fusion.34 = bf16[1,256,8192]{2,1,0:T(8,128)(2,1)} fusion(bf16[256,8192]{1,0:T(8,128)(2,1)} %collective-permute-done, bf16[8192,768]{1,0:T(8,128)(2,1)} %all-gather.4.cloned.1.call-done, bf16[256,256]{1,0:T(8,128)(2,1)S(1)} %collective-permute-done.3, bf16[256,512]{1,0:T(8,128)(2,1)S(1)} %collective-permute-done.2), kind=kOutput, calls=%fused_computation.50 | convolution fusion | flops 3228303360 | bytes 21364736 | tf_op jit(solution)/shard_map/dot_general | solution.py:105
  (266 shorter events, 56.1 us)
Async XLA Ops:
  6.5 106.2 %all-gather.6.cloned.1.call-start = ((), (), s32[]{:S(2)}) async-start(), calls=%async_computation.3 | async-start | bytes 8912896 | tf_op jit(solution)/shard_map/all_gather | solution.py:140
  9.7 7.8 %copy-start.3 = (bf16[1,256,512]{2,1,0:T(8,128)(2,1)S(1)}, bf16[1,256,512]{2,1,0:T(8,128)(2,1)}, u32[]{:S(2)}) copy-start(bf16[1,256,512]{2,1,0:T(8,128)(2,1)} %param.12) | copy-start | bytes 786436
  9.7 14.2 %copy-start.4 = (s32[1,32]{1,0:T(1,128)S(1)}, s32[1,32]{1,0:T(1,128)}, u32[]{:S(2)}) copy-start(s32[1,32]{1,0:T(1,128)} %param.17) | copy-start | bytes 388
  9.7 16.1 %copy-start.5 = (s32[1,8]{1,0:T(1,128)S(1)}, s32[1,8]{1,0:T(1,128)}, u32[]{:S(2)}) copy-start(s32[1,8]{1,0:T(1,128)} %param.16) | copy-start | bytes 100
  9.7 46.6 %all-to-all-start = ((bf16[16,256,256]{2,1,0:T(8,128)(2,1)}), bf16[16,256,256]{2,1,0:T(8,128)(2,1)S(1)}, u32[]{:S(2)}, u32[]{:S(2)}) async-start(bf16[16,256,256]{2,1,0:T(8,128)(2,1)} %broadcast_in_dim.76), calls=%async_computation | async-start | bytes 4194304 | tf_op jit(solution)/shard_map/all_to_all | solution.py:30
  17.4 207.0 %all-gather.4.cloned.1.call-start = ((), (), s32[]{:S(2)}) async-start(), calls=%async_computation.2 | async-start | bytes 13369344 | tf_op jit(solution)/shard_map/all_gather | solution.py:137
  17.5 29.0 %collective-permute-start.1 = (bf16[128,512]{1,0:T(8,128)(2,1)S(1)}, bf16[128,512]{1,0:T(8,128)(2,1)S(1)}, u32[]{:S(2)}, u32[]{:S(2)}) collective-permute-start(bf16[128,512]{1,0:T(8,128)(2,1)S(1)} %get-tuple-element.272), channel_id=1, source_target_pairs={{0,8},{1,9},{2,10},{3,11},{4,12},{5,13},{6,14},{7,15},{8,0},{9,1},... | collective-permute-start | bytes 393224 | tf_op jit(solution)/shard_map/ppermute | solution.py:18
  20.5 27.2 %collective-permute-start.4 = (bf16[512,768]{1,0:T(8,128)(2,1)}, bf16[512,768]{1,0:T(8,128)(2,1)}, u32[]{:S(2)}, u32[]{:S(2)}) collective-permute-start(bf16[512,768]{1,0:T(8,128)(2,1)} %bitcast.122), channel_id=1, source_target_pairs={{16,0},{32,16},{48,32},{64,48},{80,64},{96,80},{112,96},{17,1},{33... | collective-permute-start | bytes 2359304 | tf_op jit(solution)/shard_map/ppermute | solution.py:24
  60.4 1.0 copy-start
  63.8 0.8 copy-start.1
  66.7 1.0 copy-start
  70.2 0.8 copy-start.1
  73.0 1.0 copy-start
  76.5 0.8 copy-start.1
  79.3 1.1 copy-start
  82.8 0.8 copy-start.1
  85.6 1.1 copy-start
  89.1 0.8 copy-start.1
  92.0 1.0 copy-start
  95.4 0.8 copy-start.1
  98.2 1.0 copy-start
  101.7 0.8 copy-start.1
  104.5 1.0 copy-start
  108.0 0.8 copy-start.1
  108.8 111.4 %collective-permute-start = (bf16[256,8192]{1,0:T(8,128)(2,1)}, bf16[256,8192]{1,0:T(8,128)(2,1)}, u32[]{:S(2)}, u32[]{:S(2)}) collective-permute-start(bf16[256,8192]{1,0:T(8,128)(2,1)} %bitcast.121), channel_id=1, source_target_pairs={{16,0},{32,16},{48,32},{64,48},{80,64},{96,80},{112,96},{17,1},{33... | collective-permute-start | bytes 12582920 | tf_op jit(solution)/shard_map/ppermute | solution.py:24
  112.7 7.8 %copy-start.2 = (f32[1024,128]{1,0:T(8,128)S(1)}, f32[1024,128]{1,0:T(8,128)}, u32[]{:S(2)}) copy-start(f32[1024,128]{1,0:T(8,128)} %get-tuple-element.128) | copy-start | bytes 1572868
  161.7 55.0 %all-to-all-start.1 = ((bf16[16,256,256]{2,1,0:T(8,128)(2,1)}), bf16[16,256,256]{2,1,0:T(8,128)(2,1)S(1)}, u32[]{:S(2)}, u32[]{:S(2)}) async-start(bf16[16,256,256]{2,1,0:T(8,128)(2,1)} %bitcast.109), calls=%async_computation.1 | async-start | bytes 4194304 | tf_op jit(solution)/shard_map/all_to_all | solution.py:35
  169.0 51.2 %collective-permute-start.2 = (bf16[256,512]{1,0:T(8,128)(2,1)S(1)}, bf16[256,512]{1,0:T(8,128)(2,1)S(1)}, u32[]{:S(2)}, u32[]{:S(2)}) collective-permute-start(bf16[256,512]{1,0:T(8,128)(2,1)S(1)} %convert_element_type.74), channel_id=1, source_target_pairs={{16,0},{32,16},{48,32},{64,48},{80,64},{96,80},{112,96},{17,1},{33... | collective-permute-start | bytes 786440 | tf_op jit(solution)/shard_map/ppermute | solution.py:24
  217.8 6.6 %collective-permute-start.3 = (bf16[256,256]{1,0:T(8,128)(2,1)S(1)}, bf16[256,256]{1,0:T(8,128)(2,1)S(1)}, u32[]{:S(2)}, u32[]{:S(2)}) collective-permute-start(bf16[256,256]{1,0:T(8,128)(2,1)S(1)} %pad_maximum_fusion.4), channel_id=1, source_target_pairs={{16,0},{32,16},{48,32},{64,48},{80,64},{96,80},{112,96},{17,1},{33... | collective-permute-start | bytes 393224 | tf_op jit(solution)/shard_map/ppermute | solution.py:24
Sparse Core Ops, SparseCore 0:
  9.5 91.7 all-gather.5
  103.5 112.0 all-gather.3

commit v6 on v5

--- a/solution.py
+++ b/solution.py
@@ -3,6 +3,7 @@
 import jax
 import jax.numpy as jnp
 from jax import lax
+from jax.experimental import pallas as pl
 from jax.sharding import PartitionSpec as P
 
 BLOCK = 128
@@ -34,6 +35,34 @@
     count = lax.axis_size(axis)
     pieces = lax.all_to_all(value.reshape((count, -1) + value.shape[1:]), axis, 0, 0, tiled=False)
     return jnp.sum(pieces.astype(jnp.float32), axis=0)
+
+
+def projection_kernel(grad_ref, weight_ref, base_ref, out_ref):
+    product = lax.dot_general(
+        grad_ref[...], weight_ref[...], (((1,), (1,)), ((), ())), preferred_element_type=jnp.float32
+    )
+    out_ref[...] = (base_ref[...].astype(jnp.float32) + product).astype(out_ref.dtype)
+
+
+def projected_sum(grad_rows, weight, base, tile=1024):
+    rows, inner = grad_rows.shape
+    width = weight.shape[0]
+    return pl.pallas_call(
+        projection_kernel,
+        grid=(width // tile,),
+        in_specs=[
+            pl.BlockSpec((rows, inner), lambda j: (0, 0)),
+            pl.BlockSpec((tile, inner), lambda j: (j, 0)),
+            pl.BlockSpec((rows, tile), lambda j: (0, j)),
+        ],
+        out_specs=pl.BlockSpec((rows, tile), lambda j: (0, j)),
+        out_shape=jax.ShapeDtypeStruct((rows, width), base.dtype),
+        cost_estimate=pl.CostEstimate(
+            flops=2 * rows * inner * width,
+            bytes_accessed=2 * (rows * inner + width * inner + 2 * rows * width),
+            transcendentals=0,
+        ),
+    )(grad_rows, weight, base)
 
 
 def rope_tables(positions, head_dim):
@@ -230,8 +259,7 @@
         jnp.concatenate([key_grad, value_grad], axis=1), "pipe", -1
     )
     next_qkv_grad = jnp.concatenate([next_query_grad, next_keyval_grad], axis=1)
-    projected = contract_cols(next_qkv_grad, next_weight)
-    passed = (next_grad_in.astype(jnp.float32) + projected).astype(jnp.bfloat16)
+    passed = projected_sum(next_qkv_grad, next_weight, next_grad_in)
     return passed[None]
 
 

time: 247 us -> 245 us (level)
  matrix products: 68.9 us -> 54.1 us
  Pallas kernels: 0 us -> 11.8 us
    dot_general x25 -> x24, matrix products: 29 us -> 14.2 us  [contract_cols(): lax.dot_general(left_rows, right_rows, (((1,), (1,)), ((), ())), preferre...]
    pallas_call x0 -> x1, Pallas kernels: none -> 11.8 us  [projected_sum(): pl.pallas_call(projection_kernel, grid=(width // tile,), in_specs=[pl.Blo...]
where the time goes in v6:
time: 245 us; the launch traced here: 244 us
  waiting for transfers between devices  79.3 us (32%)
  matrix products  54.1 us (22%)
  local copies, waits for them, and re-layouts  44.9 us (18%)
  starting transfers between devices  26.3 us (11%)
  between operations  15 us (6%)
  Pallas kernels  11.8 us (5%)
  other arithmetic  11 us (4%)
    all_to_all x1, waiting for transfers between devices, summed_rows(): lax.all_to_all(value.reshape((count, -1) + value.shape[1:]), axis, 0, 0,...  45.9 us
    ppermute x1, waiting for transfers between devices, passed_along(): return lax.ppermute(value, axis, pairs)  19.8 us
    dot_general x8, matrix products, running_total(): jnp.dot(weights, value_wide, precision=lax.Precision.HIGHEST)  19.2 us
    squeeze x16, local copies, waits for them, and re-layouts, body(): lax.scan(running_total, start_carry, key_blocks)  15.7 us
    dot_general x24, matrix products, contract_cols(): lax.dot_general(left_rows, right_rows, (((1,), (1,)), ((), ())), preferre...  14.2 us
    pallas_call x1, Pallas kernels, projected_sum(): pl.pallas_call(projection_kernel, grid=(width // tile,), in_specs=[pl.Blo...  11.8 us
    ppermute x4, starting transfers between devices, passed_along_2(): return lax.ppermute(value, axis, pairs)  11.6 us
    while x40, local copies, waits for them, and re-layouts  9.21 us
  transfers between devices with their start and end apart: 9, of which 4 were waited for; matrix products, arithmetic and copies ran while one was open for 41% of the time, Pallas kernels for 0%

profile of v6, /device:TPU:1, one launch (start us, length us, event | category | flops | bytes accessed | tf_op | source)
XLA Modules:
  0.0 243.9 jit_solution(847312179261037542)
XLA Ops:
  7.3 2.4 broadcast_in_dim.79
  9.7 7.7 %all-to-all-start = ((bf16[16,256,256]{2,1,0:T(8,128)(2,1)}), bf16[16,256,256]{2,1,0:T(8,128)(2,1)S(1)}, u32[]{:S(2)}, u32[]{:S(2)}) async-start(bf16[16,256,256]{2,1,0:T(8,128)(2,1)} %broadcast_in_dim.79), calls=%async_computation | async-start | bytes 4194304 | tf_op jit(solution)/shard_map/all_to_all | solution.py:31
  17.5 2.9 %collective-permute-start = (bf16[128,512]{1,0:T(8,128)(2,1)S(1)}, bf16[128,512]{1,0:T(8,128)(2,1)S(1)}, u32[]{:S(2)}, u32[]{:S(2)}) collective-permute-start(bf16[128,512]{1,0:T(8,128)(2,1)S(1)} %get-tuple-element.272), channel_id=1, source_target_pairs={{0,8},{1,9},{2,10},{3,11},{4,12},{5,13},{6,14},{7,15},{8,0},{9,1},... | collective-permute-start | bytes 393224 | tf_op jit(solution)/shard_map/ppermute | solution.py:19
  20.5 3.4 %collective-permute-start.3 = (bf16[512,768]{1,0:T(8,128)(2,1)}, bf16[512,768]{1,0:T(8,128)(2,1)}, u32[]{:S(2)}, u32[]{:S(2)}) collective-permute-start(bf16[512,768]{1,0:T(8,128)(2,1)} %bitcast.120), channel_id=1, source_target_pairs={{16,0},{32,16},{48,32},{64,48},{80,64},{96,80},{112,96},{17,1},{33... | collective-permute-start | bytes 2359304 | tf_op jit(solution)/shard_map/ppermute | solution.py:25
  26.7 19.8 %collective-permute-done = bf16[128,512]{1,0:T(8,128)(2,1)S(1)} collective-permute-done((bf16[128,512]{1,0:T(8,128)(2,1)S(1)}, bf16[128,512]{1,0:T(8,128)(2,1)S(1)}, u32[]{:S(2)}, u32[]{:S(2)}) %collective-permute-start) | collective-permute-done | bytes 131104 | tf_op jit(solution)/shard_map/ppermute | solution.py:19
  47.6 8.6 %all-to-all-done = bf16[16,256,256]{2,1,0:T(8,128)(2,1)S(1)} async-done(((bf16[16,256,256]{2,1,0:T(8,128)(2,1)}), bf16[16,256,256]{2,1,0:T(8,128)(2,1)S(1)}, u32[]{:S(2)}, u32[]{:S(2)}) %all-to-all-start) | async-done | bytes 2097184 | tf_op jit(solution)/shard_map/all_to_all | solution.py:31
  56.3 2.0 gather_fusion
  58.3 50.5 %while.28 = (s32[]{:T(128)}, f32[1024]{0:T(1024)S(1)}, f32[1024]{0:T(1024)S(1)}, f32[1024,128]{1,0:T(8,128)}, s32[8,512]{1,0:T(8,128)S(1)}, /*index=5*/s32[8,512...) while((s32[]{:T(128)}, f32[1024]{0:T(1024)S(1)}, ...), condition=%wide.region_7.8_spmd.clone, body=%wide.region_4.7_spmd.clone.sunk | while | flops 949883904 | bytes 12720321 | solution.py:221
  58.3 1.0 dynamic-slice_bitcast_fusion.4
  61.4 2.4 convolution_add_fusion.4
  63.8 0.8 copy-done.1
  64.6 1.1 dynamic-slice_bitcast_fusion.4
  67.8 2.4 convolution_add_fusion.4
  70.2 0.8 copy-done.1
  71.0 1.0 dynamic-slice_bitcast_fusion.4
  74.1 2.4 convolution_add_fusion.4
  76.5 0.8 copy-done.1
  77.3 1.0 dynamic-slice_bitcast_fusion.4
  80.4 2.4 convolution_add_fusion.4
  82.8 0.8 copy-done.1
  83.6 1.0 dynamic-slice_bitcast_fusion.4
  86.7 2.4 convolution_add_fusion.4
  89.9 1.0 dynamic-slice_bitcast_fusion.4
  93.0 2.4 convolution_add_fusion.4
  96.2 1.0 dynamic-slice_bitcast_fusion.4
  99.3 2.4 convolution_add_fusion.4
  102.5 1.0 dynamic-slice_bitcast_fusion.4
  105.6 2.4 convolution_add_fusion.4
  108.0 0.8 copy-done.1
  108.8 3.9 %collective-permute-start.4 = (bf16[256,8192]{1,0:T(8,128)(2,1)}, bf16[256,8192]{1,0:T(8,128)(2,1)}, u32[]{:S(2)}, u32[]{:S(2)}) collective-permute-start(bf16[256,8192]{1,0:T(8,128)(2,1)} %bitcast.119), channel_id=1, source_target_pairs={{16,0},{32,16},{48,32},{64,48},{80,64},{96,80},{112,96},{17,1},{33... | collective-permute-start | bytes 12582920 | tf_op jit(solution)/shard_map/ppermute | solution.py:25
  112.8 7.5 %fusion.34 = bf16[256,512]{1,0:T(8,128)(2,1)S(1)} fusion(bf16[1,8192,512]{2,1,0:T(8,128)(2,1)} %all-gather.6.cloned.1.call-done, bf16[1,256,8192]{2,1,0:T(8,128)(2,1)} %param.11), kind=kOutput, calls=%fused_computation.51 | convolution fusion | flops 2147614720 | bytes 12845056 | tf_op jit(solution)/shard_map/dot_general | solution.py:167
  120.9 40.8 %while.29 = (s32[]{:T(128)}, f32[1024,128]{1,0:T(8,128)S(1)}, bf16[8,512,256]{2,1,0:T(8,128)(2,1)}, s32[8,512]{1,0:T(8,128)S(1)}, s32[8,512]{1,0:T(8,128)S(1)}, ...) while((s32[]{:T(128)}, f32[1024,128]{1,0:T(8,128)S(1)}, ...), condition=%wide.region_10.11_spmd.clone, body=%wide.region_9.10_spmd.clone.sunk | while | flops 677642240 | bytes 14342807 | solution.py:243
  120.9 1.0 dynamic-slice_bitcast_fusion.5
  126.0 1.0 dynamic-slice_bitcast_fusion.5
  131.1 1.0 dynamic-slice_bitcast_fusion.5
  136.2 1.0 dynamic-slice_bitcast_fusion.5
  141.3 1.0 dynamic-slice_bitcast_fusion.5
  146.4 1.0 dynamic-slice_bitcast_fusion.5
  151.5 1.0 dynamic-slice_bitcast_fusion.5
  156.6 1.0 dynamic-slice_bitcast_fusion.5
  161.7 3.9 %all-to-all-start.1 = ((bf16[16,256,256]{2,1,0:T(8,128)(2,1)}), bf16[16,256,256]{2,1,0:T(8,128)(2,1)S(1)}, u32[]{:S(2)}, u32[]{:S(2)}) async-start(bf16[16,256,256]{2,1,0:T(8,128)(2,1)} %bitcast.107), calls=%async_computation.1 | async-start | bytes 4194304 | tf_op jit(solution)/shard_map/all_to_all | solution.py:36
  166.4 2.4 fusion.38
  169.0 1.9 collective-permute-start.1
  170.9 45.9 %all-to-all-done.1 = bf16[16,256,256]{2,1,0:T(8,128)(2,1)S(1)} async-done(((bf16[16,256,256]{2,1,0:T(8,128)(2,1)}), bf16[16,256,256]{2,1,0:T(8,128)(2,1)S(1)}, u32[]{:S(2)}, u32[]{:S(2)}) %all-to-all-start.1) | async-done | bytes 2097184 | tf_op jit(solution)/shard_map/all_to_all | solution.py:36
  217.8 2.4 collective-permute-start.2
  220.2 4.2 %collective-permute-done.2 = bf16[256,256]{1,0:T(8,128)(2,1)S(1)} collective-permute-done((bf16[256,256]{1,0:T(8,128)(2,1)S(1)}, bf16[256,256]{1,0:T(8,128)(2,1)S(1)}, u32[]{:S(2)}, u32[]{:S(2)}) %collective-permute-start.2) | collective-permute-done | bytes 131104 | tf_op jit(solution)/shard_map/ppermute | solution.py:25
  224.4 0.8 pad_maximum_fusion.1.grad_ref
  225.2 11.8 %shard_map.73 = bf16[256,8192]{1,0:T(8,128)(2,1)} custom-call(bf16[256,768]{1,0:T(8,128)(2,1)} %pad_maximum_fusion.1.grad_ref, bf16[8192,768]{1,0:T(8,128)(2,1)} %all-gather.4.cloned.1.call-done.weight_ref, bf16[256,8192]{1,0:T(8,128)(2,1)} %collective-permute-done.4.base_ref), custom_call_target="tpu_custom_call" | custom-call | flops 3221225472 | bytes 21364736 | tf_op jit(solution)/shard_map/pallas_call | solution.py:50
  (267 shorter events, 56.9 us)
Async XLA Ops:
  6.5 106.2 %all-gather.6.cloned.1.call-start = ((), (), s32[]{:S(2)}) async-start(), calls=%async_computation.3 | async-start | bytes 8912896 | tf_op jit(solution)/shard_map/all_gather | solution.py:169
  9.7 7.8 %copy-start.3 = (bf16[1,256,512]{2,1,0:T(8,128)(2,1)S(1)}, bf16[1,256,512]{2,1,0:T(8,128)(2,1)}, u32[]{:S(2)}) copy-start(bf16[1,256,512]{2,1,0:T(8,128)(2,1)} %param.12) | copy-start | bytes 786436
  9.7 14.2 %copy-start.4 = (s32[1,32]{1,0:T(1,128)S(1)}, s32[1,32]{1,0:T(1,128)}, u32[]{:S(2)}) copy-start(s32[1,32]{1,0:T(1,128)} %param.17) | copy-start | bytes 388
  9.7 16.1 %copy-start.5 = (s32[1,8]{1,0:T(1,128)S(1)}, s32[1,8]{1,0:T(1,128)}, u32[]{:S(2)}) copy-start(s32[1,8]{1,0:T(1,128)} %param.16) | copy-start | bytes 100
  9.7 46.6 %all-to-all-start = ((bf16[16,256,256]{2,1,0:T(8,128)(2,1)}), bf16[16,256,256]{2,1,0:T(8,128)(2,1)S(1)}, u32[]{:S(2)}, u32[]{:S(2)}) async-start(bf16[16,256,256]{2,1,0:T(8,128)(2,1)} %broadcast_in_dim.79), calls=%async_computation | async-start | bytes 4194304 | tf_op jit(solution)/shard_map/all_to_all | solution.py:31
  17.4 207.8 %all-gather.4.cloned.1.call-start = ((), (), s32[]{:S(2)}) async-start(), calls=%async_computation.2 | async-start | bytes 13369344 | tf_op jit(solution)/shard_map/all_gather | solution.py:166
  17.5 29.0 %collective-permute-start = (bf16[128,512]{1,0:T(8,128)(2,1)S(1)}, bf16[128,512]{1,0:T(8,128)(2,1)S(1)}, u32[]{:S(2)}, u32[]{:S(2)}) collective-permute-start(bf16[128,512]{1,0:T(8,128)(2,1)S(1)} %get-tuple-element.272), channel_id=1, source_target_pairs={{0,8},{1,9},{2,10},{3,11},{4,12},{5,13},{6,14},{7,15},{8,0},{9,1},... | collective-permute-start | bytes 393224 | tf_op jit(solution)/shard_map/ppermute | solution.py:19
  20.5 27.2 %collective-permute-start.3 = (bf16[512,768]{1,0:T(8,128)(2,1)}, bf16[512,768]{1,0:T(8,128)(2,1)}, u32[]{:S(2)}, u32[]{:S(2)}) collective-permute-start(bf16[512,768]{1,0:T(8,128)(2,1)} %bitcast.120), channel_id=1, source_target_pairs={{16,0},{32,16},{48,32},{64,48},{80,64},{96,80},{112,96},{17,1},{33... | collective-permute-start | bytes 2359304 | tf_op jit(solution)/shard_map/ppermute | solution.py:25
  60.4 1.0 copy-start
  63.8 0.8 copy-start.1
  66.7 1.0 copy-start
  70.2 0.8 copy-start.1
  73.0 1.0 copy-start
  76.5 0.8 copy-start.1
  79.3 1.1 copy-start
  82.8 0.8 copy-start.1
  85.6 1.1 copy-start
  89.1 0.8 copy-start.1
  92.0 1.0 copy-start
  95.4 0.8 copy-start.1
  98.2 1.0 copy-start
  101.7 0.8 copy-start.1
  104.5 1.0 copy-start
  108.0 0.8 copy-start.1
  108.8 116.4 %collective-permute-start.4 = (bf16[256,8192]{1,0:T(8,128)(2,1)}, bf16[256,8192]{1,0:T(8,128)(2,1)}, u32[]{:S(2)}, u32[]{:S(2)}) collective-permute-start(bf16[256,8192]{1,0:T(8,128)(2,1)} %bitcast.119), channel_id=1, source_target_pairs={{16,0},{32,16},{48,32},{64,48},{80,64},{96,80},{112,96},{17,1},{33... | collective-permute-start | bytes 12582920 | tf_op jit(solution)/shard_map/ppermute | solution.py:25
  112.7 7.8 %copy-start.2 = (f32[1024,128]{1,0:T(8,128)S(1)}, f32[1024,128]{1,0:T(8,128)}, u32[]{:S(2)}) copy-start(f32[1024,128]{1,0:T(8,128)} %get-tuple-element.127) | copy-start | bytes 1572868
  161.7 55.0 %all-to-all-start.1 = ((bf16[16,256,256]{2,1,0:T(8,128)(2,1)}), bf16[16,256,256]{2,1,0:T(8,128)(2,1)S(1)}, u32[]{:S(2)}, u32[]{:S(2)}) async-start(bf16[16,256,256]{2,1,0:T(8,128)(2,1)} %bitcast.107), calls=%async_computation.1 | async-start | bytes 4194304 | tf_op jit(solution)/shard_map/all_to_all | solution.py:36
  169.0 51.2 %collective-permute-start.1 = (bf16[256,512]{1,0:T(8,128)(2,1)S(1)}, bf16[256,512]{1,0:T(8,128)(2,1)S(1)}, u32[]{:S(2)}, u32[]{:S(2)}) collective-permute-start(bf16[256,512]{1,0:T(8,128)(2,1)S(1)} %convert_element_type.67), channel_id=1, source_target_pairs={{16,0},{32,16},{48,32},{64,48},{80,64},{96,80},{112,96},{17,1},{33... | collective-permute-start | bytes 786440 | tf_op jit(solution)/shard_map/ppermute | solution.py:25
  217.8 6.6 %collective-permute-start.2 = (bf16[256,256]{1,0:T(8,128)(2,1)S(1)}, bf16[256,256]{1,0:T(8,128)(2,1)S(1)}, u32[]{:S(2)}, u32[]{:S(2)}) collective-permute-start(bf16[256,256]{1,0:T(8,128)(2,1)S(1)} %pad_maximum_fusion.5), channel_id=1, source_target_pairs={{16,0},{32,16},{48,32},{64,48},{80,64},{96,80},{112,96},{17,1},{33... | collective-permute-start | bytes 393224 | tf_op jit(solution)/shard_map/ppermute | solution.py:25
Sparse Core Ops, SparseCore 0:
  9.5 91.7 all-gather.5
  103.5 112.0 all-gather.3

commit v7 on v6

--- a/solution.py
+++ b/solution.py
@@ -44,7 +44,7 @@
     out_ref[...] = (base_ref[...].astype(jnp.float32) + product).astype(out_ref.dtype)
 
 
-def projected_sum(grad_rows, weight, base, tile=1024):
+def projected_sum(grad_rows, weight, base, tile=4096):
     rows, inner = grad_rows.shape
     width = weight.shape[0]
     return pl.pallas_call(
@@ -208,7 +208,7 @@
         row_total = row_total * rescale + jnp.sum(weights, axis=1)
         value_wide = pair_rows[:, head_dim:].astype(jnp.float32)
         weighted = weighted * rescale[:, None] + jnp.dot(
-            weights, value_wide, precision=lax.Precision.HIGHEST
+            weights, value_wide, precision=lax.Precision.HIGH
         )
         return ((new_top, row_total, weighted), None)
 

time: 245 us -> 235 us (0.959)
  matrix products: 54.1 us -> 47.3 us
  Pallas kernels: 11.8 us -> 9.08 us
    dot_general x8, matrix products: 19.2 us -> 12.9 us  [running_total(): jnp.dot(weights, value_wide, precision=lax.Precision.HIGH)]
    pallas_call x1, Pallas kernels: 11.8 us -> 9.08 us  [projected_sum(): pl.pallas_call(projection_kernel, grid=(width // tile,), in_specs=[pl.Blo...]
  transfers between devices with their start and end apart: 9 -> 9, of which waited for: 4 -> 4; matrix products, arithmetic and copies ran while one was open for 41% -> 40% of each run, Pallas kernels for 0% -> 0%
where the time goes in v7:
time: 235 us; the launch traced here: 234 us
  waiting for transfers between devices  79.2 us (34%)
  matrix products  47.3 us (20%)
  local copies, waits for them, and re-layouts  44.9 us (19%)
  starting transfers between devices  26.1 us (11%)
  between operations  15 us (6%)
  other arithmetic  11 us (5%)
  Pallas kernels  9.08 us (4%)
    all_to_all x1, waiting for transfers between devices, summed_rows(): lax.all_to_all(value.reshape((count, -1) + value.shape[1:]), axis, 0, 0,...  45.7 us
    ppermute x1, waiting for transfers between devices, passed_along(): return lax.ppermute(value, axis, pairs)  19.8 us
    squeeze x16, local copies, waits for them, and re-layouts, body(): lax.scan(running_total, start_carry, key_blocks)  15.7 us
    dot_general x24, matrix products, contract_cols(): lax.dot_general(left_rows, right_rows, (((1,), (1,)), ((), ())), preferre...  14.3 us
    dot_general x8, matrix products, running_total(): jnp.dot(weights, value_wide, precision=lax.Precision.HIGH)  12.9 us
    ppermute x4, starting transfers between devices, passed_along_2(): return lax.ppermute(value, axis, pairs)  11.5 us
    while x40, local copies, waits for them, and re-layouts  9.26 us
    pallas_call x1, Pallas kernels, projected_sum(): pl.pallas_call(projection_kernel, grid=(width // tile,), in_specs=[pl.Blo...  9.08 us
  transfers between devices with their start and end apart: 9, of which 4 were waited for; matrix products, arithmetic and copies ran while one was open for 40% of the time, Pallas kernels for 0%

profile of v7, /device:TPU:1, one launch (start us, length us, event | category | flops | bytes accessed | tf_op | source)
XLA Modules:
  0.0 234.3 jit_solution(14509833642054087883)
XLA Ops:
  7.3 2.4 %broadcast_in_dim.79 = bf16[16,256,256]{2,1,0:T(8,128)(2,1)} broadcast(bf16[256,256]{1,0:T(8,128)(2,1)} %bitcast.114), dimensions={1,2} | broadcast | bytes 2228224 | tf_op jit(solution)/shard_map/broadcast_in_dim | solution.py:30
  9.7 7.7 %all-to-all-start = ((bf16[16,256,256]{2,1,0:T(8,128)(2,1)}), bf16[16,256,256]{2,1,0:T(8,128)(2,1)S(1)}, u32[]{:S(2)}, u32[]{:S(2)}) async-start(bf16[16,256,256]{2,1,0:T(8,128)(2,1)} %broadcast_in_dim.79), calls=%async_computation | async-start | bytes 4194304 | tf_op jit(solution)/shard_map/all_to_all | solution.py:31
  17.5 2.9 %collective-permute-start = (bf16[128,512]{1,0:T(8,128)(2,1)S(1)}, bf16[128,512]{1,0:T(8,128)(2,1)S(1)}, u32[]{:S(2)}, u32[]{:S(2)}) collective-permute-start(bf16[128,512]{1,0:T(8,128)(2,1)S(1)} %get-tuple-element.272), channel_id=1, source_target_pairs={{0,8},{1,9},{2,10},{3,11},{4,12},{5,13},{6,14},{7,15},{8,0},{9,1},... | collective-permute-start | bytes 393224 | tf_op jit(solution)/shard_map/ppermute | solution.py:19
  20.5 3.4 %collective-permute-start.3 = (bf16[512,768]{1,0:T(8,128)(2,1)}, bf16[512,768]{1,0:T(8,128)(2,1)}, u32[]{:S(2)}, u32[]{:S(2)}) collective-permute-start(bf16[512,768]{1,0:T(8,128)(2,1)} %bitcast.120), channel_id=1, source_target_pairs={{16,0},{32,16},{48,32},{64,48},{80,64},{96,80},{112,96},{17,1},{33... | collective-permute-start | bytes 2359304 | tf_op jit(solution)/shard_map/ppermute | solution.py:25
  26.7 19.8 %collective-permute-done = bf16[128,512]{1,0:T(8,128)(2,1)S(1)} collective-permute-done((bf16[128,512]{1,0:T(8,128)(2,1)S(1)}, bf16[128,512]{1,0:T(8,128)(2,1)S(1)}, u32[]{:S(2)}, u32[]{:S(2)}) %collective-permute-start) | collective-permute-done | bytes 131104 | tf_op jit(solution)/shard_map/ppermute | solution.py:19
  47.6 8.6 %all-to-all-done = bf16[16,256,256]{2,1,0:T(8,128)(2,1)S(1)} async-done(((bf16[16,256,256]{2,1,0:T(8,128)(2,1)}), bf16[16,256,256]{2,1,0:T(8,128)(2,1)S(1)}, u32[]{:S(2)}, u32[]{:S(2)}) %all-to-all-start) | async-done | bytes 2097184 | tf_op jit(solution)/shard_map/all_to_all | solution.py:31
  56.3 2.0 gather_fusion
  58.3 44.2 %while.28 = (s32[]{:T(128)}, f32[1024]{0:T(1024)S(1)}, f32[1024]{0:T(1024)S(1)}, f32[1024,128]{1,0:T(8,128)}, s32[8,512]{1,0:T(8,128)S(1)}, /*index=5*/s32[8,512...) while((s32[]{:T(128)}, f32[1024]{0:T(1024)S(1)}, ...), condition=%wide.region_7.8_spmd.clone, body=%wide.region_4.7_spmd.clone.sunk | while | flops 547230720 | bytes 12720321 | solution.py:221
  58.3 1.0 dynamic-slice_bitcast_fusion.4
  61.4 1.6 convolution_add_fusion.4
  63.0 0.8 copy-done.1
  63.8 1.0 dynamic-slice_bitcast_fusion.4
  67.0 1.6 convolution_add_fusion.4
  68.6 0.8 copy-done.1
  69.4 1.0 dynamic-slice_bitcast_fusion.4
  72.5 1.6 convolution_add_fusion.4
  74.1 0.8 copy-done.1
  74.9 1.0 dynamic-slice_bitcast_fusion.4
  78.0 1.6 convolution_add_fusion.4
  80.5 1.0 dynamic-slice_bitcast_fusion.4
  83.6 1.6 convolution_add_fusion.4
  86.0 1.0 dynamic-slice_bitcast_fusion.4
  89.1 1.6 convolution_add_fusion.4
  91.5 1.0 dynamic-slice_bitcast_fusion.4
  94.6 1.6 convolution_add_fusion.4
  96.2 0.8 copy-done.1
  97.0 1.0 dynamic-slice_bitcast_fusion.4
  100.1 1.6 convolution_add_fusion.4
  101.7 0.8 copy-done.1
  102.5 3.9 %collective-permute-start.4 = (bf16[256,8192]{1,0:T(8,128)(2,1)}, bf16[256,8192]{1,0:T(8,128)(2,1)}, u32[]{:S(2)}, u32[]{:S(2)}) collective-permute-start(bf16[256,8192]{1,0:T(8,128)(2,1)} %bitcast.119), channel_id=1, source_target_pairs={{16,0},{32,16},{48,32},{64,48},{80,64},{96,80},{112,96},{17,1},{33... | collective-permute-start | bytes 12582920 | tf_op jit(solution)/shard_map/ppermute | solution.py:25
  106.4 7.0 %fusion.34 = bf16[256,512]{1,0:T(8,128)(2,1)S(1)} fusion(bf16[1,8192,512]{2,1,0:T(8,128)(2,1)} %all-gather.6.cloned.1.call-done, bf16[1,256,8192]{2,1,0:T(8,128)(2,1)} %param.11), kind=kOutput, calls=%fused_computation.51 | convolution fusion | flops 2147614720 | bytes 12845056 | tf_op jit(solution)/shard_map/dot_general | solution.py:167
  114.0 40.9 %while.29 = (s32[]{:T(128)}, f32[1024,128]{1,0:T(8,128)S(1)}, bf16[8,512,256]{2,1,0:T(8,128)(2,1)}, s32[8,512]{1,0:T(8,128)S(1)}, s32[8,512]{1,0:T(8,128)S(1)}, ...) while((s32[]{:T(128)}, f32[1024,128]{1,0:T(8,128)S(1)}, ...), condition=%wide.region_10.11_spmd.clone, body=%wide.region_9.10_spmd.clone.sunk | while | flops 677642240 | bytes 14342807 | solution.py:243
  114.0 1.0 dynamic-slice_bitcast_fusion.5
  119.1 1.0 dynamic-slice_bitcast_fusion.5
  124.2 1.0 dynamic-slice_bitcast_fusion.5
  129.4 1.0 dynamic-slice_bitcast_fusion.5
  134.5 1.0 dynamic-slice_bitcast_fusion.5
  139.6 1.0 dynamic-slice_bitcast_fusion.5
  144.7 1.0 dynamic-slice_bitcast_fusion.5
  149.8 1.0 dynamic-slice_bitcast_fusion.5
  154.9 3.9 %all-to-all-start.1 = ((bf16[16,256,256]{2,1,0:T(8,128)(2,1)}), bf16[16,256,256]{2,1,0:T(8,128)(2,1)S(1)}, u32[]{:S(2)}, u32[]{:S(2)}) async-start(bf16[16,256,256]{2,1,0:T(8,128)(2,1)} %bitcast.107), calls=%async_computation.1 | async-start | bytes 4194304 | tf_op jit(solution)/shard_map/all_to_all | solution.py:36
  159.6 2.4 %fusion.38 = bf16[1024,128]{1,0:T(8,128)(2,1)S(1)} fusion(f32[1024,64]{1,0:T(8,128)S(1)} %get-tuple-element.268, f32[1024,64]{1,0:T(8,128)S(1)} %get-tuple-element.267, f32[1024,128]{1,0:T(8,128)S(1)} %get-tuple-element.128, f32[1024,64]{1,0:T(8,128)S(1)} %broadcast_multiply_fusion), kind=kLoop, calls=%fused_computation.55 | loop fusion | flops 786432 | bytes 1572864 | tf_op jit(solution)/shard_map/convert_element_type | solution.py:250
  162.2 1.9 collective-permute-start.1
  164.1 45.7 %all-to-all-done.1 = bf16[16,256,256]{2,1,0:T(8,128)(2,1)S(1)} async-done(((bf16[16,256,256]{2,1,0:T(8,128)(2,1)}), bf16[16,256,256]{2,1,0:T(8,128)(2,1)S(1)}, u32[]{:S(2)}, u32[]{:S(2)}) %all-to-all-start.1) | async-done | bytes 2097184 | tf_op jit(solution)/shard_map/all_to_all | solution.py:36
  210.8 2.3 collective-permute-start.2
  213.1 4.4 %collective-permute-done.2 = bf16[256,256]{1,0:T(8,128)(2,1)S(1)} collective-permute-done((bf16[256,256]{1,0:T(8,128)(2,1)S(1)}, bf16[256,256]{1,0:T(8,128)(2,1)S(1)}, u32[]{:S(2)}, u32[]{:S(2)}) %collective-permute-start.2) | collective-permute-done | bytes 131104 | tf_op jit(solution)/shard_map/ppermute | solution.py:25
  217.5 0.8 pad_maximum_fusion.1.grad_ref
  218.3 9.1 %shard_map.73 = bf16[256,8192]{1,0:T(8,128)(2,1)} custom-call(bf16[256,768]{1,0:T(8,128)(2,1)} %pad_maximum_fusion.1.grad_ref, bf16[8192,768]{1,0:T(8,128)(2,1)} %all-gather.4.cloned.1.call-done.weight_ref, bf16[256,8192]{1,0:T(8,128)(2,1)} %collective-permute-done.4.base_ref), custom_call_target="tpu_custom_call" | custom-call | flops 3221225472 | bytes 21364736 | tf_op jit(solution)/shard_map/pallas_call | solution.py:50
  (267 shorter events, 56.9 us)
Async XLA Ops:
  6.5 99.9 %all-gather.6.cloned.1.call-start = ((), (), s32[]{:S(2)}) async-start(), calls=%async_computation.3 | async-start | bytes 8912896 | tf_op jit(solution)/shard_map/all_gather | solution.py:169
  9.7 7.8 %copy-start.3 = (bf16[1,256,512]{2,1,0:T(8,128)(2,1)S(1)}, bf16[1,256,512]{2,1,0:T(8,128)(2,1)}, u32[]{:S(2)}) copy-start(bf16[1,256,512]{2,1,0:T(8,128)(2,1)} %param.12) | copy-start | bytes 786436
  9.7 14.2 %copy-start.4 = (s32[1,32]{1,0:T(1,128)S(1)}, s32[1,32]{1,0:T(1,128)}, u32[]{:S(2)}) copy-start(s32[1,32]{1,0:T(1,128)} %param.17) | copy-start | bytes 388
  9.7 16.1 %copy-start.5 = (s32[1,8]{1,0:T(1,128)S(1)}, s32[1,8]{1,0:T(1,128)}, u32[]{:S(2)}) copy-start(s32[1,8]{1,0:T(1,128)} %param.16) | copy-start | bytes 100
  9.7 46.6 %all-to-all-start = ((bf16[16,256,256]{2,1,0:T(8,128)(2,1)}), bf16[16,256,256]{2,1,0:T(8,128)(2,1)S(1)}, u32[]{:S(2)}, u32[]{:S(2)}) async-start(bf16[16,256,256]{2,1,0:T(8,128)(2,1)} %broadcast_in_dim.79), calls=%async_computation | async-start | bytes 4194304 | tf_op jit(solution)/shard_map/all_to_all | solution.py:31
  17.4 200.9 %all-gather.4.cloned.1.call-start = ((), (), s32[]{:S(2)}) async-start(), calls=%async_computation.2 | async-start | bytes 13369344 | tf_op jit(solution)/shard_map/all_gather | solution.py:166
  17.5 29.0 %collective-permute-start = (bf16[128,512]{1,0:T(8,128)(2,1)S(1)}, bf16[128,512]{1,0:T(8,128)(2,1)S(1)}, u32[]{:S(2)}, u32[]{:S(2)}) collective-permute-start(bf16[128,512]{1,0:T(8,128)(2,1)S(1)} %get-tuple-element.272), channel_id=1, source_target_pairs={{0,8},{1,9},{2,10},{3,11},{4,12},{5,13},{6,14},{7,15},{8,0},{9,1},... | collective-permute-start | bytes 393224 | tf_op jit(solution)/shard_map/ppermute | solution.py:19
  20.5 27.2 %collective-permute-start.3 = (bf16[512,768]{1,0:T(8,128)(2,1)}, bf16[512,768]{1,0:T(8,128)(2,1)}, u32[]{:S(2)}, u32[]{:S(2)}) collective-permute-start(bf16[512,768]{1,0:T(8,128)(2,1)} %bitcast.120), channel_id=1, source_target_pairs={{16,0},{32,16},{48,32},{64,48},{80,64},{96,80},{112,96},{17,1},{33... | collective-permute-start | bytes 2359304 | tf_op jit(solution)/shard_map/ppermute | solution.py:25
  60.4 1.0 copy-start
  63.0 0.8 copy-start.1
  65.9 1.0 copy-start
  68.6 0.8 copy-start.1
  71.4 1.1 copy-start
  74.1 0.8 copy-start.1
  77.0 1.1 copy-start
  79.7 0.8 copy-start.1
  82.5 1.1 copy-start
  85.2 0.8 copy-start.1
  88.0 1.1 copy-start
  90.7 0.8 copy-start.1
  93.6 1.0 copy-start
  96.2 0.8 copy-start.1
  99.1 1.0 copy-start
  101.7 0.8 copy-start.1
  102.5 115.8 %collective-permute-start.4 = (bf16[256,8192]{1,0:T(8,128)(2,1)}, bf16[256,8192]{1,0:T(8,128)(2,1)}, u32[]{:S(2)}, u32[]{:S(2)}) collective-permute-start(bf16[256,8192]{1,0:T(8,128)(2,1)} %bitcast.119), channel_id=1, source_target_pairs={{16,0},{32,16},{48,32},{64,48},{80,64},{96,80},{112,96},{17,1},{33... | collective-permute-start | bytes 12582920 | tf_op jit(solution)/shard_map/ppermute | solution.py:25
  106.4 7.2 %copy-start.2 = (f32[1024,128]{1,0:T(8,128)S(1)}, f32[1024,128]{1,0:T(8,128)}, u32[]{:S(2)}) copy-start(f32[1024,128]{1,0:T(8,128)} %get-tuple-element.127) | copy-start | bytes 1572868
  154.9 54.8 %all-to-all-start.1 = ((bf16[16,256,256]{2,1,0:T(8,128)(2,1)}), bf16[16,256,256]{2,1,0:T(8,128)(2,1)S(1)}, u32[]{:S(2)}, u32[]{:S(2)}) async-start(bf16[16,256,256]{2,1,0:T(8,128)(2,1)} %bitcast.107), calls=%async_computation.1 | async-start | bytes 4194304 | tf_op jit(solution)/shard_map/all_to_all | solution.py:36
  162.2 50.9 %collective-permute-start.1 = (bf16[256,512]{1,0:T(8,128)(2,1)S(1)}, bf16[256,512]{1,0:T(8,128)(2,1)S(1)}, u32[]{:S(2)}, u32[]{:S(2)}) collective-permute-start(bf16[256,512]{1,0:T(8,128)(2,1)S(1)} %convert_element_type.67), channel_id=1, source_target_pairs={{16,0},{32,16},{48,32},{64,48},{80,64},{96,80},{112,96},{17,1},{33... | collective-permute-start | bytes 786440 | tf_op jit(solution)/shard_map/ppermute | solution.py:25
  210.8 6.7 %collective-permute-start.2 = (bf16[256,256]{1,0:T(8,128)(2,1)S(1)}, bf16[256,256]{1,0:T(8,128)(2,1)S(1)}, u32[]{:S(2)}, u32[]{:S(2)}) collective-permute-start(bf16[256,256]{1,0:T(8,128)(2,1)S(1)} %pad_maximum_fusion.5), channel_id=1, source_target_pairs={{16,0},{32,16},{48,32},{64,48},{80,64},{96,80},{112,96},{17,1},{33... | collective-permute-start | bytes 393224 | tf_op jit(solution)/shard_map/ppermute | solution.py:25
Sparse Core Ops, SparseCore 0:
  9.5 91.7 all-gather.5
  103.5 112.0 all-gather.3

commit v8 on v7

--- a/solution.py
+++ b/solution.py
@@ -63,6 +63,43 @@
             transcendentals=0,
         ),
     )(grad_rows, weight, base)
+
+
+RING_OFFSETS = (0, -1, 1, -2)
+RING_INDEX_OF_DELTA = (0, 2, 3, 1)
+
+
+def ring_shift(value, phase, step, side):
+    pairs = []
+    for source in range(side * side):
+        row, col = divmod(source, side)
+        if phase == 0:
+            target = row * side + (col + step) % side
+        else:
+            target = ((row + step) % side) * side + col
+        pairs.append((source, target))
+    return lax.ppermute(value, "ctx", pairs)
+
+
+def ring_four(value, phase, side):
+    from_left = ring_shift(value, phase, 1, side)
+    from_right = ring_shift(value, phase, -1, side)
+    from_far = ring_shift(from_left, phase, 1, side)
+    return jnp.stack([value, from_left, from_right, from_far])
+
+
+def ring_gather(value, first_phase, side):
+    inner = ring_four(value, first_phase, side)
+    return ring_four(inner, 1 - first_phase, side).reshape((side * side,) + value.shape)
+
+
+def ring_position(device, source, first_phase, side):
+    index_of_delta = jnp.asarray(RING_INDEX_OF_DELTA, jnp.int32)
+    row_delta = index_of_delta[(source // side - device // side) % side]
+    col_delta = index_of_delta[(source % side - device % side) % side]
+    if first_phase == 0:
+        return row_delta * side + col_delta
+    return col_delta * side + row_delta
 
 
 def rope_tables(positions, head_dim):
@@ -171,12 +208,28 @@
     ).astype(jnp.bfloat16)
     local_out_grad = out_grad
     seq_query = stored_to_seq(stored_query, block_order, device, ctx_size, per_device)
-    gathered = gathered_rows(stored_keyval, "ctx")
+    side = math.isqrt(ctx_size)
+    slot_ids = jnp.arange(block_count, dtype=jnp.int32)
+    if side == len(RING_OFFSETS) and per_device == 2:
+        gathered = jnp.concatenate(
+            [
+                ring_gather(stored_keyval[:BLOCK], 0, side),
+                ring_gather(stored_keyval[BLOCK:], 1, side),
+            ]
+        ).reshape(seq_len, 2 * head_dim)
+        holder = slot_ids // per_device
+        slot_place = jnp.where(
+            slot_ids % per_device == 0,
+            ring_position(device, holder, 0, side),
+            ctx_size + ring_position(device, holder, 1, side),
+        )
+    else:
+        gathered = gathered_rows(stored_keyval, "ctx")
+        slot_place = slot_ids
     gathered, grad_source = lax.optimization_barrier((gathered, section_grad_in))
     next_grad_in = passed_along_2(grad_source, "pipe", -1)
-    slot_ids = jnp.arange(block_count, dtype=jnp.int32)
     inverse = jnp.sum(
-        jnp.where(block_order[None, :] == slot_ids[:, None], slot_ids[None, :], 0), axis=1
+        jnp.where(block_order[None, :] == slot_ids[:, None], slot_place[None, :], 0), axis=1
     )
     all_keyval = gathered.reshape(block_count, BLOCK, 2 * head_dim)[inverse].reshape(
         seq_len, 2 * head_dim

time: 235 us -> 230 us (0.979)
  waiting for transfers between devices: 79.2 us -> 67.8 us
  starting transfers between devices: 26.1 us -> 29.5 us
  other arithmetic: 11 us -> 14 us
    ppermute x0 -> x12, waiting for transfers between devices: none -> 20.7 us  [ring_shift(): return lax.ppermute(value, 'ctx', pairs)]
    ppermute x1, waiting for transfers between devices: 19.8 us -> 0.01 us  [passed_along(): return lax.ppermute(value, axis, pairs)]
    ppermute x0 -> x12, starting transfers between devices: none -> 11.8 us  [ring_shift(): return lax.ppermute(value, 'ctx', pairs)]
    all_to_all x1 -> x0, waiting for transfers between devices: 8.63 us -> none  [gathered_rows(): lax.all_to_all(spread, axis, 0, 0, tiled=False)]
    all_to_all x1 -> x0, starting transfers between devices: 7.72 us -> none  [gathered_rows(): lax.all_to_all(spread, axis, 0, 0, tiled=False)]
    all_to_all x1, waiting for transfers between devices: 45.7 us -> 42.4 us  [summed_rows(): lax.all_to_all(value.reshape((count, -1) + value.shape[1:]), axis, 0, 0,...]
    broadcast_in_dim x1 -> x0, local copies, waits for them, and re-layouts: 2.43 us -> none  [gathered_rows(): spread = jnp.broadcast_to(value[None], (count,) + value.shape)]
  transfers between devices with their start and end apart: 9 -> 20, of which waited for: 4 -> 7; matrix products, arithmetic and copies ran while one was open for 40% -> 42% of each run, Pallas kernels for 0% -> 0%
where the time goes in v8:
time: 230 us; the launch traced here: 229 us
  waiting for transfers between devices  67.8 us (29%)
  matrix products  47.7 us (21%)
  local copies, waits for them, and re-layouts  44.4 us (19%)
  starting transfers between devices  29.5 us (13%)
  between operations  15.1 us (7%)
  other arithmetic  14 us (6%)
  Pallas kernels  9.08 us (4%)
    all_to_all x1, waiting for transfers between devices, summed_rows(): lax.all_to_all(value.reshape((count, -1) + value.shape[1:]), axis, 0, 0,...  42.4 us
    ppermute x12, waiting for transfers between devices, ring_shift(): return lax.ppermute(value, 'ctx', pairs)  20.7 us
    squeeze x16, local copies, waits for them, and re-layouts, body(): lax.scan(running_total, start_carry, key_blocks)  15.7 us
    dot_general x24, matrix products, contract_cols(): lax.dot_general(left_rows, right_rows, (((1,), (1,)), ((), ())), preferre...  14.3 us
    dot_general x8, matrix products, running_total(): jnp.dot(weights, value_wide, precision=lax.Precision.HIGH)  12.8 us
    ppermute x4, starting transfers between devices, passed_along_2(): return lax.ppermute(value, axis, pairs)  11.8 us
    ppermute x12, starting transfers between devices, ring_shift(): return lax.ppermute(value, 'ctx', pairs)  11.8 us
    while x40, local copies, waits for them, and re-layouts  9.23 us
  transfers between devices with their start and end apart: 20, of which 7 were waited for; matrix products, arithmetic and copies ran while one was open for 42% of the time, Pallas kernels for 0%

profile of v8, /device:TPU:1, one launch (start us, length us, event | category | flops | bytes accessed | tf_op | source)
XLA Modules:
  0.0 229.0 jit_solution(6490541793615795723)
XLA Ops:
  8.2 2.1 collective-permute-start
  10.3 1.3 collective-permute-start.1
  11.7 1.4 collective-permute-start.6
  13.1 1.4 collective-permute-start.7
  14.5 1.0 fusion.55
  15.5 1.7 collective-permute-start.12
  19.2 4.2 %collective-permute-start.15 = (bf16[512,768]{1,0:T(8,128)(2,1)}, bf16[512,768]{1,0:T(8,128)(2,1)}, u32[]{:S(2)}, u32[]{:S(2)}) collective-permute-start(bf16[512,768]{1,0:T(8,128)(2,1)} %bitcast.159), channel_id=1, source_target_pairs={{16,0},{32,16},{48,32},{64,48},{80,64},{96,80},{112,96},{17,1},{33... | collective-permute-start | bytes 2359304 | tf_op jit(solution)/shard_map/ppermute | solution.py:25
  24.6 5.6 %collective-permute-done.8 = bf16[128,256]{1,0:T(8,128)(2,1)S(1)} collective-permute-done((bf16[128,256]{1,0:T(8,128)(2,1)S(1)}, bf16[128,256]{1,0:T(8,128)(2,1)S(1)}, u32[]{:S(2)}, u32[]{:S(2)}) %collective-permute-start.8) | collective-permute-done | bytes 65568 | tf_op jit(solution)/shard_map/ppermute | solution.py:81
  30.2 1.3 collective-permute-start.9
  33.6 7.5 %collective-permute-done.3 = bf16[4,128,256]{2,1,0:T(8,128)(2,1)S(1)} collective-permute-done((bf16[4,128,256]{2,1,0:T(8,128)(2,1)S(1)}, bf16[4,128,256]{2,1,0:T(8,128)(2,1)S(1)}, u32[]{:S(2)}, u32[]{:S(2)}) %collective-permute-start.3) | collective-permute-done | bytes 262176 | tf_op jit(solution)/shard_map/ppermute | solution.py:81
  41.4 2.9 %collective-permute-start.10 = (bf16[4,128,256]{2,1,0:T(8,128)(2,1)S(1)}, bf16[4,128,256]{2,1,0:T(8,128)(2,1)}, u32[]{:S(2)}, u32[]{:S(2)}) collective-permute-start(bf16[4,128,256]{2,1,0:T(8,128)(2,1)S(1)} %get-tuple-element.276), channel_id=1, source_target_pairs={{0,3},{1,0},{2,1},{3,2},{4,7},{5,4},{6,5},{7,6},{8,11},{9,8},{10,9... | collective-permute-start | bytes 786440 | tf_op jit(solution)/shard_map/ppermute | solution.py:81
  45.5 3.3 %collective-permute-done.5 = bf16[4,128,256]{2,1,0:T(8,128)(2,1)S(1)} collective-permute-done((bf16[4,128,256]{2,1,0:T(8,128)(2,1)S(1)}, bf16[4,128,256]{2,1,0:T(8,128)(2,1)S(1)}, u32[]{:S(2)}, u32[]{:S(2)}) %collective-permute-start.5) | collective-permute-done | bytes 262176 | tf_op jit(solution)/shard_map/ppermute | solution.py:81
  49.8 3.5 %collective-permute-done.11 = bf16[4,128,256]{2,1,0:T(8,128)(2,1)} collective-permute-done((bf16[4,128,256]{2,1,0:T(8,128)(2,1)S(1)}, bf16[4,128,256]{2,1,0:T(8,128)(2,1)}, u32[]{:S(2)}, u32[]{:S(2)}) %collective-permute-start.11) | collective-permute-done | bytes 262176 | tf_op jit(solution)/shard_map/ppermute | solution.py:81
  53.3 1.2 pad_maximum_fusion.2
  54.6 2.1 gather_fusion
  56.7 44.1 %while.28 = (s32[]{:T(128)}, f32[1024]{0:T(1024)S(1)}, f32[1024]{0:T(1024)S(1)}, f32[1024,128]{1,0:T(8,128)}, s32[8,512]{1,0:T(8,128)S(1)}, /*index=5*/s32[8,512...) while((s32[]{:T(128)}, f32[1024]{0:T(1024)S(1)}, ...), condition=%wide.region_7.8_spmd.clone, body=%wide.region_4.7_spmd.clone.sunk | while | flops 547230720 | bytes 12720321 | solution.py:274
  56.8 1.0 dynamic-slice_bitcast_fusion.4
  59.9 1.6 convolution_add_fusion.4
  62.3 1.0 dynamic-slice_bitcast_fusion.4
  65.4 1.6 convolution_add_fusion.4
  67.8 1.0 dynamic-slice_bitcast_fusion.4
  70.9 1.6 convolution_add_fusion.4
  73.3 1.0 dynamic-slice_bitcast_fusion.4
  76.4 1.6 convolution_add_fusion.4
  78.8 1.0 dynamic-slice_bitcast_fusion.4
  81.9 1.6 convolution_add_fusion.4
  84.4 1.0 dynamic-slice_bitcast_fusion.4
  87.4 1.6 convolution_add_fusion.4
  89.8 1.0 dynamic-slice_bitcast_fusion.4
  92.9 1.6 convolution_add_fusion.4
  95.4 1.0 dynamic-slice_bitcast_fusion.4
  98.4 1.6 convolution_add_fusion.4
  100.8 3.4 %collective-permute-start.16 = (bf16[256,8192]{1,0:T(8,128)(2,1)}, bf16[256,8192]{1,0:T(8,128)(2,1)}, u32[]{:S(2)}, u32[]{:S(2)}) collective-permute-start(bf16[256,8192]{1,0:T(8,128)(2,1)} %bitcast.158), channel_id=1, source_target_pairs={{16,0},{32,16},{48,32},{64,48},{80,64},{96,80},{112,96},{17,1},{33... | collective-permute-start | bytes 12582920 | tf_op jit(solution)/shard_map/ppermute | solution.py:25
  104.3 7.2 %fusion.34 = bf16[256,512]{1,0:T(8,128)(2,1)S(1)} fusion(bf16[1,8192,512]{2,1,0:T(8,128)(2,1)} %all-gather.6.cloned.1.call-done, bf16[1,256,8192]{2,1,0:T(8,128)(2,1)} %param.13), kind=kOutput, calls=%fused_computation.52 | convolution fusion | flops 2147614720 | bytes 12845056 | tf_op jit(solution)/shard_map/dot_general | solution.py:204
  112.0 41.2 %while.29 = (s32[]{:T(128)}, f32[1024,128]{1,0:T(8,128)S(1)}, bf16[8,512,256]{2,1,0:T(8,128)(2,1)}, s32[8,512]{1,0:T(8,128)S(1)}, s32[8,512]{1,0:T(8,128)S(1)}, ...) while((s32[]{:T(128)}, f32[1024,128]{1,0:T(8,128)S(1)}, ...), condition=%wide.region_10.11_spmd.clone, body=%wide.region_9.10_spmd.clone.sunk | while | flops 677642240 | bytes 14342807 | solution.py:296
  112.0 1.0 dynamic-slice_bitcast_fusion.5
  117.1 1.0 dynamic-slice_bitcast_fusion.5
  122.3 1.0 dynamic-slice_bitcast_fusion.5
  127.4 1.0 dynamic-slice_bitcast_fusion.5
  142.9 1.0 dynamic-slice_bitcast_fusion.5
  148.0 1.0 dynamic-slice_bitcast_fusion.5
  153.2 4.1 %all-to-all-start = ((bf16[16,256,256]{2,1,0:T(8,128)(2,1)}), bf16[16,256,256]{2,1,0:T(8,128)(2,1)S(1)}, u32[]{:S(2)}, u32[]{:S(2)}) async-start(bf16[16,256,256]{2,1,0:T(8,128)(2,1)} %bitcast.137), calls=%async_computation | async-start | bytes 4194304 | tf_op jit(solution)/shard_map/all_to_all | solution.py:36
  158.1 2.4 %fusion.38 = bf16[1024,128]{1,0:T(8,128)(2,1)S(1)} fusion(f32[1024,64]{1,0:T(8,128)S(1)} %get-tuple-element.268, f32[1024,64]{1,0:T(8,128)S(1)} %get-tuple-element.267, f32[1024,128]{1,0:T(8,128)S(1)} %get-tuple-element.128, f32[1024,64]{1,0:T(8,128)S(1)} %broadcast_multiply_fusion), kind=kLoop, calls=%fused_computation.58 | loop fusion | flops 786432 | bytes 1572864 | tf_op jit(solution)/shard_map/convert_element_type | solution.py:303
  160.7 1.9 collective-permute-start.13
  162.6 42.4 %all-to-all-done = bf16[16,256,256]{2,1,0:T(8,128)(2,1)S(1)} async-done(((bf16[16,256,256]{2,1,0:T(8,128)(2,1)}), bf16[16,256,256]{2,1,0:T(8,128)(2,1)S(1)}, u32[]{:S(2)}, u32[]{:S(2)}) %all-to-all-start) | async-done | bytes 2097184 | tf_op jit(solution)/shard_map/all_to_all | solution.py:36
  206.0 2.3 %collective-permute-start.14 = (bf16[256,256]{1,0:T(8,128)(2,1)S(1)}, bf16[256,256]{1,0:T(8,128)(2,1)S(1)}, u32[]{:S(2)}, u32[]{:S(2)}) collective-permute-start(bf16[256,256]{1,0:T(8,128)(2,1)S(1)} %pad_maximum_fusion.10), channel_id=1, source_target_pairs={{16,0},{32,16},{48,32},{64,48},{80,64},{96,80},{112,96},{17,1},{33... | collective-permute-start | bytes 393224 | tf_op jit(solution)/shard_map/ppermute | solution.py:25
  208.3 4.0 %collective-permute-done.14 = bf16[256,256]{1,0:T(8,128)(2,1)S(1)} collective-permute-done((bf16[256,256]{1,0:T(8,128)(2,1)S(1)}, bf16[256,256]{1,0:T(8,128)(2,1)S(1)}, u32[]{:S(2)}, u32[]{:S(2)}) %collective-permute-start.14) | collective-permute-done | bytes 131104 | tf_op jit(solution)/shard_map/ppermute | solution.py:25
  213.1 9.1 %shard_map.91 = bf16[256,8192]{1,0:T(8,128)(2,1)} custom-call(bf16[256,768]{1,0:T(8,128)(2,1)} %pad_maximum_fusion.4.grad_ref, bf16[8192,768]{1,0:T(8,128)(2,1)} %all-gather.4.cloned.1.call-done.weight_ref, bf16[256,8192]{1,0:T(8,128)(2,1)} %collective-permute-done.16.base_ref), custom_call_target="tpu_custom_call" | custom-call | flops 3221225472 | bytes 21364736 | tf_op jit(solution)/shard_map/pallas_call | solution.py:50
  (291 shorter events, 68.7 us)
Async XLA Ops:
  6.5 25.0 %copy-start.3 = (s32[1,32]{1,0:T(1,128)S(1)}, s32[1,32]{1,0:T(1,128)}, u32[]{:S(2)}) copy-start(s32[1,32]{1,0:T(1,128)} %param.19) | copy-start | bytes 388
  6.5 97.7 %all-gather.6.cloned.1.call-start = ((), (), s32[]{:S(2)}) async-start(), calls=%async_computation.2 | async-start | bytes 8912896 | tf_op jit(solution)/shard_map/all_gather | solution.py:206
  7.3 205.8 %all-gather.4.cloned.1.call-start = ((), (), s32[]{:S(2)}) async-start(), calls=%async_computation.1 | async-start | bytes 13369344 | tf_op jit(solution)/shard_map/all_gather | solution.py:203
  8.2 10.8 %collective-permute-start = (bf16[128,256]{1,0:T(8,128)(2,1)S(1)}, bf16[128,256]{1,0:T(8,128)(2,1)S(1)}, u32[]{:S(2)}, u32[]{:S(2)}) collective-permute-start(bf16[128,256]{1,0:T(8,128)(2,1)S(1)} %get-tuple-element.278), channel_id=1, source_target_pairs={{0,1},{1,2},{2,3},{3,0},{4,5},{5,6},{6,7},{7,4},{8,9},{9,10},{10,1... | collective-permute-start | bytes 196616 | tf_op jit(solution)/shard_map/ppermute | solution.py:81
  10.3 8.9 %collective-permute-start.1 = (bf16[128,256]{1,0:T(8,128)(2,1)S(1)}, bf16[128,256]{1,0:T(8,128)(2,1)S(1)}, u32[]{:S(2)}, u32[]{:S(2)}) collective-permute-start(bf16[128,256]{1,0:T(8,128)(2,1)S(1)} %get-tuple-element.278), channel_id=1, source_target_pairs={{0,3},{1,0},{2,1},{3,2},{4,7},{5,4},{6,5},{7,6},{8,11},{9,8},{10,9... | collective-permute-start | bytes 196616 | tf_op jit(solution)/shard_map/ppermute | solution.py:81
  11.7 11.8 %collective-permute-start.6 = (bf16[128,256]{1,0:T(8,128)(2,1)S(1)}, bf16[128,256]{1,0:T(8,128)(2,1)S(1)}, u32[]{:S(2)}, u32[]{:S(2)}) collective-permute-start(bf16[128,256]{1,0:T(8,128)(2,1)S(1)} %get-tuple-element.279), channel_id=1, source_target_pairs={{0,4},{1,5},{2,6},{3,7},{4,8},{5,9},{6,10},{7,11},{8,12},{9,13},{1... | collective-permute-start | bytes 196616 | tf_op jit(solution)/shard_map/ppermute | solution.py:81
  13.1 11.5 %collective-permute-start.7 = (bf16[128,256]{1,0:T(8,128)(2,1)S(1)}, bf16[128,256]{1,0:T(8,128)(2,1)S(1)}, u32[]{:S(2)}, u32[]{:S(2)}) collective-permute-start(bf16[128,256]{1,0:T(8,128)(2,1)S(1)} %get-tuple-element.279), channel_id=1, source_target_pairs={{0,12},{1,13},{2,14},{3,15},{4,0},{5,1},{6,2},{7,3},{8,4},{9,5},{1... | collective-permute-start | bytes 196616 | tf_op jit(solution)/shard_map/ppermute | solution.py:81
  15.5 25.9 %collective-permute-start.12 = (bf16[128,512]{1,0:T(8,128)(2,1)S(1)}, bf16[128,512]{1,0:T(8,128)(2,1)S(1)}, u32[]{:S(2)}, u32[]{:S(2)}) collective-permute-start(bf16[128,512]{1,0:T(8,128)(2,1)S(1)} %get-tuple-element.272), channel_id=1, source_target_pairs={{0,8},{1,9},{2,10},{3,11},{4,12},{5,13},{6,14},{7,15},{8,0},{9,1},... | collective-permute-start | bytes 393224 | tf_op jit(solution)/shard_map/ppermute | solution.py:19
  19.0 4.9 %collective-permute-start.2 = (bf16[128,256]{1,0:T(8,128)(2,1)S(1)}, bf16[128,256]{1,0:T(8,128)(2,1)S(1)}, u32[]{:S(2)}, u32[]{:S(2)}) collective-permute-start(bf16[128,256]{1,0:T(8,128)(2,1)S(1)} %collective-permute-done), channel_id=1, source_target_pairs={{0,1},{1,2},{2,3},{3,0},{4,5},{5,6},{6,7},{7,4},{8,9},{9,10},{10,1... | collective-permute-start | bytes 196616 | tf_op jit(solution)/shard_map/ppermute | solution.py:81
  19.2 37.5 %collective-permute-start.15 = (bf16[512,768]{1,0:T(8,128)(2,1)}, bf16[512,768]{1,0:T(8,128)(2,1)}, u32[]{:S(2)}, u32[]{:S(2)}) collective-permute-start(bf16[512,768]{1,0:T(8,128)(2,1)} %bitcast.159), channel_id=1, source_target_pairs={{16,0},{32,16},{48,32},{64,48},{80,64},{96,80},{112,96},{17,1},{33... | collective-permute-start | bytes 2359304 | tf_op jit(solution)/shard_map/ppermute | solution.py:25
  23.5 6.7 %collective-permute-start.8 = (bf16[128,256]{1,0:T(8,128)(2,1)S(1)}, bf16[128,256]{1,0:T(8,128)(2,1)S(1)}, u32[]{:S(2)}, u32[]{:S(2)}) collective-permute-start(bf16[128,256]{1,0:T(8,128)(2,1)S(1)} %collective-permute-done.6), channel_id=1, source_target_pairs={{0,4},{1,5},{2,6},{3,7},{4,8},{5,9},{6,10},{7,11},{8,12},{9,13},{1... | collective-permute-start | bytes 196616 | tf_op jit(solution)/shard_map/ppermute | solution.py:81
  24.0 17.1 %collective-permute-start.3 = (bf16[4,128,256]{2,1,0:T(8,128)(2,1)S(1)}, bf16[4,128,256]{2,1,0:T(8,128)(2,1)S(1)}, u32[]{:S(2)}, u32[]{:S(2)}) collective-permute-start(bf16[4,128,256]{2,1,0:T(8,128)(2,1)S(1)} %get-tuple-element.274), channel_id=1, source_target_pairs={{0,4},{1,5},{2,6},{3,7},{4,8},{5,9},{6,10},{7,11},{8,12},{9,13},{1... | collective-permute-start | bytes 786440 | tf_op jit(solution)/shard_map/ppermute | solution.py:81
  30.2 14.3 %collective-permute-start.9 = (bf16[4,128,256]{2,1,0:T(8,128)(2,1)S(1)}, bf16[4,128,256]{2,1,0:T(8,128)(2,1)S(1)}, u32[]{:S(2)}, u32[]{:S(2)}) collective-permute-start(bf16[4,128,256]{2,1,0:T(8,128)(2,1)S(1)} %get-tuple-element.276), channel_id=1, source_target_pairs={{0,1},{1,2},{2,3},{3,0},{4,5},{5,6},{6,7},{7,4},{8,9},{9,10},{10,1... | collective-permute-start | bytes 786440 | tf_op jit(solution)/shard_map/ppermute | solution.py:81
  33.5 12.1 %collective-permute-start.4 = (bf16[4,128,256]{2,1,0:T(8,128)(2,1)S(1)}, bf16[4,128,256]{2,1,0:T(8,128)(2,1)S(1)}, u32[]{:S(2)}, u32[]{:S(2)}) collective-permute-start(bf16[4,128,256]{2,1,0:T(8,128)(2,1)S(1)} %get-tuple-element.274), channel_id=1, source_target_pairs={{0,12},{1,13},{2,14},{3,15},{4,0},{5,1},{6,2},{7,3},{8,4},{9,5},{1... | collective-permute-start | bytes 786440 | tf_op jit(solution)/shard_map/ppermute | solution.py:81
  41.1 7.7 %collective-permute-start.5 = (bf16[4,128,256]{2,1,0:T(8,128)(2,1)S(1)}, bf16[4,128,256]{2,1,0:T(8,128)(2,1)S(1)}, u32[]{:S(2)}, u32[]{:S(2)}) collective-permute-start(bf16[4,128,256]{2,1,0:T(8,128)(2,1)S(1)} %collective-permute-done.3), channel_id=1, source_target_pairs={{0,4},{1,5},{2,6},{3,7},{4,8},{5,9},{6,10},{7,11},{8,12},{9,13},{1... | collective-permute-start | bytes 786440 | tf_op jit(solution)/shard_map/ppermute | solution.py:81
  41.4 8.4 %collective-permute-start.10 = (bf16[4,128,256]{2,1,0:T(8,128)(2,1)S(1)}, bf16[4,128,256]{2,1,0:T(8,128)(2,1)}, u32[]{:S(2)}, u32[]{:S(2)}) collective-permute-start(bf16[4,128,256]{2,1,0:T(8,128)(2,1)S(1)} %get-tuple-element.276), channel_id=1, source_target_pairs={{0,3},{1,0},{2,1},{3,2},{4,7},{5,4},{6,5},{7,6},{8,11},{9,8},{10,9... | collective-permute-start | bytes 786440 | tf_op jit(solution)/shard_map/ppermute | solution.py:81
  44.5 8.8 %collective-permute-start.11 = (bf16[4,128,256]{2,1,0:T(8,128)(2,1)S(1)}, bf16[4,128,256]{2,1,0:T(8,128)(2,1)}, u32[]{:S(2)}, u32[]{:S(2)}) collective-permute-start(bf16[4,128,256]{2,1,0:T(8,128)(2,1)S(1)} %collective-permute-done.9), channel_id=1, source_target_pairs={{0,1},{1,2},{2,3},{3,0},{4,5},{5,6},{6,7},{7,4},{8,9},{9,10},{10,1... | collective-permute-start | bytes 786440 | tf_op jit(solution)/shard_map/ppermute | solution.py:81
  58.8 1.1 copy-start
  61.5 0.8 copy-start.1
  64.3 1.1 copy-start
  67.0 0.8 copy-start.1
  69.8 1.1 copy-start
  72.5 0.8 copy-start.1
  75.4 1.1 copy-start
  78.0 0.8 copy-start.1
  80.9 1.0 copy-start
  83.5 0.8 copy-start.1
  86.4 1.0 copy-start
  89.0 0.8 copy-start.1
  91.9 1.0 copy-start
  94.5 0.8 copy-start.1
  97.4 1.0 copy-start
  100.1 0.8 copy-start.1
  100.8 112.2 %collective-permute-start.16 = (bf16[256,8192]{1,0:T(8,128)(2,1)}, bf16[256,8192]{1,0:T(8,128)(2,1)}, u32[]{:S(2)}, u32[]{:S(2)}) collective-permute-start(bf16[256,8192]{1,0:T(8,128)(2,1)} %bitcast.158), channel_id=1, source_target_pairs={{16,0},{32,16},{48,32},{64,48},{80,64},{96,80},{112,96},{17,1},{33... | collective-permute-start | bytes 12582920 | tf_op jit(solution)/shard_map/ppermute | solution.py:25
  104.2 7.4 %copy-start.2 = (f32[1024,128]{1,0:T(8,128)S(1)}, f32[1024,128]{1,0:T(8,128)}, u32[]{:S(2)}) copy-start(f32[1024,128]{1,0:T(8,128)} %get-tuple-element.127) | copy-start | bytes 1572868
  153.2 51.8 %all-to-all-start = ((bf16[16,256,256]{2,1,0:T(8,128)(2,1)}), bf16[16,256,256]{2,1,0:T(8,128)(2,1)S(1)}, u32[]{:S(2)}, u32[]{:S(2)}) async-start(bf16[16,256,256]{2,1,0:T(8,128)(2,1)} %bitcast.137), calls=%async_computation | async-start | bytes 4194304 | tf_op jit(solution)/shard_map/all_to_all | solution.py:36
  160.7 47.6 %collective-permute-start.13 = (bf16[256,512]{1,0:T(8,128)(2,1)S(1)}, bf16[256,512]{1,0:T(8,128)(2,1)S(1)}, u32[]{:S(2)}, u32[]{:S(2)}) collective-permute-start(bf16[256,512]{1,0:T(8,128)(2,1)S(1)} %convert_element_type.67), channel_id=1, source_target_pairs={{16,0},{32,16},{48,32},{64,48},{80,64},{96,80},{112,96},{17,1},{33... | collective-permute-start | bytes 786440 | tf_op jit(solution)/shard_map/ppermute | solution.py:25
  206.0 6.3 %collective-permute-start.14 = (bf16[256,256]{1,0:T(8,128)(2,1)S(1)}, bf16[256,256]{1,0:T(8,128)(2,1)S(1)}, u32[]{:S(2)}, u32[]{:S(2)}) collective-permute-start(bf16[256,256]{1,0:T(8,128)(2,1)S(1)} %pad_maximum_fusion.10), channel_id=1, source_target_pairs={{16,0},{32,16},{48,32},{64,48},{80,64},{96,80},{112,96},{17,1},{33... | collective-permute-start | bytes 393224 | tf_op jit(solution)/shard_map/ppermute | solution.py:25
Sparse Core Ops, SparseCore 0:
  9.5 79.0 all-gather.5
  90.7 110.7 all-gather.3

commit v9 on v8

--- a/solution.py
+++ b/solution.py
@@ -91,6 +91,28 @@
 def ring_gather(value, first_phase, side):
     inner = ring_four(value, first_phase, side)
     return ring_four(inner, 1 - first_phase, side).reshape((side * side,) + value.shape)
+
+
+def ring_reduce(chunks, phase, device, side):
+    me = device % side if phase == 0 else device // side
+    rel = lax.dynamic_slice_in_dim(jnp.concatenate([chunks, chunks]), me, side, axis=0)
+    from_far = ring_shift(rel[2].astype(jnp.bfloat16), phase, 1, side)
+    from_right = ring_shift(rel[3].astype(jnp.bfloat16), phase, -1, side)
+    carried = (rel[1] + from_far.astype(jnp.float32)).astype(jnp.bfloat16)
+    from_left = ring_shift(carried, phase, 1, side)
+    return rel[0] + from_right.astype(jnp.float32) + from_left.astype(jnp.float32)
+
+
+def ring_scatter_sum(rows, device, side):
+    region = rows.shape[0] // (side * side)
+    width = rows.shape[1]
+    tiles = rows.reshape(side, side, region, width)
+    half = width // 2
+    first = ring_reduce(jnp.moveaxis(tiles[..., :half], 1, 0), 0, device, side)
+    first = ring_reduce(first, 1, device, side)
+    second = ring_reduce(tiles[..., half:], 1, device, side)
+    second = ring_reduce(second, 0, device, side)
+    return jnp.concatenate([first, second], axis=1)
 
 
 def ring_position(device, source, first_phase, side):
@@ -303,9 +325,12 @@
         .astype(jnp.bfloat16)
     )
     next_query_grad = passed_along_2(query_grad, "pipe", -1)
-    keyval_grad = summed_rows(
-        key_terms.reshape(seq_len, 2 * head_dim).astype(jnp.bfloat16), "ctx"
-    )
+    if side == len(RING_OFFSETS):
+        keyval_grad = ring_scatter_sum(key_terms.reshape(seq_len, 2 * head_dim), device, side)
+    else:
+        keyval_grad = summed_rows(
+            key_terms.reshape(seq_len, 2 * head_dim).astype(jnp.bfloat16), "ctx"
+        )
     key_grad = unrotate(keyval_grad[:, :head_dim], own_positions).astype(jnp.bfloat16)
     value_grad = keyval_grad[:, head_dim:].astype(jnp.bfloat16)
     next_keyval_grad = passed_along_2(

time: 230 us -> 235 us (1.022)
  waiting for transfers between devices: 67.8 us -> 50.3 us
  starting transfers between devices: 29.5 us -> 38.4 us
  other arithmetic: 14 us -> 21.1 us
  local copies, waits for them, and re-layouts: 44.4 us -> 49.5 us
    all_to_all x1 -> x0, waiting for transfers between devices: 42.4 us -> none  [summed_rows(): lax.all_to_all(value.reshape((count, -1) + value.shape[1:]), axis, 0, 0,...]
    ppermute x12 -> x24, waiting for transfers between devices: 20.7 us -> 43.9 us  [ring_shift(): return lax.ppermute(value, 'ctx', pairs)]
    ppermute x12 -> x24, starting transfers between devices: 11.8 us -> 22.1 us  [ring_shift(): return lax.ppermute(value, 'ctx', pairs)]
    all_to_all x1 -> x0, starting transfers between devices: 4.15 us -> none  [summed_rows(): lax.all_to_all(value.reshape((count, -1) + value.shape[1:]), axis, 0, 0,...]
    convert_element_type x0 -> x6, other arithmetic: none -> 2.88 us  [the longest x4 1.9 us: ring_reduce(): carried = (rel[1] + from_far.astype(jnp.float32)).astype(jnp.bfloat16)]
    transpose x0 -> x1, local copies, waits for them, and re-layouts: none -> 2.73 us  [ring_scatter_sum(): first = ring_reduce(jnp.moveaxis(tiles[..., :half], 1, 0), 0, device, side)]
    ppermute x4, starting transfers between devices: 11.8 us -> 14.5 us  [passed_along_2(): return lax.ppermute(value, axis, pairs)]
    while x40 -> x136, local copies, waits for them, and re-layouts: 9.23 us -> 9.56 us
  transfers between devices with their start and end apart: 20 -> 31, of which waited for: 7 -> 13; matrix products, arithmetic and copies ran while one was open for 42% -> 47% of each run, Pallas kernels for 0% -> 0%
where the time goes in v9:
time: 235 us; the launch traced here: 233 us
  waiting for transfers between devices  50.3 us (21%)
  local copies, waits for them, and re-layouts  49.5 us (21%)
  matrix products  47.5 us (20%)
  starting transfers between devices  38.4 us (16%)
  other arithmetic  21.1 us (9%)
  between operations  15.2 us (6%)
  Pallas kernels  9.08 us (4%)
    ppermute x24, waiting for transfers between devices, ring_shift(): return lax.ppermute(value, 'ctx', pairs)  43.9 us
    ppermute x24, starting transfers between devices, ring_shift(): return lax.ppermute(value, 'ctx', pairs)  22.1 us
    squeeze x16, local copies, waits for them, and re-layouts, body(): lax.scan(running_total, start_carry, key_blocks)  15.6 us
    ppermute x4, starting transfers between devices, passed_along_2(): return lax.ppermute(value, axis, pairs)  14.5 us
    dot_general x24, matrix products, contract_cols(): lax.dot_general(left_rows, right_rows, (((1,), (1,)), ((), ())), preferre...  14.3 us
    dot_general x8, matrix products, running_total(): jnp.dot(weights, value_wide, precision=lax.Precision.HIGH)  12.9 us
    while x136, local copies, waits for them, and re-layouts  9.56 us
    pallas_call x1, Pallas kernels, projected_sum(): pl.pallas_call(projection_kernel, grid=(width // tile,), in_specs=[pl.Blo...  9.08 us
  transfers between devices with their start and end apart: 31, of which 13 were waited for; matrix products, arithmetic and copies ran while one was open for 47% of the time, Pallas kernels for 0%

profile of v9, /device:TPU:1, one launch (start us, length us, event | category | flops | bytes accessed | tf_op | source)
XLA Modules:
  0.0 233.2 jit_solution(6878067993669082866)
XLA Ops:
  8.2 2.1 collective-permute-start
  10.3 1.3 collective-permute-start.1
  11.7 1.4 collective-permute-start.6
  13.1 1.4 collective-permute-start.7
  14.5 1.0 fusion.82
  15.5 1.7 collective-permute-start.12
  19.3 4.2 %collective-permute-start.27 = (bf16[512,768]{1,0:T(8,128)(2,1)}, bf16[512,768]{1,0:T(8,128)(2,1)}, u32[]{:S(2)}, u32[]{:S(2)}) collective-permute-start(bf16[512,768]{1,0:T(8,128)(2,1)} %bitcast.226), channel_id=1, source_target_pairs={{16,0},{32,16},{48,32},{64,48},{80,64},{96,80},{112,96},{17,1},{33... | collective-permute-start | bytes 2359304 | tf_op jit(solution)/shard_map/ppermute | solution.py:25
  24.7 5.5 %collective-permute-done.8 = bf16[128,256]{1,0:T(8,128)(2,1)S(1)} collective-permute-done((bf16[128,256]{1,0:T(8,128)(2,1)S(1)}, bf16[128,256]{1,0:T(8,128)(2,1)S(1)}, u32[]{:S(2)}, u32[]{:S(2)}) %collective-permute-start.8) | collective-permute-done | bytes 65568 | tf_op jit(solution)/shard_map/ppermute | solution.py:81
  30.2 1.3 collective-permute-start.9
  33.5 7.5 %collective-permute-done.3 = bf16[4,128,256]{2,1,0:T(8,128)(2,1)S(1)} collective-permute-done((bf16[4,128,256]{2,1,0:T(8,128)(2,1)S(1)}, bf16[4,128,256]{2,1,0:T(8,128)(2,1)S(1)}, u32[]{:S(2)}, u32[]{:S(2)}) %collective-permute-start.3) | collective-permute-done | bytes 262176 | tf_op jit(solution)/shard_map/ppermute | solution.py:81
  41.6 3.1 %collective-permute-start.10 = (bf16[4,128,256]{2,1,0:T(8,128)(2,1)S(1)}, bf16[4,128,256]{2,1,0:T(8,128)(2,1)}, u32[]{:S(2)}, u32[]{:S(2)}) collective-permute-start(bf16[4,128,256]{2,1,0:T(8,128)(2,1)S(1)} %get-tuple-element.290), channel_id=1, source_target_pairs={{0,3},{1,0},{2,1},{3,2},{4,7},{5,4},{6,5},{7,6},{8,11},{9,8},{10,9... | collective-permute-start | bytes 786440 | tf_op jit(solution)/shard_map/ppermute | solution.py:81
  45.9 2.8 %collective-permute-done.5 = bf16[4,128,256]{2,1,0:T(8,128)(2,1)} collective-permute-done((bf16[4,128,256]{2,1,0:T(8,128)(2,1)S(1)}, bf16[4,128,256]{2,1,0:T(8,128)(2,1)}, u32[]{:S(2)}, u32[]{:S(2)}) %collective-permute-start.5) | collective-permute-done | bytes 262176 | tf_op jit(solution)/shard_map/ppermute | solution.py:81
  48.7 1.1 pad_maximum_fusion.1
  50.1 3.5 %collective-permute-done.11 = bf16[4,128,256]{2,1,0:T(8,128)(2,1)} collective-permute-done((bf16[4,128,256]{2,1,0:T(8,128)(2,1)S(1)}, bf16[4,128,256]{2,1,0:T(8,128)(2,1)}, u32[]{:S(2)}, u32[]{:S(2)}) %collective-permute-start.11) | collective-permute-done | bytes 262176 | tf_op jit(solution)/shard_map/ppermute | solution.py:81
  53.6 1.2 pad_maximum_fusion.2
  54.9 2.0 gather_fusion
  57.0 44.3 %while.28 = (s32[]{:T(128)}, f32[1024]{0:T(1024)S(1)}, f32[1024]{0:T(1024)S(1)}, f32[1024,128]{1,0:T(8,128)}, s32[8,512]{1,0:T(8,128)S(1)}, /*index=5*/s32[8,512...) while((s32[]{:T(128)}, f32[1024]{0:T(1024)S(1)}, ...), condition=%wide.region_7.8_spmd.clone, body=%wide.region_4.7_spmd.clone.sunk | while | flops 547230720 | bytes 12720321 | solution.py:296
  60.1 1.6 convolution_add_fusion.4
  65.6 1.6 convolution_add_fusion.4
  71.2 1.6 convolution_add_fusion.4
  76.7 1.6 convolution_add_fusion.4
  82.2 1.6 convolution_add_fusion.4
  87.8 1.6 convolution_add_fusion.4
  93.3 1.6 convolution_add_fusion.4
  98.8 1.6 convolution_add_fusion.4
  101.2 3.5 %collective-permute-start.28 = (bf16[256,8192]{1,0:T(8,128)(2,1)}, bf16[256,8192]{1,0:T(8,128)(2,1)}, u32[]{:S(2)}, u32[]{:S(2)}) collective-permute-start(bf16[256,8192]{1,0:T(8,128)(2,1)} %bitcast.225), channel_id=1, source_target_pairs={{16,0},{32,16},{48,32},{64,48},{80,64},{96,80},{112,96},{17,1},{33... | collective-permute-start | bytes 12582920 | tf_op jit(solution)/shard_map/ppermute | solution.py:25
  104.8 7.2 %fusion.36 = bf16[256,512]{1,0:T(8,128)(2,1)S(1)} fusion(bf16[1,8192,512]{2,1,0:T(8,128)(2,1)} %all-gather.6.cloned.1.call-done, bf16[1,256,8192]{2,1,0:T(8,128)(2,1)} %param.13), kind=kOutput, calls=%fused_computation.58 | convolution fusion | flops 2147614720 | bytes 12845056 | tf_op jit(solution)/shard_map/dot_general | solution.py:226
  112.5 43.4 %while.29 = (s32[]{:T(128)}, f32[1024,128]{1,0:T(8,128)S(1)}, f32[8,512,256]{2,1,0:T(8,128)}, s32[8,512]{1,0:T(8,128)S(1)}, s32[8,512]{1,0:T(8,128)S(1)}, /*inde...) while((s32[]{:T(128)}, f32[1024,128]{1,0:T(8,128)S(1)}, ...), condition=%wide.region_10.11_spmd.clone, body=%wide.region_9.10_spmd.clone.sunk | while | flops 677249024 | bytes 16472895 | solution.py:318
  134.3 1.0 dynamic-slice_bitcast_fusion.5
  139.7 1.0 dynamic-slice_bitcast_fusion.5
  155.9 2.7 %slice_bitcast_fusion = (f32[4,4,256,128]{3,2,0,1:T(8,128)S(1)}, f32[4,4,256,128]{3,2,1,0:T(8,128)S(1)}) fusion(f32[4,4,256,256]{3,2,1,0:T(8,128)} %bitcast.203), kind=kLoop, calls=%fused_computation.55 | loop fusion | bytes 8388608 | tf_op jit(solution)/shard_map/transpose | solution.py:111
  160.9 2.8 %collective-permute-start.20 = (bf16[4,256,128]{2,1,0:T(8,128)(2,1)}, bf16[4,256,128]{2,1,0:T(8,128)(2,1)S(1)}, u32[]{:S(2)}, u32[]{:S(2)}) collective-permute-start(bf16[4,256,128]{2,1,0:T(8,128)(2,1)} %get-tuple-element.277), channel_id=1, source_target_pairs={{0,12},{1,13},{2,14},{3,15},{4,0},{5,1},{6,2},{7,3},{8,4},{9,5},{1... | collective-permute-start | bytes 786440 | tf_op jit(solution)/shard_map/ppermute | solution.py:81
  164.0 2.4 %fusion.50 = bf16[1024,128]{1,0:T(8,128)(2,1)S(1)} fusion(f32[1024,64]{1,0:T(8,128)S(1)} %get-tuple-element.280, f32[1024,64]{1,0:T(8,128)S(1)} %get-tuple-element.279, f32[1024,128]{1,0:T(8,128)S(1)} %get-tuple-element.128, f32[1024,64]{1,0:T(8,128)S(1)} %get-tuple-element.299), kind=kLoop, calls=%fused_computation.82 | loop fusion | flops 786432 | bytes 1572864 | tf_op jit(solution)/shard_map/convert_element_type | solution.py:325
  166.4 9.7 %collective-permute-done.21 = bf16[4,256,128]{2,1,0:T(8,128)(2,1)S(1)} collective-permute-done((bf16[4,256,128]{2,1,0:T(8,128)(2,1)S(1)}, bf16[4,256,128]{2,1,0:T(8,128)(2,1)S(1)}, u32[]{:S(2)}, u32[]{:S(2)}) %collective-permute-start.21) | collective-permute-done | bytes 262176 | tf_op jit(solution)/shard_map/ppermute | solution.py:81
  176.8 1.6 fusion.35
  178.6 1.9 collective-permute-start.13
  180.5 3.0 %collective-permute-start.14 = (bf16[4,256,128]{2,1,0:T(8,128)(2,1)}, bf16[4,256,128]{2,1,0:T(8,128)(2,1)S(1)}, u32[]{:S(2)}, u32[]{:S(2)}) collective-permute-start(bf16[4,256,128]{2,1,0:T(8,128)(2,1)} %get-tuple-element.275), channel_id=1, source_target_pairs={{0,3},{1,0},{2,1},{3,2},{4,7},{5,4},{6,5},{7,6},{8,11},{9,8},{10,9... | collective-permute-start | bytes 786440 | tf_op jit(solution)/shard_map/ppermute | solution.py:81
  183.6 1.1 fusion.46
  184.7 6.4 %collective-permute-done.22 = bf16[4,256,128]{2,1,0:T(8,128)(2,1)S(1)} collective-permute-done((bf16[4,256,128]{2,1,0:T(8,128)(2,1)}, bf16[4,256,128]{2,1,0:T(8,128)(2,1)S(1)}, u32[]{:S(2)}, u32[]{:S(2)}) %collective-permute-start.22) | collective-permute-done | bytes 262176 | tf_op jit(solution)/shard_map/ppermute | solution.py:81
  191.1 1.1 fusion.44
  192.9 1.3 collective-permute-done.16
  195.1 2.4 %collective-permute-start.17 = (bf16[256,128]{1,0:T(8,128)(2,1)S(1)}, bf16[256,128]{1,0:T(8,128)(2,1)S(1)}, u32[]{:S(2)}, u32[]{:S(2)}) collective-permute-start(bf16[256,128]{1,0:T(8,128)(2,1)S(1)} %get-tuple-element.281), channel_id=1, source_target_pairs={{0,12},{1,13},{2,14},{3,15},{4,0},{5,1},{6,2},{7,3},{8,4},{9,5},{1... | collective-permute-start | bytes 196616 | tf_op jit(solution)/shard_map/ppermute | solution.py:81
  199.1 1.5 collective-permute-done.23
  200.6 2.8 %collective-permute-done.25 = bf16[256,128]{1,0:T(8,128)(2,1)S(1)} collective-permute-done((bf16[256,128]{1,0:T(8,128)(2,1)S(1)}, bf16[256,128]{1,0:T(8,128)(2,1)S(1)}, u32[]{:S(2)}, u32[]{:S(2)}) %collective-permute-start.25) | collective-permute-done | bytes 65568 | tf_op jit(solution)/shard_map/ppermute | solution.py:81
  203.5 1.8 collective-permute-done.19
  206.0 4.9 %collective-permute-start.26 = (bf16[256,256]{1,0:T(8,128)(2,1)S(1)}, bf16[256,256]{1,0:T(8,128)(2,1)S(1)}, u32[]{:S(2)}, u32[]{:S(2)}) collective-permute-start(bf16[256,256]{1,0:T(8,128)(2,1)S(1)} %pad_maximum_fusion.10), channel_id=1, source_target_pairs={{16,0},{32,16},{48,32},{64,48},{80,64},{96,80},{112,96},{17,1},{33... | collective-permute-start | bytes 393224 | tf_op jit(solution)/shard_map/ppermute | solution.py:25
  210.9 5.6 %collective-permute-done.26 = bf16[256,256]{1,0:T(8,128)(2,1)S(1)} collective-permute-done((bf16[256,256]{1,0:T(8,128)(2,1)S(1)}, bf16[256,256]{1,0:T(8,128)(2,1)S(1)}, u32[]{:S(2)}, u32[]{:S(2)}) %collective-permute-start.26) | collective-permute-done | bytes 131104 | tf_op jit(solution)/shard_map/ppermute | solution.py:25
  217.3 9.1 %shard_map.91 = bf16[256,8192]{1,0:T(8,128)(2,1)} custom-call(bf16[256,768]{1,0:T(8,128)(2,1)} %pad_maximum_fusion.4.grad_ref, bf16[8192,768]{1,0:T(8,128)(2,1)} %all-gather.4.cloned.1.call-done.weight_ref, bf16[256,8192]{1,0:T(8,128)(2,1)} %collective-permute-done.28.base_ref), custom_call_target="tpu_custom_call" | custom-call | flops 3221225472 | bytes 21364736 | tf_op jit(solution)/shard_map/pallas_call | solution.py:50
  (429 shorter events, 87.1 us)
Async XLA Ops:
  6.5 25.0 %copy-start.10 = (s32[1,32]{1,0:T(1,128)S(1)}, s32[1,32]{1,0:T(1,128)}, u32[]{:S(2)}) copy-start(s32[1,32]{1,0:T(1,128)} %param.19) | copy-start | bytes 388
  6.5 98.2 %all-gather.6.cloned.1.call-start = ((), (), s32[]{:S(2)}) async-start(), calls=%async_computation.1 | async-start | bytes 8912896 | tf_op jit(solution)/shard_map/all_gather | solution.py:228
  7.3 210.0 %all-gather.4.cloned.1.call-start = ((), (), s32[]{:S(2)}) async-start(), calls=%async_computation | async-start | bytes 13369344 | tf_op jit(solution)/shard_map/all_gather | solution.py:225
  8.2 10.9 %collective-permute-start = (bf16[128,256]{1,0:T(8,128)(2,1)S(1)}, bf16[128,256]{1,0:T(8,128)(2,1)S(1)}, u32[]{:S(2)}, u32[]{:S(2)}) collective-permute-start(bf16[128,256]{1,0:T(8,128)(2,1)S(1)} %get-tuple-element.294), channel_id=1, source_target_pairs={{0,1},{1,2},{2,3},{3,0},{4,5},{5,6},{6,7},{7,4},{8,9},{9,10},{10,1... | collective-permute-start | bytes 196616 | tf_op jit(solution)/shard_map/ppermute | solution.py:81
  10.3 9.0 %collective-permute-start.1 = (bf16[128,256]{1,0:T(8,128)(2,1)S(1)}, bf16[128,256]{1,0:T(8,128)(2,1)S(1)}, u32[]{:S(2)}, u32[]{:S(2)}) collective-permute-start(bf16[128,256]{1,0:T(8,128)(2,1)S(1)} %get-tuple-element.294), channel_id=1, source_target_pairs={{0,3},{1,0},{2,1},{3,2},{4,7},{5,4},{6,5},{7,6},{8,11},{9,8},{10,9... | collective-permute-start | bytes 196616 | tf_op jit(solution)/shard_map/ppermute | solution.py:81
  11.7 11.9 %collective-permute-start.6 = (bf16[128,256]{1,0:T(8,128)(2,1)S(1)}, bf16[128,256]{1,0:T(8,128)(2,1)S(1)}, u32[]{:S(2)}, u32[]{:S(2)}) collective-permute-start(bf16[128,256]{1,0:T(8,128)(2,1)S(1)} %get-tuple-element.295), channel_id=1, source_target_pairs={{0,4},{1,5},{2,6},{3,7},{4,8},{5,9},{6,10},{7,11},{8,12},{9,13},{1... | collective-permute-start | bytes 196616 | tf_op jit(solution)/shard_map/ppermute | solution.py:81
  13.1 11.7 %collective-permute-start.7 = (bf16[128,256]{1,0:T(8,128)(2,1)S(1)}, bf16[128,256]{1,0:T(8,128)(2,1)S(1)}, u32[]{:S(2)}, u32[]{:S(2)}) collective-permute-start(bf16[128,256]{1,0:T(8,128)(2,1)S(1)} %get-tuple-element.295), channel_id=1, source_target_pairs={{0,12},{1,13},{2,14},{3,15},{4,0},{5,1},{6,2},{7,3},{8,4},{9,5},{1... | collective-permute-start | bytes 196616 | tf_op jit(solution)/shard_map/ppermute | solution.py:81
  15.5 26.0 %collective-permute-start.12 = (bf16[128,512]{1,0:T(8,128)(2,1)S(1)}, bf16[128,512]{1,0:T(8,128)(2,1)S(1)}, u32[]{:S(2)}, u32[]{:S(2)}) collective-permute-start(bf16[128,512]{1,0:T(8,128)(2,1)S(1)} %get-tuple-element.286), channel_id=1, source_target_pairs={{0,8},{1,9},{2,10},{3,11},{4,12},{5,13},{6,14},{7,15},{8,0},{9,1},... | collective-permute-start | bytes 393224 | tf_op jit(solution)/shard_map/ppermute | solution.py:19
  18.1 27.6 %copy-start.11 = (f32[64]{0:T(128)}, f32[64]{0:T(128)S(1)}, u32[]{:S(2)}) copy-start(f32[64]{0:T(128)S(1)} %negate_power_fusion) | copy-start | bytes 772
  19.2 4.9 %collective-permute-start.2 = (bf16[128,256]{1,0:T(8,128)(2,1)S(1)}, bf16[128,256]{1,0:T(8,128)(2,1)S(1)}, u32[]{:S(2)}, u32[]{:S(2)}) collective-permute-start(bf16[128,256]{1,0:T(8,128)(2,1)S(1)} %collective-permute-done), channel_id=1, source_target_pairs={{0,1},{1,2},{2,3},{3,0},{4,5},{5,6},{6,7},{7,4},{8,9},{9,10},{10,1... | collective-permute-start | bytes 196616 | tf_op jit(solution)/shard_map/ppermute | solution.py:81
  19.3 37.6 %collective-permute-start.27 = (bf16[512,768]{1,0:T(8,128)(2,1)}, bf16[512,768]{1,0:T(8,128)(2,1)}, u32[]{:S(2)}, u32[]{:S(2)}) collective-permute-start(bf16[512,768]{1,0:T(8,128)(2,1)} %bitcast.226), channel_id=1, source_target_pairs={{16,0},{32,16},{48,32},{64,48},{80,64},{96,80},{112,96},{17,1},{33... | collective-permute-start | bytes 2359304 | tf_op jit(solution)/shard_map/ppermute | solution.py:25
  23.6 6.6 %collective-permute-start.8 = (bf16[128,256]{1,0:T(8,128)(2,1)S(1)}, bf16[128,256]{1,0:T(8,128)(2,1)S(1)}, u32[]{:S(2)}, u32[]{:S(2)}) collective-permute-start(bf16[128,256]{1,0:T(8,128)(2,1)S(1)} %collective-permute-done.6), channel_id=1, source_target_pairs={{0,4},{1,5},{2,6},{3,7},{4,8},{5,9},{6,10},{7,11},{8,12},{9,13},{1... | collective-permute-start | bytes 196616 | tf_op jit(solution)/shard_map/ppermute | solution.py:81
  24.1 16.9 %collective-permute-start.3 = (bf16[4,128,256]{2,1,0:T(8,128)(2,1)S(1)}, bf16[4,128,256]{2,1,0:T(8,128)(2,1)S(1)}, u32[]{:S(2)}, u32[]{:S(2)}) collective-permute-start(bf16[4,128,256]{2,1,0:T(8,128)(2,1)S(1)} %get-tuple-element.288), channel_id=1, source_target_pairs={{0,4},{1,5},{2,6},{3,7},{4,8},{5,9},{6,10},{7,11},{8,12},{9,13},{1... | collective-permute-start | bytes 786440 | tf_op jit(solution)/shard_map/ppermute | solution.py:81
  30.2 14.6 %collective-permute-start.9 = (bf16[4,128,256]{2,1,0:T(8,128)(2,1)S(1)}, bf16[4,128,256]{2,1,0:T(8,128)(2,1)S(1)}, u32[]{:S(2)}, u32[]{:S(2)}) collective-permute-start(bf16[4,128,256]{2,1,0:T(8,128)(2,1)S(1)} %get-tuple-element.290), channel_id=1, source_target_pairs={{0,1},{1,2},{2,3},{3,0},{4,5},{5,6},{6,7},{7,4},{8,9},{9,10},{10,1... | collective-permute-start | bytes 786440 | tf_op jit(solution)/shard_map/ppermute | solution.py:81
  33.4 12.5 %collective-permute-start.4 = (bf16[4,128,256]{2,1,0:T(8,128)(2,1)S(1)}, bf16[4,128,256]{2,1,0:T(8,128)(2,1)S(1)}, u32[]{:S(2)}, u32[]{:S(2)}) collective-permute-start(bf16[4,128,256]{2,1,0:T(8,128)(2,1)S(1)} %get-tuple-element.288), channel_id=1, source_target_pairs={{0,12},{1,13},{2,14},{3,15},{4,0},{5,1},{6,2},{7,3},{8,4},{9,5},{1... | collective-permute-start | bytes 786440 | tf_op jit(solution)/shard_map/ppermute | solution.py:81
  41.0 7.7 %collective-permute-start.5 = (bf16[4,128,256]{2,1,0:T(8,128)(2,1)S(1)}, bf16[4,128,256]{2,1,0:T(8,128)(2,1)}, u32[]{:S(2)}, u32[]{:S(2)}) collective-permute-start(bf16[4,128,256]{2,1,0:T(8,128)(2,1)S(1)} %collective-permute-done.3), channel_id=1, source_target_pairs={{0,4},{1,5},{2,6},{3,7},{4,8},{5,9},{6,10},{7,11},{8,12},{9,13},{1... | collective-permute-start | bytes 786440 | tf_op jit(solution)/shard_map/ppermute | solution.py:81
  41.6 8.5 %collective-permute-start.10 = (bf16[4,128,256]{2,1,0:T(8,128)(2,1)S(1)}, bf16[4,128,256]{2,1,0:T(8,128)(2,1)}, u32[]{:S(2)}, u32[]{:S(2)}) collective-permute-start(bf16[4,128,256]{2,1,0:T(8,128)(2,1)S(1)} %get-tuple-element.290), channel_id=1, source_target_pairs={{0,3},{1,0},{2,1},{3,2},{4,7},{5,4},{6,5},{7,6},{8,11},{9,8},{10,9... | collective-permute-start | bytes 786440 | tf_op jit(solution)/shard_map/ppermute | solution.py:81
  44.9 8.7 %collective-permute-start.11 = (bf16[4,128,256]{2,1,0:T(8,128)(2,1)S(1)}, bf16[4,128,256]{2,1,0:T(8,128)(2,1)}, u32[]{:S(2)}, u32[]{:S(2)}) collective-permute-start(bf16[4,128,256]{2,1,0:T(8,128)(2,1)S(1)} %collective-permute-done.9), channel_id=1, source_target_pairs={{0,1},{1,2},{2,3},{3,0},{4,5},{5,6},{6,7},{7,4},{8,9},{9,10},{10,1... | collective-permute-start | bytes 786440 | tf_op jit(solution)/shard_map/ppermute | solution.py:81
  101.2 116.1 %collective-permute-start.28 = (bf16[256,8192]{1,0:T(8,128)(2,1)}, bf16[256,8192]{1,0:T(8,128)(2,1)}, u32[]{:S(2)}, u32[]{:S(2)}) collective-permute-start(bf16[256,8192]{1,0:T(8,128)(2,1)} %bitcast.225), channel_id=1, source_target_pairs={{16,0},{32,16},{48,32},{64,48},{80,64},{96,80},{112,96},{17,1},{33... | collective-permute-start | bytes 12582920 | tf_op jit(solution)/shard_map/ppermute | solution.py:25
  104.7 7.4 %copy-start.3 = (f32[1024,128]{1,0:T(8,128)S(1)}, f32[1024,128]{1,0:T(8,128)}, u32[]{:S(2)}) copy-start(f32[1024,128]{1,0:T(8,128)} %get-tuple-element.127) | copy-start | bytes 1572868
  134.2 2.2 copy-start.4
  134.2 2.2 copy-start.6
  134.2 2.2 copy-start.8
  139.7 2.2 copy-start.4
  139.7 2.2 copy-start.6
  139.7 2.2 copy-start.8
  145.1 2.2 copy-start.4
  145.1 2.2 copy-start.6
  145.1 2.2 copy-start.8
  150.5 2.2 copy-start.4
  150.5 2.2 copy-start.6
  150.5 2.2 copy-start.8
  159.6 20.9 %collective-permute-start.15 = (bf16[4,256,128]{2,1,0:T(8,128)(2,1)}, bf16[4,256,128]{2,1,0:T(8,128)(2,1)S(1)}, u32[]{:S(2)}, u32[]{:S(2)}) collective-permute-start(bf16[4,256,128]{2,1,0:T(8,128)(2,1)} %get-tuple-element.276), channel_id=1, source_target_pairs={{0,1},{1,2},{2,3},{3,0},{4,5},{5,6},{6,7},{7,4},{8,9},{9,10},{10,1... | collective-permute-start | bytes 786440 | tf_op jit(solution)/shard_map/ppermute | solution.py:81
  159.6 4.0 %copy-start.12 = (f32[64]{0:T(128)S(1)}, f32[64]{0:T(128)}, u32[]{:S(2)}) copy-start(f32[64]{0:T(128)} %copy-done.11) | copy-start | bytes 772
  160.1 16.0 %copy-start = (f32[4,4,256,128]{3,2,1,0:T(8,128)}, f32[4,4,256,128]{3,2,1,0:T(8,128)S(1)}, u32[]{:S(2)}) copy-start(f32[4,4,256,128]{3,2,1,0:T(8,128)S(1)} %get-tuple-element.266) | copy-start | bytes 6291460
  160.9 15.2 %collective-permute-start.21 = (bf16[4,256,128]{2,1,0:T(8,128)(2,1)S(1)}, bf16[4,256,128]{2,1,0:T(8,128)(2,1)S(1)}, u32[]{:S(2)}, u32[]{:S(2)}) collective-permute-start(bf16[4,256,128]{2,1,0:T(8,128)(2,1)S(1)} %get-tuple-element.278), channel_id=1, source_target_pairs={{0,4},{1,5},{2,6},{3,7},{4,8},{5,9},{6,10},{7,11},{8,12},{9,13},{1... | collective-permute-start | bytes 786440 | tf_op jit(solution)/shard_map/ppermute | solution.py:81
  160.9 23.8 %collective-permute-start.20 = (bf16[4,256,128]{2,1,0:T(8,128)(2,1)}, bf16[4,256,128]{2,1,0:T(8,128)(2,1)S(1)}, u32[]{:S(2)}, u32[]{:S(2)}) collective-permute-start(bf16[4,256,128]{2,1,0:T(8,128)(2,1)} %get-tuple-element.277), channel_id=1, source_target_pairs={{0,12},{1,13},{2,14},{3,15},{4,0},{5,1},{6,2},{7,3},{8,4},{9,5},{1... | collective-permute-start | bytes 786440 | tf_op jit(solution)/shard_map/ppermute | solution.py:81
  176.8 14.3 %collective-permute-start.22 = (bf16[4,256,128]{2,1,0:T(8,128)(2,1)}, bf16[4,256,128]{2,1,0:T(8,128)(2,1)S(1)}, u32[]{:S(2)}, u32[]{:S(2)}) collective-permute-start(bf16[4,256,128]{2,1,0:T(8,128)(2,1)} %fusion.42), channel_id=1, source_target_pairs={{0,4},{1,5},{2,6},{3,7},{4,8},{5,9},{6,10},{7,11},{8,12},{9,13},{1... | collective-permute-start | bytes 786440 | tf_op jit(solution)/shard_map/ppermute | solution.py:81
  178.6 32.3 %collective-permute-start.13 = (bf16[256,512]{1,0:T(8,128)(2,1)S(1)}, bf16[256,512]{1,0:T(8,128)(2,1)S(1)}, u32[]{:S(2)}, u32[]{:S(2)}) collective-permute-start(bf16[256,512]{1,0:T(8,128)(2,1)S(1)} %convert_element_type.139), channel_id=1, source_target_pairs={{16,0},{32,16},{48,32},{64,48},{80,64},{96,80},{112,96},{17,1},{33... | collective-permute-start | bytes 786440 | tf_op jit(solution)/shard_map/ppermute | solution.py:25
  180.5 12.3 %collective-permute-start.14 = (bf16[4,256,128]{2,1,0:T(8,128)(2,1)}, bf16[4,256,128]{2,1,0:T(8,128)(2,1)S(1)}, u32[]{:S(2)}, u32[]{:S(2)}) collective-permute-start(bf16[4,256,128]{2,1,0:T(8,128)(2,1)} %get-tuple-element.275), channel_id=1, source_target_pairs={{0,3},{1,0},{2,1},{3,2},{4,7},{5,4},{6,5},{7,6},{8,11},{9,8},{10,9... | collective-permute-start | bytes 786440 | tf_op jit(solution)/shard_map/ppermute | solution.py:81
  184.7 9.5 %collective-permute-start.16 = (bf16[4,256,128]{2,1,0:T(8,128)(2,1)S(1)}, bf16[4,256,128]{2,1,0:T(8,128)(2,1)S(1)}, u32[]{:S(2)}, u32[]{:S(2)}) collective-permute-start(bf16[4,256,128]{2,1,0:T(8,128)(2,1)S(1)} %fusion.46), channel_id=1, source_target_pairs={{0,1},{1,2},{2,3},{3,0},{4,5},{5,6},{6,7},{7,4},{8,9},{9,10},{10,1... | collective-permute-start | bytes 786440 | tf_op jit(solution)/shard_map/ppermute | solution.py:81
  192.4 5.1 %collective-permute-start.24 = (bf16[256,128]{1,0:T(8,128)(2,1)S(1)}, bf16[256,128]{1,0:T(8,128)(2,1)S(1)}, u32[]{:S(2)}, u32[]{:S(2)}) collective-permute-start(bf16[256,128]{1,0:T(8,128)(2,1)S(1)} %get-tuple-element.284), channel_id=1, source_target_pairs={{0,1},{1,2},{2,3},{3,0},{4,5},{5,6},{6,7},{7,4},{8,9},{9,10},{10,1... | collective-permute-start | bytes 196616 | tf_op jit(solution)/shard_map/ppermute | solution.py:81
  194.4 4.7 %collective-permute-start.18 = (bf16[256,128]{1,0:T(8,128)(2,1)S(1)}, bf16[256,128]{1,0:T(8,128)(2,1)S(1)}, u32[]{:S(2)}, u32[]{:S(2)}) collective-permute-start(bf16[256,128]{1,0:T(8,128)(2,1)S(1)} %get-tuple-element.282), channel_id=1, source_target_pairs={{0,4},{1,5},{2,6},{3,7},{4,8},{5,9},{6,10},{7,11},{8,12},{9,13},{1... | collective-permute-start | bytes 196616 | tf_op jit(solution)/shard_map/ppermute | solution.py:81
  195.1 8.4 %collective-permute-start.17 = (bf16[256,128]{1,0:T(8,128)(2,1)S(1)}, bf16[256,128]{1,0:T(8,128)(2,1)S(1)}, u32[]{:S(2)}, u32[]{:S(2)}) collective-permute-start(bf16[256,128]{1,0:T(8,128)(2,1)S(1)} %get-tuple-element.281), channel_id=1, source_target_pairs={{0,12},{1,13},{2,14},{3,15},{4,0},{5,1},{6,2},{7,3},{8,4},{9,5},{1... | collective-permute-start | bytes 196616 | tf_op jit(solution)/shard_map/ppermute | solution.py:81
  197.5 3.1 %collective-permute-start.23 = (bf16[256,128]{1,0:T(8,128)(2,1)S(1)}, bf16[256,128]{1,0:T(8,128)(2,1)S(1)}, u32[]{:S(2)}, u32[]{:S(2)}) collective-permute-start(bf16[256,128]{1,0:T(8,128)(2,1)S(1)} %get-tuple-element.283), channel_id=1, source_target_pairs={{0,3},{1,0},{2,1},{3,2},{4,7},{5,4},{6,5},{7,6},{8,11},{9,8},{10,9... | collective-permute-start | bytes 196616 | tf_op jit(solution)/shard_map/ppermute | solution.py:81
  199.1 4.3 %collective-permute-start.25 = (bf16[256,128]{1,0:T(8,128)(2,1)S(1)}, bf16[256,128]{1,0:T(8,128)(2,1)S(1)}, u32[]{:S(2)}, u32[]{:S(2)}) collective-permute-start(bf16[256,128]{1,0:T(8,128)(2,1)S(1)} %fusion.53), channel_id=1, source_target_pairs={{0,1},{1,2},{2,3},{3,0},{4,5},{5,6},{6,7},{7,4},{8,9},{9,10},{10,1... | collective-permute-start | bytes 196616 | tf_op jit(solution)/shard_map/ppermute | solution.py:81
  200.6 4.6 %collective-permute-start.19 = (bf16[256,128]{1,0:T(8,128)(2,1)S(1)}, bf16[256,128]{1,0:T(8,128)(2,1)S(1)}, u32[]{:S(2)}, u32[]{:S(2)}) collective-permute-start(bf16[256,128]{1,0:T(8,128)(2,1)S(1)} %fusion.58), channel_id=1, source_target_pairs={{0,4},{1,5},{2,6},{3,7},{4,8},{5,9},{6,10},{7,11},{8,12},{9,13},{1... | collective-permute-start | bytes 196616 | tf_op jit(solution)/shard_map/ppermute | solution.py:81
  206.0 10.5 %collective-permute-start.26 = (bf16[256,256]{1,0:T(8,128)(2,1)S(1)}, bf16[256,256]{1,0:T(8,128)(2,1)S(1)}, u32[]{:S(2)}, u32[]{:S(2)}) collective-permute-start(bf16[256,256]{1,0:T(8,128)(2,1)S(1)} %pad_maximum_fusion.10), channel_id=1, source_target_pairs={{16,0},{32,16},{48,32},{64,48},{80,64},{96,80},{112,96},{17,1},{33... | collective-permute-start | bytes 393224 | tf_op jit(solution)/shard_map/ppermute | solution.py:25
  (52 other events, 76.9 us)
Sparse Core Ops, SparseCore 0:
  9.5 78.9 all-gather.5
  90.6 99.6 all-gather.3

commit v10 on v9

--- a/solution.py
+++ b/solution.py
@@ -84,7 +84,7 @@
 def ring_four(value, phase, side):
     from_left = ring_shift(value, phase, 1, side)
     from_right = ring_shift(value, phase, -1, side)
-    from_far = ring_shift(from_left, phase, 1, side)
+    from_far = ring_shift(value, phase, 2, side)
     return jnp.stack([value, from_left, from_right, from_far])
 
 
@@ -96,11 +96,15 @@
 def ring_reduce(chunks, phase, device, side):
     me = device % side if phase == 0 else device // side
     rel = lax.dynamic_slice_in_dim(jnp.concatenate([chunks, chunks]), me, side, axis=0)
-    from_far = ring_shift(rel[2].astype(jnp.bfloat16), phase, 1, side)
+    from_left = ring_shift(rel[1].astype(jnp.bfloat16), phase, 1, side)
+    from_far = ring_shift(rel[2].astype(jnp.bfloat16), phase, 2, side)
     from_right = ring_shift(rel[3].astype(jnp.bfloat16), phase, -1, side)
-    carried = (rel[1] + from_far.astype(jnp.float32)).astype(jnp.bfloat16)
-    from_left = ring_shift(carried, phase, 1, side)
-    return rel[0] + from_right.astype(jnp.float32) + from_left.astype(jnp.float32)
+    return (
+        rel[0]
+        + from_right.astype(jnp.float32)
+        + from_far.astype(jnp.float32)
+        + from_left.astype(jnp.float32)
+    )
 
 
 def ring_scatter_sum(rows, device, side):

time: 235 us -> 242 us (1.030)
  starting transfers between devices: 38.4 us -> 59.2 us
  waiting for transfers between devices: 50.3 us -> 42.7 us
  other arithmetic: 21.1 us -> 15.8 us
    ppermute x24, starting transfers between devices: 22.1 us -> 39.3 us  [ring_shift(): return lax.ppermute(value, 'ctx', pairs)]
    ppermute x24, waiting for transfers between devices: 43.9 us -> 35.7 us  [ring_shift(): return lax.ppermute(value, 'ctx', pairs)]
    ppermute x4, starting transfers between devices: 14.5 us -> 19.7 us  [passed_along_2(): return lax.ppermute(value, axis, pairs)]
    convert_element_type x5 -> x0, other arithmetic: 2.86 us -> none  [the longest x4 1.9 us: ring_reduce(): carried = (rel[1] + from_far.astype(jnp.float32)).astype(jnp.bfloat16)]
  transfers between devices with their start and end apart: 31 -> 31, of which waited for: 13 -> 10; matrix products, arithmetic and copies ran while one was open for 47% -> 43% of each run, Pallas kernels for 0% -> 0%
where the time goes in v10:
time: 242 us; the launch traced here: 241 us
  starting transfers between devices  59.2 us (24%)
  local copies, waits for them, and re-layouts  48.9 us (20%)
  matrix products  48.1 us (20%)
  waiting for transfers between devices  42.7 us (18%)
  other arithmetic  15.8 us (7%)
  between operations  15.2 us (6%)
  Pallas kernels  9.07 us (4%)
    ppermute x24, starting transfers between devices, ring_shift(): return lax.ppermute(value, 'ctx', pairs)  39.3 us
    ppermute x24, waiting for transfers between devices, ring_shift(): return lax.ppermute(value, 'ctx', pairs)  35.7 us
    ppermute x4, starting transfers between devices, passed_along_2(): return lax.ppermute(value, axis, pairs)  19.7 us
    squeeze x16, local copies, waits for them, and re-layouts, body(): lax.scan(running_total, start_carry, key_blocks)  15.7 us
    dot_general x24, matrix products, contract_cols(): lax.dot_general(left_rows, right_rows, (((1,), (1,)), ((), ())), preferre...  14.2 us
    dot_general x8, matrix products, running_total(): jnp.dot(weights, value_wide, precision=lax.Precision.HIGH)  12.9 us
    while x136, local copies, waits for them, and re-layouts  9.6 us
    pallas_call x1, Pallas kernels, projected_sum(): pl.pallas_call(projection_kernel, grid=(width // tile,), in_specs=[pl.Blo...  9.07 us
  transfers between devices with their start and end apart: 31, of which 10 were waited for; matrix products, arithmetic and copies ran while one was open for 43% of the time, Pallas kernels for 0%

profile of v10, /device:TPU:1, one launch (start us, length us, event | category | flops | bytes accessed | tf_op | source)
XLA Modules:
  0.0 241.2 jit_solution(603656628722348333)
XLA Ops:
  8.2 2.1 collective-permute-start
  10.3 1.3 collective-permute-start.1
  11.7 1.6 collective-permute-start.2
  13.3 1.3 collective-permute-start.6
  14.6 1.4 collective-permute-start.7
  18.1 1.0 fusion.80
  19.1 1.7 collective-permute-start.8
  21.3 2.3 collective-permute-start.4
  26.3 5.0 %collective-permute-start.27 = (bf16[512,768]{1,0:T(8,128)(2,1)}, bf16[512,768]{1,0:T(8,128)(2,1)}, u32[]{:S(2)}, u32[]{:S(2)}) collective-permute-start(bf16[512,768]{1,0:T(8,128)(2,1)} %bitcast.224), channel_id=1, source_target_pairs={{16,0},{32,16},{48,32},{64,48},{80,64},{96,80},{112,96},{17,1},{33... | collective-permute-start | bytes 2359304 | tf_op jit(solution)/shard_map/ppermute | solution.py:25
  31.3 3.0 %collective-permute-start.5 = (bf16[4,128,256]{2,1,0:T(8,128)(2,1)S(1)}, bf16[4,128,256]{2,1,0:T(8,128)(2,1)S(1)}, u32[]{:S(2)}, u32[]{:S(2)}) collective-permute-start(bf16[4,128,256]{2,1,0:T(8,128)(2,1)S(1)} %get-tuple-element.294), channel_id=1, source_target_pairs={{0,8},{1,9},{2,10},{3,11},{4,12},{5,13},{6,14},{7,15},{8,0},{9,1},... | collective-permute-start | bytes 786440 | tf_op jit(solution)/shard_map/ppermute | solution.py:81
  35.4 2.6 %collective-permute-start.10 = (bf16[4,128,256]{2,1,0:T(8,128)(2,1)S(1)}, bf16[4,128,256]{2,1,0:T(8,128)(2,1)}, u32[]{:S(2)}, u32[]{:S(2)}) collective-permute-start(bf16[4,128,256]{2,1,0:T(8,128)(2,1)S(1)} %get-tuple-element.296), channel_id=1, source_target_pairs={{0,3},{1,0},{2,1},{3,2},{4,7},{5,4},{6,5},{7,6},{8,11},{9,8},{10,9... | collective-permute-start | bytes 786440 | tf_op jit(solution)/shard_map/ppermute | solution.py:81
  39.1 6.3 %collective-permute-done.5 = bf16[4,128,256]{2,1,0:T(8,128)(2,1)S(1)} collective-permute-done((bf16[4,128,256]{2,1,0:T(8,128)(2,1)S(1)}, bf16[4,128,256]{2,1,0:T(8,128)(2,1)S(1)}, u32[]{:S(2)}, u32[]{:S(2)}) %collective-permute-start.5) | collective-permute-done | bytes 262176 | tf_op jit(solution)/shard_map/ppermute | solution.py:81
  45.6 2.3 collective-permute-done.11
  47.8 1.2 pad_maximum_fusion.2
  49.3 2.0 gather_fusion
  51.3 44.3 %while.28 = (s32[]{:T(128)}, f32[1024]{0:T(1024)S(1)}, f32[1024]{0:T(1024)S(1)}, f32[1024,128]{1,0:T(8,128)}, s32[8,512]{1,0:T(8,128)S(1)}, /*index=5*/s32[8,512...) while((s32[]{:T(128)}, f32[1024]{0:T(1024)S(1)}, ...), condition=%wide.region_7.8_spmd.clone, body=%wide.region_4.7_spmd.clone.sunk | while | flops 547230720 | bytes 12720321 | solution.py:300
  54.4 1.6 convolution_add_fusion.4
  56.9 1.0 dynamic-slice_bitcast_fusion.4
  60.0 1.6 convolution_add_fusion.4
  65.5 1.6 convolution_add_fusion.4
  71.1 1.6 convolution_add_fusion.4
  76.6 1.6 convolution_add_fusion.4
  82.2 1.6 convolution_add_fusion.4
  87.7 1.6 convolution_add_fusion.4
  93.2 1.6 convolution_add_fusion.4
  95.6 9.1 %collective-permute-start.28 = (bf16[256,8192]{1,0:T(8,128)(2,1)}, bf16[256,8192]{1,0:T(8,128)(2,1)}, u32[]{:S(2)}, u32[]{:S(2)}) collective-permute-start(bf16[256,8192]{1,0:T(8,128)(2,1)} %bitcast.223), channel_id=1, source_target_pairs={{16,0},{32,16},{48,32},{64,48},{80,64},{96,80},{112,96},{17,1},{33... | collective-permute-start | bytes 12582920 | tf_op jit(solution)/shard_map/ppermute | solution.py:25
  104.8 7.8 %fusion.36 = bf16[256,512]{1,0:T(8,128)(2,1)S(1)} fusion(bf16[1,8192,512]{2,1,0:T(8,128)(2,1)} %all-gather.6.cloned.1.call-done, bf16[1,256,8192]{2,1,0:T(8,128)(2,1)} %param.13), kind=kOutput, calls=%fused_computation.58 | convolution fusion | flops 2147614720 | bytes 12845056 | tf_op jit(solution)/shard_map/dot_general | solution.py:230
  113.1 43.4 %while.29 = (s32[]{:T(128)}, f32[1024,128]{1,0:T(8,128)S(1)}, f32[8,512,256]{2,1,0:T(8,128)}, s32[8,512]{1,0:T(8,128)S(1)}, s32[8,512]{1,0:T(8,128)S(1)}, /*inde...) while((s32[]{:T(128)}, f32[1024,128]{1,0:T(8,128)S(1)}, ...), condition=%wide.region_10.11_spmd.clone, body=%wide.region_9.10_spmd.clone.sunk | while | flops 677249024 | bytes 16472895 | solution.py:322
  145.7 1.0 dynamic-slice_bitcast_fusion.5
  156.5 1.0 slice_negate_fusion
  157.5 2.4 fusion.48
  160.0 1.9 collective-permute-start.13
  162.0 2.8 %slice_bitcast_fusion = (f32[4,4,256,128]{3,2,0,1:T(8,128)S(1)}, f32[4,4,256,128]{3,2,1,0:T(8,128)S(1)}) fusion(f32[4,4,256,256]{3,2,1,0:T(8,128)} %bitcast.201), kind=kLoop, calls=%fused_computation.55 | loop fusion | bytes 8388608 | tf_op jit(solution)/shard_map/transpose | solution.py:115
  165.2 2.4 %collective-permute-start.14 = (bf16[4,256,128]{2,1,0:T(8,128)(2,1)S(1)}, bf16[4,256,128]{2,1,0:T(8,128)(2,1)S(1)}, u32[]{:S(2)}, u32[]{:S(2)}) collective-permute-start(bf16[4,256,128]{2,1,0:T(8,128)(2,1)S(1)} %get-tuple-element.277), channel_id=1, source_target_pairs={{0,3},{1,0},{2,1},{3,2},{4,7},{5,4},{6,5},{7,6},{8,11},{9,8},{10,9... | collective-permute-start | bytes 786440 | tf_op jit(solution)/shard_map/ppermute | solution.py:81
  168.8 11.3 %collective-permute-done.14 = bf16[4,256,128]{2,1,0:T(8,128)(2,1)S(1)} collective-permute-done((bf16[4,256,128]{2,1,0:T(8,128)(2,1)S(1)}, bf16[4,256,128]{2,1,0:T(8,128)(2,1)S(1)}, u32[]{:S(2)}, u32[]{:S(2)}) %collective-permute-start.14) | collective-permute-done | bytes 262176 | tf_op jit(solution)/shard_map/ppermute | solution.py:81
  180.2 2.1 collective-permute-start.20
  183.7 6.6 %collective-permute-done.16 = bf16[4,256,128]{2,1,0:T(8,128)(2,1)S(1)} collective-permute-done((bf16[4,256,128]{2,1,0:T(8,128)(2,1)S(1)}, bf16[4,256,128]{2,1,0:T(8,128)(2,1)S(1)}, u32[]{:S(2)}, u32[]{:S(2)}) %collective-permute-start.16) | collective-permute-done | bytes 262176 | tf_op jit(solution)/shard_map/ppermute | solution.py:81
  190.4 1.7 collective-permute-start.22
  192.3 1.0 collective-permute-start.17
  193.4 1.2 collective-permute-start.18
  194.6 5.2 %collective-permute-done.22 = bf16[4,256,128]{2,1,0:T(8,128)(2,1)S(1)} collective-permute-done((bf16[4,256,128]{2,1,0:T(8,128)(2,1)S(1)}, bf16[4,256,128]{2,1,0:T(8,128)(2,1)S(1)}, u32[]{:S(2)}, u32[]{:S(2)}) %collective-permute-start.22) | collective-permute-done | bytes 262176 | tf_op jit(solution)/shard_map/ppermute | solution.py:81
  200.4 7.9 %collective-permute-start.23 = (bf16[256,128]{1,0:T(8,128)(2,1)S(1)}, bf16[256,128]{1,0:T(8,128)(2,1)S(1)}, u32[]{:S(2)}, u32[]{:S(2)}) collective-permute-start(bf16[256,128]{1,0:T(8,128)(2,1)S(1)} %get-tuple-element.288), channel_id=1, source_target_pairs={{0,3},{1,0},{2,1},{3,2},{4,7},{5,4},{6,5},{7,6},{8,11},{9,8},{10,9... | collective-permute-start | bytes 196616 | tf_op jit(solution)/shard_map/ppermute | solution.py:81
  208.9 2.2 collective-permute-start.25
  211.2 1.7 collective-permute-done.24
  213.0 1.7 collective-permute-done.25
  215.3 3.7 %collective-permute-start.26 = (bf16[256,256]{1,0:T(8,128)(2,1)S(1)}, bf16[256,256]{1,0:T(8,128)(2,1)S(1)}, u32[]{:S(2)}, u32[]{:S(2)}) collective-permute-start(bf16[256,256]{1,0:T(8,128)(2,1)S(1)} %pad_maximum_fusion.10), channel_id=1, source_target_pairs={{16,0},{32,16},{48,32},{64,48},{80,64},{96,80},{112,96},{17,1},{33... | collective-permute-start | bytes 393224 | tf_op jit(solution)/shard_map/ppermute | solution.py:25
  219.0 5.5 %collective-permute-done.26 = bf16[256,256]{1,0:T(8,128)(2,1)S(1)} collective-permute-done((bf16[256,256]{1,0:T(8,128)(2,1)S(1)}, bf16[256,256]{1,0:T(8,128)(2,1)S(1)}, u32[]{:S(2)}, u32[]{:S(2)}) %collective-permute-start.26) | collective-permute-done | bytes 131104 | tf_op jit(solution)/shard_map/ppermute | solution.py:25
  225.3 9.1 %shard_map.91 = bf16[256,8192]{1,0:T(8,128)(2,1)} custom-call(bf16[256,768]{1,0:T(8,128)(2,1)} %pad_maximum_fusion.4.grad_ref, bf16[8192,768]{1,0:T(8,128)(2,1)} %all-gather.4.cloned.1.call-done.weight_ref, bf16[256,8192]{1,0:T(8,128)(2,1)} %collective-permute-done.28.base_ref), custom_call_target="tpu_custom_call" | custom-call | flops 3221225472 | bytes 21364736 | tf_op jit(solution)/shard_map/pallas_call | solution.py:50
  (421 shorter events, 85.2 us)
Async XLA Ops:
  6.5 17.1 %copy-start.9 = (s32[1,32]{1,0:T(1,128)S(1)}, s32[1,32]{1,0:T(1,128)}, u32[]{:S(2)}) copy-start(s32[1,32]{1,0:T(1,128)} %param.19) | copy-start | bytes 388
  6.5 98.2 %all-gather.6.cloned.1.call-start = ((), (), s32[]{:S(2)}) async-start(), calls=%async_computation.1 | async-start | bytes 8912896 | tf_op jit(solution)/shard_map/all_gather | solution.py:232
  7.3 218.0 %all-gather.4.cloned.1.call-start = ((), (), s32[]{:S(2)}) async-start(), calls=%async_computation | async-start | bytes 13369344 | tf_op jit(solution)/shard_map/all_gather | solution.py:229
  8.2 10.9 %collective-permute-start = (bf16[128,256]{1,0:T(8,128)(2,1)S(1)}, bf16[128,256]{1,0:T(8,128)(2,1)S(1)}, u32[]{:S(2)}, u32[]{:S(2)}) collective-permute-start(bf16[128,256]{1,0:T(8,128)(2,1)S(1)} %get-tuple-element.300), channel_id=1, source_target_pairs={{0,1},{1,2},{2,3},{3,0},{4,5},{5,6},{6,7},{7,4},{8,9},{9,10},{10,1... | collective-permute-start | bytes 196616 | tf_op jit(solution)/shard_map/ppermute | solution.py:81
  10.3 10.5 %collective-permute-start.1 = (bf16[128,256]{1,0:T(8,128)(2,1)S(1)}, bf16[128,256]{1,0:T(8,128)(2,1)S(1)}, u32[]{:S(2)}, u32[]{:S(2)}) collective-permute-start(bf16[128,256]{1,0:T(8,128)(2,1)S(1)} %get-tuple-element.300), channel_id=1, source_target_pairs={{0,3},{1,0},{2,1},{3,2},{4,7},{5,4},{6,5},{7,6},{8,11},{9,8},{10,9... | collective-permute-start | bytes 196616 | tf_op jit(solution)/shard_map/ppermute | solution.py:81
  11.7 9.1 %collective-permute-start.2 = (bf16[128,256]{1,0:T(8,128)(2,1)S(1)}, bf16[128,256]{1,0:T(8,128)(2,1)S(1)}, u32[]{:S(2)}, u32[]{:S(2)}) collective-permute-start(bf16[128,256]{1,0:T(8,128)(2,1)S(1)} %get-tuple-element.300), channel_id=1, source_target_pairs={{0,2},{1,3},{2,0},{3,1},{4,6},{5,7},{6,4},{7,5},{8,10},{9,11},{10,... | collective-permute-start | bytes 196616 | tf_op jit(solution)/shard_map/ppermute | solution.py:81
  13.3 12.2 %collective-permute-start.6 = (bf16[128,256]{1,0:T(8,128)(2,1)S(1)}, bf16[128,256]{1,0:T(8,128)(2,1)S(1)}, u32[]{:S(2)}, u32[]{:S(2)}) collective-permute-start(bf16[128,256]{1,0:T(8,128)(2,1)S(1)} %get-tuple-element.301), channel_id=1, source_target_pairs={{0,4},{1,5},{2,6},{3,7},{4,8},{5,9},{6,10},{7,11},{8,12},{9,13},{1... | collective-permute-start | bytes 196616 | tf_op jit(solution)/shard_map/ppermute | solution.py:81
  14.6 11.7 %collective-permute-start.7 = (bf16[128,256]{1,0:T(8,128)(2,1)S(1)}, bf16[128,256]{1,0:T(8,128)(2,1)S(1)}, u32[]{:S(2)}, u32[]{:S(2)}) collective-permute-start(bf16[128,256]{1,0:T(8,128)(2,1)S(1)} %get-tuple-element.301), channel_id=1, source_target_pairs={{0,12},{1,13},{2,14},{3,15},{4,0},{5,1},{6,2},{7,3},{8,4},{9,5},{1... | collective-permute-start | bytes 196616 | tf_op jit(solution)/shard_map/ppermute | solution.py:81
  16.9 8.6 %copy-start.10 = (f32[64]{0:T(128)}, f32[64]{0:T(128)S(1)}, u32[]{:S(2)}) copy-start(f32[64]{0:T(128)S(1)} %negate_power_fusion) | copy-start | bytes 772
  19.1 12.3 %collective-permute-start.8 = (bf16[128,256]{1,0:T(8,128)(2,1)S(1)}, bf16[128,256]{1,0:T(8,128)(2,1)S(1)}, u32[]{:S(2)}, u32[]{:S(2)}) collective-permute-start(bf16[128,256]{1,0:T(8,128)(2,1)S(1)} %get-tuple-element.301), channel_id=1, source_target_pairs={{0,8},{1,9},{2,10},{3,11},{4,12},{5,13},{6,14},{7,15},{8,0},{9,1},... | collective-permute-start | bytes 196616 | tf_op jit(solution)/shard_map/ppermute | solution.py:81
  20.8 14.6 %collective-permute-start.3 = (bf16[4,128,256]{2,1,0:T(8,128)(2,1)S(1)}, bf16[4,128,256]{2,1,0:T(8,128)(2,1)S(1)}, u32[]{:S(2)}, u32[]{:S(2)}) collective-permute-start(bf16[4,128,256]{2,1,0:T(8,128)(2,1)S(1)} %get-tuple-element.294), channel_id=1, source_target_pairs={{0,4},{1,5},{2,6},{3,7},{4,8},{5,9},{6,10},{7,11},{8,12},{9,13},{1... | collective-permute-start | bytes 786440 | tf_op jit(solution)/shard_map/ppermute | solution.py:81
  21.3 16.8 %collective-permute-start.4 = (bf16[4,128,256]{2,1,0:T(8,128)(2,1)S(1)}, bf16[4,128,256]{2,1,0:T(8,128)(2,1)S(1)}, u32[]{:S(2)}, u32[]{:S(2)}) collective-permute-start(bf16[4,128,256]{2,1,0:T(8,128)(2,1)S(1)} %get-tuple-element.294), channel_id=1, source_target_pairs={{0,12},{1,13},{2,14},{3,15},{4,0},{5,1},{6,2},{7,3},{8,4},{9,5},{1... | collective-permute-start | bytes 786440 | tf_op jit(solution)/shard_map/ppermute | solution.py:81
  25.5 9.6 %collective-permute-start.12 = (bf16[128,512]{1,0:T(8,128)(2,1)S(1)}, bf16[128,512]{1,0:T(8,128)(2,1)S(1)}, u32[]{:S(2)}, u32[]{:S(2)}) collective-permute-start(bf16[128,512]{1,0:T(8,128)(2,1)S(1)} %get-tuple-element.292), channel_id=1, source_target_pairs={{0,8},{1,9},{2,10},{3,11},{4,12},{5,13},{6,14},{7,15},{8,0},{9,1},... | collective-permute-start | bytes 393224 | tf_op jit(solution)/shard_map/ppermute | solution.py:19
  26.3 25.0 %collective-permute-start.27 = (bf16[512,768]{1,0:T(8,128)(2,1)}, bf16[512,768]{1,0:T(8,128)(2,1)}, u32[]{:S(2)}, u32[]{:S(2)}) collective-permute-start(bf16[512,768]{1,0:T(8,128)(2,1)} %bitcast.224), channel_id=1, source_target_pairs={{16,0},{32,16},{48,32},{64,48},{80,64},{96,80},{112,96},{17,1},{33... | collective-permute-start | bytes 2359304 | tf_op jit(solution)/shard_map/ppermute | solution.py:25
  31.3 14.1 %collective-permute-start.5 = (bf16[4,128,256]{2,1,0:T(8,128)(2,1)S(1)}, bf16[4,128,256]{2,1,0:T(8,128)(2,1)S(1)}, u32[]{:S(2)}, u32[]{:S(2)}) collective-permute-start(bf16[4,128,256]{2,1,0:T(8,128)(2,1)S(1)} %get-tuple-element.294), channel_id=1, source_target_pairs={{0,8},{1,9},{2,10},{3,11},{4,12},{5,13},{6,14},{7,15},{8,0},{9,1},... | collective-permute-start | bytes 786440 | tf_op jit(solution)/shard_map/ppermute | solution.py:81
  35.1 10.4 %collective-permute-start.9 = (bf16[4,128,256]{2,1,0:T(8,128)(2,1)S(1)}, bf16[4,128,256]{2,1,0:T(8,128)(2,1)}, u32[]{:S(2)}, u32[]{:S(2)}) collective-permute-start(bf16[4,128,256]{2,1,0:T(8,128)(2,1)S(1)} %get-tuple-element.296), channel_id=1, source_target_pairs={{0,1},{1,2},{2,3},{3,0},{4,5},{5,6},{6,7},{7,4},{8,9},{9,10},{10,1... | collective-permute-start | bytes 786440 | tf_op jit(solution)/shard_map/ppermute | solution.py:81
  35.4 10.1 %collective-permute-start.10 = (bf16[4,128,256]{2,1,0:T(8,128)(2,1)S(1)}, bf16[4,128,256]{2,1,0:T(8,128)(2,1)}, u32[]{:S(2)}, u32[]{:S(2)}) collective-permute-start(bf16[4,128,256]{2,1,0:T(8,128)(2,1)S(1)} %get-tuple-element.296), channel_id=1, source_target_pairs={{0,3},{1,0},{2,1},{3,2},{4,7},{5,4},{6,5},{7,6},{8,11},{9,8},{10,9... | collective-permute-start | bytes 786440 | tf_op jit(solution)/shard_map/ppermute | solution.py:81
  38.1 9.7 %collective-permute-start.11 = (bf16[4,128,256]{2,1,0:T(8,128)(2,1)S(1)}, bf16[4,128,256]{2,1,0:T(8,128)(2,1)}, u32[]{:S(2)}, u32[]{:S(2)}) collective-permute-start(bf16[4,128,256]{2,1,0:T(8,128)(2,1)S(1)} %get-tuple-element.296), channel_id=1, source_target_pairs={{0,2},{1,3},{2,0},{3,1},{4,6},{5,7},{6,4},{7,5},{8,10},{9,11},{10,... | collective-permute-start | bytes 786440 | tf_op jit(solution)/shard_map/ppermute | solution.py:81
  95.6 129.6 %collective-permute-start.28 = (bf16[256,8192]{1,0:T(8,128)(2,1)}, bf16[256,8192]{1,0:T(8,128)(2,1)}, u32[]{:S(2)}, u32[]{:S(2)}) collective-permute-start(bf16[256,8192]{1,0:T(8,128)(2,1)} %bitcast.223), channel_id=1, source_target_pairs={{16,0},{32,16},{48,32},{64,48},{80,64},{96,80},{112,96},{17,1},{33... | collective-permute-start | bytes 12582920 | tf_op jit(solution)/shard_map/ppermute | solution.py:25
  104.7 8.0 %copy-start.2 = (f32[1024,128]{1,0:T(8,128)S(1)}, f32[1024,128]{1,0:T(8,128)}, u32[]{:S(2)}) copy-start(f32[1024,128]{1,0:T(8,128)} %get-tuple-element.127) | copy-start | bytes 1572868
  123.9 2.2 copy-start.3
  123.9 2.2 copy-start.5
  124.0 2.2 copy-start.7
  129.4 2.2 copy-start.3
  129.4 2.2 copy-start.5
  129.4 2.2 copy-start.7
  134.8 2.2 copy-start.3
  134.8 2.2 copy-start.5
  140.2 2.2 copy-start.3
  140.2 2.2 copy-start.5
  140.2 2.2 copy-start.7
  145.6 2.2 copy-start.3
  145.6 2.2 copy-start.5
  145.6 2.2 copy-start.7
  160.0 59.0 %collective-permute-start.13 = (bf16[256,512]{1,0:T(8,128)(2,1)S(1)}, bf16[256,512]{1,0:T(8,128)(2,1)S(1)}, u32[]{:S(2)}, u32[]{:S(2)}) collective-permute-start(bf16[256,512]{1,0:T(8,128)(2,1)S(1)} %convert_element_type.143), channel_id=1, source_target_pairs={{16,0},{32,16},{48,32},{64,48},{80,64},{96,80},{112,96},{17,1},{33... | collective-permute-start | bytes 786440 | tf_op jit(solution)/shard_map/ppermute | solution.py:25
  165.2 14.9 %collective-permute-start.14 = (bf16[4,256,128]{2,1,0:T(8,128)(2,1)S(1)}, bf16[4,256,128]{2,1,0:T(8,128)(2,1)S(1)}, u32[]{:S(2)}, u32[]{:S(2)}) collective-permute-start(bf16[4,256,128]{2,1,0:T(8,128)(2,1)S(1)} %get-tuple-element.277), channel_id=1, source_target_pairs={{0,3},{1,0},{2,1},{3,2},{4,7},{5,4},{6,5},{7,6},{8,11},{9,8},{10,9... | collective-permute-start | bytes 786440 | tf_op jit(solution)/shard_map/ppermute | solution.py:81
  167.7 15.2 %collective-permute-start.15 = (bf16[4,256,128]{2,1,0:T(8,128)(2,1)S(1)}, bf16[4,256,128]{2,1,0:T(8,128)(2,1)S(1)}, u32[]{:S(2)}, u32[]{:S(2)}) collective-permute-start(bf16[4,256,128]{2,1,0:T(8,128)(2,1)S(1)} %get-tuple-element.279), channel_id=1, source_target_pairs={{0,2},{1,3},{2,0},{3,1},{4,6},{5,7},{6,4},{7,5},{8,10},{9,11},{10,... | collective-permute-start | bytes 786440 | tf_op jit(solution)/shard_map/ppermute | solution.py:81
  167.7 22.7 %collective-permute-start.16 = (bf16[4,256,128]{2,1,0:T(8,128)(2,1)S(1)}, bf16[4,256,128]{2,1,0:T(8,128)(2,1)S(1)}, u32[]{:S(2)}, u32[]{:S(2)}) collective-permute-start(bf16[4,256,128]{2,1,0:T(8,128)(2,1)S(1)} %get-tuple-element.278), channel_id=1, source_target_pairs={{0,1},{1,2},{2,3},{3,0},{4,5},{5,6},{6,7},{7,4},{8,9},{9,10},{10,1... | collective-permute-start | bytes 786440 | tf_op jit(solution)/shard_map/ppermute | solution.py:81
  180.2 12.1 %collective-permute-start.20 = (bf16[4,256,128]{2,1,0:T(8,128)(2,1)S(1)}, bf16[4,256,128]{2,1,0:T(8,128)(2,1)S(1)}, u32[]{:S(2)}, u32[]{:S(2)}) collective-permute-start(bf16[4,256,128]{2,1,0:T(8,128)(2,1)S(1)} %get-tuple-element.280), channel_id=1, source_target_pairs={{0,12},{1,13},{2,14},{3,15},{4,0},{5,1},{6,2},{7,3},{8,4},{9,5},{1... | collective-permute-start | bytes 786440 | tf_op jit(solution)/shard_map/ppermute | solution.py:81
  182.8 10.5 %collective-permute-start.21 = (bf16[4,256,128]{2,1,0:T(8,128)(2,1)S(1)}, bf16[4,256,128]{2,1,0:T(8,128)(2,1)S(1)}, u32[]{:S(2)}, u32[]{:S(2)}) collective-permute-start(bf16[4,256,128]{2,1,0:T(8,128)(2,1)S(1)} %get-tuple-element.282), channel_id=1, source_target_pairs={{0,8},{1,9},{2,10},{3,11},{4,12},{5,13},{6,14},{7,15},{8,0},{9,1},... | collective-permute-start | bytes 786440 | tf_op jit(solution)/shard_map/ppermute | solution.py:81
  190.4 9.5 %collective-permute-start.22 = (bf16[4,256,128]{2,1,0:T(8,128)(2,1)S(1)}, bf16[4,256,128]{2,1,0:T(8,128)(2,1)S(1)}, u32[]{:S(2)}, u32[]{:S(2)}) collective-permute-start(bf16[4,256,128]{2,1,0:T(8,128)(2,1)S(1)} %get-tuple-element.281), channel_id=1, source_target_pairs={{0,4},{1,5},{2,6},{3,7},{4,8},{5,9},{6,10},{7,11},{8,12},{9,13},{1... | collective-permute-start | bytes 786440 | tf_op jit(solution)/shard_map/ppermute | solution.py:81
  192.3 8.1 %collective-permute-start.17 = (bf16[256,128]{1,0:T(8,128)(2,1)S(1)}, bf16[256,128]{1,0:T(8,128)(2,1)S(1)}, u32[]{:S(2)}, u32[]{:S(2)}) collective-permute-start(bf16[256,128]{1,0:T(8,128)(2,1)S(1)} %get-tuple-element.285), channel_id=1, source_target_pairs={{0,12},{1,13},{2,14},{3,15},{4,0},{5,1},{6,2},{7,3},{8,4},{9,5},{1... | collective-permute-start | bytes 196616 | tf_op jit(solution)/shard_map/ppermute | solution.py:81
  193.4 15.0 %collective-permute-start.18 = (bf16[256,128]{1,0:T(8,128)(2,1)S(1)}, bf16[256,128]{1,0:T(8,128)(2,1)S(1)}, u32[]{:S(2)}, u32[]{:S(2)}) collective-permute-start(bf16[256,128]{1,0:T(8,128)(2,1)S(1)} %get-tuple-element.287), channel_id=1, source_target_pairs={{0,8},{1,9},{2,10},{3,11},{4,12},{5,13},{6,14},{7,15},{8,0},{9,1},... | collective-permute-start | bytes 196616 | tf_op jit(solution)/shard_map/ppermute | solution.py:81
  199.8 9.0 %collective-permute-start.19 = (bf16[256,128]{1,0:T(8,128)(2,1)S(1)}, bf16[256,128]{1,0:T(8,128)(2,1)S(1)}, u32[]{:S(2)}, u32[]{:S(2)}) collective-permute-start(bf16[256,128]{1,0:T(8,128)(2,1)S(1)} %get-tuple-element.286), channel_id=1, source_target_pairs={{0,4},{1,5},{2,6},{3,7},{4,8},{5,9},{6,10},{7,11},{8,12},{9,13},{1... | collective-permute-start | bytes 196616 | tf_op jit(solution)/shard_map/ppermute | solution.py:81
  200.4 10.8 %collective-permute-start.23 = (bf16[256,128]{1,0:T(8,128)(2,1)S(1)}, bf16[256,128]{1,0:T(8,128)(2,1)S(1)}, u32[]{:S(2)}, u32[]{:S(2)}) collective-permute-start(bf16[256,128]{1,0:T(8,128)(2,1)S(1)} %get-tuple-element.288), channel_id=1, source_target_pairs={{0,3},{1,0},{2,1},{3,2},{4,7},{5,4},{6,5},{7,6},{8,11},{9,8},{10,9... | collective-permute-start | bytes 196616 | tf_op jit(solution)/shard_map/ppermute | solution.py:81
  208.3 4.6 %collective-permute-start.24 = (bf16[256,128]{1,0:T(8,128)(2,1)S(1)}, bf16[256,128]{1,0:T(8,128)(2,1)S(1)}, u32[]{:S(2)}, u32[]{:S(2)}) collective-permute-start(bf16[256,128]{1,0:T(8,128)(2,1)S(1)} %get-tuple-element.290), channel_id=1, source_target_pairs={{0,2},{1,3},{2,0},{3,1},{4,6},{5,7},{6,4},{7,5},{8,10},{9,11},{10,... | collective-permute-start | bytes 196616 | tf_op jit(solution)/shard_map/ppermute | solution.py:81
  208.9 5.8 %collective-permute-start.25 = (bf16[256,128]{1,0:T(8,128)(2,1)S(1)}, bf16[256,128]{1,0:T(8,128)(2,1)S(1)}, u32[]{:S(2)}, u32[]{:S(2)}) collective-permute-start(bf16[256,128]{1,0:T(8,128)(2,1)S(1)} %get-tuple-element.289), channel_id=1, source_target_pairs={{0,1},{1,2},{2,3},{3,0},{4,5},{5,6},{6,7},{7,4},{8,9},{9,10},{10,1... | collective-permute-start | bytes 196616 | tf_op jit(solution)/shard_map/ppermute | solution.py:81
  215.3 9.1 %collective-permute-start.26 = (bf16[256,256]{1,0:T(8,128)(2,1)S(1)}, bf16[256,256]{1,0:T(8,128)(2,1)S(1)}, u32[]{:S(2)}, u32[]{:S(2)}) collective-permute-start(bf16[256,256]{1,0:T(8,128)(2,1)S(1)} %pad_maximum_fusion.10), channel_id=1, source_target_pairs={{16,0},{32,16},{48,32},{64,48},{80,64},{96,80},{112,96},{17,1},{33... | collective-permute-start | bytes 393224 | tf_op jit(solution)/shard_map/ppermute | solution.py:25
  (50 other events, 72.5 us)
Sparse Core Ops, SparseCore 0:
  9.5 84.7 all-gather.5
  96.4 100.6 all-gather.3

commit v11 on v8

--- a/solution.py
+++ b/solution.py
@@ -293,9 +293,12 @@
         value_term = contract_rows(attn_prob.astype(jnp.bfloat16), flat_grad)
         return (summed, jnp.concatenate([key_term, value_term], axis=1))
 
-    query_grad_rot, key_terms = lax.scan(
-        grad_step, jnp.zeros((flat_rows, head_dim), jnp.float32), key_blocks
-    )
+    query_grad_rot = jnp.zeros((flat_rows, head_dim), jnp.float32)
+    term_list = []
+    for step in range(key_steps):
+        query_grad_rot, term = grad_step(query_grad_rot, tuple(part[step] for part in key_blocks))
+        term_list.append(term)
+    key_terms = jnp.stack(term_list)
     own_positions = first_row + jnp.arange(local_rows, dtype=jnp.int32)
     query_grad = (
         unrotate(query_grad_rot, flat_pos)

time: 230 us -> 238 us (1.035)
  matrix products: 47.7 us -> 70 us
  local copies, waits for them, and re-layouts: 44.4 us -> 30.3 us
  waiting for transfers between devices: 67.8 us -> 55.6 us
  other arithmetic: 14 us -> 22.7 us
  starting transfers between devices: 29.5 us -> 32.1 us
    dot_general x8, matrix products: 12.8 us -> 26.3 us  [running_total(): jnp.dot(weights, value_wide, precision=lax.Precision.HIGH)]
    all_to_all x1, waiting for transfers between devices: 42.4 us -> 29.5 us  [summed_rows(): lax.all_to_all(value.reshape((count, -1) + value.shape[1:]), axis, 0, 0,...]
    dot_general x24, matrix products: 14.3 us -> 26.2 us  [contract_cols(): lax.dot_general(left_rows, right_rows, (((1,), (1,)), ((), ())), preferre...]
    while x40 -> x8, local copies, waits for them, and re-layouts: 9.23 us -> 0.02 us
    squeeze x16 -> x8, local copies, waits for them, and re-layouts: 15.7 us -> 7.79 us  [body(): lax.scan(running_total, start_carry, key_blocks)]
    dynamic_update_slice x16 -> x0, local copies, waits for them, and re-layouts: 6.87 us -> none  [body(): lax.scan(grad_step, jnp.zeros((flat_rows, head_dim), jnp.float32), key_bl...]
    unnamed x5 -> x109, local copies, waits for them, and re-layouts: 0.21 us -> 6.48 us
    unnamed x4 -> x10, other arithmetic: 0.01 us -> 5.07 us
  transfers between devices with their start and end apart: 20 -> 20, of which waited for: 7 -> 7; matrix products, arithmetic and copies ran while one was open for 42% -> 49% of each run, Pallas kernels for 0% -> 0%
where the time goes in v11:
time: 238 us; the launch traced here: 236 us
  matrix products  70 us (29%)
  waiting for transfers between devices  55.6 us (23%)
  starting transfers between devices  32.1 us (13%)
  local copies, waits for them, and re-layouts  30.3 us (13%)
  other arithmetic  22.7 us (10%)
  between operations  15.7 us (7%)
  Pallas kernels  9.08 us (4%)
    all_to_all x1, waiting for transfers between devices, summed_rows(): lax.all_to_all(value.reshape((count, -1) + value.shape[1:]), axis, 0, 0,...  29.5 us
    dot_general x8, matrix products, running_total(): jnp.dot(weights, value_wide, precision=lax.Precision.HIGH)  26.3 us
    dot_general x24, matrix products, contract_cols(): lax.dot_general(left_rows, right_rows, (((1,), (1,)), ((), ())), preferre...  26.2 us
    ppermute x12, waiting for transfers between devices, ring_shift(): return lax.ppermute(value, 'ctx', pairs)  21.4 us
    ppermute x4, starting transfers between devices, passed_along_2(): return lax.ppermute(value, axis, pairs)  13.8 us
    ppermute x12, starting transfers between devices, ring_shift(): return lax.ppermute(value, 'ctx', pairs)  11.7 us
    pallas_call x1, Pallas kernels, projected_sum(): pl.pallas_call(projection_kernel, grid=(width // tile,), in_specs=[pl.Blo...  9.08 us
    squeeze x8, local copies, waits for them, and re-layouts, body(): lax.scan(running_total, start_carry, key_blocks)  7.79 us
  transfers between devices with their start and end apart: 20, of which 7 were waited for; matrix products, arithmetic and copies ran while one was open for 49% of the time, Pallas kernels for 0%

profile of v11, /device:TPU:1, one launch (start us, length us, event | category | flops | bytes accessed | tf_op | source)
XLA Modules:
  0.0 236.0 jit_solution(10052654214206874771)
XLA Ops:
  8.2 2.2 collective-permute-start.7
  10.4 1.5 collective-permute-start.8
  11.9 1.2 collective-permute-start.1
  13.1 1.5 collective-permute-start.2
  14.6 1.0 fusion.91
  15.6 1.6 collective-permute-start
  20.9 4.3 %collective-permute-start.15 = (bf16[512,768]{1,0:T(8,128)(2,1)}, bf16[512,768]{1,0:T(8,128)(2,1)S(1)}, u32[]{:S(2)}, u32[]{:S(2)}) collective-permute-start(bf16[512,768]{1,0:T(8,128)(2,1)} %bitcast.239), channel_id=1, source_target_pairs={{16,0},{32,16},{48,32},{64,48},{80,64},{96,80},{112,96},{17,1},{33... | collective-permute-start | bytes 2359304 | tf_op jit(solution)/shard_map/ppermute | solution.py:25
  25.3 1.3 collective-permute-start.10
  26.6 5.3 %collective-permute-done.3 = bf16[128,256]{1,0:T(8,128)(2,1)S(1)} collective-permute-done((bf16[128,256]{1,0:T(8,128)(2,1)S(1)}, bf16[128,256]{1,0:T(8,128)(2,1)S(1)}, u32[]{:S(2)}, u32[]{:S(2)}) %collective-permute-start.3) | collective-permute-done | bytes 65568 | tf_op jit(solution)/shard_map/ppermute | solution.py:81
  34.4 7.8 %collective-permute-done.10 = bf16[4,128,256]{2,1,0:T(8,128)(2,1)S(1)} collective-permute-done((bf16[4,128,256]{2,1,0:T(8,128)(2,1)S(1)}, bf16[4,128,256]{2,1,0:T(8,128)(2,1)S(1)}, u32[]{:S(2)}, u32[]{:S(2)}) %collective-permute-start.10) | collective-permute-done | bytes 262176 | tf_op jit(solution)/shard_map/ppermute | solution.py:81
  42.9 2.9 %collective-permute-start.5 = (bf16[4,128,256]{2,1,0:T(8,128)(2,1)S(1)}, bf16[4,128,256]{2,1,0:T(8,128)(2,1)}, u32[]{:S(2)}, u32[]{:S(2)}) collective-permute-start(bf16[4,128,256]{2,1,0:T(8,128)(2,1)S(1)} %get-tuple-element.144), channel_id=1, source_target_pairs={{0,12},{1,13},{2,14},{3,15},{4,0},{5,1},{6,2},{7,3},{8,4},{9,5},{1... | collective-permute-start | bytes 786440 | tf_op jit(solution)/shard_map/ppermute | solution.py:81
  47.1 3.5 %collective-permute-done.12 = bf16[4,128,256]{2,1,0:T(8,128)(2,1)} collective-permute-done((bf16[4,128,256]{2,1,0:T(8,128)(2,1)S(1)}, bf16[4,128,256]{2,1,0:T(8,128)(2,1)}, u32[]{:S(2)}, u32[]{:S(2)}) %collective-permute-start.12) | collective-permute-done | bytes 262176 | tf_op jit(solution)/shard_map/ppermute | solution.py:81
  50.6 1.2 pad_maximum_fusion.2
  52.8 3.8 %collective-permute-done.6 = bf16[4,128,256]{2,1,0:T(8,128)(2,1)} collective-permute-done((bf16[4,128,256]{2,1,0:T(8,128)(2,1)}, bf16[4,128,256]{2,1,0:T(8,128)(2,1)}, u32[]{:S(2)}, u32[]{:S(2)}) %collective-permute-start.6) | collective-permute-done | bytes 262176 | tf_op jit(solution)/shard_map/ppermute | solution.py:81
  56.6 1.2 pad_maximum_fusion.1
  58.1 5.3 %collective-permute-start.16 = (bf16[256,8192]{1,0:T(8,128)(2,1)}, bf16[256,8192]{1,0:T(8,128)(2,1)}, u32[]{:S(2)}, u32[]{:S(2)}) collective-permute-start(bf16[256,8192]{1,0:T(8,128)(2,1)} %bitcast.29), channel_id=1, source_target_pairs={{16,0},{32,16},{48,32},{64,48},{80,64},{96,80},{112,96},{17,1},{33... | collective-permute-start | bytes 12582920 | tf_op jit(solution)/shard_map/ppermute | solution.py:25
  63.4 2.0 gather_fusion
  66.3 48.3 %while.15 = (s32[]{:T(128)}, f32[1024]{0:T(1024)S(1)}, f32[1024]{0:T(1024)S(1)}, f32[1024,128]{1,0:T(8,128)}, s32[8,512]{1,0:T(8,128)S(1)}, /*index=5*/s32[8,512...) while((s32[]{:T(128)}, f32[1024]{0:T(1024)S(1)}, ...), condition=%wide.region_7.8_spmd.clone, body=%wide.region_4.7_spmd.clone.sunk | while | flops 547230720 | bytes 8525969 | solution.py:274
  69.0 2.4 %convolution_add_fusion.9 = f32[1024,128]{1,0:T(8,128)} fusion(f32[512,1024]{1,0:T(8,128)S(1)} %get-tuple-element.242, f32[1024]{0:T(1024)S(1)} %select_maximum_fusion.2, s32[1024]{0:T(1024)S(1)} %le.219, s32[1024]{0:T(1024)S(1)} %eq.269, s32[512]{0:T(512)S(1)} %bitcast.219, s32[512]{0:T(512)S(1)} %bitcast.222, f32[1024,128]{1,0:T(8,128)} %get-tuple-element.260, ...), kind=kOutput, calls=%fused_computation.9.clone.1 | convolution fusion | flops 406192128 | bytes 3297281 | tf_op jit(solution)/shard_map/while/body/eval_jaxpr/dot_general | solution.py:263
  74.2 3.4 %convolution_add_fusion.9 = f32[1024,128]{1,0:T(8,128)} fusion(f32[512,1024]{1,0:T(8,128)S(1)} %get-tuple-element.242, f32[1024]{0:T(1024)S(1)} %select_maximum_fusion.2, s32[1024]{0:T(1024)S(1)} %le.219, s32[1024]{0:T(1024)S(1)} %eq.269, s32[512]{0:T(512)S(1)} %bitcast.219, s32[512]{0:T(512)S(1)} %bitcast.222, f32[1024,128]{1,0:T(8,128)} %get-tuple-element.260, ...), kind=kOutput, calls=%fused_computation.9.clone.1 | convolution fusion | flops 406192128 | bytes 3297281 | tf_op jit(solution)/shard_map/while/body/eval_jaxpr/dot_general | solution.py:263
  80.4 3.4 %convolution_add_fusion.9 = f32[1024,128]{1,0:T(8,128)} fusion(f32[512,1024]{1,0:T(8,128)S(1)} %get-tuple-element.242, f32[1024]{0:T(1024)S(1)} %select_maximum_fusion.2, s32[1024]{0:T(1024)S(1)} %le.219, s32[1024]{0:T(1024)S(1)} %eq.269, s32[512]{0:T(512)S(1)} %bitcast.219, s32[512]{0:T(512)S(1)} %bitcast.222, f32[1024,128]{1,0:T(8,128)} %get-tuple-element.260, ...), kind=kOutput, calls=%fused_computation.9.clone.1 | convolution fusion | flops 406192128 | bytes 3297281 | tf_op jit(solution)/shard_map/while/body/eval_jaxpr/dot_general | solution.py:263
  86.5 3.4 %convolution_add_fusion.9 = f32[1024,128]{1,0:T(8,128)} fusion(f32[512,1024]{1,0:T(8,128)S(1)} %get-tuple-element.242, f32[1024]{0:T(1024)S(1)} %select_maximum_fusion.2, s32[1024]{0:T(1024)S(1)} %le.219, s32[1024]{0:T(1024)S(1)} %eq.269, s32[512]{0:T(512)S(1)} %bitcast.219, s32[512]{0:T(512)S(1)} %bitcast.222, f32[1024,128]{1,0:T(8,128)} %get-tuple-element.260, ...), kind=kOutput, calls=%fused_computation.9.clone.1 | convolution fusion | flops 406192128 | bytes 3297281 | tf_op jit(solution)/shard_map/while/body/eval_jaxpr/dot_general | solution.py:263
  92.7 3.4 %convolution_add_fusion.9 = f32[1024,128]{1,0:T(8,128)} fusion(f32[512,1024]{1,0:T(8,128)S(1)} %get-tuple-element.242, f32[1024]{0:T(1024)S(1)} %select_maximum_fusion.2, s32[1024]{0:T(1024)S(1)} %le.219, s32[1024]{0:T(1024)S(1)} %eq.269, s32[512]{0:T(512)S(1)} %bitcast.219, s32[512]{0:T(512)S(1)} %bitcast.222, f32[1024,128]{1,0:T(8,128)} %get-tuple-element.260, ...), kind=kOutput, calls=%fused_computation.9.clone.1 | convolution fusion | flops 406192128 | bytes 3297281 | tf_op jit(solution)/shard_map/while/body/eval_jaxpr/dot_general | solution.py:263
  98.8 3.4 %convolution_add_fusion.9 = f32[1024,128]{1,0:T(8,128)} fusion(f32[512,1024]{1,0:T(8,128)S(1)} %get-tuple-element.242, f32[1024]{0:T(1024)S(1)} %select_maximum_fusion.2, s32[1024]{0:T(1024)S(1)} %le.219, s32[1024]{0:T(1024)S(1)} %eq.269, s32[512]{0:T(512)S(1)} %bitcast.219, s32[512]{0:T(512)S(1)} %bitcast.222, f32[1024,128]{1,0:T(8,128)} %get-tuple-element.260, ...), kind=kOutput, calls=%fused_computation.9.clone.1 | convolution fusion | flops 406192128 | bytes 3297281 | tf_op jit(solution)/shard_map/while/body/eval_jaxpr/dot_general | solution.py:263
  105.0 3.4 %convolution_add_fusion.9 = f32[1024,128]{1,0:T(8,128)} fusion(f32[512,1024]{1,0:T(8,128)S(1)} %get-tuple-element.242, f32[1024]{0:T(1024)S(1)} %select_maximum_fusion.2, s32[1024]{0:T(1024)S(1)} %le.219, s32[1024]{0:T(1024)S(1)} %eq.269, s32[512]{0:T(512)S(1)} %bitcast.219, s32[512]{0:T(512)S(1)} %bitcast.222, f32[1024,128]{1,0:T(8,128)} %get-tuple-element.260, ...), kind=kOutput, calls=%fused_computation.9.clone.1 | convolution fusion | flops 406192128 | bytes 3297281 | tf_op jit(solution)/shard_map/while/body/eval_jaxpr/dot_general | solution.py:263
  108.9 1.0 dynamic-slice_bitcast_fusion.2
  111.2 3.4 %convolution_add_fusion.9 = f32[1024,128]{1,0:T(8,128)} fusion(f32[512,1024]{1,0:T(8,128)S(1)} %get-tuple-element.242, f32[1024]{0:T(1024)S(1)} %select_maximum_fusion.2, s32[1024]{0:T(1024)S(1)} %le.219, s32[1024]{0:T(1024)S(1)} %eq.269, s32[512]{0:T(512)S(1)} %bitcast.219, s32[512]{0:T(512)S(1)} %bitcast.222, f32[1024,128]{1,0:T(8,128)} %get-tuple-element.260, ...), kind=kOutput, calls=%fused_computation.9.clone.1 | convolution fusion | flops 406192128 | bytes 3297281 | tf_op jit(solution)/shard_map/while/body/eval_jaxpr/dot_general | solution.py:263
  114.6 1.7 fusion.90
  116.4 2.0 exponential_select_fusion.7
  118.4 2.0 exponential_select_fusion.6
  120.4 2.1 exponential_select_fusion.5
  122.5 2.0 exponential_select_fusion.4
  124.6 2.0 exponential_select_fusion.3
  126.6 2.0 exponential_select_fusion.2
  128.6 2.0 exponential_select_fusion.1
  130.6 2.0 exponential_select_fusion
  132.6 7.2 %fusion.24 = bf16[256,512]{1,0:T(8,128)(2,1)S(1)} fusion(bf16[1,8192,512]{2,1,0:T(8,128)(2,1)} %all-gather.6.cloned.1.call-done, bf16[1,256,8192]{2,1,0:T(8,128)(2,1)} %param.11), kind=kOutput, calls=%fused_computation.59 | convolution fusion | flops 2147614720 | bytes 12845056 | tf_op jit(solution)/shard_map/dot_general | solution.py:204
  140.0 1.4 multiply_reduce_fusion
  141.4 2.2 multiply_convert_fusion.7
  162.7 3.9 %copy.21 = bf16[8,512,256]{2,1,0:T(8,128)(2,1)} copy(bf16[8,512,256]{1,2,0:T(8,128)(2,1)} %fusion.49) | data formatting | bytes 4194304 | tf_op jit(solution)/shard_map/stack | solution.py:301
  166.6 4.9 %all-to-all-start = ((bf16[16,256,256]{2,1,0:T(8,128)(2,1)}), bf16[16,256,256]{2,1,0:T(8,128)(2,1)}, u32[]{:S(2)}, u32[]{:S(2)}) async-start(bf16[16,256,256]{2,1,0:T(8,128)(2,1)} %bitcast.189), calls=%async_computation | async-start | bytes 4194304 | tf_op jit(solution)/shard_map/all_to_all | solution.py:36
  176.6 2.0 fusion.39
  178.9 1.9 collective-permute-start.13
  180.9 29.5 %all-to-all-done = bf16[16,256,256]{2,1,0:T(8,128)(2,1)} async-done(((bf16[16,256,256]{2,1,0:T(8,128)(2,1)}), bf16[16,256,256]{2,1,0:T(8,128)(2,1)}, u32[]{:S(2)}, u32[]{:S(2)}) %all-to-all-start) | async-done | bytes 2097184 | tf_op jit(solution)/shard_map/all_to_all | solution.py:36
  210.4 1.9 convert_reduce_fusion
  213.1 2.3 collective-permute-start.14
  215.4 3.9 %collective-permute-done.14 = bf16[256,256]{1,0:T(8,128)(2,1)S(1)} collective-permute-done((bf16[256,256]{1,0:T(8,128)(2,1)S(1)}, bf16[256,256]{1,0:T(8,128)(2,1)S(1)}, u32[]{:S(2)}, u32[]{:S(2)}) %collective-permute-start.14) | collective-permute-done | bytes 131104 | tf_op jit(solution)/shard_map/ppermute | solution.py:25
  220.1 9.1 %shard_map.91 = bf16[256,8192]{1,0:T(8,128)(2,1)} custom-call(bf16[256,768]{1,0:T(8,128)(2,1)} %pad_maximum_fusion.4.grad_ref, bf16[8192,768]{1,0:T(8,128)(2,1)} %all-gather.4.cloned.1.call-done.weight_ref, bf16[256,8192]{1,0:T(8,128)(2,1)} %collective-permute-done.16.base_ref), custom_call_target="tpu_custom_call" | custom-call | flops 3221225472 | bytes 21364736 | tf_op jit(solution)/shard_map/pallas_call | solution.py:50
  (303 shorter events, 56.7 us)
Async XLA Ops:
  6.5 25.9 %copy-start.53 = (s32[1,32]{1,0:T(1,128)S(1)}, s32[1,32]{1,0:T(1,128)}, u32[]{:S(2)}) copy-start(s32[1,32]{1,0:T(1,128)} %param.17) | copy-start | bytes 388
  6.5 126.0 %all-gather.6.cloned.1.call-start = ((), (), s32[]{:S(2)}) async-start(), calls=%async_computation.2 | async-start | bytes 8912896 | tf_op jit(solution)/shard_map/all_gather | solution.py:206
  7.3 212.9 %all-gather.4.cloned.1.call-start = ((), (), s32[]{:S(2)}) async-start(), calls=%async_computation.1 | async-start | bytes 13369344 | tf_op jit(solution)/shard_map/all_gather | solution.py:203
  8.2 12.2 %collective-permute-start.7 = (bf16[128,256]{1,0:T(8,128)(2,1)S(1)}, bf16[128,256]{1,0:T(8,128)(2,1)S(1)}, u32[]{:S(2)}, u32[]{:S(2)}) collective-permute-start(bf16[128,256]{1,0:T(8,128)(2,1)S(1)} %get-tuple-element.151), channel_id=1, source_target_pairs={{0,4},{1,5},{2,6},{3,7},{4,8},{5,9},{6,10},{7,11},{8,12},{9,13},{1... | collective-permute-start | bytes 196616 | tf_op jit(solution)/shard_map/ppermute | solution.py:81
  10.4 10.5 %collective-permute-start.8 = (bf16[128,256]{1,0:T(8,128)(2,1)S(1)}, bf16[128,256]{1,0:T(8,128)(2,1)S(1)}, u32[]{:S(2)}, u32[]{:S(2)}) collective-permute-start(bf16[128,256]{1,0:T(8,128)(2,1)S(1)} %get-tuple-element.151), channel_id=1, source_target_pairs={{0,12},{1,13},{2,14},{3,15},{4,0},{5,1},{6,2},{7,3},{8,4},{9,5},{1... | collective-permute-start | bytes 196616 | tf_op jit(solution)/shard_map/ppermute | solution.py:81
  11.9 13.2 %collective-permute-start.1 = (bf16[128,256]{1,0:T(8,128)(2,1)S(1)}, bf16[128,256]{1,0:T(8,128)(2,1)S(1)}, u32[]{:S(2)}, u32[]{:S(2)}) collective-permute-start(bf16[128,256]{1,0:T(8,128)(2,1)S(1)} %get-tuple-element.150), channel_id=1, source_target_pairs={{0,1},{1,2},{2,3},{3,0},{4,5},{5,6},{6,7},{7,4},{8,9},{9,10},{10,1... | collective-permute-start | bytes 196616 | tf_op jit(solution)/shard_map/ppermute | solution.py:81
  13.1 13.4 %collective-permute-start.2 = (bf16[128,256]{1,0:T(8,128)(2,1)S(1)}, bf16[128,256]{1,0:T(8,128)(2,1)S(1)}, u32[]{:S(2)}, u32[]{:S(2)}) collective-permute-start(bf16[128,256]{1,0:T(8,128)(2,1)S(1)} %get-tuple-element.150), channel_id=1, source_target_pairs={{0,3},{1,0},{2,1},{3,2},{4,7},{5,4},{6,5},{7,6},{8,11},{9,8},{10,9... | collective-permute-start | bytes 196616 | tf_op jit(solution)/shard_map/ppermute | solution.py:81
  15.6 27.3 %collective-permute-start = (bf16[128,512]{1,0:T(8,128)(2,1)S(1)}, bf16[128,512]{1,0:T(8,128)(2,1)S(1)}, u32[]{:S(2)}, u32[]{:S(2)}) collective-permute-start(bf16[128,512]{1,0:T(8,128)(2,1)S(1)} %get-tuple-element.148), channel_id=1, source_target_pairs={{0,8},{1,9},{2,10},{3,11},{4,12},{5,13},{6,14},{7,15},{8,0},{9,1},... | collective-permute-start | bytes 393224 | tf_op jit(solution)/shard_map/ppermute | solution.py:19
  18.1 2.3 copy-start.35
  20.4 4.8 %collective-permute-start.9 = (bf16[128,256]{1,0:T(8,128)(2,1)S(1)}, bf16[128,256]{1,0:T(8,128)(2,1)S(1)}, u32[]{:S(2)}, u32[]{:S(2)}) collective-permute-start(bf16[128,256]{1,0:T(8,128)(2,1)S(1)} %collective-permute-done.7), channel_id=1, source_target_pairs={{0,4},{1,5},{2,6},{3,7},{4,8},{5,9},{6,10},{7,11},{8,12},{9,13},{1... | collective-permute-start | bytes 196616 | tf_op jit(solution)/shard_map/ppermute | solution.py:81
  20.9 44.5 %collective-permute-start.15 = (bf16[512,768]{1,0:T(8,128)(2,1)}, bf16[512,768]{1,0:T(8,128)(2,1)S(1)}, u32[]{:S(2)}, u32[]{:S(2)}) collective-permute-start(bf16[512,768]{1,0:T(8,128)(2,1)} %bitcast.239), channel_id=1, source_target_pairs={{16,0},{32,16},{48,32},{64,48},{80,64},{96,80},{112,96},{17,1},{33... | collective-permute-start | bytes 2359304 | tf_op jit(solution)/shard_map/ppermute | solution.py:25
  25.2 6.7 %collective-permute-start.3 = (bf16[128,256]{1,0:T(8,128)(2,1)S(1)}, bf16[128,256]{1,0:T(8,128)(2,1)S(1)}, u32[]{:S(2)}, u32[]{:S(2)}) collective-permute-start(bf16[128,256]{1,0:T(8,128)(2,1)S(1)} %collective-permute-done.1), channel_id=1, source_target_pairs={{0,1},{1,2},{2,3},{3,0},{4,5},{5,6},{6,7},{7,4},{8,9},{9,10},{10,1... | collective-permute-start | bytes 196616 | tf_op jit(solution)/shard_map/ppermute | solution.py:81
  25.3 16.9 %collective-permute-start.10 = (bf16[4,128,256]{2,1,0:T(8,128)(2,1)S(1)}, bf16[4,128,256]{2,1,0:T(8,128)(2,1)S(1)}, u32[]{:S(2)}, u32[]{:S(2)}) collective-permute-start(bf16[4,128,256]{2,1,0:T(8,128)(2,1)S(1)} %get-tuple-element.146), channel_id=1, source_target_pairs={{0,1},{1,2},{2,3},{3,0},{4,5},{5,6},{6,7},{7,4},{8,9},{9,10},{10,1... | collective-permute-start | bytes 786440 | tf_op jit(solution)/shard_map/ppermute | solution.py:81
  31.9 14.1 %collective-permute-start.4 = (bf16[4,128,256]{2,1,0:T(8,128)(2,1)S(1)}, bf16[4,128,256]{2,1,0:T(8,128)(2,1)}, u32[]{:S(2)}, u32[]{:S(2)}) collective-permute-start(bf16[4,128,256]{2,1,0:T(8,128)(2,1)S(1)} %get-tuple-element.144), channel_id=1, source_target_pairs={{0,4},{1,5},{2,6},{3,7},{4,8},{5,9},{6,10},{7,11},{8,12},{9,13},{1... | collective-permute-start | bytes 786440 | tf_op jit(solution)/shard_map/ppermute | solution.py:81
  34.3 12.8 %collective-permute-start.11 = (bf16[4,128,256]{2,1,0:T(8,128)(2,1)S(1)}, bf16[4,128,256]{2,1,0:T(8,128)(2,1)}, u32[]{:S(2)}, u32[]{:S(2)}) collective-permute-start(bf16[4,128,256]{2,1,0:T(8,128)(2,1)S(1)} %get-tuple-element.146), channel_id=1, source_target_pairs={{0,3},{1,0},{2,1},{3,2},{4,7},{5,4},{6,5},{7,6},{8,11},{9,8},{10,9... | collective-permute-start | bytes 786440 | tf_op jit(solution)/shard_map/ppermute | solution.py:81
  42.2 8.5 %collective-permute-start.12 = (bf16[4,128,256]{2,1,0:T(8,128)(2,1)S(1)}, bf16[4,128,256]{2,1,0:T(8,128)(2,1)}, u32[]{:S(2)}, u32[]{:S(2)}) collective-permute-start(bf16[4,128,256]{2,1,0:T(8,128)(2,1)S(1)} %collective-permute-done.10), channel_id=1, source_target_pairs={{0,1},{1,2},{2,3},{3,0},{4,5},{5,6},{6,7},{7,4},{8,9},{9,10},{10,1... | collective-permute-start | bytes 786440 | tf_op jit(solution)/shard_map/ppermute | solution.py:81
  42.9 9.9 %collective-permute-start.5 = (bf16[4,128,256]{2,1,0:T(8,128)(2,1)S(1)}, bf16[4,128,256]{2,1,0:T(8,128)(2,1)}, u32[]{:S(2)}, u32[]{:S(2)}) collective-permute-start(bf16[4,128,256]{2,1,0:T(8,128)(2,1)S(1)} %get-tuple-element.144), channel_id=1, source_target_pairs={{0,12},{1,13},{2,14},{3,15},{4,0},{5,1},{6,2},{7,3},{8,4},{9,5},{1... | collective-permute-start | bytes 786440 | tf_op jit(solution)/shard_map/ppermute | solution.py:81
  46.1 10.6 %collective-permute-start.6 = (bf16[4,128,256]{2,1,0:T(8,128)(2,1)}, bf16[4,128,256]{2,1,0:T(8,128)(2,1)}, u32[]{:S(2)}, u32[]{:S(2)}) collective-permute-start(bf16[4,128,256]{2,1,0:T(8,128)(2,1)} %collective-permute-done.4), channel_id=1, source_target_pairs={{0,4},{1,5},{2,6},{3,7},{4,8},{5,9},{6,10},{7,11},{8,12},{9,13},{1... | collective-permute-start | bytes 786440 | tf_op jit(solution)/shard_map/ppermute | solution.py:81
  58.1 162.1 %collective-permute-start.16 = (bf16[256,8192]{1,0:T(8,128)(2,1)}, bf16[256,8192]{1,0:T(8,128)(2,1)}, u32[]{:S(2)}, u32[]{:S(2)}) collective-permute-start(bf16[256,8192]{1,0:T(8,128)(2,1)} %bitcast.29), channel_id=1, source_target_pairs={{16,0},{32,16},{48,32},{64,48},{80,64},{96,80},{112,96},{17,1},{33... | collective-permute-start | bytes 12582920 | tf_op jit(solution)/shard_map/ppermute | solution.py:25
  116.3 2.1 copy-start.29
  116.3 4.1 %copy-start.26 = (bf16[4,128,256]{2,1,0:T(8,128)(2,1)}, bf16[4,128,256]{2,1,0:T(8,128)(2,1)S(1)}, u32[]{:S(2)}) copy-start(bf16[4,128,256]{2,1,0:T(8,128)(2,1)S(1)} %get-tuple-element.136) | copy-start | bytes 786436
  116.3 6.2 %copy-start.23 = (bf16[4,128,256]{2,1,0:T(8,128)(2,1)}, bf16[4,128,256]{2,1,0:T(8,128)(2,1)S(1)}, u32[]{:S(2)}) copy-start(bf16[4,128,256]{2,1,0:T(8,128)(2,1)S(1)} %get-tuple-element.135) | copy-start | bytes 786436
  116.3 8.2 %copy-start.20 = (bf16[4,128,256]{2,1,0:T(8,128)(2,1)}, bf16[4,128,256]{2,1,0:T(8,128)(2,1)S(1)}, u32[]{:S(2)}) copy-start(bf16[4,128,256]{2,1,0:T(8,128)(2,1)S(1)} %get-tuple-element.134) | copy-start | bytes 786436
  116.3 25.1 %copy-start.32 = (bf16[4,128,256]{2,1,0:T(8,128)(2,1)}, bf16[4,128,256]{2,1,0:T(8,128)(2,1)S(1)}, u32[]{:S(2)}) copy-start(bf16[4,128,256]{2,1,0:T(8,128)(2,1)S(1)} %get-tuple-element.138) | copy-start | bytes 786436
  116.3 2.0 copy-start.45
  116.4 2.0 copy-start.51
  118.4 2.0 copy-start.43
  118.4 2.0 copy-start.50
  120.4 2.1 copy-start.42
  120.4 2.1 copy-start.49
  122.5 2.1 copy-start.40
  122.5 2.0 copy-start.48
  124.5 2.0 copy-start.39
  124.6 2.0 copy-start.46
  126.6 2.0 copy-start.38
  126.6 2.0 copy-start.44
  141.4 2.6 %copy-start.19 = (f32[1024,512]{1,0:T(8,128)S(1)}, f32[1024,512]{1,0:T(8,128)}, u32[]{:S(2)}) copy-start(f32[1024,512]{1,0:T(8,128)} %exponential_select_fusion.7) | copy-start | bytes 6291460
  147.9 2.1 copy-start.16
  147.9 2.1 copy-start.24
  150.5 2.1 copy-start.15
  150.5 2.1 copy-start.21
  153.1 2.1 copy-start.14
  155.6 2.1 copy-start.12
  166.6 4.9 %copy-start.33 = (bf16[4,128,256]{2,1,0:T(8,128)(2,1)S(1)}, bf16[4,128,256]{2,1,0:T(8,128)(2,1)}, u32[]{:S(2)}) copy-start(bf16[4,128,256]{2,1,0:T(8,128)(2,1)} %copy-done.32) | copy-start | bytes 786436
  166.6 5.4 %copy-start.31 = (bf16[4,128,256]{2,1,0:T(8,128)(2,1)S(1)}, bf16[4,128,256]{2,1,0:T(8,128)(2,1)}, u32[]{:S(2)}) copy-start(bf16[4,128,256]{2,1,0:T(8,128)(2,1)} %copy-done.29) | copy-start | bytes 786436
  166.6 43.8 %all-to-all-start = ((bf16[16,256,256]{2,1,0:T(8,128)(2,1)}), bf16[16,256,256]{2,1,0:T(8,128)(2,1)}, u32[]{:S(2)}, u32[]{:S(2)}) async-start(bf16[16,256,256]{2,1,0:T(8,128)(2,1)} %bitcast.189), calls=%async_computation | async-start | bytes 4194304 | tf_op jit(solution)/shard_map/all_to_all | solution.py:36
  178.9 36.5 %collective-permute-start.13 = (bf16[256,512]{1,0:T(8,128)(2,1)S(1)}, bf16[256,512]{1,0:T(8,128)(2,1)S(1)}, u32[]{:S(2)}, u32[]{:S(2)}) collective-permute-start(bf16[256,512]{1,0:T(8,128)(2,1)S(1)} %convert_element_type.112), channel_id=1, source_target_pairs={{16,0},{32,16},{48,32},{64,48},{80,64},{96,80},{112,96},{17,1},{33... | collective-permute-start | bytes 786440 | tf_op jit(solution)/shard_map/ppermute | solution.py:25
  213.1 6.3 %collective-permute-start.14 = (bf16[256,256]{1,0:T(8,128)(2,1)S(1)}, bf16[256,256]{1,0:T(8,128)(2,1)S(1)}, u32[]{:S(2)}, u32[]{:S(2)}) collective-permute-start(bf16[256,256]{1,0:T(8,128)(2,1)S(1)} %pad_maximum_fusion.10), channel_id=1, source_target_pairs={{16,0},{32,16},{48,32},{64,48},{80,64},{96,80},{112,96},{17,1},{33... | collective-permute-start | bytes 393224 | tf_op jit(solution)/shard_map/ppermute | solution.py:25
  (26 other events, 38.1 us)
Sparse Core Ops, SparseCore 0:
  9.5 80.4 all-gather.5
  92.2 101.4 all-gather.3

commit v12 on v8

--- a/solution.py
+++ b/solution.py
@@ -44,22 +44,23 @@
     out_ref[...] = (base_ref[...].astype(jnp.float32) + product).astype(out_ref.dtype)
 
 
-def projected_sum(grad_rows, weight, base, tile=4096):
+def projected_sum(grad_rows, weight, base, first_column, out_dtype, tile=4096):
     rows, inner = grad_rows.shape
     width = weight.shape[0]
+    column_block = first_column // inner
     return pl.pallas_call(
         projection_kernel,
         grid=(width // tile,),
         in_specs=[
             pl.BlockSpec((rows, inner), lambda j: (0, 0)),
-            pl.BlockSpec((tile, inner), lambda j: (j, 0)),
+            pl.BlockSpec((tile, inner), lambda j: (j, column_block)),
             pl.BlockSpec((rows, tile), lambda j: (0, j)),
         ],
         out_specs=pl.BlockSpec((rows, tile), lambda j: (0, j)),
-        out_shape=jax.ShapeDtypeStruct((rows, width), base.dtype),
+        out_shape=jax.ShapeDtypeStruct((rows, width), out_dtype),
         cost_estimate=pl.CostEstimate(
             flops=2 * rows * inner * width,
-            bytes_accessed=2 * (rows * inner + width * inner + 2 * rows * width),
+            bytes_accessed=2 * (rows * inner + width * inner) + 6 * rows * width,
             transcendentals=0,
         ),
     )(grad_rows, weight, base)
@@ -311,8 +312,9 @@
     next_keyval_grad = passed_along_2(
         jnp.concatenate([key_grad, value_grad], axis=1), "pipe", -1
     )
-    next_qkv_grad = jnp.concatenate([next_query_grad, next_keyval_grad], axis=1)
-    passed = projected_sum(next_qkv_grad, next_weight, next_grad_in)
+    query_width = next_query_grad.shape[1]
+    partial = projected_sum(next_query_grad, next_weight, next_grad_in, 0, jnp.float32)
+    passed = projected_sum(next_keyval_grad, next_weight, partial, query_width, jnp.bfloat16)
     return passed[None]
 
 

time: 230 us -> 239 us (1.039)
  matrix products: 47.7 us -> 83.9 us
  local copies, waits for them, and re-layouts: 44.4 us -> 23.1 us
  waiting for transfers between devices: 67.8 us -> 50.8 us
  Pallas kernels: 9.08 us -> 15.6 us
  other arithmetic: 14 us -> 16.6 us
    dot_general x24, matrix products: 14.3 us -> 29.7 us  [contract_cols(): lax.dot_general(left_rows, right_rows, (((1,), (1,)), ((), ())), preferre...]
    squeeze x16, local copies, waits for them, and re-layouts: 15.7 us -> 0.42 us  [body(): lax.scan(running_total, start_carry, key_blocks)]
    dot_general x8, matrix products: 12.8 us -> 26.3 us  [running_total(): jnp.dot(weights, value_wide, precision=lax.Precision.HIGH)]
    all_to_all x1, waiting for transfers between devices: 42.4 us -> 32.4 us  [summed_rows(): lax.all_to_all(value.reshape((count, -1) + value.shape[1:]), axis, 0, 0,...]
    while x40 -> x8, local copies, waits for them, and re-layouts: 9.23 us -> 0.01 us
    dot_general x16, matrix products: 7.86 us -> 15.3 us  [contract_rows(): lax.dot_general(left_rows, right_rows, (((0,), (0,)), ((), ())), preferre...]
    pallas_call x1 -> x2, Pallas kernels: 9.08 us -> 15.6 us  [projected_sum(): pl.pallas_call(projection_kernel, grid=(width // tile,), in_specs=[pl.Blo...]
    ppermute x4, waiting for transfers between devices: 3.97 us -> 0.01 us  [passed_along_2(): return lax.ppermute(value, axis, pairs)]
  transfers between devices with their start and end apart: 20 -> 20, of which waited for: 7 -> 5; matrix products, arithmetic and copies ran while one was open for 42% -> 51% of each run, Pallas kernels for 0% -> 4%
where the time goes in v12:
time: 239 us; the launch traced here: 237 us
  matrix products  83.9 us (35%)
  waiting for transfers between devices  50.8 us (21%)
  starting transfers between devices  30.8 us (13%)
  local copies, waits for them, and re-layouts  23.1 us (10%)
  other arithmetic  16.6 us (7%)
  Pallas kernels  15.6 us (7%)
  between operations  15.2 us (6%)
    all_to_all x1, waiting for transfers between devices, summed_rows(): lax.all_to_all(value.reshape((count, -1) + value.shape[1:]), axis, 0, 0,...  32.4 us
    dot_general x24, matrix products, contract_cols(): lax.dot_general(left_rows, right_rows, (((1,), (1,)), ((), ())), preferre...  29.7 us
    dot_general x8, matrix products, running_total(): jnp.dot(weights, value_wide, precision=lax.Precision.HIGH)  26.3 us
    ppermute x12, waiting for transfers between devices, ring_shift(): return lax.ppermute(value, 'ctx', pairs)  17.6 us
    pallas_call x2, Pallas kernels, projected_sum(): pl.pallas_call(projection_kernel, grid=(width // tile,), in_specs=[pl.Blo...  15.6 us
    dot_general x16, matrix products, contract_rows(): lax.dot_general(left_rows, right_rows, (((0,), (0,)), ((), ())), preferre...  15.3 us
    ppermute x4, starting transfers between devices, passed_along_2(): return lax.ppermute(value, axis, pairs)  12.9 us
    ppermute x12, starting transfers between devices, ring_shift(): return lax.ppermute(value, 'ctx', pairs)  11.9 us
  transfers between devices with their start and end apart: 20, of which 5 were waited for; matrix products, arithmetic and copies ran while one was open for 51% of the time, Pallas kernels for 4%

profile of v12, /device:TPU:1, one launch (start us, length us, event | category | flops | bytes accessed | tf_op | source)
XLA Modules:
  0.0 237.2 jit_solution(13105123696159715883)
XLA Ops:
  8.2 3.4 %collective-permute-start.1 = (bf16[128,256]{1,0:T(8,128)(2,1)S(1)}, bf16[128,256]{1,0:T(8,128)(2,1)S(1)}, u32[]{:S(2)}, u32[]{:S(2)}) collective-permute-start(bf16[128,256]{1,0:T(8,128)(2,1)S(1)} %get-tuple-element.278), channel_id=1, source_target_pairs={{0,3},{1,0},{2,1},{3,2},{4,7},{5,4},{6,5},{7,6},{8,11},{9,8},{10,9... | collective-permute-start | bytes 196616 | tf_op jit(solution)/shard_map/ppermute | solution.py:82
  11.6 2.7 %collective-permute-start.7 = (bf16[128,256]{1,0:T(8,128)(2,1)S(1)}, bf16[128,256]{1,0:T(8,128)(2,1)S(1)}, u32[]{:S(2)}, u32[]{:S(2)}) collective-permute-start(bf16[128,256]{1,0:T(8,128)(2,1)S(1)} %get-tuple-element.279), channel_id=1, source_target_pairs={{0,12},{1,13},{2,14},{3,15},{4,0},{5,1},{6,2},{7,3},{8,4},{9,5},{1... | collective-permute-start | bytes 196616 | tf_op jit(solution)/shard_map/ppermute | solution.py:82
  15.3 1.7 collective-permute-start.12
  19.2 4.3 %collective-permute-start.14 = (bf16[512,768]{1,0:T(8,128)(2,1)}, bf16[512,768]{1,0:T(8,128)(2,1)S(1)}, u32[]{:S(2)}, u32[]{:S(2)}) collective-permute-start(bf16[512,768]{1,0:T(8,128)(2,1)} %bitcast.157), channel_id=1, source_target_pairs={{16,0},{32,16},{48,32},{64,48},{80,64},{96,80},{112,96},{17,1},{33... | collective-permute-start | bytes 2359304 | tf_op jit(solution)/shard_map/ppermute | solution.py:25
  23.5 1.7 collective-permute-start.8
  25.3 4.9 %collective-permute-done.8 = bf16[128,256]{1,0:T(8,128)(2,1)S(1)} collective-permute-done((bf16[128,256]{1,0:T(8,128)(2,1)S(1)}, bf16[128,256]{1,0:T(8,128)(2,1)S(1)}, u32[]{:S(2)}, u32[]{:S(2)}) %collective-permute-start.8) | collective-permute-done | bytes 65568 | tf_op jit(solution)/shard_map/ppermute | solution.py:82
  33.7 7.6 %collective-permute-done.3 = bf16[4,128,256]{2,1,0:T(8,128)(2,1)S(1)} collective-permute-done((bf16[4,128,256]{2,1,0:T(8,128)(2,1)S(1)}, bf16[4,128,256]{2,1,0:T(8,128)(2,1)S(1)}, u32[]{:S(2)}, u32[]{:S(2)}) %collective-permute-start.3) | collective-permute-done | bytes 262176 | tf_op jit(solution)/shard_map/ppermute | solution.py:82
  41.5 2.3 collective-permute-start.10
  45.7 3.8 %collective-permute-done.5 = bf16[4,128,256]{2,1,0:T(8,128)(2,1)} collective-permute-done((bf16[4,128,256]{2,1,0:T(8,128)(2,1)S(1)}, bf16[4,128,256]{2,1,0:T(8,128)(2,1)}, u32[]{:S(2)}, u32[]{:S(2)}) %collective-permute-start.5) | collective-permute-done | bytes 262176 | tf_op jit(solution)/shard_map/ppermute | solution.py:82
  53.3 1.5 pad_maximum_fusion
  54.8 2.3 gather_fusion
  58.1 48.4 %while.28 = (s32[]{:T(128)}, f32[1024]{0:T(1024)S(1)}, f32[1024]{0:T(1024)S(1)}, f32[1024,128]{1,0:T(8,128)}, s32[8,512]{1,0:T(8,128)S(1)}, /*index=5*/s32[8,512...) while((s32[]{:T(128)}, f32[1024]{0:T(1024)S(1)}, ...), condition=%wide.region_7.8_spmd.clone, body=%wide.region_4.7_spmd.clone.sunk | while | flops 547230720 | bytes 8525969 | solution.py:275
  58.6 1.6 fusion.87
  60.8 2.4 %convolution_add_fusion.4 = f32[1024,128]{1,0:T(8,128)} fusion(f32[512,1024]{1,0:T(8,128)S(1)} %get-tuple-element.416, f32[1024]{0:T(1024)S(1)} %select_maximum_fusion.2, s32[1024]{0:T(1024)S(1)} %le.90, s32[1024]{0:T(1024)S(1)} %eq.164, s32[512]{0:T(512)S(1)} %bitcast.142, s32[512]{0:T(512)S(1)} %bitcast.145, f32[1024,128]{1,0:T(8,128)} %get-tuple-element.448, ...), kind=kOutput, calls=%fused_computation.11.clone.1 | convolution fusion | flops 406192128 | bytes 3297281 | tf_op jit(solution)/shard_map/while/body/eval_jaxpr/dot_general | solution.py:264
  63.7 1.6 fusion.87
  66.0 3.4 %convolution_add_fusion.4 = f32[1024,128]{1,0:T(8,128)} fusion(f32[512,1024]{1,0:T(8,128)S(1)} %get-tuple-element.416, f32[1024]{0:T(1024)S(1)} %select_maximum_fusion.2, s32[1024]{0:T(1024)S(1)} %le.90, s32[1024]{0:T(1024)S(1)} %eq.164, s32[512]{0:T(512)S(1)} %bitcast.142, s32[512]{0:T(512)S(1)} %bitcast.145, f32[1024,128]{1,0:T(8,128)} %get-tuple-element.448, ...), kind=kOutput, calls=%fused_computation.11.clone.1 | convolution fusion | flops 406192128 | bytes 3297281 | tf_op jit(solution)/shard_map/while/body/eval_jaxpr/dot_general | solution.py:264
  69.9 1.6 fusion.87
  72.2 3.4 %convolution_add_fusion.4 = f32[1024,128]{1,0:T(8,128)} fusion(f32[512,1024]{1,0:T(8,128)S(1)} %get-tuple-element.416, f32[1024]{0:T(1024)S(1)} %select_maximum_fusion.2, s32[1024]{0:T(1024)S(1)} %le.90, s32[1024]{0:T(1024)S(1)} %eq.164, s32[512]{0:T(512)S(1)} %bitcast.142, s32[512]{0:T(512)S(1)} %bitcast.145, f32[1024,128]{1,0:T(8,128)} %get-tuple-element.448, ...), kind=kOutput, calls=%fused_computation.11.clone.1 | convolution fusion | flops 406192128 | bytes 3297281 | tf_op jit(solution)/shard_map/while/body/eval_jaxpr/dot_general | solution.py:264
  76.1 1.6 fusion.87
  78.4 3.4 %convolution_add_fusion.4 = f32[1024,128]{1,0:T(8,128)} fusion(f32[512,1024]{1,0:T(8,128)S(1)} %get-tuple-element.416, f32[1024]{0:T(1024)S(1)} %select_maximum_fusion.2, s32[1024]{0:T(1024)S(1)} %le.90, s32[1024]{0:T(1024)S(1)} %eq.164, s32[512]{0:T(512)S(1)} %bitcast.142, s32[512]{0:T(512)S(1)} %bitcast.145, f32[1024,128]{1,0:T(8,128)} %get-tuple-element.448, ...), kind=kOutput, calls=%fused_computation.11.clone.1 | convolution fusion | flops 406192128 | bytes 3297281 | tf_op jit(solution)/shard_map/while/body/eval_jaxpr/dot_general | solution.py:264
  82.3 1.6 fusion.87
  84.5 3.4 %convolution_add_fusion.4 = f32[1024,128]{1,0:T(8,128)} fusion(f32[512,1024]{1,0:T(8,128)S(1)} %get-tuple-element.416, f32[1024]{0:T(1024)S(1)} %select_maximum_fusion.2, s32[1024]{0:T(1024)S(1)} %le.90, s32[1024]{0:T(1024)S(1)} %eq.164, s32[512]{0:T(512)S(1)} %bitcast.142, s32[512]{0:T(512)S(1)} %bitcast.145, f32[1024,128]{1,0:T(8,128)} %get-tuple-element.448, ...), kind=kOutput, calls=%fused_computation.11.clone.1 | convolution fusion | flops 406192128 | bytes 3297281 | tf_op jit(solution)/shard_map/while/body/eval_jaxpr/dot_general | solution.py:264
  88.4 1.6 fusion.87
  90.7 3.4 %convolution_add_fusion.4 = f32[1024,128]{1,0:T(8,128)} fusion(f32[512,1024]{1,0:T(8,128)S(1)} %get-tuple-element.416, f32[1024]{0:T(1024)S(1)} %select_maximum_fusion.2, s32[1024]{0:T(1024)S(1)} %le.90, s32[1024]{0:T(1024)S(1)} %eq.164, s32[512]{0:T(512)S(1)} %bitcast.142, s32[512]{0:T(512)S(1)} %bitcast.145, f32[1024,128]{1,0:T(8,128)} %get-tuple-element.448, ...), kind=kOutput, calls=%fused_computation.11.clone.1 | convolution fusion | flops 406192128 | bytes 3297281 | tf_op jit(solution)/shard_map/while/body/eval_jaxpr/dot_general | solution.py:264
  94.6 1.6 fusion.87
  96.9 3.4 %convolution_add_fusion.4 = f32[1024,128]{1,0:T(8,128)} fusion(f32[512,1024]{1,0:T(8,128)S(1)} %get-tuple-element.416, f32[1024]{0:T(1024)S(1)} %select_maximum_fusion.2, s32[1024]{0:T(1024)S(1)} %le.90, s32[1024]{0:T(1024)S(1)} %eq.164, s32[512]{0:T(512)S(1)} %bitcast.142, s32[512]{0:T(512)S(1)} %bitcast.145, f32[1024,128]{1,0:T(8,128)} %get-tuple-element.448, ...), kind=kOutput, calls=%fused_computation.11.clone.1 | convolution fusion | flops 406192128 | bytes 3297281 | tf_op jit(solution)/shard_map/while/body/eval_jaxpr/dot_general | solution.py:264
  100.8 1.6 fusion.87
  103.0 3.4 %convolution_add_fusion.4 = f32[1024,128]{1,0:T(8,128)} fusion(f32[512,1024]{1,0:T(8,128)S(1)} %get-tuple-element.416, f32[1024]{0:T(1024)S(1)} %select_maximum_fusion.2, s32[1024]{0:T(1024)S(1)} %le.90, s32[1024]{0:T(1024)S(1)} %eq.164, s32[512]{0:T(512)S(1)} %bitcast.142, s32[512]{0:T(512)S(1)} %bitcast.145, f32[1024,128]{1,0:T(8,128)} %get-tuple-element.448, ...), kind=kOutput, calls=%fused_computation.11.clone.1 | convolution fusion | flops 406192128 | bytes 3297281 | tf_op jit(solution)/shard_map/while/body/eval_jaxpr/dot_general | solution.py:264
  106.5 4.4 %collective-permute-start.16 = (bf16[256,8192]{1,0:T(8,128)(2,1)}, bf16[256,8192]{1,0:T(8,128)(2,1)}, u32[]{:S(2)}, u32[]{:S(2)}) collective-permute-start(bf16[256,8192]{1,0:T(8,128)(2,1)} %bitcast.156), channel_id=1, source_target_pairs={{16,0},{32,16},{48,32},{64,48},{80,64},{96,80},{112,96},{17,1},{33... | collective-permute-start | bytes 12582920 | tf_op jit(solution)/shard_map/ppermute | solution.py:25
  110.9 7.1 %fusion.34 = bf16[256,512]{1,0:T(8,128)(2,1)S(1)} fusion(bf16[1,8192,512]{2,1,0:T(8,128)(2,1)} %all-gather.6.cloned.1.call-done, bf16[1,256,8192]{2,1,0:T(8,128)(2,1)} %param.13), kind=kOutput, calls=%fused_computation.52 | convolution fusion | flops 2147614720 | bytes 12845056 | tf_op jit(solution)/shard_map/dot_general | solution.py:205
  119.6 48.4 %while.29 = (s32[]{:T(128)}, f32[1024,128]{1,0:T(8,128)S(1)}, bf16[8,512,256]{2,1,0:T(8,128)(2,1)}, s32[8,512]{1,0:T(8,128)S(1)}, s32[8,512]{1,0:T(8,128)S(1)}, ...) while((s32[]{:T(128)}, f32[1024,128]{1,0:T(8,128)S(1)}, ...), condition=%wide.region_10.11_spmd.clone, body=%wide.region_9.10_spmd.clone.sunk | while | flops 677642240 | bytes 14342307 | solution.py:297
  120.1 1.7 bitcast_select_fusion.3
  126.2 1.8 bitcast_select_fusion.3
  132.3 1.7 bitcast_select_fusion.3
  134.9 1.4 fusion.102
  138.3 1.7 bitcast_select_fusion.3
  144.4 1.7 bitcast_select_fusion.3
  150.4 1.7 bitcast_select_fusion.3
  156.4 1.7 bitcast_select_fusion.3
  159.1 1.4 fusion.102
  162.5 1.7 bitcast_select_fusion.3
  168.0 4.2 %all-to-all-start = ((bf16[16,256,256]{2,1,0:T(8,128)(2,1)}), bf16[16,256,256]{2,1,0:T(8,128)(2,1)S(1)}, u32[]{:S(2)}, u32[]{:S(2)}) async-start(bf16[16,256,256]{2,1,0:T(8,128)(2,1)} %bitcast.138), calls=%async_computation | async-start | bytes 4194304 | tf_op jit(solution)/shard_map/all_to_all | solution.py:36
  173.1 2.4 fusion.38
  175.6 1.9 collective-permute-start.15
  177.5 32.4 %all-to-all-done = bf16[16,256,256]{2,1,0:T(8,128)(2,1)S(1)} async-done(((bf16[16,256,256]{2,1,0:T(8,128)(2,1)}), bf16[16,256,256]{2,1,0:T(8,128)(2,1)S(1)}, u32[]{:S(2)}, u32[]{:S(2)}) %all-to-all-start) | async-done | bytes 2097184 | tf_op jit(solution)/shard_map/all_to_all | solution.py:36
  211.0 2.4 collective-permute-start.13
  214.1 8.8 %shard_map.91.base_ref = f32[256,8192]{1,0:T(8,128)} custom-call(bf16[256,512]{1,0:T(8,128)(2,1)} %copy-done.1, bf16[8192,768]{1,0:T(8,128)(2,1)} %all-gather.4.cloned.1.call-done.weight_ref, bf16[256,8192]{1,0:T(8,128)(2,1)} %collective-permute-done.16.base_ref), custom_call_target="tpu_custom_call" | custom-call | flops 2147483648 | bytes 21233664 | tf_op jit(solution)/shard_map/pallas_call | solution.py:51
  223.6 6.8 %shard_map.92 = bf16[256,8192]{1,0:T(8,128)(2,1)} custom-call(bf16[256,256]{1,0:T(8,128)(2,1)} %copy-done.2, bf16[8192,768]{1,0:T(8,128)(2,1)} %all-gather.4.cloned.1.call-done.weight_ref, f32[256,8192]{1,0:T(8,128)} %shard_map.91.base_ref), custom_call_target="tpu_custom_call" | custom-call | flops 1073741824 | bytes 16908288 | tf_op jit(solution)/shard_map/pallas_call | solution.py:51
  (263 shorter events, 58.9 us)
Async XLA Ops:
  6.5 25.0 %copy-start.3 = (s32[1,32]{1,0:T(1,128)S(1)}, s32[1,32]{1,0:T(1,128)}, u32[]{:S(2)}) copy-start(s32[1,32]{1,0:T(1,128)} %param.19) | copy-start | bytes 388
  6.5 104.4 %all-gather.6.cloned.1.call-start = ((), (), s32[]{:S(2)}) async-start(), calls=%async_computation.2 | async-start | bytes 8912896 | tf_op jit(solution)/shard_map/all_gather | solution.py:207
  7.3 206.2 %all-gather.4.cloned.1.call-start = ((), (), s32[]{:S(2)}) async-start(), calls=%async_computation.1 | async-start | bytes 13369344 | tf_op jit(solution)/shard_map/all_gather | solution.py:204
  8.2 11.0 %collective-permute-start.1 = (bf16[128,256]{1,0:T(8,128)(2,1)S(1)}, bf16[128,256]{1,0:T(8,128)(2,1)S(1)}, u32[]{:S(2)}, u32[]{:S(2)}) collective-permute-start(bf16[128,256]{1,0:T(8,128)(2,1)S(1)} %get-tuple-element.278), channel_id=1, source_target_pairs={{0,3},{1,0},{2,1},{3,2},{4,7},{5,4},{6,5},{7,6},{8,11},{9,8},{10,9... | collective-permute-start | bytes 196616 | tf_op jit(solution)/shard_map/ppermute | solution.py:82
  11.6 7.2 %collective-permute-start = (bf16[128,256]{1,0:T(8,128)(2,1)S(1)}, bf16[128,256]{1,0:T(8,128)(2,1)S(1)}, u32[]{:S(2)}, u32[]{:S(2)}) collective-permute-start(bf16[128,256]{1,0:T(8,128)(2,1)S(1)} %get-tuple-element.278), channel_id=1, source_target_pairs={{0,1},{1,2},{2,3},{3,0},{4,5},{5,6},{6,7},{7,4},{8,9},{9,10},{10,1... | collective-permute-start | bytes 196616 | tf_op jit(solution)/shard_map/ppermute | solution.py:82
  11.6 13.7 %collective-permute-start.7 = (bf16[128,256]{1,0:T(8,128)(2,1)S(1)}, bf16[128,256]{1,0:T(8,128)(2,1)S(1)}, u32[]{:S(2)}, u32[]{:S(2)}) collective-permute-start(bf16[128,256]{1,0:T(8,128)(2,1)S(1)} %get-tuple-element.279), channel_id=1, source_target_pairs={{0,12},{1,13},{2,14},{3,15},{4,0},{5,1},{6,2},{7,3},{8,4},{9,5},{1... | collective-permute-start | bytes 196616 | tf_op jit(solution)/shard_map/ppermute | solution.py:82
  14.3 9.1 %collective-permute-start.6 = (bf16[128,256]{1,0:T(8,128)(2,1)S(1)}, bf16[128,256]{1,0:T(8,128)(2,1)S(1)}, u32[]{:S(2)}, u32[]{:S(2)}) collective-permute-start(bf16[128,256]{1,0:T(8,128)(2,1)S(1)} %get-tuple-element.279), channel_id=1, source_target_pairs={{0,4},{1,5},{2,6},{3,7},{4,8},{5,9},{6,10},{7,11},{8,12},{9,13},{1... | collective-permute-start | bytes 196616 | tf_op jit(solution)/shard_map/ppermute | solution.py:82
  15.3 26.2 %collective-permute-start.12 = (bf16[128,512]{1,0:T(8,128)(2,1)S(1)}, bf16[128,512]{1,0:T(8,128)(2,1)S(1)}, u32[]{:S(2)}, u32[]{:S(2)}) collective-permute-start(bf16[128,512]{1,0:T(8,128)(2,1)S(1)} %get-tuple-element.272), channel_id=1, source_target_pairs={{0,8},{1,9},{2,10},{3,11},{4,12},{5,13},{6,14},{7,15},{8,0},{9,1},... | collective-permute-start | bytes 393224 | tf_op jit(solution)/shard_map/ppermute | solution.py:19
  18.8 6.3 %collective-permute-start.2 = (bf16[128,256]{1,0:T(8,128)(2,1)S(1)}, bf16[128,256]{1,0:T(8,128)(2,1)S(1)}, u32[]{:S(2)}, u32[]{:S(2)}) collective-permute-start(bf16[128,256]{1,0:T(8,128)(2,1)S(1)} %collective-permute-done), channel_id=1, source_target_pairs={{0,1},{1,2},{2,3},{3,0},{4,5},{5,6},{6,7},{7,4},{8,9},{9,10},{10,1... | collective-permute-start | bytes 196616 | tf_op jit(solution)/shard_map/ppermute | solution.py:82
  19.2 37.9 %collective-permute-start.14 = (bf16[512,768]{1,0:T(8,128)(2,1)}, bf16[512,768]{1,0:T(8,128)(2,1)S(1)}, u32[]{:S(2)}, u32[]{:S(2)}) collective-permute-start(bf16[512,768]{1,0:T(8,128)(2,1)} %bitcast.157), channel_id=1, source_target_pairs={{16,0},{32,16},{48,32},{64,48},{80,64},{96,80},{112,96},{17,1},{33... | collective-permute-start | bytes 2359304 | tf_op jit(solution)/shard_map/ppermute | solution.py:25
  23.5 6.7 %collective-permute-start.8 = (bf16[128,256]{1,0:T(8,128)(2,1)S(1)}, bf16[128,256]{1,0:T(8,128)(2,1)S(1)}, u32[]{:S(2)}, u32[]{:S(2)}) collective-permute-start(bf16[128,256]{1,0:T(8,128)(2,1)S(1)} %collective-permute-done.6), channel_id=1, source_target_pairs={{0,4},{1,5},{2,6},{3,7},{4,8},{5,9},{6,10},{7,11},{8,12},{9,13},{1... | collective-permute-start | bytes 196616 | tf_op jit(solution)/shard_map/ppermute | solution.py:82
  25.2 16.0 %collective-permute-start.3 = (bf16[4,128,256]{2,1,0:T(8,128)(2,1)S(1)}, bf16[4,128,256]{2,1,0:T(8,128)(2,1)S(1)}, u32[]{:S(2)}, u32[]{:S(2)}) collective-permute-start(bf16[4,128,256]{2,1,0:T(8,128)(2,1)S(1)} %get-tuple-element.274), channel_id=1, source_target_pairs={{0,4},{1,5},{2,6},{3,7},{4,8},{5,9},{6,10},{7,11},{8,12},{9,13},{1... | collective-permute-start | bytes 786440 | tf_op jit(solution)/shard_map/ppermute | solution.py:82
  30.2 13.8 %collective-permute-start.9 = (bf16[4,128,256]{2,1,0:T(8,128)(2,1)S(1)}, bf16[4,128,256]{2,1,0:T(8,128)(2,1)}, u32[]{:S(2)}, u32[]{:S(2)}) collective-permute-start(bf16[4,128,256]{2,1,0:T(8,128)(2,1)S(1)} %get-tuple-element.276), channel_id=1, source_target_pairs={{0,1},{1,2},{2,3},{3,0},{4,5},{5,6},{6,7},{7,4},{8,9},{9,10},{10,1... | collective-permute-start | bytes 786440 | tf_op jit(solution)/shard_map/ppermute | solution.py:82
  33.6 12.2 %collective-permute-start.4 = (bf16[4,128,256]{2,1,0:T(8,128)(2,1)S(1)}, bf16[4,128,256]{2,1,0:T(8,128)(2,1)}, u32[]{:S(2)}, u32[]{:S(2)}) collective-permute-start(bf16[4,128,256]{2,1,0:T(8,128)(2,1)S(1)} %get-tuple-element.274), channel_id=1, source_target_pairs={{0,12},{1,13},{2,14},{3,15},{4,0},{5,1},{6,2},{7,3},{8,4},{9,5},{1... | collective-permute-start | bytes 786440 | tf_op jit(solution)/shard_map/ppermute | solution.py:82
  41.2 8.3 %collective-permute-start.5 = (bf16[4,128,256]{2,1,0:T(8,128)(2,1)S(1)}, bf16[4,128,256]{2,1,0:T(8,128)(2,1)}, u32[]{:S(2)}, u32[]{:S(2)}) collective-permute-start(bf16[4,128,256]{2,1,0:T(8,128)(2,1)S(1)} %collective-permute-done.3), channel_id=1, source_target_pairs={{0,4},{1,5},{2,6},{3,7},{4,8},{5,9},{6,10},{7,11},{8,12},{9,13},{1... | collective-permute-start | bytes 786440 | tf_op jit(solution)/shard_map/ppermute | solution.py:82
  41.5 9.2 %collective-permute-start.10 = (bf16[4,128,256]{2,1,0:T(8,128)(2,1)S(1)}, bf16[4,128,256]{2,1,0:T(8,128)(2,1)}, u32[]{:S(2)}, u32[]{:S(2)}) collective-permute-start(bf16[4,128,256]{2,1,0:T(8,128)(2,1)S(1)} %get-tuple-element.276), channel_id=1, source_target_pairs={{0,3},{1,0},{2,1},{3,2},{4,7},{5,4},{6,5},{7,6},{8,11},{9,8},{10,9... | collective-permute-start | bytes 786440 | tf_op jit(solution)/shard_map/ppermute | solution.py:82
  44.0 8.0 %collective-permute-start.11 = (bf16[4,128,256]{2,1,0:T(8,128)(2,1)}, bf16[4,128,256]{2,1,0:T(8,128)(2,1)}, u32[]{:S(2)}, u32[]{:S(2)}) collective-permute-start(bf16[4,128,256]{2,1,0:T(8,128)(2,1)} %collective-permute-done.9), channel_id=1, source_target_pairs={{0,1},{1,2},{2,3},{3,0},{4,5},{5,6},{6,7},{7,4},{8,9},{9,10},{10,1... | collective-permute-start | bytes 786440 | tf_op jit(solution)/shard_map/ppermute | solution.py:82
  57.1 1.0 copy-start
  106.5 106.9 %collective-permute-start.16 = (bf16[256,8192]{1,0:T(8,128)(2,1)}, bf16[256,8192]{1,0:T(8,128)(2,1)}, u32[]{:S(2)}, u32[]{:S(2)}) collective-permute-start(bf16[256,8192]{1,0:T(8,128)(2,1)} %bitcast.156), channel_id=1, source_target_pairs={{16,0},{32,16},{48,32},{64,48},{80,64},{96,80},{112,96},{17,1},{33... | collective-permute-start | bytes 12582920 | tf_op jit(solution)/shard_map/ppermute | solution.py:25
  168.0 41.9 %all-to-all-start = ((bf16[16,256,256]{2,1,0:T(8,128)(2,1)}), bf16[16,256,256]{2,1,0:T(8,128)(2,1)S(1)}, u32[]{:S(2)}, u32[]{:S(2)}) async-start(bf16[16,256,256]{2,1,0:T(8,128)(2,1)} %bitcast.138), calls=%async_computation | async-start | bytes 4194304 | tf_op jit(solution)/shard_map/all_to_all | solution.py:36
  175.6 37.8 %collective-permute-start.15 = (bf16[256,512]{1,0:T(8,128)(2,1)S(1)}, bf16[256,512]{1,0:T(8,128)(2,1)S(1)}, u32[]{:S(2)}, u32[]{:S(2)}) collective-permute-start(bf16[256,512]{1,0:T(8,128)(2,1)S(1)} %convert_element_type.71), channel_id=1, source_target_pairs={{16,0},{32,16},{48,32},{64,48},{80,64},{96,80},{112,96},{17,1},{33... | collective-permute-start | bytes 786440 | tf_op jit(solution)/shard_map/ppermute | solution.py:25
  211.0 11.9 %collective-permute-start.13 = (bf16[256,256]{1,0:T(8,128)(2,1)S(1)}, bf16[256,256]{1,0:T(8,128)(2,1)S(1)}, u32[]{:S(2)}, u32[]{:S(2)}) collective-permute-start(bf16[256,256]{1,0:T(8,128)(2,1)S(1)} %pad_maximum_fusion.9), channel_id=1, source_target_pairs={{16,0},{32,16},{48,32},{64,48},{80,64},{96,80},{112,96},{17,1},{33... | collective-permute-start | bytes 393224 | tf_op jit(solution)/shard_map/ppermute | solution.py:25
  213.4 0.7 copy-start.1
  222.9 0.7 copy-start.2
Sparse Core Ops, SparseCore 0:
  9.5 78.3 all-gather.5
  90.0 100.7 all-gather.3

commit v13 on v8

--- a/solution.py
+++ b/solution.py
@@ -91,6 +91,19 @@
 def ring_gather(value, first_phase, side):
     inner = ring_four(value, first_phase, side)
     return ring_four(inner, 1 - first_phase, side).reshape((side * side,) + value.shape)
+
+
+def grid_scatter_sum(rows, side):
+    region = rows.shape[0] // (side * side)
+    tiles = rows.reshape(side, side, region, rows.shape[1])
+    along_x = [[row * side + col for col in range(side)] for row in range(side)]
+    along_y = [[row * side + col for row in range(side)] for col in range(side)]
+    first = lax.all_to_all(
+        jnp.moveaxis(tiles, 1, 0).astype(jnp.bfloat16), "ctx", 0, 0, axis_index_groups=along_x
+    )
+    first = jnp.sum(first.astype(jnp.float32), axis=0)
+    second = lax.all_to_all(first.astype(jnp.bfloat16), "ctx", 0, 0, axis_index_groups=along_y)
+    return jnp.sum(second.astype(jnp.float32), axis=0)
 
 
 def ring_position(device, source, first_phase, side):
@@ -303,9 +316,12 @@
         .astype(jnp.bfloat16)
     )
     next_query_grad = passed_along_2(query_grad, "pipe", -1)
-    keyval_grad = summed_rows(
-        key_terms.reshape(seq_len, 2 * head_dim).astype(jnp.bfloat16), "ctx"
-    )
+    if side == len(RING_OFFSETS):
+        keyval_grad = grid_scatter_sum(key_terms.reshape(seq_len, 2 * head_dim), side)
+    else:
+        keyval_grad = summed_rows(
+            key_terms.reshape(seq_len, 2 * head_dim).astype(jnp.bfloat16), "ctx"
+        )
     key_grad = unrotate(keyval_grad[:, :head_dim], own_positions).astype(jnp.bfloat16)
     value_grad = keyval_grad[:, head_dim:].astype(jnp.bfloat16)
     next_keyval_grad = passed_along_2(

time: 230 us -> 243 us (1.057)
  starting transfers between devices: 29.5 us -> 34.9 us
  waiting for transfers between devices: 67.8 us -> 71.1 us
  local copies, waits for them, and re-layouts: 44.4 us -> 47.3 us
    all_to_all x1 -> x2, starting transfers between devices: 4.15 us -> 7.71 us  [the longest x1 4.11 us: grid_scatter_sum(): lax.all_to_all(first.astype(jnp.bfloat16), 'ctx', 0, 0, axis_index_groups...]
    all_to_all x1 -> x2, waiting for transfers between devices: 42.4 us -> 45.9 us  [the longest x1 42.4 us: grid_scatter_sum(): lax.all_to_all(jnp.moveaxis(tiles, 1, 0).astype(jnp.bfloat16), 'ctx', 0,...]
    convert_element_type x0 -> x1, local copies, waits for them, and re-layouts: none -> 3.12 us  [grid_scatter_sum(): jnp.moveaxis(tiles, 1, 0).astype(jnp.bfloat16)]
  transfers between devices with their start and end apart: 20 -> 21, of which waited for: 7 -> 8; matrix products, arithmetic and copies ran while one was open for 42% -> 42% of each run, Pallas kernels for 0% -> 0%
where the time goes in v13:
time: 243 us; the launch traced here: 242 us
  waiting for transfers between devices  71.1 us (29%)
  matrix products  47.6 us (20%)
  local copies, waits for them, and re-layouts  47.3 us (19%)
  starting transfers between devices  34.9 us (14%)
  between operations  15.1 us (6%)
  other arithmetic  15 us (6%)
  Pallas kernels  9.07 us (4%)
    all_to_all x1, waiting for transfers between devices, grid_scatter_sum(): lax.all_to_all(jnp.moveaxis(tiles, 1, 0).astype(jnp.bfloat16), 'ctx', 0,...  42.4 us
    ppermute x12, waiting for transfers between devices, ring_shift(): return lax.ppermute(value, 'ctx', pairs)  20.8 us
    squeeze x16, local copies, waits for them, and re-layouts, body(): lax.scan(running_total, start_carry, key_blocks)  15.7 us
    dot_general x24, matrix products, contract_cols(): lax.dot_general(left_rows, right_rows, (((1,), (1,)), ((), ())), preferre...  14.3 us
    ppermute x4, starting transfers between devices, passed_along_2(): return lax.ppermute(value, axis, pairs)  13.7 us
    dot_general x8, matrix products, running_total(): jnp.dot(weights, value_wide, precision=lax.Precision.HIGH)  12.9 us
    ppermute x12, starting transfers between devices, ring_shift(): return lax.ppermute(value, 'ctx', pairs)  11.8 us
    while x40, local copies, waits for them, and re-layouts  9.15 us
  transfers between devices with their start and end apart: 21, of which 8 were waited for; matrix products, arithmetic and copies ran while one was open for 42% of the time, Pallas kernels for 0%

profile of v13, /device:TPU:1, one launch (start us, length us, event | category | flops | bytes accessed | tf_op | source)
XLA Modules:
  0.0 241.6 jit_solution(16171032194248883476)
XLA Ops:
  8.2 2.1 collective-permute-start
  10.3 1.3 collective-permute-start.1
  11.7 1.4 collective-permute-start.6
  13.1 1.4 collective-permute-start.7
  14.5 1.0 fusion.55
  15.5 1.7 collective-permute-start.12
  19.2 4.2 %collective-permute-start.15 = (bf16[512,768]{1,0:T(8,128)(2,1)}, bf16[512,768]{1,0:T(8,128)(2,1)}, u32[]{:S(2)}, u32[]{:S(2)}) collective-permute-start(bf16[512,768]{1,0:T(8,128)(2,1)} %bitcast.161), channel_id=1, source_target_pairs={{16,0},{32,16},{48,32},{64,48},{80,64},{96,80},{112,96},{17,1},{33... | collective-permute-start | bytes 2359304 | tf_op jit(solution)/shard_map/ppermute | solution.py:25
  24.6 5.6 %collective-permute-done.8 = bf16[128,256]{1,0:T(8,128)(2,1)S(1)} collective-permute-done((bf16[128,256]{1,0:T(8,128)(2,1)S(1)}, bf16[128,256]{1,0:T(8,128)(2,1)S(1)}, u32[]{:S(2)}, u32[]{:S(2)}) %collective-permute-start.8) | collective-permute-done | bytes 65568 | tf_op jit(solution)/shard_map/ppermute | solution.py:81
  30.2 1.3 collective-permute-start.9
  33.5 7.6 %collective-permute-done.3 = bf16[4,128,256]{2,1,0:T(8,128)(2,1)S(1)} collective-permute-done((bf16[4,128,256]{2,1,0:T(8,128)(2,1)S(1)}, bf16[4,128,256]{2,1,0:T(8,128)(2,1)S(1)}, u32[]{:S(2)}, u32[]{:S(2)}) %collective-permute-start.3) | collective-permute-done | bytes 262176 | tf_op jit(solution)/shard_map/ppermute | solution.py:81
  41.4 2.9 %collective-permute-start.10 = (bf16[4,128,256]{2,1,0:T(8,128)(2,1)S(1)}, bf16[4,128,256]{2,1,0:T(8,128)(2,1)}, u32[]{:S(2)}, u32[]{:S(2)}) collective-permute-start(bf16[4,128,256]{2,1,0:T(8,128)(2,1)S(1)} %get-tuple-element.276), channel_id=1, source_target_pairs={{0,3},{1,0},{2,1},{3,2},{4,7},{5,4},{6,5},{7,6},{8,11},{9,8},{10,9... | collective-permute-start | bytes 786440 | tf_op jit(solution)/shard_map/ppermute | solution.py:81
  45.5 3.3 %collective-permute-done.5 = bf16[4,128,256]{2,1,0:T(8,128)(2,1)S(1)} collective-permute-done((bf16[4,128,256]{2,1,0:T(8,128)(2,1)S(1)}, bf16[4,128,256]{2,1,0:T(8,128)(2,1)S(1)}, u32[]{:S(2)}, u32[]{:S(2)}) %collective-permute-start.5) | collective-permute-done | bytes 262176 | tf_op jit(solution)/shard_map/ppermute | solution.py:81
  49.8 3.5 %collective-permute-done.11 = bf16[4,128,256]{2,1,0:T(8,128)(2,1)} collective-permute-done((bf16[4,128,256]{2,1,0:T(8,128)(2,1)S(1)}, bf16[4,128,256]{2,1,0:T(8,128)(2,1)}, u32[]{:S(2)}, u32[]{:S(2)}) %collective-permute-start.11) | collective-permute-done | bytes 262176 | tf_op jit(solution)/shard_map/ppermute | solution.py:81
  53.3 1.2 pad_maximum_fusion.2
  54.6 2.1 gather_fusion
  56.7 44.0 %while.28 = (s32[]{:T(128)}, f32[1024]{0:T(1024)S(1)}, f32[1024]{0:T(1024)S(1)}, f32[1024,128]{1,0:T(8,128)}, s32[8,512]{1,0:T(8,128)S(1)}, /*index=5*/s32[8,512...) while((s32[]{:T(128)}, f32[1024]{0:T(1024)S(1)}, ...), condition=%wide.region_7.8_spmd.clone, body=%wide.region_4.7_spmd.clone.sunk | while | flops 547230720 | bytes 12720321 | solution.py:287
  56.8 1.0 dynamic-slice_bitcast_fusion.4
  59.9 1.6 convolution_add_fusion.4
  62.3 1.0 dynamic-slice_bitcast_fusion.4
  65.4 1.6 convolution_add_fusion.4
  67.8 1.0 dynamic-slice_bitcast_fusion.4
  70.9 1.6 convolution_add_fusion.4
  73.3 1.0 dynamic-slice_bitcast_fusion.4
  76.4 1.6 convolution_add_fusion.4
  78.8 1.0 dynamic-slice_bitcast_fusion.4
  81.9 1.6 convolution_add_fusion.4
  87.4 1.6 convolution_add_fusion.4
  89.8 1.0 dynamic-slice_bitcast_fusion.4
  92.9 1.6 convolution_add_fusion.4
  95.3 1.0 dynamic-slice_bitcast_fusion.4
  98.4 1.6 convolution_add_fusion.4
  100.8 3.4 %collective-permute-start.16 = (bf16[256,8192]{1,0:T(8,128)(2,1)}, bf16[256,8192]{1,0:T(8,128)(2,1)}, u32[]{:S(2)}, u32[]{:S(2)}) collective-permute-start(bf16[256,8192]{1,0:T(8,128)(2,1)} %bitcast.160), channel_id=1, source_target_pairs={{16,0},{32,16},{48,32},{64,48},{80,64},{96,80},{112,96},{17,1},{33... | collective-permute-start | bytes 12582920 | tf_op jit(solution)/shard_map/ppermute | solution.py:25
  104.2 7.2 %fusion.34 = bf16[256,512]{1,0:T(8,128)(2,1)S(1)} fusion(bf16[1,8192,512]{2,1,0:T(8,128)(2,1)} %all-gather.6.cloned.1.call-done, bf16[1,256,8192]{2,1,0:T(8,128)(2,1)} %param.13), kind=kOutput, calls=%fused_computation.51 | convolution fusion | flops 2147614720 | bytes 12845056 | tf_op jit(solution)/shard_map/dot_general | solution.py:217
  111.9 41.1 %while.29 = (s32[]{:T(128)}, f32[1024,128]{1,0:T(8,128)S(1)}, bf16[8,512,256]{2,1,0:T(8,128)(2,1)}, s32[8,512]{1,0:T(8,128)S(1)}, s32[8,512]{1,0:T(8,128)S(1)}, ...) while((s32[]{:T(128)}, f32[1024,128]{1,0:T(8,128)S(1)}, ...), condition=%wide.region_10.11_spmd.clone, body=%wide.region_9.10_spmd.clone.sunk | while | flops 677642240 | bytes 14342807 | solution.py:309
  127.3 1.0 dynamic-slice_bitcast_fusion.5
  142.8 1.0 dynamic-slice_bitcast_fusion.5
  147.9 1.0 dynamic-slice_bitcast_fusion.5
  153.0 3.1 %copy.24 = bf16[4,4,256,256]{3,2,1,0:T(8,128)(2,1)} copy(bf16[4,4,256,256]{3,2,0,1:T(8,128)(2,1)} %bitcast.139) | data formatting | bytes 4194304 | tf_op jit(solution)/shard_map/convert_element_type | solution.py:102
  156.2 3.6 %all-to-all-start = ((bf16[4,4,256,256]{3,2,1,0:T(8,128)(2,1)}), bf16[4,4,256,256]{3,2,1,0:T(8,128)(2,1)S(1)}, u32[]{:S(2)}, u32[]{:S(2)}) async-start(bf16[4,4,256,256]{3,2,1,0:T(8,128)(2,1)} %copy.24), calls=%async_computation | async-start | bytes 4194304 | tf_op jit(solution)/shard_map/all_to_all | solution.py:101
  160.3 42.4 %all-to-all-done = bf16[4,4,256,256]{3,2,1,0:T(8,128)(2,1)S(1)} async-done(((bf16[4,4,256,256]{3,2,1,0:T(8,128)(2,1)}), bf16[4,4,256,256]{3,2,1,0:T(8,128)(2,1)S(1)}, u32[]{:S(2)}, u32[]{:S(2)}) %all-to-all-start) | async-done | bytes 2097184 | tf_op jit(solution)/shard_map/all_to_all | solution.py:101
  202.7 1.2 reduce_sum.73
  204.0 4.1 %all-to-all-start.1 = ((bf16[4,256,256]{2,1,0:T(8,128)(2,1)}), bf16[4,256,256]{2,1,0:T(8,128)(2,1)S(1)}, u32[]{:S(2)}, u32[]{:S(2)}) async-start(bf16[4,256,256]{2,1,0:T(8,128)(2,1)} %reduce_sum.73), calls=%async_computation.1 | async-start | bytes 1048576 | tf_op jit(solution)/shard_map/all_to_all | solution.py:105
  208.3 2.4 fusion.38
  210.9 2.6 %collective-permute-start.13 = (bf16[256,512]{1,0:T(8,128)(2,1)S(1)}, bf16[256,512]{1,0:T(8,128)(2,1)S(1)}, u32[]{:S(2)}, u32[]{:S(2)}) collective-permute-start(bf16[256,512]{1,0:T(8,128)(2,1)S(1)} %convert_element_type.71), channel_id=1, source_target_pairs={{16,0},{32,16},{48,32},{64,48},{80,64},{96,80},{112,96},{17,1},{33... | collective-permute-start | bytes 786440 | tf_op jit(solution)/shard_map/ppermute | solution.py:25
  213.5 3.5 %all-to-all-done.1 = bf16[4,256,256]{2,1,0:T(8,128)(2,1)S(1)} async-done(((bf16[4,256,256]{2,1,0:T(8,128)(2,1)}), bf16[4,256,256]{2,1,0:T(8,128)(2,1)S(1)}, u32[]{:S(2)}, u32[]{:S(2)}) %all-to-all-start.1) | async-done | bytes 524320 | tf_op jit(solution)/shard_map/all_to_all | solution.py:105
  217.8 3.5 %collective-permute-start.14 = (bf16[256,256]{1,0:T(8,128)(2,1)S(1)}, bf16[256,256]{1,0:T(8,128)(2,1)S(1)}, u32[]{:S(2)}, u32[]{:S(2)}) collective-permute-start(bf16[256,256]{1,0:T(8,128)(2,1)S(1)} %pad_maximum_fusion.10), channel_id=1, source_target_pairs={{16,0},{32,16},{48,32},{64,48},{80,64},{96,80},{112,96},{17,1},{33... | collective-permute-start | bytes 393224 | tf_op jit(solution)/shard_map/ppermute | solution.py:25
  221.3 3.6 %collective-permute-done.14 = bf16[256,256]{1,0:T(8,128)(2,1)S(1)} collective-permute-done((bf16[256,256]{1,0:T(8,128)(2,1)S(1)}, bf16[256,256]{1,0:T(8,128)(2,1)S(1)}, u32[]{:S(2)}, u32[]{:S(2)}) %collective-permute-start.14) | collective-permute-done | bytes 131104 | tf_op jit(solution)/shard_map/ppermute | solution.py:25
  225.7 9.1 %shard_map.91 = bf16[256,8192]{1,0:T(8,128)(2,1)} custom-call(bf16[256,768]{1,0:T(8,128)(2,1)} %pad_maximum_fusion.4.grad_ref, bf16[8192,768]{1,0:T(8,128)(2,1)} %all-gather.4.cloned.1.call-done.weight_ref, bf16[256,8192]{1,0:T(8,128)(2,1)} %collective-permute-done.16.base_ref), custom_call_target="tpu_custom_call" | custom-call | flops 3221225472 | bytes 21364736 | tf_op jit(solution)/shard_map/pallas_call | solution.py:50
  (295 shorter events, 72.1 us)
Async XLA Ops:
  6.5 25.0 %copy-start.3 = (s32[1,32]{1,0:T(1,128)S(1)}, s32[1,32]{1,0:T(1,128)}, u32[]{:S(2)}) copy-start(s32[1,32]{1,0:T(1,128)} %param.19) | copy-start | bytes 388
  6.5 97.6 %all-gather.6.cloned.1.call-start = ((), (), s32[]{:S(2)}) async-start(), calls=%async_computation.3 | async-start | bytes 8912896 | tf_op jit(solution)/shard_map/all_gather | solution.py:219
  7.3 218.4 %all-gather.4.cloned.1.call-start = ((), (), s32[]{:S(2)}) async-start(), calls=%async_computation.2 | async-start | bytes 13369344 | tf_op jit(solution)/shard_map/all_gather | solution.py:216
  8.2 10.8 %collective-permute-start = (bf16[128,256]{1,0:T(8,128)(2,1)S(1)}, bf16[128,256]{1,0:T(8,128)(2,1)S(1)}, u32[]{:S(2)}, u32[]{:S(2)}) collective-permute-start(bf16[128,256]{1,0:T(8,128)(2,1)S(1)} %get-tuple-element.278), channel_id=1, source_target_pairs={{0,1},{1,2},{2,3},{3,0},{4,5},{5,6},{6,7},{7,4},{8,9},{9,10},{10,1... | collective-permute-start | bytes 196616 | tf_op jit(solution)/shard_map/ppermute | solution.py:81
  10.3 8.9 %collective-permute-start.1 = (bf16[128,256]{1,0:T(8,128)(2,1)S(1)}, bf16[128,256]{1,0:T(8,128)(2,1)S(1)}, u32[]{:S(2)}, u32[]{:S(2)}) collective-permute-start(bf16[128,256]{1,0:T(8,128)(2,1)S(1)} %get-tuple-element.278), channel_id=1, source_target_pairs={{0,3},{1,0},{2,1},{3,2},{4,7},{5,4},{6,5},{7,6},{8,11},{9,8},{10,9... | collective-permute-start | bytes 196616 | tf_op jit(solution)/shard_map/ppermute | solution.py:81
  11.7 11.8 %collective-permute-start.6 = (bf16[128,256]{1,0:T(8,128)(2,1)S(1)}, bf16[128,256]{1,0:T(8,128)(2,1)S(1)}, u32[]{:S(2)}, u32[]{:S(2)}) collective-permute-start(bf16[128,256]{1,0:T(8,128)(2,1)S(1)} %get-tuple-element.279), channel_id=1, source_target_pairs={{0,4},{1,5},{2,6},{3,7},{4,8},{5,9},{6,10},{7,11},{8,12},{9,13},{1... | collective-permute-start | bytes 196616 | tf_op jit(solution)/shard_map/ppermute | solution.py:81
  13.1 11.5 %collective-permute-start.7 = (bf16[128,256]{1,0:T(8,128)(2,1)S(1)}, bf16[128,256]{1,0:T(8,128)(2,1)S(1)}, u32[]{:S(2)}, u32[]{:S(2)}) collective-permute-start(bf16[128,256]{1,0:T(8,128)(2,1)S(1)} %get-tuple-element.279), channel_id=1, source_target_pairs={{0,12},{1,13},{2,14},{3,15},{4,0},{5,1},{6,2},{7,3},{8,4},{9,5},{1... | collective-permute-start | bytes 196616 | tf_op jit(solution)/shard_map/ppermute | solution.py:81
  15.5 25.9 %collective-permute-start.12 = (bf16[128,512]{1,0:T(8,128)(2,1)S(1)}, bf16[128,512]{1,0:T(8,128)(2,1)S(1)}, u32[]{:S(2)}, u32[]{:S(2)}) collective-permute-start(bf16[128,512]{1,0:T(8,128)(2,1)S(1)} %get-tuple-element.272), channel_id=1, source_target_pairs={{0,8},{1,9},{2,10},{3,11},{4,12},{5,13},{6,14},{7,15},{8,0},{9,1},... | collective-permute-start | bytes 393224 | tf_op jit(solution)/shard_map/ppermute | solution.py:19
  19.0 4.9 %collective-permute-start.2 = (bf16[128,256]{1,0:T(8,128)(2,1)S(1)}, bf16[128,256]{1,0:T(8,128)(2,1)S(1)}, u32[]{:S(2)}, u32[]{:S(2)}) collective-permute-start(bf16[128,256]{1,0:T(8,128)(2,1)S(1)} %collective-permute-done), channel_id=1, source_target_pairs={{0,1},{1,2},{2,3},{3,0},{4,5},{5,6},{6,7},{7,4},{8,9},{9,10},{10,1... | collective-permute-start | bytes 196616 | tf_op jit(solution)/shard_map/ppermute | solution.py:81
  19.2 37.5 %collective-permute-start.15 = (bf16[512,768]{1,0:T(8,128)(2,1)}, bf16[512,768]{1,0:T(8,128)(2,1)}, u32[]{:S(2)}, u32[]{:S(2)}) collective-permute-start(bf16[512,768]{1,0:T(8,128)(2,1)} %bitcast.161), channel_id=1, source_target_pairs={{16,0},{32,16},{48,32},{64,48},{80,64},{96,80},{112,96},{17,1},{33... | collective-permute-start | bytes 2359304 | tf_op jit(solution)/shard_map/ppermute | solution.py:25
  23.5 6.7 %collective-permute-start.8 = (bf16[128,256]{1,0:T(8,128)(2,1)S(1)}, bf16[128,256]{1,0:T(8,128)(2,1)S(1)}, u32[]{:S(2)}, u32[]{:S(2)}) collective-permute-start(bf16[128,256]{1,0:T(8,128)(2,1)S(1)} %collective-permute-done.6), channel_id=1, source_target_pairs={{0,4},{1,5},{2,6},{3,7},{4,8},{5,9},{6,10},{7,11},{8,12},{9,13},{1... | collective-permute-start | bytes 196616 | tf_op jit(solution)/shard_map/ppermute | solution.py:81
  24.0 17.1 %collective-permute-start.3 = (bf16[4,128,256]{2,1,0:T(8,128)(2,1)S(1)}, bf16[4,128,256]{2,1,0:T(8,128)(2,1)S(1)}, u32[]{:S(2)}, u32[]{:S(2)}) collective-permute-start(bf16[4,128,256]{2,1,0:T(8,128)(2,1)S(1)} %get-tuple-element.274), channel_id=1, source_target_pairs={{0,4},{1,5},{2,6},{3,7},{4,8},{5,9},{6,10},{7,11},{8,12},{9,13},{1... | collective-permute-start | bytes 786440 | tf_op jit(solution)/shard_map/ppermute | solution.py:81
  30.2 14.3 %collective-permute-start.9 = (bf16[4,128,256]{2,1,0:T(8,128)(2,1)S(1)}, bf16[4,128,256]{2,1,0:T(8,128)(2,1)S(1)}, u32[]{:S(2)}, u32[]{:S(2)}) collective-permute-start(bf16[4,128,256]{2,1,0:T(8,128)(2,1)S(1)} %get-tuple-element.276), channel_id=1, source_target_pairs={{0,1},{1,2},{2,3},{3,0},{4,5},{5,6},{6,7},{7,4},{8,9},{9,10},{10,1... | collective-permute-start | bytes 786440 | tf_op jit(solution)/shard_map/ppermute | solution.py:81
  33.4 12.1 %collective-permute-start.4 = (bf16[4,128,256]{2,1,0:T(8,128)(2,1)S(1)}, bf16[4,128,256]{2,1,0:T(8,128)(2,1)S(1)}, u32[]{:S(2)}, u32[]{:S(2)}) collective-permute-start(bf16[4,128,256]{2,1,0:T(8,128)(2,1)S(1)} %get-tuple-element.274), channel_id=1, source_target_pairs={{0,12},{1,13},{2,14},{3,15},{4,0},{5,1},{6,2},{7,3},{8,4},{9,5},{1... | collective-permute-start | bytes 786440 | tf_op jit(solution)/shard_map/ppermute | solution.py:81
  41.1 7.7 %collective-permute-start.5 = (bf16[4,128,256]{2,1,0:T(8,128)(2,1)S(1)}, bf16[4,128,256]{2,1,0:T(8,128)(2,1)S(1)}, u32[]{:S(2)}, u32[]{:S(2)}) collective-permute-start(bf16[4,128,256]{2,1,0:T(8,128)(2,1)S(1)} %collective-permute-done.3), channel_id=1, source_target_pairs={{0,4},{1,5},{2,6},{3,7},{4,8},{5,9},{6,10},{7,11},{8,12},{9,13},{1... | collective-permute-start | bytes 786440 | tf_op jit(solution)/shard_map/ppermute | solution.py:81
  41.4 8.4 %collective-permute-start.10 = (bf16[4,128,256]{2,1,0:T(8,128)(2,1)S(1)}, bf16[4,128,256]{2,1,0:T(8,128)(2,1)}, u32[]{:S(2)}, u32[]{:S(2)}) collective-permute-start(bf16[4,128,256]{2,1,0:T(8,128)(2,1)S(1)} %get-tuple-element.276), channel_id=1, source_target_pairs={{0,3},{1,0},{2,1},{3,2},{4,7},{5,4},{6,5},{7,6},{8,11},{9,8},{10,9... | collective-permute-start | bytes 786440 | tf_op jit(solution)/shard_map/ppermute | solution.py:81
  44.5 8.8 %collective-permute-start.11 = (bf16[4,128,256]{2,1,0:T(8,128)(2,1)S(1)}, bf16[4,128,256]{2,1,0:T(8,128)(2,1)}, u32[]{:S(2)}, u32[]{:S(2)}) collective-permute-start(bf16[4,128,256]{2,1,0:T(8,128)(2,1)S(1)} %collective-permute-done.9), channel_id=1, source_target_pairs={{0,1},{1,2},{2,3},{3,0},{4,5},{5,6},{6,7},{7,4},{8,9},{9,10},{10,1... | collective-permute-start | bytes 786440 | tf_op jit(solution)/shard_map/ppermute | solution.py:81
  58.8 1.1 copy-start
  61.5 0.8 copy-start.1
  64.3 1.1 copy-start
  67.0 0.8 copy-start.1
  69.8 1.1 copy-start
  72.5 0.8 copy-start.1
  75.3 1.1 copy-start
  78.0 0.8 copy-start.1
  80.9 1.0 copy-start
  83.5 0.8 copy-start.1
  86.3 1.0 copy-start
  89.0 0.8 copy-start.1
  91.8 1.0 copy-start
  94.5 0.8 copy-start.1
  97.3 1.0 copy-start
  100.0 0.8 copy-start.1
  100.8 124.9 %collective-permute-start.16 = (bf16[256,8192]{1,0:T(8,128)(2,1)}, bf16[256,8192]{1,0:T(8,128)(2,1)}, u32[]{:S(2)}, u32[]{:S(2)}) collective-permute-start(bf16[256,8192]{1,0:T(8,128)(2,1)} %bitcast.160), channel_id=1, source_target_pairs={{16,0},{32,16},{48,32},{64,48},{80,64},{96,80},{112,96},{17,1},{33... | collective-permute-start | bytes 12582920 | tf_op jit(solution)/shard_map/ppermute | solution.py:25
  104.1 7.4 %copy-start.2 = (f32[1024,128]{1,0:T(8,128)S(1)}, f32[1024,128]{1,0:T(8,128)}, u32[]{:S(2)}) copy-start(f32[1024,128]{1,0:T(8,128)} %get-tuple-element.127) | copy-start | bytes 1572868
  156.2 46.6 %all-to-all-start = ((bf16[4,4,256,256]{3,2,1,0:T(8,128)(2,1)}), bf16[4,4,256,256]{3,2,1,0:T(8,128)(2,1)S(1)}, u32[]{:S(2)}, u32[]{:S(2)}) async-start(bf16[4,4,256,256]{3,2,1,0:T(8,128)(2,1)} %copy.24), calls=%async_computation | async-start | bytes 4194304 | tf_op jit(solution)/shard_map/all_to_all | solution.py:101
  204.0 13.0 %all-to-all-start.1 = ((bf16[4,256,256]{2,1,0:T(8,128)(2,1)}), bf16[4,256,256]{2,1,0:T(8,128)(2,1)S(1)}, u32[]{:S(2)}, u32[]{:S(2)}) async-start(bf16[4,256,256]{2,1,0:T(8,128)(2,1)} %reduce_sum.73), calls=%async_computation.1 | async-start | bytes 1048576 | tf_op jit(solution)/shard_map/all_to_all | solution.py:105
  210.9 10.4 %collective-permute-start.13 = (bf16[256,512]{1,0:T(8,128)(2,1)S(1)}, bf16[256,512]{1,0:T(8,128)(2,1)S(1)}, u32[]{:S(2)}, u32[]{:S(2)}) collective-permute-start(bf16[256,512]{1,0:T(8,128)(2,1)S(1)} %convert_element_type.71), channel_id=1, source_target_pairs={{16,0},{32,16},{48,32},{64,48},{80,64},{96,80},{112,96},{17,1},{33... | collective-permute-start | bytes 786440 | tf_op jit(solution)/shard_map/ppermute | solution.py:25
  217.8 7.1 %collective-permute-start.14 = (bf16[256,256]{1,0:T(8,128)(2,1)S(1)}, bf16[256,256]{1,0:T(8,128)(2,1)S(1)}, u32[]{:S(2)}, u32[]{:S(2)}) collective-permute-start(bf16[256,256]{1,0:T(8,128)(2,1)S(1)} %pad_maximum_fusion.10), channel_id=1, source_target_pairs={{16,0},{32,16},{48,32},{64,48},{80,64},{96,80},{112,96},{17,1},{33... | collective-permute-start | bytes 393224 | tf_op jit(solution)/shard_map/ppermute | solution.py:25
Sparse Core Ops, SparseCore 0:
  9.5 79.0 all-gather.5
  90.7 105.3 all-gather.3

commit v14 on v8

--- a/solution.py
+++ b/solution.py
@@ -261,7 +261,7 @@
         row_total = row_total * rescale + jnp.sum(weights, axis=1)
         value_wide = pair_rows[:, head_dim:].astype(jnp.float32)
         weighted = weighted * rescale[:, None] + jnp.dot(
-            weights, value_wide, precision=lax.Precision.HIGH
+            weights, value_wide, precision=lax.Precision.DEFAULT
         )
         return ((new_top, row_total, weighted), None)
 

time: 230 us -> 230 us (level)
  matrix products: 47.7 us -> 43.2 us
  waiting for transfers between devices: 67.8 us -> 71.7 us
    dot_general x8, matrix products: 12.8 us -> 7.73 us  [running_total(): jnp.dot(weights, value_wide, precision=lax.Precision.DEFAULT)]
    all_to_all x1, waiting for transfers between devices: 42.4 us -> 46 us  [summed_rows(): lax.all_to_all(value.reshape((count, -1) + value.shape[1:]), axis, 0, 0,...]
  transfers between devices with their start and end apart: 20 -> 20, of which waited for: 7 -> 7; matrix products, arithmetic and copies ran while one was open for 42% -> 40% of each run, Pallas kernels for 0% -> 0%
where the time goes in v14:
time: 230 us; the launch traced here: 229 us
  waiting for transfers between devices  71.7 us (31%)
  local copies, waits for them, and re-layouts  44.3 us (19%)
  matrix products  43.2 us (19%)
  starting transfers between devices  29.8 us (13%)
  between operations  15.1 us (7%)
  other arithmetic  14 us (6%)
  Pallas kernels  9.08 us (4%)
    all_to_all x1, waiting for transfers between devices, summed_rows(): lax.all_to_all(value.reshape((count, -1) + value.shape[1:]), axis, 0, 0,...  46 us
    ppermute x12, waiting for transfers between devices, ring_shift(): return lax.ppermute(value, 'ctx', pairs)  20.7 us
    squeeze x16, local copies, waits for them, and re-layouts, body(): lax.scan(running_total, start_carry, key_blocks)  15.6 us
    dot_general x24, matrix products, contract_cols(): lax.dot_general(left_rows, right_rows, (((1,), (1,)), ((), ())), preferre...  14.3 us
    ppermute x4, starting transfers between devices, passed_along_2(): return lax.ppermute(value, axis, pairs)  12.2 us
    ppermute x12, starting transfers between devices, ring_shift(): return lax.ppermute(value, 'ctx', pairs)  11.8 us
    while x40, local copies, waits for them, and re-layouts  9.22 us
    pallas_call x1, Pallas kernels, projected_sum(): pl.pallas_call(projection_kernel, grid=(width // tile,), in_specs=[pl.Blo...  9.08 us
  transfers between devices with their start and end apart: 20, of which 7 were waited for; matrix products, arithmetic and copies ran while one was open for 40% of the time, Pallas kernels for 0%

profile of v14, /device:TPU:1, one launch (start us, length us, event | category | flops | bytes accessed | tf_op | source)
XLA Modules:
  0.0 228.6 jit_solution(11506989715346326721)
XLA Ops:
  8.2 2.1 collective-permute-start
  10.3 1.3 collective-permute-start.1
  11.7 1.4 collective-permute-start.6
  13.1 1.4 collective-permute-start.7
  14.5 1.0 fusion.55
  15.5 1.7 collective-permute-start.12
  19.2 4.2 %collective-permute-start.15 = (bf16[512,768]{1,0:T(8,128)(2,1)}, bf16[512,768]{1,0:T(8,128)(2,1)}, u32[]{:S(2)}, u32[]{:S(2)}) collective-permute-start(bf16[512,768]{1,0:T(8,128)(2,1)} %bitcast.159), channel_id=1, source_target_pairs={{16,0},{32,16},{48,32},{64,48},{80,64},{96,80},{112,96},{17,1},{33... | collective-permute-start | bytes 2359304 | tf_op jit(solution)/shard_map/ppermute | solution.py:25
  24.6 5.6 %collective-permute-done.8 = bf16[128,256]{1,0:T(8,128)(2,1)S(1)} collective-permute-done((bf16[128,256]{1,0:T(8,128)(2,1)S(1)}, bf16[128,256]{1,0:T(8,128)(2,1)S(1)}, u32[]{:S(2)}, u32[]{:S(2)}) %collective-permute-start.8) | collective-permute-done | bytes 65568 | tf_op jit(solution)/shard_map/ppermute | solution.py:81
  30.2 1.3 collective-permute-start.9
  33.6 7.5 %collective-permute-done.3 = bf16[4,128,256]{2,1,0:T(8,128)(2,1)S(1)} collective-permute-done((bf16[4,128,256]{2,1,0:T(8,128)(2,1)S(1)}, bf16[4,128,256]{2,1,0:T(8,128)(2,1)S(1)}, u32[]{:S(2)}, u32[]{:S(2)}) %collective-permute-start.3) | collective-permute-done | bytes 262176 | tf_op jit(solution)/shard_map/ppermute | solution.py:81
  41.4 2.9 %collective-permute-start.10 = (bf16[4,128,256]{2,1,0:T(8,128)(2,1)S(1)}, bf16[4,128,256]{2,1,0:T(8,128)(2,1)}, u32[]{:S(2)}, u32[]{:S(2)}) collective-permute-start(bf16[4,128,256]{2,1,0:T(8,128)(2,1)S(1)} %get-tuple-element.276), channel_id=1, source_target_pairs={{0,3},{1,0},{2,1},{3,2},{4,7},{5,4},{6,5},{7,6},{8,11},{9,8},{10,9... | collective-permute-start | bytes 786440 | tf_op jit(solution)/shard_map/ppermute | solution.py:81
  45.5 3.3 %collective-permute-done.5 = bf16[4,128,256]{2,1,0:T(8,128)(2,1)S(1)} collective-permute-done((bf16[4,128,256]{2,1,0:T(8,128)(2,1)S(1)}, bf16[4,128,256]{2,1,0:T(8,128)(2,1)S(1)}, u32[]{:S(2)}, u32[]{:S(2)}) %collective-permute-start.5) | collective-permute-done | bytes 262176 | tf_op jit(solution)/shard_map/ppermute | solution.py:81
  49.8 3.5 %collective-permute-done.11 = bf16[4,128,256]{2,1,0:T(8,128)(2,1)} collective-permute-done((bf16[4,128,256]{2,1,0:T(8,128)(2,1)S(1)}, bf16[4,128,256]{2,1,0:T(8,128)(2,1)}, u32[]{:S(2)}, u32[]{:S(2)}) %collective-permute-start.11) | collective-permute-done | bytes 262176 | tf_op jit(solution)/shard_map/ppermute | solution.py:81
  53.3 1.2 pad_maximum_fusion.2
  54.6 2.1 gather_fusion
  56.7 39.0 %while.28 = (s32[]{:T(128)}, f32[1024]{0:T(1024)S(1)}, f32[1024]{0:T(1024)S(1)}, f32[1024,128]{1,0:T(8,128)}, s32[8,512]{1,0:T(8,128)S(1)}, /*index=5*/s32[8,512...) while((s32[]{:T(128)}, f32[1024]{0:T(1024)S(1)}, ...), condition=%wide.region_7.8_spmd.clone, body=%wide.region_4.7_spmd.clone.sunk | while | flops 278795264 | bytes 12720321 | solution.py:274
  56.8 1.0 dynamic-slice_bitcast_fusion.4
  59.9 1.0 convolution_add_fusion.4
  61.6 1.0 dynamic-slice_bitcast_fusion.4
  64.8 1.0 convolution_add_fusion.4
  66.5 1.0 dynamic-slice_bitcast_fusion.4
  69.6 1.0 convolution_add_fusion.4
  71.4 1.0 dynamic-slice_bitcast_fusion.4
  74.5 1.0 convolution_add_fusion.4
  76.3 1.0 dynamic-slice_bitcast_fusion.4
  81.1 1.0 dynamic-slice_bitcast_fusion.4
  84.2 1.0 convolution_add_fusion.4
  86.0 1.0 dynamic-slice_bitcast_fusion.4
  89.1 1.0 convolution_add_fusion.4
  90.9 1.0 dynamic-slice_bitcast_fusion.4
  95.7 3.4 %collective-permute-start.16 = (bf16[256,8192]{1,0:T(8,128)(2,1)}, bf16[256,8192]{1,0:T(8,128)(2,1)}, u32[]{:S(2)}, u32[]{:S(2)}) collective-permute-start(bf16[256,8192]{1,0:T(8,128)(2,1)} %bitcast.158), channel_id=1, source_target_pairs={{16,0},{32,16},{48,32},{64,48},{80,64},{96,80},{112,96},{17,1},{33... | collective-permute-start | bytes 12582920 | tf_op jit(solution)/shard_map/ppermute | solution.py:25
  99.2 7.7 %fusion.34 = bf16[256,512]{1,0:T(8,128)(2,1)S(1)} fusion(bf16[1,8192,512]{2,1,0:T(8,128)(2,1)} %all-gather.6.cloned.1.call-done, bf16[1,256,8192]{2,1,0:T(8,128)(2,1)} %param.13), kind=kOutput, calls=%fused_computation.52 | convolution fusion | flops 2147614720 | bytes 12845056 | tf_op jit(solution)/shard_map/dot_general | solution.py:204
  107.5 41.2 %while.29 = (s32[]{:T(128)}, f32[1024,128]{1,0:T(8,128)S(1)}, bf16[8,512,256]{2,1,0:T(8,128)(2,1)}, s32[8,512]{1,0:T(8,128)S(1)}, s32[8,512]{1,0:T(8,128)S(1)}, ...) while((s32[]{:T(128)}, f32[1024,128]{1,0:T(8,128)S(1)}, ...), condition=%wide.region_10.11_spmd.clone, body=%wide.region_9.10_spmd.clone.sunk | while | flops 677642240 | bytes 14342807 | solution.py:296
  107.5 1.0 dynamic-slice_bitcast_fusion.5
  112.7 1.0 dynamic-slice_bitcast_fusion.5
  117.8 1.0 dynamic-slice_bitcast_fusion.5
  122.9 1.0 dynamic-slice_bitcast_fusion.5
  128.1 1.0 dynamic-slice_bitcast_fusion.5
  133.2 1.0 dynamic-slice_bitcast_fusion.5
  138.4 1.0 dynamic-slice_bitcast_fusion.5
  143.5 1.0 dynamic-slice_bitcast_fusion.5
  148.7 4.0 %all-to-all-start = ((bf16[16,256,256]{2,1,0:T(8,128)(2,1)}), bf16[16,256,256]{2,1,0:T(8,128)(2,1)S(1)}, u32[]{:S(2)}, u32[]{:S(2)}) async-start(bf16[16,256,256]{2,1,0:T(8,128)(2,1)} %bitcast.137), calls=%async_computation | async-start | bytes 4194304 | tf_op jit(solution)/shard_map/all_to_all | solution.py:36
  153.5 2.4 %fusion.38 = bf16[1024,128]{1,0:T(8,128)(2,1)S(1)} fusion(f32[1024,64]{1,0:T(8,128)S(1)} %get-tuple-element.268, f32[1024,64]{1,0:T(8,128)S(1)} %get-tuple-element.267, f32[1024,128]{1,0:T(8,128)S(1)} %get-tuple-element.128, f32[1024,64]{1,0:T(8,128)S(1)} %broadcast_multiply_fusion), kind=kLoop, calls=%fused_computation.58 | loop fusion | flops 786432 | bytes 1572864 | tf_op jit(solution)/shard_map/convert_element_type | solution.py:303
  156.0 1.9 collective-permute-start.13
  158.0 46.0 %all-to-all-done = bf16[16,256,256]{2,1,0:T(8,128)(2,1)S(1)} async-done(((bf16[16,256,256]{2,1,0:T(8,128)(2,1)}), bf16[16,256,256]{2,1,0:T(8,128)(2,1)S(1)}, u32[]{:S(2)}, u32[]{:S(2)}) %all-to-all-start) | async-done | bytes 2097184 | tf_op jit(solution)/shard_map/all_to_all | solution.py:36
  205.0 2.6 %collective-permute-start.14 = (bf16[256,256]{1,0:T(8,128)(2,1)S(1)}, bf16[256,256]{1,0:T(8,128)(2,1)S(1)}, u32[]{:S(2)}, u32[]{:S(2)}) collective-permute-start(bf16[256,256]{1,0:T(8,128)(2,1)S(1)} %pad_maximum_fusion.10), channel_id=1, source_target_pairs={{16,0},{32,16},{48,32},{64,48},{80,64},{96,80},{112,96},{17,1},{33... | collective-permute-start | bytes 393224 | tf_op jit(solution)/shard_map/ppermute | solution.py:25
  207.6 4.3 %collective-permute-done.14 = bf16[256,256]{1,0:T(8,128)(2,1)S(1)} collective-permute-done((bf16[256,256]{1,0:T(8,128)(2,1)S(1)}, bf16[256,256]{1,0:T(8,128)(2,1)S(1)}, u32[]{:S(2)}, u32[]{:S(2)}) %collective-permute-start.14) | collective-permute-done | bytes 131104 | tf_op jit(solution)/shard_map/ppermute | solution.py:25
  212.7 9.1 %shard_map.91 = bf16[256,8192]{1,0:T(8,128)(2,1)} custom-call(bf16[256,768]{1,0:T(8,128)(2,1)} %pad_maximum_fusion.4.grad_ref, bf16[8192,768]{1,0:T(8,128)(2,1)} %all-gather.4.cloned.1.call-done.weight_ref, bf16[256,8192]{1,0:T(8,128)(2,1)} %collective-permute-done.16.base_ref), custom_call_target="tpu_custom_call" | custom-call | flops 3221225472 | bytes 21364736 | tf_op jit(solution)/shard_map/pallas_call | solution.py:50
  (291 shorter events, 68.7 us)
Async XLA Ops:
  6.5 25.0 %copy-start.3 = (s32[1,32]{1,0:T(1,128)S(1)}, s32[1,32]{1,0:T(1,128)}, u32[]{:S(2)}) copy-start(s32[1,32]{1,0:T(1,128)} %param.19) | copy-start | bytes 388
  6.5 92.7 %all-gather.6.cloned.1.call-start = ((), (), s32[]{:S(2)}) async-start(), calls=%async_computation.2 | async-start | bytes 8912896 | tf_op jit(solution)/shard_map/all_gather | solution.py:206
  7.3 205.4 %all-gather.4.cloned.1.call-start = ((), (), s32[]{:S(2)}) async-start(), calls=%async_computation.1 | async-start | bytes 13369344 | tf_op jit(solution)/shard_map/all_gather | solution.py:203
  8.2 10.8 %collective-permute-start = (bf16[128,256]{1,0:T(8,128)(2,1)S(1)}, bf16[128,256]{1,0:T(8,128)(2,1)S(1)}, u32[]{:S(2)}, u32[]{:S(2)}) collective-permute-start(bf16[128,256]{1,0:T(8,128)(2,1)S(1)} %get-tuple-element.278), channel_id=1, source_target_pairs={{0,1},{1,2},{2,3},{3,0},{4,5},{5,6},{6,7},{7,4},{8,9},{9,10},{10,1... | collective-permute-start | bytes 196616 | tf_op jit(solution)/shard_map/ppermute | solution.py:81
  10.3 8.9 %collective-permute-start.1 = (bf16[128,256]{1,0:T(8,128)(2,1)S(1)}, bf16[128,256]{1,0:T(8,128)(2,1)S(1)}, u32[]{:S(2)}, u32[]{:S(2)}) collective-permute-start(bf16[128,256]{1,0:T(8,128)(2,1)S(1)} %get-tuple-element.278), channel_id=1, source_target_pairs={{0,3},{1,0},{2,1},{3,2},{4,7},{5,4},{6,5},{7,6},{8,11},{9,8},{10,9... | collective-permute-start | bytes 196616 | tf_op jit(solution)/shard_map/ppermute | solution.py:81
  11.7 11.8 %collective-permute-start.6 = (bf16[128,256]{1,0:T(8,128)(2,1)S(1)}, bf16[128,256]{1,0:T(8,128)(2,1)S(1)}, u32[]{:S(2)}, u32[]{:S(2)}) collective-permute-start(bf16[128,256]{1,0:T(8,128)(2,1)S(1)} %get-tuple-element.279), channel_id=1, source_target_pairs={{0,4},{1,5},{2,6},{3,7},{4,8},{5,9},{6,10},{7,11},{8,12},{9,13},{1... | collective-permute-start | bytes 196616 | tf_op jit(solution)/shard_map/ppermute | solution.py:81
  13.1 11.5 %collective-permute-start.7 = (bf16[128,256]{1,0:T(8,128)(2,1)S(1)}, bf16[128,256]{1,0:T(8,128)(2,1)S(1)}, u32[]{:S(2)}, u32[]{:S(2)}) collective-permute-start(bf16[128,256]{1,0:T(8,128)(2,1)S(1)} %get-tuple-element.279), channel_id=1, source_target_pairs={{0,12},{1,13},{2,14},{3,15},{4,0},{5,1},{6,2},{7,3},{8,4},{9,5},{1... | collective-permute-start | bytes 196616 | tf_op jit(solution)/shard_map/ppermute | solution.py:81
  15.5 25.9 %collective-permute-start.12 = (bf16[128,512]{1,0:T(8,128)(2,1)S(1)}, bf16[128,512]{1,0:T(8,128)(2,1)S(1)}, u32[]{:S(2)}, u32[]{:S(2)}) collective-permute-start(bf16[128,512]{1,0:T(8,128)(2,1)S(1)} %get-tuple-element.272), channel_id=1, source_target_pairs={{0,8},{1,9},{2,10},{3,11},{4,12},{5,13},{6,14},{7,15},{8,0},{9,1},... | collective-permute-start | bytes 393224 | tf_op jit(solution)/shard_map/ppermute | solution.py:19
  19.0 4.9 %collective-permute-start.2 = (bf16[128,256]{1,0:T(8,128)(2,1)S(1)}, bf16[128,256]{1,0:T(8,128)(2,1)S(1)}, u32[]{:S(2)}, u32[]{:S(2)}) collective-permute-start(bf16[128,256]{1,0:T(8,128)(2,1)S(1)} %collective-permute-done), channel_id=1, source_target_pairs={{0,1},{1,2},{2,3},{3,0},{4,5},{5,6},{6,7},{7,4},{8,9},{9,10},{10,1... | collective-permute-start | bytes 196616 | tf_op jit(solution)/shard_map/ppermute | solution.py:81
  19.2 37.5 %collective-permute-start.15 = (bf16[512,768]{1,0:T(8,128)(2,1)}, bf16[512,768]{1,0:T(8,128)(2,1)}, u32[]{:S(2)}, u32[]{:S(2)}) collective-permute-start(bf16[512,768]{1,0:T(8,128)(2,1)} %bitcast.159), channel_id=1, source_target_pairs={{16,0},{32,16},{48,32},{64,48},{80,64},{96,80},{112,96},{17,1},{33... | collective-permute-start | bytes 2359304 | tf_op jit(solution)/shard_map/ppermute | solution.py:25
  23.5 6.7 %collective-permute-start.8 = (bf16[128,256]{1,0:T(8,128)(2,1)S(1)}, bf16[128,256]{1,0:T(8,128)(2,1)S(1)}, u32[]{:S(2)}, u32[]{:S(2)}) collective-permute-start(bf16[128,256]{1,0:T(8,128)(2,1)S(1)} %collective-permute-done.6), channel_id=1, source_target_pairs={{0,4},{1,5},{2,6},{3,7},{4,8},{5,9},{6,10},{7,11},{8,12},{9,13},{1... | collective-permute-start | bytes 196616 | tf_op jit(solution)/shard_map/ppermute | solution.py:81
  24.0 17.1 %collective-permute-start.3 = (bf16[4,128,256]{2,1,0:T(8,128)(2,1)S(1)}, bf16[4,128,256]{2,1,0:T(8,128)(2,1)S(1)}, u32[]{:S(2)}, u32[]{:S(2)}) collective-permute-start(bf16[4,128,256]{2,1,0:T(8,128)(2,1)S(1)} %get-tuple-element.274), channel_id=1, source_target_pairs={{0,4},{1,5},{2,6},{3,7},{4,8},{5,9},{6,10},{7,11},{8,12},{9,13},{1... | collective-permute-start | bytes 786440 | tf_op jit(solution)/shard_map/ppermute | solution.py:81
  30.2 14.3 %collective-permute-start.9 = (bf16[4,128,256]{2,1,0:T(8,128)(2,1)S(1)}, bf16[4,128,256]{2,1,0:T(8,128)(2,1)S(1)}, u32[]{:S(2)}, u32[]{:S(2)}) collective-permute-start(bf16[4,128,256]{2,1,0:T(8,128)(2,1)S(1)} %get-tuple-element.276), channel_id=1, source_target_pairs={{0,1},{1,2},{2,3},{3,0},{4,5},{5,6},{6,7},{7,4},{8,9},{9,10},{10,1... | collective-permute-start | bytes 786440 | tf_op jit(solution)/shard_map/ppermute | solution.py:81
  33.5 12.1 %collective-permute-start.4 = (bf16[4,128,256]{2,1,0:T(8,128)(2,1)S(1)}, bf16[4,128,256]{2,1,0:T(8,128)(2,1)S(1)}, u32[]{:S(2)}, u32[]{:S(2)}) collective-permute-start(bf16[4,128,256]{2,1,0:T(8,128)(2,1)S(1)} %get-tuple-element.274), channel_id=1, source_target_pairs={{0,12},{1,13},{2,14},{3,15},{4,0},{5,1},{6,2},{7,3},{8,4},{9,5},{1... | collective-permute-start | bytes 786440 | tf_op jit(solution)/shard_map/ppermute | solution.py:81
  41.1 7.7 %collective-permute-start.5 = (bf16[4,128,256]{2,1,0:T(8,128)(2,1)S(1)}, bf16[4,128,256]{2,1,0:T(8,128)(2,1)S(1)}, u32[]{:S(2)}, u32[]{:S(2)}) collective-permute-start(bf16[4,128,256]{2,1,0:T(8,128)(2,1)S(1)} %collective-permute-done.3), channel_id=1, source_target_pairs={{0,4},{1,5},{2,6},{3,7},{4,8},{5,9},{6,10},{7,11},{8,12},{9,13},{1... | collective-permute-start | bytes 786440 | tf_op jit(solution)/shard_map/ppermute | solution.py:81
  41.4 8.4 %collective-permute-start.10 = (bf16[4,128,256]{2,1,0:T(8,128)(2,1)S(1)}, bf16[4,128,256]{2,1,0:T(8,128)(2,1)}, u32[]{:S(2)}, u32[]{:S(2)}) collective-permute-start(bf16[4,128,256]{2,1,0:T(8,128)(2,1)S(1)} %get-tuple-element.276), channel_id=1, source_target_pairs={{0,3},{1,0},{2,1},{3,2},{4,7},{5,4},{6,5},{7,6},{8,11},{9,8},{10,9... | collective-permute-start | bytes 786440 | tf_op jit(solution)/shard_map/ppermute | solution.py:81
  44.5 8.8 %collective-permute-start.11 = (bf16[4,128,256]{2,1,0:T(8,128)(2,1)S(1)}, bf16[4,128,256]{2,1,0:T(8,128)(2,1)}, u32[]{:S(2)}, u32[]{:S(2)}) collective-permute-start(bf16[4,128,256]{2,1,0:T(8,128)(2,1)S(1)} %collective-permute-done.9), channel_id=1, source_target_pairs={{0,1},{1,2},{2,3},{3,0},{4,5},{5,6},{6,7},{7,4},{8,9},{9,10},{10,1... | collective-permute-start | bytes 786440 | tf_op jit(solution)/shard_map/ppermute | solution.py:81
  58.8 1.1 copy-start
  60.8 0.8 copy-start.1
  63.7 1.1 copy-start
  65.7 0.8 copy-start.1
  68.6 1.0 copy-start
  70.6 0.8 copy-start.1
  73.4 1.0 copy-start
  75.5 0.8 copy-start.1
  78.3 1.1 copy-start
  80.3 0.8 copy-start.1
  83.2 1.0 copy-start
  85.2 0.8 copy-start.1
  88.0 1.0 copy-start
  90.1 0.8 copy-start.1
  92.9 1.0 copy-start
  94.9 0.8 copy-start.1
  95.7 116.9 %collective-permute-start.16 = (bf16[256,8192]{1,0:T(8,128)(2,1)}, bf16[256,8192]{1,0:T(8,128)(2,1)}, u32[]{:S(2)}, u32[]{:S(2)}) collective-permute-start(bf16[256,8192]{1,0:T(8,128)(2,1)} %bitcast.158), channel_id=1, source_target_pairs={{16,0},{32,16},{48,32},{64,48},{80,64},{96,80},{112,96},{17,1},{33... | collective-permute-start | bytes 12582920 | tf_op jit(solution)/shard_map/ppermute | solution.py:25
  99.2 7.9 %copy-start.2 = (f32[1024,128]{1,0:T(8,128)S(1)}, f32[1024,128]{1,0:T(8,128)}, u32[]{:S(2)}) copy-start(f32[1024,128]{1,0:T(8,128)} %get-tuple-element.127) | copy-start | bytes 1572868
  148.7 55.3 %all-to-all-start = ((bf16[16,256,256]{2,1,0:T(8,128)(2,1)}), bf16[16,256,256]{2,1,0:T(8,128)(2,1)S(1)}, u32[]{:S(2)}, u32[]{:S(2)}) async-start(bf16[16,256,256]{2,1,0:T(8,128)(2,1)} %bitcast.137), calls=%async_computation | async-start | bytes 4194304 | tf_op jit(solution)/shard_map/all_to_all | solution.py:36
  156.0 51.6 %collective-permute-start.13 = (bf16[256,512]{1,0:T(8,128)(2,1)S(1)}, bf16[256,512]{1,0:T(8,128)(2,1)S(1)}, u32[]{:S(2)}, u32[]{:S(2)}) collective-permute-start(bf16[256,512]{1,0:T(8,128)(2,1)S(1)} %convert_element_type.67), channel_id=1, source_target_pairs={{16,0},{32,16},{48,32},{64,48},{80,64},{96,80},{112,96},{17,1},{33... | collective-permute-start | bytes 786440 | tf_op jit(solution)/shard_map/ppermute | solution.py:25
  205.0 6.9 %collective-permute-start.14 = (bf16[256,256]{1,0:T(8,128)(2,1)S(1)}, bf16[256,256]{1,0:T(8,128)(2,1)S(1)}, u32[]{:S(2)}, u32[]{:S(2)}) collective-permute-start(bf16[256,256]{1,0:T(8,128)(2,1)S(1)} %pad_maximum_fusion.10), channel_id=1, source_target_pairs={{16,0},{32,16},{48,32},{64,48},{80,64},{96,80},{112,96},{17,1},{33... | collective-permute-start | bytes 393224 | tf_op jit(solution)/shard_map/ppermute | solution.py:25
Sparse Core Ops, SparseCore 0:
  9.5 79.0 all-gather.5
  90.7 112.0 all-gather.3

commit v15 on v9

--- a/solution.py
+++ b/solution.py
@@ -283,7 +283,7 @@
         row_total = row_total * rescale + jnp.sum(weights, axis=1)
         value_wide = pair_rows[:, head_dim:].astype(jnp.float32)
         weighted = weighted * rescale[:, None] + jnp.dot(
-            weights, value_wide, precision=lax.Precision.HIGH
+            weights, value_wide, precision=lax.Precision.DEFAULT
         )
         return ((new_top, row_total, weighted), None)
 

time: 235 us -> 231 us (0.983)
  matrix products: 47.5 us -> 42.8 us
    dot_general x8, matrix products: 12.9 us -> 7.71 us  [running_total(): jnp.dot(weights, value_wide, precision=lax.Precision.DEFAULT)]
  transfers between devices with their start and end apart: 31 -> 31, of which waited for: 13 -> 13; matrix products, arithmetic and copies ran while one was open for 47% -> 45% of each run, Pallas kernels for 0% -> 0%
where the time goes in v15:
time: 231 us; the launch traced here: 229 us
  waiting for transfers between devices  51.3 us (22%)
  local copies, waits for them, and re-layouts  49.5 us (21%)
  matrix products  42.8 us (19%)
  starting transfers between devices  37.6 us (16%)
  other arithmetic  21.1 us (9%)
  between operations  15.2 us (7%)
  Pallas kernels  9.08 us (4%)
    ppermute x24, waiting for transfers between devices, ring_shift(): return lax.ppermute(value, 'ctx', pairs)  46.1 us
    ppermute x24, starting transfers between devices, ring_shift(): return lax.ppermute(value, 'ctx', pairs)  21.2 us
    squeeze x16, local copies, waits for them, and re-layouts, body(): lax.scan(running_total, start_carry, key_blocks)  15.6 us
    ppermute x4, starting transfers between devices, passed_along_2(): return lax.ppermute(value, axis, pairs)  14.7 us
    dot_general x24, matrix products, contract_cols(): lax.dot_general(left_rows, right_rows, (((1,), (1,)), ((), ())), preferre...  14.3 us
    while x136, local copies, waits for them, and re-layouts  9.6 us
    pallas_call x1, Pallas kernels, projected_sum(): pl.pallas_call(projection_kernel, grid=(width // tile,), in_specs=[pl.Blo...  9.08 us
    dynamic_update_slice x16, local copies, waits for them, and re-layouts, body(): lax.scan(grad_step, jnp.zeros((flat_rows, head_dim), jnp.float32), key_bl...  8.24 us
  transfers between devices with their start and end apart: 31, of which 13 were waited for; matrix products, arithmetic and copies ran while one was open for 45% of the time, Pallas kernels for 0%

profile of v15, /device:TPU:1, one launch (start us, length us, event | category | flops | bytes accessed | tf_op | source)
XLA Modules:
  0.0 228.8 jit_solution(14077844121586927473)
XLA Ops:
  8.2 2.1 collective-permute-start
  10.3 1.3 collective-permute-start.1
  11.7 1.4 collective-permute-start.6
  13.1 1.4 collective-permute-start.7
  14.5 1.0 fusion.82
  15.5 1.7 collective-permute-start.12
  19.3 4.2 %collective-permute-start.27 = (bf16[512,768]{1,0:T(8,128)(2,1)}, bf16[512,768]{1,0:T(8,128)(2,1)}, u32[]{:S(2)}, u32[]{:S(2)}) collective-permute-start(bf16[512,768]{1,0:T(8,128)(2,1)} %bitcast.226), channel_id=1, source_target_pairs={{16,0},{32,16},{48,32},{64,48},{80,64},{96,80},{112,96},{17,1},{33... | collective-permute-start | bytes 2359304 | tf_op jit(solution)/shard_map/ppermute | solution.py:25
  24.7 5.5 %collective-permute-done.8 = bf16[128,256]{1,0:T(8,128)(2,1)S(1)} collective-permute-done((bf16[128,256]{1,0:T(8,128)(2,1)S(1)}, bf16[128,256]{1,0:T(8,128)(2,1)S(1)}, u32[]{:S(2)}, u32[]{:S(2)}) %collective-permute-start.8) | collective-permute-done | bytes 65568 | tf_op jit(solution)/shard_map/ppermute | solution.py:81
  30.2 1.3 collective-permute-start.9
  33.5 7.5 %collective-permute-done.3 = bf16[4,128,256]{2,1,0:T(8,128)(2,1)S(1)} collective-permute-done((bf16[4,128,256]{2,1,0:T(8,128)(2,1)S(1)}, bf16[4,128,256]{2,1,0:T(8,128)(2,1)S(1)}, u32[]{:S(2)}, u32[]{:S(2)}) %collective-permute-start.3) | collective-permute-done | bytes 262176 | tf_op jit(solution)/shard_map/ppermute | solution.py:81
  41.6 3.1 %collective-permute-start.10 = (bf16[4,128,256]{2,1,0:T(8,128)(2,1)S(1)}, bf16[4,128,256]{2,1,0:T(8,128)(2,1)}, u32[]{:S(2)}, u32[]{:S(2)}) collective-permute-start(bf16[4,128,256]{2,1,0:T(8,128)(2,1)S(1)} %get-tuple-element.290), channel_id=1, source_target_pairs={{0,3},{1,0},{2,1},{3,2},{4,7},{5,4},{6,5},{7,6},{8,11},{9,8},{10,9... | collective-permute-start | bytes 786440 | tf_op jit(solution)/shard_map/ppermute | solution.py:81
  45.9 2.8 %collective-permute-done.5 = bf16[4,128,256]{2,1,0:T(8,128)(2,1)} collective-permute-done((bf16[4,128,256]{2,1,0:T(8,128)(2,1)S(1)}, bf16[4,128,256]{2,1,0:T(8,128)(2,1)}, u32[]{:S(2)}, u32[]{:S(2)}) %collective-permute-start.5) | collective-permute-done | bytes 262176 | tf_op jit(solution)/shard_map/ppermute | solution.py:81
  48.7 1.1 pad_maximum_fusion.1
  50.1 3.5 %collective-permute-done.11 = bf16[4,128,256]{2,1,0:T(8,128)(2,1)} collective-permute-done((bf16[4,128,256]{2,1,0:T(8,128)(2,1)S(1)}, bf16[4,128,256]{2,1,0:T(8,128)(2,1)}, u32[]{:S(2)}, u32[]{:S(2)}) %collective-permute-start.11) | collective-permute-done | bytes 262176 | tf_op jit(solution)/shard_map/ppermute | solution.py:81
  53.6 1.2 pad_maximum_fusion.2
  54.9 2.0 gather_fusion
  57.0 39.1 %while.28 = (s32[]{:T(128)}, f32[1024]{0:T(1024)S(1)}, f32[1024]{0:T(1024)S(1)}, f32[1024,128]{1,0:T(8,128)}, s32[8,512]{1,0:T(8,128)S(1)}, /*index=5*/s32[8,512...) while((s32[]{:T(128)}, f32[1024]{0:T(1024)S(1)}, ...), condition=%wide.region_7.8_spmd.clone, body=%wide.region_4.7_spmd.clone.sunk | while | flops 278795264 | bytes 12720321 | solution.py:296
  61.9 1.0 dynamic-slice_bitcast_fusion.4
  66.8 1.0 dynamic-slice_bitcast_fusion.4
  71.7 1.0 dynamic-slice_bitcast_fusion.4
  76.6 1.0 dynamic-slice_bitcast_fusion.4
  86.3 1.0 dynamic-slice_bitcast_fusion.4
  96.1 3.5 %collective-permute-start.28 = (bf16[256,8192]{1,0:T(8,128)(2,1)}, bf16[256,8192]{1,0:T(8,128)(2,1)}, u32[]{:S(2)}, u32[]{:S(2)}) collective-permute-start(bf16[256,8192]{1,0:T(8,128)(2,1)} %bitcast.225), channel_id=1, source_target_pairs={{16,0},{32,16},{48,32},{64,48},{80,64},{96,80},{112,96},{17,1},{33... | collective-permute-start | bytes 12582920 | tf_op jit(solution)/shard_map/ppermute | solution.py:25
  99.7 7.6 %fusion.36 = bf16[256,512]{1,0:T(8,128)(2,1)S(1)} fusion(bf16[1,8192,512]{2,1,0:T(8,128)(2,1)} %all-gather.6.cloned.1.call-done, bf16[1,256,8192]{2,1,0:T(8,128)(2,1)} %param.13), kind=kOutput, calls=%fused_computation.58 | convolution fusion | flops 2147614720 | bytes 12845056 | tf_op jit(solution)/shard_map/dot_general | solution.py:226
  107.8 43.4 %while.29 = (s32[]{:T(128)}, f32[1024,128]{1,0:T(8,128)S(1)}, f32[8,512,256]{2,1,0:T(8,128)}, s32[8,512]{1,0:T(8,128)S(1)}, s32[8,512]{1,0:T(8,128)S(1)}, /*inde...) while((s32[]{:T(128)}, f32[1024,128]{1,0:T(8,128)S(1)}, ...), condition=%wide.region_10.11_spmd.clone, body=%wide.region_9.10_spmd.clone.sunk | while | flops 677249024 | bytes 16472895 | solution.py:318
  107.9 1.0 dynamic-slice_bitcast_fusion.5
  113.3 1.0 dynamic-slice_bitcast_fusion.5
  135.0 1.0 dynamic-slice_bitcast_fusion.5
  151.2 2.8 %slice_bitcast_fusion = (f32[4,4,256,128]{3,2,0,1:T(8,128)S(1)}, f32[4,4,256,128]{3,2,1,0:T(8,128)S(1)}) fusion(f32[4,4,256,256]{3,2,1,0:T(8,128)} %bitcast.203), kind=kLoop, calls=%fused_computation.55 | loop fusion | bytes 8388608 | tf_op jit(solution)/shard_map/transpose | solution.py:111
  156.2 2.7 %collective-permute-start.20 = (bf16[4,256,128]{2,1,0:T(8,128)(2,1)}, bf16[4,256,128]{2,1,0:T(8,128)(2,1)S(1)}, u32[]{:S(2)}, u32[]{:S(2)}) collective-permute-start(bf16[4,256,128]{2,1,0:T(8,128)(2,1)} %get-tuple-element.277), channel_id=1, source_target_pairs={{0,12},{1,13},{2,14},{3,15},{4,0},{5,1},{6,2},{7,3},{8,4},{9,5},{1... | collective-permute-start | bytes 786440 | tf_op jit(solution)/shard_map/ppermute | solution.py:81
  159.2 2.4 %fusion.50 = bf16[1024,128]{1,0:T(8,128)(2,1)S(1)} fusion(f32[1024,64]{1,0:T(8,128)S(1)} %get-tuple-element.280, f32[1024,64]{1,0:T(8,128)S(1)} %get-tuple-element.279, f32[1024,128]{1,0:T(8,128)S(1)} %get-tuple-element.128, f32[1024,64]{1,0:T(8,128)S(1)} %get-tuple-element.299), kind=kLoop, calls=%fused_computation.82 | loop fusion | flops 786432 | bytes 1572864 | tf_op jit(solution)/shard_map/convert_element_type | solution.py:325
  161.6 9.8 %collective-permute-done.21 = bf16[4,256,128]{2,1,0:T(8,128)(2,1)S(1)} collective-permute-done((bf16[4,256,128]{2,1,0:T(8,128)(2,1)S(1)}, bf16[4,256,128]{2,1,0:T(8,128)(2,1)S(1)}, u32[]{:S(2)}, u32[]{:S(2)}) %collective-permute-start.21) | collective-permute-done | bytes 262176 | tf_op jit(solution)/shard_map/ppermute | solution.py:81
  172.2 1.6 fusion.35
  173.9 2.1 collective-permute-start.13
  176.1 3.0 %collective-permute-start.14 = (bf16[4,256,128]{2,1,0:T(8,128)(2,1)}, bf16[4,256,128]{2,1,0:T(8,128)(2,1)S(1)}, u32[]{:S(2)}, u32[]{:S(2)}) collective-permute-start(bf16[4,256,128]{2,1,0:T(8,128)(2,1)} %get-tuple-element.275), channel_id=1, source_target_pairs={{0,3},{1,0},{2,1},{3,2},{4,7},{5,4},{6,5},{7,6},{8,11},{9,8},{10,9... | collective-permute-start | bytes 786440 | tf_op jit(solution)/shard_map/ppermute | solution.py:81
  179.1 1.1 fusion.46
  180.3 7.1 %collective-permute-done.22 = bf16[4,256,128]{2,1,0:T(8,128)(2,1)S(1)} collective-permute-done((bf16[4,256,128]{2,1,0:T(8,128)(2,1)}, bf16[4,256,128]{2,1,0:T(8,128)(2,1)S(1)}, u32[]{:S(2)}, u32[]{:S(2)}) %collective-permute-start.22) | collective-permute-done | bytes 262176 | tf_op jit(solution)/shard_map/ppermute | solution.py:81
  187.4 1.1 fusion.44
  188.7 2.6 %collective-permute-done.16 = bf16[4,256,128]{2,1,0:T(8,128)(2,1)S(1)} collective-permute-done((bf16[4,256,128]{2,1,0:T(8,128)(2,1)S(1)}, bf16[4,256,128]{2,1,0:T(8,128)(2,1)S(1)}, u32[]{:S(2)}, u32[]{:S(2)}) %collective-permute-start.16) | collective-permute-done | bytes 262176 | tf_op jit(solution)/shard_map/ppermute | solution.py:81
  191.6 1.2 collective-permute-start.18
  192.7 1.6 collective-permute-start.17
  195.0 1.0 collective-permute-done.18
  196.0 1.4 collective-permute-done.23
  197.4 2.9 %collective-permute-done.25 = bf16[256,128]{1,0:T(8,128)(2,1)S(1)} collective-permute-done((bf16[256,128]{1,0:T(8,128)(2,1)S(1)}, bf16[256,128]{1,0:T(8,128)(2,1)S(1)}, u32[]{:S(2)}, u32[]{:S(2)}) %collective-permute-start.25) | collective-permute-done | bytes 65568 | tf_op jit(solution)/shard_map/ppermute | solution.py:81
  200.3 1.7 collective-permute-done.19
  202.8 4.8 %collective-permute-start.26 = (bf16[256,256]{1,0:T(8,128)(2,1)S(1)}, bf16[256,256]{1,0:T(8,128)(2,1)S(1)}, u32[]{:S(2)}, u32[]{:S(2)}) collective-permute-start(bf16[256,256]{1,0:T(8,128)(2,1)S(1)} %pad_maximum_fusion.10), channel_id=1, source_target_pairs={{16,0},{32,16},{48,32},{64,48},{80,64},{96,80},{112,96},{17,1},{33... | collective-permute-start | bytes 393224 | tf_op jit(solution)/shard_map/ppermute | solution.py:25
  207.6 4.4 %collective-permute-done.26 = bf16[256,256]{1,0:T(8,128)(2,1)S(1)} collective-permute-done((bf16[256,256]{1,0:T(8,128)(2,1)S(1)}, bf16[256,256]{1,0:T(8,128)(2,1)S(1)}, u32[]{:S(2)}, u32[]{:S(2)}) %collective-permute-start.26) | collective-permute-done | bytes 131104 | tf_op jit(solution)/shard_map/ppermute | solution.py:25
  212.8 9.1 %shard_map.91 = bf16[256,8192]{1,0:T(8,128)(2,1)} custom-call(bf16[256,768]{1,0:T(8,128)(2,1)} %pad_maximum_fusion.4.grad_ref, bf16[8192,768]{1,0:T(8,128)(2,1)} %all-gather.4.cloned.1.call-done.weight_ref, bf16[256,8192]{1,0:T(8,128)(2,1)} %collective-permute-done.28.base_ref), custom_call_target="tpu_custom_call" | custom-call | flops 3221225472 | bytes 21364736 | tf_op jit(solution)/shard_map/pallas_call | solution.py:50
  (429 shorter events, 87.0 us)
Async XLA Ops:
  6.5 25.0 %copy-start.10 = (s32[1,32]{1,0:T(1,128)S(1)}, s32[1,32]{1,0:T(1,128)}, u32[]{:S(2)}) copy-start(s32[1,32]{1,0:T(1,128)} %param.19) | copy-start | bytes 388
  6.5 93.1 %all-gather.6.cloned.1.call-start = ((), (), s32[]{:S(2)}) async-start(), calls=%async_computation.1 | async-start | bytes 8912896 | tf_op jit(solution)/shard_map/all_gather | solution.py:228
  7.3 205.6 %all-gather.4.cloned.1.call-start = ((), (), s32[]{:S(2)}) async-start(), calls=%async_computation | async-start | bytes 13369344 | tf_op jit(solution)/shard_map/all_gather | solution.py:225
  8.2 10.9 %collective-permute-start = (bf16[128,256]{1,0:T(8,128)(2,1)S(1)}, bf16[128,256]{1,0:T(8,128)(2,1)S(1)}, u32[]{:S(2)}, u32[]{:S(2)}) collective-permute-start(bf16[128,256]{1,0:T(8,128)(2,1)S(1)} %get-tuple-element.294), channel_id=1, source_target_pairs={{0,1},{1,2},{2,3},{3,0},{4,5},{5,6},{6,7},{7,4},{8,9},{9,10},{10,1... | collective-permute-start | bytes 196616 | tf_op jit(solution)/shard_map/ppermute | solution.py:81
  10.3 9.0 %collective-permute-start.1 = (bf16[128,256]{1,0:T(8,128)(2,1)S(1)}, bf16[128,256]{1,0:T(8,128)(2,1)S(1)}, u32[]{:S(2)}, u32[]{:S(2)}) collective-permute-start(bf16[128,256]{1,0:T(8,128)(2,1)S(1)} %get-tuple-element.294), channel_id=1, source_target_pairs={{0,3},{1,0},{2,1},{3,2},{4,7},{5,4},{6,5},{7,6},{8,11},{9,8},{10,9... | collective-permute-start | bytes 196616 | tf_op jit(solution)/shard_map/ppermute | solution.py:81
  11.7 11.9 %collective-permute-start.6 = (bf16[128,256]{1,0:T(8,128)(2,1)S(1)}, bf16[128,256]{1,0:T(8,128)(2,1)S(1)}, u32[]{:S(2)}, u32[]{:S(2)}) collective-permute-start(bf16[128,256]{1,0:T(8,128)(2,1)S(1)} %get-tuple-element.295), channel_id=1, source_target_pairs={{0,4},{1,5},{2,6},{3,7},{4,8},{5,9},{6,10},{7,11},{8,12},{9,13},{1... | collective-permute-start | bytes 196616 | tf_op jit(solution)/shard_map/ppermute | solution.py:81
  13.1 11.7 %collective-permute-start.7 = (bf16[128,256]{1,0:T(8,128)(2,1)S(1)}, bf16[128,256]{1,0:T(8,128)(2,1)S(1)}, u32[]{:S(2)}, u32[]{:S(2)}) collective-permute-start(bf16[128,256]{1,0:T(8,128)(2,1)S(1)} %get-tuple-element.295), channel_id=1, source_target_pairs={{0,12},{1,13},{2,14},{3,15},{4,0},{5,1},{6,2},{7,3},{8,4},{9,5},{1... | collective-permute-start | bytes 196616 | tf_op jit(solution)/shard_map/ppermute | solution.py:81
  15.5 26.0 %collective-permute-start.12 = (bf16[128,512]{1,0:T(8,128)(2,1)S(1)}, bf16[128,512]{1,0:T(8,128)(2,1)S(1)}, u32[]{:S(2)}, u32[]{:S(2)}) collective-permute-start(bf16[128,512]{1,0:T(8,128)(2,1)S(1)} %get-tuple-element.286), channel_id=1, source_target_pairs={{0,8},{1,9},{2,10},{3,11},{4,12},{5,13},{6,14},{7,15},{8,0},{9,1},... | collective-permute-start | bytes 393224 | tf_op jit(solution)/shard_map/ppermute | solution.py:19
  18.1 27.6 %copy-start.11 = (f32[64]{0:T(128)}, f32[64]{0:T(128)S(1)}, u32[]{:S(2)}) copy-start(f32[64]{0:T(128)S(1)} %negate_power_fusion) | copy-start | bytes 772
  19.2 4.9 %collective-permute-start.2 = (bf16[128,256]{1,0:T(8,128)(2,1)S(1)}, bf16[128,256]{1,0:T(8,128)(2,1)S(1)}, u32[]{:S(2)}, u32[]{:S(2)}) collective-permute-start(bf16[128,256]{1,0:T(8,128)(2,1)S(1)} %collective-permute-done), channel_id=1, source_target_pairs={{0,1},{1,2},{2,3},{3,0},{4,5},{5,6},{6,7},{7,4},{8,9},{9,10},{10,1... | collective-permute-start | bytes 196616 | tf_op jit(solution)/shard_map/ppermute | solution.py:81
  19.3 37.6 %collective-permute-start.27 = (bf16[512,768]{1,0:T(8,128)(2,1)}, bf16[512,768]{1,0:T(8,128)(2,1)}, u32[]{:S(2)}, u32[]{:S(2)}) collective-permute-start(bf16[512,768]{1,0:T(8,128)(2,1)} %bitcast.226), channel_id=1, source_target_pairs={{16,0},{32,16},{48,32},{64,48},{80,64},{96,80},{112,96},{17,1},{33... | collective-permute-start | bytes 2359304 | tf_op jit(solution)/shard_map/ppermute | solution.py:25
  23.6 6.6 %collective-permute-start.8 = (bf16[128,256]{1,0:T(8,128)(2,1)S(1)}, bf16[128,256]{1,0:T(8,128)(2,1)S(1)}, u32[]{:S(2)}, u32[]{:S(2)}) collective-permute-start(bf16[128,256]{1,0:T(8,128)(2,1)S(1)} %collective-permute-done.6), channel_id=1, source_target_pairs={{0,4},{1,5},{2,6},{3,7},{4,8},{5,9},{6,10},{7,11},{8,12},{9,13},{1... | collective-permute-start | bytes 196616 | tf_op jit(solution)/shard_map/ppermute | solution.py:81
  24.1 16.9 %collective-permute-start.3 = (bf16[4,128,256]{2,1,0:T(8,128)(2,1)S(1)}, bf16[4,128,256]{2,1,0:T(8,128)(2,1)S(1)}, u32[]{:S(2)}, u32[]{:S(2)}) collective-permute-start(bf16[4,128,256]{2,1,0:T(8,128)(2,1)S(1)} %get-tuple-element.288), channel_id=1, source_target_pairs={{0,4},{1,5},{2,6},{3,7},{4,8},{5,9},{6,10},{7,11},{8,12},{9,13},{1... | collective-permute-start | bytes 786440 | tf_op jit(solution)/shard_map/ppermute | solution.py:81
  30.2 14.6 %collective-permute-start.9 = (bf16[4,128,256]{2,1,0:T(8,128)(2,1)S(1)}, bf16[4,128,256]{2,1,0:T(8,128)(2,1)S(1)}, u32[]{:S(2)}, u32[]{:S(2)}) collective-permute-start(bf16[4,128,256]{2,1,0:T(8,128)(2,1)S(1)} %get-tuple-element.290), channel_id=1, source_target_pairs={{0,1},{1,2},{2,3},{3,0},{4,5},{5,6},{6,7},{7,4},{8,9},{9,10},{10,1... | collective-permute-start | bytes 786440 | tf_op jit(solution)/shard_map/ppermute | solution.py:81
  33.4 12.5 %collective-permute-start.4 = (bf16[4,128,256]{2,1,0:T(8,128)(2,1)S(1)}, bf16[4,128,256]{2,1,0:T(8,128)(2,1)S(1)}, u32[]{:S(2)}, u32[]{:S(2)}) collective-permute-start(bf16[4,128,256]{2,1,0:T(8,128)(2,1)S(1)} %get-tuple-element.288), channel_id=1, source_target_pairs={{0,12},{1,13},{2,14},{3,15},{4,0},{5,1},{6,2},{7,3},{8,4},{9,5},{1... | collective-permute-start | bytes 786440 | tf_op jit(solution)/shard_map/ppermute | solution.py:81
  41.0 7.7 %collective-permute-start.5 = (bf16[4,128,256]{2,1,0:T(8,128)(2,1)S(1)}, bf16[4,128,256]{2,1,0:T(8,128)(2,1)}, u32[]{:S(2)}, u32[]{:S(2)}) collective-permute-start(bf16[4,128,256]{2,1,0:T(8,128)(2,1)S(1)} %collective-permute-done.3), channel_id=1, source_target_pairs={{0,4},{1,5},{2,6},{3,7},{4,8},{5,9},{6,10},{7,11},{8,12},{9,13},{1... | collective-permute-start | bytes 786440 | tf_op jit(solution)/shard_map/ppermute | solution.py:81
  41.6 8.5 %collective-permute-start.10 = (bf16[4,128,256]{2,1,0:T(8,128)(2,1)S(1)}, bf16[4,128,256]{2,1,0:T(8,128)(2,1)}, u32[]{:S(2)}, u32[]{:S(2)}) collective-permute-start(bf16[4,128,256]{2,1,0:T(8,128)(2,1)S(1)} %get-tuple-element.290), channel_id=1, source_target_pairs={{0,3},{1,0},{2,1},{3,2},{4,7},{5,4},{6,5},{7,6},{8,11},{9,8},{10,9... | collective-permute-start | bytes 786440 | tf_op jit(solution)/shard_map/ppermute | solution.py:81
  44.9 8.7 %collective-permute-start.11 = (bf16[4,128,256]{2,1,0:T(8,128)(2,1)S(1)}, bf16[4,128,256]{2,1,0:T(8,128)(2,1)}, u32[]{:S(2)}, u32[]{:S(2)}) collective-permute-start(bf16[4,128,256]{2,1,0:T(8,128)(2,1)S(1)} %collective-permute-done.9), channel_id=1, source_target_pairs={{0,1},{1,2},{2,3},{3,0},{4,5},{5,6},{6,7},{7,4},{8,9},{9,10},{10,1... | collective-permute-start | bytes 786440 | tf_op jit(solution)/shard_map/ppermute | solution.py:81
  96.1 116.8 %collective-permute-start.28 = (bf16[256,8192]{1,0:T(8,128)(2,1)}, bf16[256,8192]{1,0:T(8,128)(2,1)}, u32[]{:S(2)}, u32[]{:S(2)}) collective-permute-start(bf16[256,8192]{1,0:T(8,128)(2,1)} %bitcast.225), channel_id=1, source_target_pairs={{16,0},{32,16},{48,32},{64,48},{80,64},{96,80},{112,96},{17,1},{33... | collective-permute-start | bytes 12582920 | tf_op jit(solution)/shard_map/ppermute | solution.py:25
  99.6 7.8 %copy-start.3 = (f32[1024,128]{1,0:T(8,128)S(1)}, f32[1024,128]{1,0:T(8,128)}, u32[]{:S(2)}) copy-start(f32[1024,128]{1,0:T(8,128)} %get-tuple-element.127) | copy-start | bytes 1572868
  118.7 2.2 copy-start.4
  118.7 2.2 copy-start.6
  118.7 2.2 copy-start.8
  124.1 2.2 copy-start.4
  124.1 2.2 copy-start.6
  124.1 2.2 copy-start.8
  134.9 2.2 copy-start.4
  134.9 2.2 copy-start.6
  134.9 2.2 copy-start.8
  145.8 2.2 copy-start.4
  145.8 2.2 copy-start.6
  145.8 2.2 copy-start.8
  154.9 21.2 %collective-permute-start.15 = (bf16[4,256,128]{2,1,0:T(8,128)(2,1)}, bf16[4,256,128]{2,1,0:T(8,128)(2,1)S(1)}, u32[]{:S(2)}, u32[]{:S(2)}) collective-permute-start(bf16[4,256,128]{2,1,0:T(8,128)(2,1)} %get-tuple-element.276), channel_id=1, source_target_pairs={{0,1},{1,2},{2,3},{3,0},{4,5},{5,6},{6,7},{7,4},{8,9},{9,10},{10,1... | collective-permute-start | bytes 786440 | tf_op jit(solution)/shard_map/ppermute | solution.py:81
  154.9 4.0 %copy-start.12 = (f32[64]{0:T(128)S(1)}, f32[64]{0:T(128)}, u32[]{:S(2)}) copy-start(f32[64]{0:T(128)} %copy-done.11) | copy-start | bytes 772
  155.4 16.1 %copy-start = (f32[4,4,256,128]{3,2,1,0:T(8,128)}, f32[4,4,256,128]{3,2,1,0:T(8,128)S(1)}, u32[]{:S(2)}) copy-start(f32[4,4,256,128]{3,2,1,0:T(8,128)S(1)} %get-tuple-element.266) | copy-start | bytes 6291460
  156.2 15.2 %collective-permute-start.21 = (bf16[4,256,128]{2,1,0:T(8,128)(2,1)S(1)}, bf16[4,256,128]{2,1,0:T(8,128)(2,1)S(1)}, u32[]{:S(2)}, u32[]{:S(2)}) collective-permute-start(bf16[4,256,128]{2,1,0:T(8,128)(2,1)S(1)} %get-tuple-element.278), channel_id=1, source_target_pairs={{0,4},{1,5},{2,6},{3,7},{4,8},{5,9},{6,10},{7,11},{8,12},{9,13},{1... | collective-permute-start | bytes 786440 | tf_op jit(solution)/shard_map/ppermute | solution.py:81
  156.2 24.0 %collective-permute-start.20 = (bf16[4,256,128]{2,1,0:T(8,128)(2,1)}, bf16[4,256,128]{2,1,0:T(8,128)(2,1)S(1)}, u32[]{:S(2)}, u32[]{:S(2)}) collective-permute-start(bf16[4,256,128]{2,1,0:T(8,128)(2,1)} %get-tuple-element.277), channel_id=1, source_target_pairs={{0,12},{1,13},{2,14},{3,15},{4,0},{5,1},{6,2},{7,3},{8,4},{9,5},{1... | collective-permute-start | bytes 786440 | tf_op jit(solution)/shard_map/ppermute | solution.py:81
  172.2 15.2 %collective-permute-start.22 = (bf16[4,256,128]{2,1,0:T(8,128)(2,1)}, bf16[4,256,128]{2,1,0:T(8,128)(2,1)S(1)}, u32[]{:S(2)}, u32[]{:S(2)}) collective-permute-start(bf16[4,256,128]{2,1,0:T(8,128)(2,1)} %fusion.42), channel_id=1, source_target_pairs={{0,4},{1,5},{2,6},{3,7},{4,8},{5,9},{6,10},{7,11},{8,12},{9,13},{1... | collective-permute-start | bytes 786440 | tf_op jit(solution)/shard_map/ppermute | solution.py:81
  173.9 33.7 %collective-permute-start.13 = (bf16[256,512]{1,0:T(8,128)(2,1)S(1)}, bf16[256,512]{1,0:T(8,128)(2,1)S(1)}, u32[]{:S(2)}, u32[]{:S(2)}) collective-permute-start(bf16[256,512]{1,0:T(8,128)(2,1)S(1)} %convert_element_type.139), channel_id=1, source_target_pairs={{16,0},{32,16},{48,32},{64,48},{80,64},{96,80},{112,96},{17,1},{33... | collective-permute-start | bytes 786440 | tf_op jit(solution)/shard_map/ppermute | solution.py:25
  176.1 12.6 %collective-permute-start.14 = (bf16[4,256,128]{2,1,0:T(8,128)(2,1)}, bf16[4,256,128]{2,1,0:T(8,128)(2,1)S(1)}, u32[]{:S(2)}, u32[]{:S(2)}) collective-permute-start(bf16[4,256,128]{2,1,0:T(8,128)(2,1)} %get-tuple-element.275), channel_id=1, source_target_pairs={{0,3},{1,0},{2,1},{3,2},{4,7},{5,4},{6,5},{7,6},{8,11},{9,8},{10,9... | collective-permute-start | bytes 786440 | tf_op jit(solution)/shard_map/ppermute | solution.py:81
  180.2 11.1 %collective-permute-start.16 = (bf16[4,256,128]{2,1,0:T(8,128)(2,1)S(1)}, bf16[4,256,128]{2,1,0:T(8,128)(2,1)S(1)}, u32[]{:S(2)}, u32[]{:S(2)}) collective-permute-start(bf16[4,256,128]{2,1,0:T(8,128)(2,1)S(1)} %fusion.46), channel_id=1, source_target_pairs={{0,1},{1,2},{2,3},{3,0},{4,5},{5,6},{6,7},{7,4},{8,9},{9,10},{10,1... | collective-permute-start | bytes 786440 | tf_op jit(solution)/shard_map/ppermute | solution.py:81
  188.7 5.7 %collective-permute-start.24 = (bf16[256,128]{1,0:T(8,128)(2,1)S(1)}, bf16[256,128]{1,0:T(8,128)(2,1)S(1)}, u32[]{:S(2)}, u32[]{:S(2)}) collective-permute-start(bf16[256,128]{1,0:T(8,128)(2,1)S(1)} %get-tuple-element.284), channel_id=1, source_target_pairs={{0,1},{1,2},{2,3},{3,0},{4,5},{5,6},{6,7},{7,4},{8,9},{9,10},{10,1... | collective-permute-start | bytes 196616 | tf_op jit(solution)/shard_map/ppermute | solution.py:81
  191.6 4.4 %collective-permute-start.18 = (bf16[256,128]{1,0:T(8,128)(2,1)S(1)}, bf16[256,128]{1,0:T(8,128)(2,1)S(1)}, u32[]{:S(2)}, u32[]{:S(2)}) collective-permute-start(bf16[256,128]{1,0:T(8,128)(2,1)S(1)} %get-tuple-element.282), channel_id=1, source_target_pairs={{0,4},{1,5},{2,6},{3,7},{4,8},{5,9},{6,10},{7,11},{8,12},{9,13},{1... | collective-permute-start | bytes 196616 | tf_op jit(solution)/shard_map/ppermute | solution.py:81
  192.7 7.6 %collective-permute-start.17 = (bf16[256,128]{1,0:T(8,128)(2,1)S(1)}, bf16[256,128]{1,0:T(8,128)(2,1)S(1)}, u32[]{:S(2)}, u32[]{:S(2)}) collective-permute-start(bf16[256,128]{1,0:T(8,128)(2,1)S(1)} %get-tuple-element.281), channel_id=1, source_target_pairs={{0,12},{1,13},{2,14},{3,15},{4,0},{5,1},{6,2},{7,3},{8,4},{9,5},{1... | collective-permute-start | bytes 196616 | tf_op jit(solution)/shard_map/ppermute | solution.py:81
  194.3 3.1 %collective-permute-start.23 = (bf16[256,128]{1,0:T(8,128)(2,1)S(1)}, bf16[256,128]{1,0:T(8,128)(2,1)S(1)}, u32[]{:S(2)}, u32[]{:S(2)}) collective-permute-start(bf16[256,128]{1,0:T(8,128)(2,1)S(1)} %get-tuple-element.283), channel_id=1, source_target_pairs={{0,3},{1,0},{2,1},{3,2},{4,7},{5,4},{6,5},{7,6},{8,11},{9,8},{10,9... | collective-permute-start | bytes 196616 | tf_op jit(solution)/shard_map/ppermute | solution.py:81
  196.0 4.3 %collective-permute-start.25 = (bf16[256,128]{1,0:T(8,128)(2,1)S(1)}, bf16[256,128]{1,0:T(8,128)(2,1)S(1)}, u32[]{:S(2)}, u32[]{:S(2)}) collective-permute-start(bf16[256,128]{1,0:T(8,128)(2,1)S(1)} %fusion.53), channel_id=1, source_target_pairs={{0,1},{1,2},{2,3},{3,0},{4,5},{5,6},{6,7},{7,4},{8,9},{9,10},{10,1... | collective-permute-start | bytes 196616 | tf_op jit(solution)/shard_map/ppermute | solution.py:81
  197.4 4.6 %collective-permute-start.19 = (bf16[256,128]{1,0:T(8,128)(2,1)S(1)}, bf16[256,128]{1,0:T(8,128)(2,1)S(1)}, u32[]{:S(2)}, u32[]{:S(2)}) collective-permute-start(bf16[256,128]{1,0:T(8,128)(2,1)S(1)} %fusion.58), channel_id=1, source_target_pairs={{0,4},{1,5},{2,6},{3,7},{4,8},{5,9},{6,10},{7,11},{8,12},{9,13},{1... | collective-permute-start | bytes 196616 | tf_op jit(solution)/shard_map/ppermute | solution.py:81
  202.8 9.2 %collective-permute-start.26 = (bf16[256,256]{1,0:T(8,128)(2,1)S(1)}, bf16[256,256]{1,0:T(8,128)(2,1)S(1)}, u32[]{:S(2)}, u32[]{:S(2)}) collective-permute-start(bf16[256,256]{1,0:T(8,128)(2,1)S(1)} %pad_maximum_fusion.10), channel_id=1, source_target_pairs={{16,0},{32,16},{48,32},{64,48},{80,64},{96,80},{112,96},{17,1},{33... | collective-permute-start | bytes 393224 | tf_op jit(solution)/shard_map/ppermute | solution.py:25
  (52 other events, 76.9 us)
Sparse Core Ops, SparseCore 0:
  9.5 78.9 all-gather.5
  90.6 100.8 all-gather.3

commit v16 on v15

--- a/solution.py
+++ b/solution.py
@@ -44,22 +44,23 @@
     out_ref[...] = (base_ref[...].astype(jnp.float32) + product).astype(out_ref.dtype)
 
 
-def projected_sum(grad_rows, weight, base, tile=4096):
+def projected_sum(grad_rows, weight, base, first_column, out_dtype, tile=4096):
     rows, inner = grad_rows.shape
     width = weight.shape[0]
+    column_block = first_column // inner
     return pl.pallas_call(
         projection_kernel,
         grid=(width // tile,),
         in_specs=[
             pl.BlockSpec((rows, inner), lambda j: (0, 0)),
-            pl.BlockSpec((tile, inner), lambda j: (j, 0)),
+            pl.BlockSpec((tile, inner), lambda j: (j, column_block)),
             pl.BlockSpec((rows, tile), lambda j: (0, j)),
         ],
         out_specs=pl.BlockSpec((rows, tile), lambda j: (0, j)),
-        out_shape=jax.ShapeDtypeStruct((rows, width), base.dtype),
+        out_shape=jax.ShapeDtypeStruct((rows, width), out_dtype),
         cost_estimate=pl.CostEstimate(
             flops=2 * rows * inner * width,
-            bytes_accessed=2 * (rows * inner + width * inner + 2 * rows * width),
+            bytes_accessed=2 * (rows * inner + width * inner) + 6 * rows * width,
             transcendentals=0,
         ),
     )(grad_rows, weight, base)
@@ -336,8 +337,9 @@
     next_keyval_grad = passed_along_2(
         jnp.concatenate([key_grad, value_grad], axis=1), "pipe", -1
     )
-    next_qkv_grad = jnp.concatenate([next_query_grad, next_keyval_grad], axis=1)
-    passed = projected_sum(next_qkv_grad, next_weight, next_grad_in)
+    query_width = next_query_grad.shape[1]
+    partial = projected_sum(next_query_grad, next_weight, next_grad_in, 0, jnp.float32)
+    passed = projected_sum(next_keyval_grad, next_weight, partial, query_width, jnp.bfloat16)
     return passed[None]
 
 

time: 231 us -> 248 us (1.074)
  the two profiles are of different devices: /device:TPU:1 before, /device:TPU:103 now
where the time goes in v16:
time: 248 us; the launch traced here: 244 us
  local copies, waits for them, and re-layouts  54.1 us (22%)
  starting transfers between devices  49.7 us (20%)
  matrix products  43.5 us (18%)
  waiting for transfers between devices  41.7 us (17%)
  other arithmetic  23.3 us (9%)
  Pallas kernels  15.7 us (6%)
  between operations  15.1 us (6%)
    ppermute x24, waiting for transfers between devices, ring_shift(): return lax.ppermute(value, 'ctx', pairs)  40.9 us
    ppermute x24, starting transfers between devices, ring_shift(): return lax.ppermute(value, 'ctx', pairs)  27.5 us
    ppermute x4, starting transfers between devices, passed_along_2(): return lax.ppermute(value, axis, pairs)  20.4 us
    pallas_call x2, Pallas kernels, projected_sum(): pl.pallas_call(projection_kernel, grid=(width // tile,), in_specs=[pl.Blo...  15.7 us
    squeeze x16, local copies, waits for them, and re-layouts, body(): lax.scan(running_total, start_carry, key_blocks)  15.6 us
    dot_general x24, matrix products, contract_cols(): lax.dot_general(left_rows, right_rows, (((1,), (1,)), ((), ())), preferre...  14.3 us
    dynamic_slice x16, local copies, waits for them, and re-layouts, body(): lax.scan(running_total, start_carry, key_blocks)  11.9 us
    dynamic_update_slice x16, local copies, waits for them, and re-layouts, body(): lax.scan(grad_step, jnp.zeros((flat_rows, head_dim), jnp.float32), key_bl...  8.24 us
  transfers between devices with their start and end apart: 31, of which 10 were waited for; matrix products, arithmetic and copies ran while one was open for 49% of the time, Pallas kernels for 4%

profile of v16, /device:TPU:103, one launch (start us, length us, event | category | flops | bytes accessed | tf_op | source)
XLA Modules:
  0.0 244.3 jit_solution(7523736268807303569)
XLA Ops:
  8.8 2.1 collective-permute-start
  10.9 2.7 %collective-permute-start.7 = (bf16[128,256]{1,0:T(8,128)(2,1)S(1)}, bf16[128,256]{1,0:T(8,128)(2,1)S(1)}, u32[]{:S(2)}, u32[]{:S(2)}) collective-permute-start(bf16[128,256]{1,0:T(8,128)(2,1)S(1)} %get-tuple-element.295), channel_id=1, source_target_pairs={{0,12},{1,13},{2,14},{3,15},{4,0},{5,1},{6,2},{7,3},{8,4},{9,5},{1... | collective-permute-start | bytes 196616 | tf_op jit(solution)/shard_map/ppermute | solution.py:82
  14.7 1.7 collective-permute-start.12
  18.5 4.9 %collective-permute-start.26 = (bf16[512,768]{1,0:T(8,128)(2,1)}, bf16[512,768]{1,0:T(8,128)(2,1)}, u32[]{:S(2)}, u32[]{:S(2)}) collective-permute-start(bf16[512,768]{1,0:T(8,128)(2,1)} %bitcast.224), channel_id=1, source_target_pairs={{16,0},{32,16},{48,32},{64,48},{80,64},{96,80},{112,96},{17,1},{33... | collective-permute-start | bytes 2359304 | tf_op jit(solution)/shard_map/ppermute | solution.py:25
  23.4 1.6 collective-permute-start.8
  25.1 4.9 %collective-permute-done.8 = bf16[128,256]{1,0:T(8,128)(2,1)S(1)} collective-permute-done((bf16[128,256]{1,0:T(8,128)(2,1)S(1)}, bf16[128,256]{1,0:T(8,128)(2,1)S(1)}, u32[]{:S(2)}, u32[]{:S(2)}) %collective-permute-start.8) | collective-permute-done | bytes 65568 | tf_op jit(solution)/shard_map/ppermute | solution.py:82
  33.3 7.4 %collective-permute-done.3 = bf16[4,128,256]{2,1,0:T(8,128)(2,1)S(1)} collective-permute-done((bf16[4,128,256]{2,1,0:T(8,128)(2,1)S(1)}, bf16[4,128,256]{2,1,0:T(8,128)(2,1)S(1)}, u32[]{:S(2)}, u32[]{:S(2)}) %collective-permute-start.3) | collective-permute-done | bytes 262176 | tf_op jit(solution)/shard_map/ppermute | solution.py:82
  42.9 1.2 collective-permute-start.10
  44.3 1.6 collective-permute-start.11
  45.9 1.4 convolution_convert_fusion
  47.5 1.8 collective-permute-done.5
  49.3 1.3 pad_maximum_fusion.1
  50.6 2.8 %collective-permute-done.10 = bf16[4,128,256]{2,1,0:T(8,128)(2,1)} collective-permute-done((bf16[4,128,256]{2,1,0:T(8,128)(2,1)S(1)}, bf16[4,128,256]{2,1,0:T(8,128)(2,1)}, u32[]{:S(2)}, u32[]{:S(2)}) %collective-permute-start.10) | collective-permute-done | bytes 262176 | tf_op jit(solution)/shard_map/ppermute | solution.py:82
  53.5 1.2 pad_maximum_fusion.2
  55.0 2.2 gather_fusion
  57.2 36.1 %while.28 = (s32[]{:T(128)}, f32[1024]{0:T(1024)S(1)}, f32[1024]{0:T(1024)S(1)}, f32[1024,128]{1,0:T(8,128)S(1)}, s32[8,512]{1,0:T(8,128)}, /*index=5*/s32[8,512...) while((s32[]{:T(128)}, f32[1024]{0:T(1024)S(1)}, ...), condition=%wide.region_7.8_spmd.clone, body=%wide.region_4.7_spmd.clone.sunk | while | flops 278795264 | bytes 8525969 | solution.py:297
  60.6 1.0 convolution_add_fusion.4
  65.2 1.0 convolution_add_fusion.4
  69.7 1.0 convolution_add_fusion.4
  74.2 1.0 convolution_add_fusion.4
  78.7 1.0 convolution_add_fusion.4
  83.2 1.0 convolution_add_fusion.4
  87.7 1.0 convolution_add_fusion.4
  92.3 1.0 convolution_add_fusion.4
  93.3 8.2 %collective-permute-start.28 = (bf16[256,8192]{1,0:T(8,128)(2,1)}, bf16[256,8192]{1,0:T(8,128)(2,1)}, u32[]{:S(2)}, u32[]{:S(2)}) collective-permute-start(bf16[256,8192]{1,0:T(8,128)(2,1)} %bitcast.223), channel_id=1, source_target_pairs={{16,0},{32,16},{48,32},{64,48},{80,64},{96,80},{112,96},{17,1},{33... | collective-permute-start | bytes 12582920 | tf_op jit(solution)/shard_map/ppermute | solution.py:25
  101.5 7.2 %fusion.36 = bf16[256,512]{1,0:T(8,128)(2,1)S(1)} fusion(bf16[1,8192,512]{2,1,0:T(8,128)(2,1)} %all-gather.6.cloned.1.call-done, bf16[1,256,8192]{2,1,0:T(8,128)(2,1)} %param.13), kind=kOutput, calls=%fused_computation.58 | convolution fusion | flops 2147614720 | bytes 12845056 | tf_op jit(solution)/shard_map/dot_general | solution.py:227
  109.3 48.1 %while.29 = (s32[]{:T(128)}, f32[1024,128]{1,0:T(8,128)S(1)}, f32[8,512,256]{2,1,0:T(8,128)}, s32[8,512]{1,0:T(8,128)}, s32[8,512]{1,0:T(8,128)}, /*index=5*/bf1...) while((s32[]{:T(128)}, f32[1024,128]{1,0:T(8,128)S(1)}, ...), condition=%wide.region_10.11_spmd.clone, body=%wide.region_9.10_spmd.clone.sunk | while | flops 677249024 | bytes 16177315 | solution.py:319
  157.4 2.5 %slice_bitcast_fusion = (f32[4,4,256,128]{3,2,0,1:T(8,128)S(1)}, f32[4,4,256,128]{3,2,1,0:T(8,128)S(1)}) fusion(f32[4,4,256,256]{3,2,1,0:T(8,128)} %bitcast.203), kind=kLoop, calls=%fused_computation.55 | loop fusion | bytes 8388608 | tf_op jit(solution)/shard_map/transpose | solution.py:112
  159.9 1.1 slice_bitcast_fusion.8
  161.0 3.4 %collective-permute-start.14 = (bf16[4,256,128]{2,1,0:T(8,128)(2,1)}, bf16[4,256,128]{2,1,0:T(8,128)(2,1)S(1)}, u32[]{:S(2)}, u32[]{:S(2)}) collective-permute-start(bf16[4,256,128]{2,1,0:T(8,128)(2,1)} %get-tuple-element.276), channel_id=1, source_target_pairs={{0,1},{1,2},{2,3},{3,0},{4,5},{5,6},{6,7},{7,4},{8,9},{9,10},{10,1... | collective-permute-start | bytes 786440 | tf_op jit(solution)/shard_map/ppermute | solution.py:82
  165.6 3.3 %collective-permute-start.19 = (bf16[4,256,128]{2,1,0:T(8,128)(2,1)}, bf16[4,256,128]{2,1,0:T(8,128)(2,1)S(1)}, u32[]{:S(2)}, u32[]{:S(2)}) collective-permute-start(bf16[4,256,128]{2,1,0:T(8,128)(2,1)} %get-tuple-element.277), channel_id=1, source_target_pairs={{0,12},{1,13},{2,14},{3,15},{4,0},{5,1},{6,2},{7,3},{8,4},{9,5},{1... | collective-permute-start | bytes 786440 | tf_op jit(solution)/shard_map/ppermute | solution.py:82
  168.8 1.6 fusion.35
  170.8 12.9 %collective-permute-done.20 = bf16[4,256,128]{2,1,0:T(8,128)(2,1)S(1)} collective-permute-done((bf16[4,256,128]{2,1,0:T(8,128)(2,1)S(1)}, bf16[4,256,128]{2,1,0:T(8,128)(2,1)S(1)}, u32[]{:S(2)}, u32[]{:S(2)}) %collective-permute-start.20) | collective-permute-done | bytes 262176 | tf_op jit(solution)/shard_map/ppermute | solution.py:82
  184.5 2.4 fusion.50
  187.0 1.4 collective-permute-start.27
  188.5 1.1 fusion.46
  189.6 1.7 collective-permute-start.15
  191.3 2.4 collective-permute-done.21
  193.7 1.0 fusion.44
  195.0 2.7 %collective-permute-start.23 = (bf16[256,128]{1,0:T(8,128)(2,1)S(1)}, bf16[256,128]{1,0:T(8,128)(2,1)S(1)}, u32[]{:S(2)}, u32[]{:S(2)}) collective-permute-start(bf16[256,128]{1,0:T(8,128)(2,1)S(1)} %get-tuple-element.284), channel_id=1, source_target_pairs={{0,1},{1,2},{2,3},{3,0},{4,5},{5,6},{6,7},{7,4},{8,9},{9,10},{10,1... | collective-permute-start | bytes 196616 | tf_op jit(solution)/shard_map/ppermute | solution.py:82
  197.7 1.1 fusion.48
  198.9 2.8 %collective-permute-start.16 = (bf16[256,128]{1,0:T(8,128)(2,1)S(1)}, bf16[256,128]{1,0:T(8,128)(2,1)S(1)}, u32[]{:S(2)}, u32[]{:S(2)}) collective-permute-start(bf16[256,128]{1,0:T(8,128)(2,1)S(1)} %get-tuple-element.281), channel_id=1, source_target_pairs={{0,12},{1,13},{2,14},{3,15},{4,0},{5,1},{6,2},{7,3},{8,4},{9,5},{1... | collective-permute-start | bytes 196616 | tf_op jit(solution)/shard_map/ppermute | solution.py:82
  201.7 4.3 %collective-permute-done.17 = bf16[256,128]{1,0:T(8,128)(2,1)S(1)} collective-permute-done((bf16[256,128]{1,0:T(8,128)(2,1)S(1)}, bf16[256,128]{1,0:T(8,128)(2,1)S(1)}, u32[]{:S(2)}, u32[]{:S(2)}) %collective-permute-start.17) | collective-permute-done | bytes 65568 | tf_op jit(solution)/shard_map/ppermute | solution.py:82
  206.0 3.0 %collective-permute-start.24 = (bf16[256,128]{1,0:T(8,128)(2,1)S(1)}, bf16[256,128]{1,0:T(8,128)(2,1)S(1)}, u32[]{:S(2)}, u32[]{:S(2)}) collective-permute-start(bf16[256,128]{1,0:T(8,128)(2,1)S(1)} %fusion.53), channel_id=1, source_target_pairs={{0,1},{1,2},{2,3},{3,0},{4,5},{5,6},{6,7},{7,4},{8,9},{9,10},{10,1... | collective-permute-start | bytes 196616 | tf_op jit(solution)/shard_map/ppermute | solution.py:82
  210.4 3.3 %collective-permute-done.18 = bf16[256,128]{1,0:T(8,128)(2,1)S(1)} collective-permute-done((bf16[256,128]{1,0:T(8,128)(2,1)S(1)}, bf16[256,128]{1,0:T(8,128)(2,1)S(1)}, u32[]{:S(2)}, u32[]{:S(2)}) %collective-permute-start.18) | collective-permute-done | bytes 65568 | tf_op jit(solution)/shard_map/ppermute | solution.py:82
  214.4 5.9 %collective-permute-start.25 = (bf16[256,256]{1,0:T(8,128)(2,1)S(1)}, bf16[256,256]{1,0:T(8,128)(2,1)S(1)}, u32[]{:S(2)}, u32[]{:S(2)}) collective-permute-start(bf16[256,256]{1,0:T(8,128)(2,1)S(1)} %pad_maximum_fusion.9), channel_id=1, source_target_pairs={{16,0},{32,16},{48,32},{64,48},{80,64},{96,80},{112,96},{17,1},{33... | collective-permute-start | bytes 393224 | tf_op jit(solution)/shard_map/ppermute | solution.py:25
  221.1 8.9 %shard_map.91.base_ref = f32[256,8192]{1,0:T(8,128)} custom-call(bf16[256,512]{1,0:T(8,128)(2,1)} %copy-done.2, bf16[8192,768]{1,0:T(8,128)(2,1)} %all-gather.4.cloned.1.call-done.weight_ref, bf16[256,8192]{1,0:T(8,128)(2,1)} %collective-permute-done.28.base_ref), custom_call_target="tpu_custom_call" | custom-call | flops 2147483648 | bytes 21233664 | tf_op jit(solution)/shard_map/pallas_call | solution.py:51
  230.6 6.8 %shard_map.92 = bf16[256,8192]{1,0:T(8,128)(2,1)} custom-call(bf16[256,256]{1,0:T(8,128)(2,1)} %copy-done.3, bf16[8192,768]{1,0:T(8,128)(2,1)} %all-gather.4.cloned.1.call-done.weight_ref, f32[256,8192]{1,0:T(8,128)} %shard_map.91.base_ref), custom_call_target="tpu_custom_call" | custom-call | flops 1073741824 | bytes 16908288 | tf_op jit(solution)/shard_map/pallas_call | solution.py:51
  (307 shorter events, 92.0 us)
Async XLA Ops:
  6.5 24.8 %copy-start.5 = (s32[1,32]{1,0:T(1,128)S(1)}, s32[1,32]{1,0:T(1,128)}, u32[]{:S(2)}) copy-start(s32[1,32]{1,0:T(1,128)} %param.19) | copy-start | bytes 388
  6.5 95.0 %all-gather.6.cloned.1.call-start = ((), (), s32[]{:S(2)}) async-start(), calls=%async_computation.1 | async-start | bytes 8912896 | tf_op jit(solution)/shard_map/all_gather | solution.py:229
  7.3 213.2 %all-gather.4.cloned.1.call-start = ((), (), s32[]{:S(2)}) async-start(), calls=%async_computation | async-start | bytes 13369344 | tf_op jit(solution)/shard_map/all_gather | solution.py:226
  8.2 10.3 %collective-permute-start.1 = (bf16[128,256]{1,0:T(8,128)(2,1)S(1)}, bf16[128,256]{1,0:T(8,128)(2,1)S(1)}, u32[]{:S(2)}, u32[]{:S(2)}) collective-permute-start(bf16[128,256]{1,0:T(8,128)(2,1)S(1)} %get-tuple-element.294), channel_id=1, source_target_pairs={{0,3},{1,0},{2,1},{3,2},{4,7},{5,4},{6,5},{7,6},{8,11},{9,8},{10,9... | collective-permute-start | bytes 196616 | tf_op jit(solution)/shard_map/ppermute | solution.py:82
  8.8 9.5 %collective-permute-start = (bf16[128,256]{1,0:T(8,128)(2,1)S(1)}, bf16[128,256]{1,0:T(8,128)(2,1)S(1)}, u32[]{:S(2)}, u32[]{:S(2)}) collective-permute-start(bf16[128,256]{1,0:T(8,128)(2,1)S(1)} %get-tuple-element.294), channel_id=1, source_target_pairs={{0,1},{1,2},{2,3},{3,0},{4,5},{5,6},{6,7},{7,4},{8,9},{9,10},{10,1... | collective-permute-start | bytes 196616 | tf_op jit(solution)/shard_map/ppermute | solution.py:82
  10.9 14.2 %collective-permute-start.7 = (bf16[128,256]{1,0:T(8,128)(2,1)S(1)}, bf16[128,256]{1,0:T(8,128)(2,1)S(1)}, u32[]{:S(2)}, u32[]{:S(2)}) collective-permute-start(bf16[128,256]{1,0:T(8,128)(2,1)S(1)} %get-tuple-element.295), channel_id=1, source_target_pairs={{0,12},{1,13},{2,14},{3,15},{4,0},{5,1},{6,2},{7,3},{8,4},{9,5},{1... | collective-permute-start | bytes 196616 | tf_op jit(solution)/shard_map/ppermute | solution.py:82
  13.7 9.7 %collective-permute-start.6 = (bf16[128,256]{1,0:T(8,128)(2,1)S(1)}, bf16[128,256]{1,0:T(8,128)(2,1)S(1)}, u32[]{:S(2)}, u32[]{:S(2)}) collective-permute-start(bf16[128,256]{1,0:T(8,128)(2,1)S(1)} %get-tuple-element.295), channel_id=1, source_target_pairs={{0,4},{1,5},{2,6},{3,7},{4,8},{5,9},{6,10},{7,11},{8,12},{9,13},{1... | collective-permute-start | bytes 196616 | tf_op jit(solution)/shard_map/ppermute | solution.py:82
  14.7 28.2 %collective-permute-start.12 = (bf16[128,512]{1,0:T(8,128)(2,1)S(1)}, bf16[128,512]{1,0:T(8,128)(2,1)S(1)}, u32[]{:S(2)}, u32[]{:S(2)}) collective-permute-start(bf16[128,512]{1,0:T(8,128)(2,1)S(1)} %get-tuple-element.286), channel_id=1, source_target_pairs={{0,8},{1,9},{2,10},{3,11},{4,12},{5,13},{6,14},{7,15},{8,0},{9,1},... | collective-permute-start | bytes 393224 | tf_op jit(solution)/shard_map/ppermute | solution.py:19
  17.2 1.1 copy-start.6
  18.3 6.6 %collective-permute-start.2 = (bf16[128,256]{1,0:T(8,128)(2,1)S(1)}, bf16[128,256]{1,0:T(8,128)(2,1)S(1)}, u32[]{:S(2)}, u32[]{:S(2)}) collective-permute-start(bf16[128,256]{1,0:T(8,128)(2,1)S(1)} %collective-permute-done), channel_id=1, source_target_pairs={{0,1},{1,2},{2,3},{3,0},{4,5},{5,6},{6,7},{7,4},{8,9},{9,10},{10,1... | collective-permute-start | bytes 196616 | tf_op jit(solution)/shard_map/ppermute | solution.py:82
  18.5 38.6 %collective-permute-start.26 = (bf16[512,768]{1,0:T(8,128)(2,1)}, bf16[512,768]{1,0:T(8,128)(2,1)}, u32[]{:S(2)}, u32[]{:S(2)}) collective-permute-start(bf16[512,768]{1,0:T(8,128)(2,1)} %bitcast.224), channel_id=1, source_target_pairs={{16,0},{32,16},{48,32},{64,48},{80,64},{96,80},{112,96},{17,1},{33... | collective-permute-start | bytes 2359304 | tf_op jit(solution)/shard_map/ppermute | solution.py:25
  23.4 6.7 %collective-permute-start.8 = (bf16[128,256]{1,0:T(8,128)(2,1)S(1)}, bf16[128,256]{1,0:T(8,128)(2,1)S(1)}, u32[]{:S(2)}, u32[]{:S(2)}) collective-permute-start(bf16[128,256]{1,0:T(8,128)(2,1)S(1)} %collective-permute-done.6), channel_id=1, source_target_pairs={{0,4},{1,5},{2,6},{3,7},{4,8},{5,9},{6,10},{7,11},{8,12},{9,13},{1... | collective-permute-start | bytes 196616 | tf_op jit(solution)/shard_map/ppermute | solution.py:82
  25.0 15.6 %collective-permute-start.3 = (bf16[4,128,256]{2,1,0:T(8,128)(2,1)S(1)}, bf16[4,128,256]{2,1,0:T(8,128)(2,1)S(1)}, u32[]{:S(2)}, u32[]{:S(2)}) collective-permute-start(bf16[4,128,256]{2,1,0:T(8,128)(2,1)S(1)} %get-tuple-element.288), channel_id=1, source_target_pairs={{0,4},{1,5},{2,6},{3,7},{4,8},{5,9},{6,10},{7,11},{8,12},{9,13},{1... | collective-permute-start | bytes 786440 | tf_op jit(solution)/shard_map/ppermute | solution.py:82
  30.1 14.2 %collective-permute-start.9 = (bf16[4,128,256]{2,1,0:T(8,128)(2,1)S(1)}, bf16[4,128,256]{2,1,0:T(8,128)(2,1)}, u32[]{:S(2)}, u32[]{:S(2)}) collective-permute-start(bf16[4,128,256]{2,1,0:T(8,128)(2,1)S(1)} %get-tuple-element.290), channel_id=1, source_target_pairs={{0,1},{1,2},{2,3},{3,0},{4,5},{5,6},{6,7},{7,4},{8,9},{9,10},{10,1... | collective-permute-start | bytes 786440 | tf_op jit(solution)/shard_map/ppermute | solution.py:82
  33.2 14.3 %collective-permute-start.4 = (bf16[4,128,256]{2,1,0:T(8,128)(2,1)S(1)}, bf16[4,128,256]{2,1,0:T(8,128)(2,1)}, u32[]{:S(2)}, u32[]{:S(2)}) collective-permute-start(bf16[4,128,256]{2,1,0:T(8,128)(2,1)S(1)} %get-tuple-element.288), channel_id=1, source_target_pairs={{0,12},{1,13},{2,14},{3,15},{4,0},{5,1},{6,2},{7,3},{8,4},{9,5},{1... | collective-permute-start | bytes 786440 | tf_op jit(solution)/shard_map/ppermute | solution.py:82
  40.6 8.7 %collective-permute-start.5 = (bf16[4,128,256]{2,1,0:T(8,128)(2,1)S(1)}, bf16[4,128,256]{2,1,0:T(8,128)(2,1)}, u32[]{:S(2)}, u32[]{:S(2)}) collective-permute-start(bf16[4,128,256]{2,1,0:T(8,128)(2,1)S(1)} %collective-permute-done.3), channel_id=1, source_target_pairs={{0,4},{1,5},{2,6},{3,7},{4,8},{5,9},{6,10},{7,11},{8,12},{9,13},{1... | collective-permute-start | bytes 786440 | tf_op jit(solution)/shard_map/ppermute | solution.py:82
  42.9 10.5 %collective-permute-start.10 = (bf16[4,128,256]{2,1,0:T(8,128)(2,1)S(1)}, bf16[4,128,256]{2,1,0:T(8,128)(2,1)}, u32[]{:S(2)}, u32[]{:S(2)}) collective-permute-start(bf16[4,128,256]{2,1,0:T(8,128)(2,1)S(1)} %get-tuple-element.290), channel_id=1, source_target_pairs={{0,3},{1,0},{2,1},{3,2},{4,7},{5,4},{6,5},{7,6},{8,11},{9,8},{10,9... | collective-permute-start | bytes 786440 | tf_op jit(solution)/shard_map/ppermute | solution.py:82
  44.3 9.2 %collective-permute-start.11 = (bf16[4,128,256]{2,1,0:T(8,128)(2,1)}, bf16[4,128,256]{2,1,0:T(8,128)(2,1)}, u32[]{:S(2)}, u32[]{:S(2)}) collective-permute-start(bf16[4,128,256]{2,1,0:T(8,128)(2,1)} %collective-permute-done.9), channel_id=1, source_target_pairs={{0,1},{1,2},{2,3},{3,0},{4,5},{5,6},{6,7},{7,4},{8,9},{9,10},{10,1... | collective-permute-start | bytes 786440 | tf_op jit(solution)/shard_map/ppermute | solution.py:82
  93.3 127.1 %collective-permute-start.28 = (bf16[256,8192]{1,0:T(8,128)(2,1)}, bf16[256,8192]{1,0:T(8,128)(2,1)}, u32[]{:S(2)}, u32[]{:S(2)}) collective-permute-start(bf16[256,8192]{1,0:T(8,128)(2,1)} %bitcast.223), channel_id=1, source_target_pairs={{16,0},{32,16},{48,32},{64,48},{80,64},{96,80},{112,96},{17,1},{33... | collective-permute-start | bytes 12582920 | tf_op jit(solution)/shard_map/ppermute | solution.py:25
  159.9 9.0 %copy-start = (f32[4,4,256,128]{3,2,0,1:T(8,128)}, f32[4,4,256,128]{3,2,0,1:T(8,128)S(1)}, u32[]{:S(2)}) copy-start(f32[4,4,256,128]{3,2,0,1:T(8,128)S(1)} %get-tuple-element.273) | copy-start | bytes 6291460
  161.0 34.0 %collective-permute-start.13 = (bf16[4,256,128]{2,1,0:T(8,128)(2,1)}, bf16[4,256,128]{2,1,0:T(8,128)(2,1)}, u32[]{:S(2)}, u32[]{:S(2)}) collective-permute-start(bf16[4,256,128]{2,1,0:T(8,128)(2,1)} %get-tuple-element.275), channel_id=1, source_target_pairs={{0,3},{1,0},{2,1},{3,2},{4,7},{5,4},{6,5},{7,6},{8,11},{9,8},{10,9... | collective-permute-start | bytes 786440 | tf_op jit(solution)/shard_map/ppermute | solution.py:82
  161.0 26.1 %collective-permute-start.14 = (bf16[4,256,128]{2,1,0:T(8,128)(2,1)}, bf16[4,256,128]{2,1,0:T(8,128)(2,1)S(1)}, u32[]{:S(2)}, u32[]{:S(2)}) collective-permute-start(bf16[4,256,128]{2,1,0:T(8,128)(2,1)} %get-tuple-element.276), channel_id=1, source_target_pairs={{0,1},{1,2},{2,3},{3,0},{4,5},{5,6},{6,7},{7,4},{8,9},{9,10},{10,1... | collective-permute-start | bytes 786440 | tf_op jit(solution)/shard_map/ppermute | solution.py:82
  165.6 24.0 %collective-permute-start.19 = (bf16[4,256,128]{2,1,0:T(8,128)(2,1)}, bf16[4,256,128]{2,1,0:T(8,128)(2,1)S(1)}, u32[]{:S(2)}, u32[]{:S(2)}) collective-permute-start(bf16[4,256,128]{2,1,0:T(8,128)(2,1)} %get-tuple-element.277), channel_id=1, source_target_pairs={{0,12},{1,13},{2,14},{3,15},{4,0},{5,1},{6,2},{7,3},{8,4},{9,5},{1... | collective-permute-start | bytes 786440 | tf_op jit(solution)/shard_map/ppermute | solution.py:82
  168.8 1.6 copy-start.4
  168.8 1.6 copy-start.7
  168.8 14.9 %collective-permute-start.20 = (bf16[4,256,128]{2,1,0:T(8,128)(2,1)S(1)}, bf16[4,256,128]{2,1,0:T(8,128)(2,1)S(1)}, u32[]{:S(2)}, u32[]{:S(2)}) collective-permute-start(bf16[4,256,128]{2,1,0:T(8,128)(2,1)S(1)} %get-tuple-element.278), channel_id=1, source_target_pairs={{0,4},{1,5},{2,6},{3,7},{4,8},{5,9},{6,10},{7,11},{8,12},{9,13},{1... | collective-permute-start | bytes 786440 | tf_op jit(solution)/shard_map/ppermute | solution.py:82
  184.5 9.2 %collective-permute-start.21 = (bf16[4,256,128]{2,1,0:T(8,128)(2,1)}, bf16[4,256,128]{2,1,0:T(8,128)(2,1)}, u32[]{:S(2)}, u32[]{:S(2)}) collective-permute-start(bf16[4,256,128]{2,1,0:T(8,128)(2,1)} %fusion.42), channel_id=1, source_target_pairs={{0,4},{1,5},{2,6},{3,7},{4,8},{5,9},{6,10},{7,11},{8,12},{9,13},{1... | collective-permute-start | bytes 786440 | tf_op jit(solution)/shard_map/ppermute | solution.py:82
  187.0 10.7 %copy-start.1 = (f32[4,4,256,128]{3,2,0,1:T(8,128)S(1)}, f32[4,4,256,128]{3,2,0,1:T(8,128)}, u32[]{:S(2)}) copy-start(f32[4,4,256,128]{3,2,0,1:T(8,128)} %copy-done) | copy-start | bytes 6291460
  187.0 33.4 %collective-permute-start.27 = (bf16[256,512]{1,0:T(8,128)(2,1)S(1)}, bf16[256,512]{1,0:T(8,128)(2,1)S(1)}, u32[]{:S(2)}, u32[]{:S(2)}) collective-permute-start(bf16[256,512]{1,0:T(8,128)(2,1)S(1)} %convert_element_type.165), channel_id=1, source_target_pairs={{16,0},{32,16},{48,32},{64,48},{80,64},{96,80},{112,96},{17,1},{33... | collective-permute-start | bytes 786440 | tf_op jit(solution)/shard_map/ppermute | solution.py:25
  189.6 8.1 %collective-permute-start.15 = (bf16[4,256,128]{2,1,0:T(8,128)(2,1)S(1)}, bf16[4,256,128]{2,1,0:T(8,128)(2,1)S(1)}, u32[]{:S(2)}, u32[]{:S(2)}) collective-permute-start(bf16[4,256,128]{2,1,0:T(8,128)(2,1)S(1)} %fusion.46), channel_id=1, source_target_pairs={{0,1},{1,2},{2,3},{3,0},{4,5},{5,6},{6,7},{7,4},{8,9},{9,10},{10,1... | collective-permute-start | bytes 786440 | tf_op jit(solution)/shard_map/ppermute | solution.py:82
  194.9 14.2 %collective-permute-start.22 = (bf16[256,128]{1,0:T(8,128)(2,1)S(1)}, bf16[256,128]{1,0:T(8,128)(2,1)S(1)}, u32[]{:S(2)}, u32[]{:S(2)}) collective-permute-start(bf16[256,128]{1,0:T(8,128)(2,1)S(1)} %get-tuple-element.283), channel_id=1, source_target_pairs={{0,3},{1,0},{2,1},{3,2},{4,7},{5,4},{6,5},{7,6},{8,11},{9,8},{10,9... | collective-permute-start | bytes 196616 | tf_op jit(solution)/shard_map/ppermute | solution.py:82
  195.0 6.7 %collective-permute-start.23 = (bf16[256,128]{1,0:T(8,128)(2,1)S(1)}, bf16[256,128]{1,0:T(8,128)(2,1)S(1)}, u32[]{:S(2)}, u32[]{:S(2)}) collective-permute-start(bf16[256,128]{1,0:T(8,128)(2,1)S(1)} %get-tuple-element.284), channel_id=1, source_target_pairs={{0,1},{1,2},{2,3},{3,0},{4,5},{5,6},{6,7},{7,4},{8,9},{9,10},{10,1... | collective-permute-start | bytes 196616 | tf_op jit(solution)/shard_map/ppermute | solution.py:82
  198.9 11.5 %collective-permute-start.16 = (bf16[256,128]{1,0:T(8,128)(2,1)S(1)}, bf16[256,128]{1,0:T(8,128)(2,1)S(1)}, u32[]{:S(2)}, u32[]{:S(2)}) collective-permute-start(bf16[256,128]{1,0:T(8,128)(2,1)S(1)} %get-tuple-element.281), channel_id=1, source_target_pairs={{0,12},{1,13},{2,14},{3,15},{4,0},{5,1},{6,2},{7,3},{8,4},{9,5},{1... | collective-permute-start | bytes 196616 | tf_op jit(solution)/shard_map/ppermute | solution.py:82
  201.7 4.3 %collective-permute-start.17 = (bf16[256,128]{1,0:T(8,128)(2,1)S(1)}, bf16[256,128]{1,0:T(8,128)(2,1)S(1)}, u32[]{:S(2)}, u32[]{:S(2)}) collective-permute-start(bf16[256,128]{1,0:T(8,128)(2,1)S(1)} %get-tuple-element.282), channel_id=1, source_target_pairs={{0,4},{1,5},{2,6},{3,7},{4,8},{5,9},{6,10},{7,11},{8,12},{9,13},{1... | collective-permute-start | bytes 196616 | tf_op jit(solution)/shard_map/ppermute | solution.py:82
  206.0 4.4 %collective-permute-start.24 = (bf16[256,128]{1,0:T(8,128)(2,1)S(1)}, bf16[256,128]{1,0:T(8,128)(2,1)S(1)}, u32[]{:S(2)}, u32[]{:S(2)}) collective-permute-start(bf16[256,128]{1,0:T(8,128)(2,1)S(1)} %fusion.53), channel_id=1, source_target_pairs={{0,1},{1,2},{2,3},{3,0},{4,5},{5,6},{6,7},{7,4},{8,9},{9,10},{10,1... | collective-permute-start | bytes 196616 | tf_op jit(solution)/shard_map/ppermute | solution.py:82
  209.1 4.6 %collective-permute-start.18 = (bf16[256,128]{1,0:T(8,128)(2,1)S(1)}, bf16[256,128]{1,0:T(8,128)(2,1)S(1)}, u32[]{:S(2)}, u32[]{:S(2)}) collective-permute-start(bf16[256,128]{1,0:T(8,128)(2,1)S(1)} %fusion.58), channel_id=1, source_target_pairs={{0,4},{1,5},{2,6},{3,7},{4,8},{5,9},{6,10},{7,11},{8,12},{9,13},{1... | collective-permute-start | bytes 196616 | tf_op jit(solution)/shard_map/ppermute | solution.py:82
  214.4 15.5 %collective-permute-start.25 = (bf16[256,256]{1,0:T(8,128)(2,1)S(1)}, bf16[256,256]{1,0:T(8,128)(2,1)S(1)}, u32[]{:S(2)}, u32[]{:S(2)}) collective-permute-start(bf16[256,256]{1,0:T(8,128)(2,1)S(1)} %pad_maximum_fusion.9), channel_id=1, source_target_pairs={{16,0},{32,16},{48,32},{64,48},{80,64},{96,80},{112,96},{17,1},{33... | collective-permute-start | bytes 393224 | tf_op jit(solution)/shard_map/ppermute | solution.py:25
  220.4 0.7 copy-start.2
  230.0 0.7 copy-start.3
Sparse Core Ops, SparseCore 0:
  9.5 77.5 all-gather.5
  89.2 96.3 all-gather.3

commit v17 on v15

--- a/solution.py
+++ b/solution.py
@@ -110,8 +110,7 @@
     half = width // 2
     first = ring_reduce(jnp.moveaxis(tiles[..., :half], 1, 0), 0, device, side)
     first = ring_reduce(first, 1, device, side)
-    second = ring_reduce(tiles[..., half:], 1, device, side)
-    second = ring_reduce(second, 0, device, side)
+    second = summed_rows(rows[:, half:].astype(jnp.bfloat16), "ctx")
     return jnp.concatenate([first, second], axis=1)
 
 

time: 231 us -> 231 us (level)
  starting transfers between devices: 37.6 us -> 45.2 us
  waiting for transfers between devices: 51.3 us -> 48 us
    all_to_all x0 -> x1, starting transfers between devices: none -> 6.46 us  [summed_rows(): lax.all_to_all(value.reshape((count, -1) + value.shape[1:]), axis, 0, 0,...]
    ppermute x24 -> x18, waiting for transfers between devices: 46.1 us -> 40.7 us  [ring_shift(): return lax.ppermute(value, 'ctx', pairs)]
    ppermute x4, starting transfers between devices: 14.7 us -> 19.5 us  [passed_along_2(): return lax.ppermute(value, axis, pairs)]
    ppermute x24 -> x18, starting transfers between devices: 21.2 us -> 17.6 us  [ring_shift(): return lax.ppermute(value, 'ctx', pairs)]
    all_to_all x0 -> x1, waiting for transfers between devices: none -> 2.7 us  [summed_rows(): lax.all_to_all(value.reshape((count, -1) + value.shape[1:]), axis, 0, 0,...]
    another operation x4, other arithmetic: 1.49 us -> 3.85 us
    while x136 -> x40, local copies, waits for them, and re-layouts: 9.6 us -> 9.28 us
  transfers between devices with their start and end apart: 31 -> 26, of which waited for: 13 -> 10; matrix products, arithmetic and copies ran while one was open for 45% -> 44% of each run, Pallas kernels for 0% -> 0%
where the time goes in v17:
time: 231 us; the launch traced here: 229 us
  local copies, waits for them, and re-layouts  48.6 us (21%)
  waiting for transfers between devices  48 us (21%)
  starting transfers between devices  45.2 us (20%)
  matrix products  42.8 us (19%)
  other arithmetic  19.1 us (8%)
  between operations  15.2 us (7%)
  Pallas kernels  9.08 us (4%)
    ppermute x18, waiting for transfers between devices, ring_shift(): return lax.ppermute(value, 'ctx', pairs)  40.7 us
    ppermute x4, starting transfers between devices, passed_along_2(): return lax.ppermute(value, axis, pairs)  19.5 us
    ppermute x18, starting transfers between devices, ring_shift(): return lax.ppermute(value, 'ctx', pairs)  17.6 us
    squeeze x16, local copies, waits for them, and re-layouts, body(): lax.scan(running_total, start_carry, key_blocks)  15.6 us
    dot_general x24, matrix products, contract_cols(): lax.dot_general(left_rows, right_rows, (((1,), (1,)), ((), ())), preferre...  14.2 us
    while x40, local copies, waits for them, and re-layouts  9.28 us
    pallas_call x1, Pallas kernels, projected_sum(): pl.pallas_call(projection_kernel, grid=(width // tile,), in_specs=[pl.Blo...  9.08 us
    dynamic_update_slice x16, local copies, waits for them, and re-layouts, body(): lax.scan(grad_step, jnp.zeros((flat_rows, head_dim), jnp.float32), key_bl...  8.24 us
  transfers between devices with their start and end apart: 26, of which 10 were waited for; matrix products, arithmetic and copies ran while one was open for 44% of the time, Pallas kernels for 0%

profile of v17, /device:TPU:1, one launch (start us, length us, event | category | flops | bytes accessed | tf_op | source)
XLA Modules:
  0.0 229.3 jit_solution(3026138421215328115)
XLA Ops:
  8.2 2.1 collective-permute-start
  10.3 1.3 collective-permute-start.1
  11.7 1.4 collective-permute-start.6
  13.1 1.4 collective-permute-start.7
  14.5 1.0 fusion.69
  15.5 1.7 collective-permute-start.12
  19.2 4.2 %collective-permute-start.21 = (bf16[512,768]{1,0:T(8,128)(2,1)}, bf16[512,768]{1,0:T(8,128)(2,1)}, u32[]{:S(2)}, u32[]{:S(2)}) collective-permute-start(bf16[512,768]{1,0:T(8,128)(2,1)} %bitcast.197), channel_id=1, source_target_pairs={{16,0},{32,16},{48,32},{64,48},{80,64},{96,80},{112,96},{17,1},{33... | collective-permute-start | bytes 2359304 | tf_op jit(solution)/shard_map/ppermute | solution.py:25
  24.6 5.6 %collective-permute-done.8 = bf16[128,256]{1,0:T(8,128)(2,1)S(1)} collective-permute-done((bf16[128,256]{1,0:T(8,128)(2,1)S(1)}, bf16[128,256]{1,0:T(8,128)(2,1)S(1)}, u32[]{:S(2)}, u32[]{:S(2)}) %collective-permute-start.8) | collective-permute-done | bytes 65568 | tf_op jit(solution)/shard_map/ppermute | solution.py:81
  30.2 1.3 collective-permute-start.9
  33.6 7.5 %collective-permute-done.3 = bf16[4,128,256]{2,1,0:T(8,128)(2,1)S(1)} collective-permute-done((bf16[4,128,256]{2,1,0:T(8,128)(2,1)S(1)}, bf16[4,128,256]{2,1,0:T(8,128)(2,1)S(1)}, u32[]{:S(2)}, u32[]{:S(2)}) %collective-permute-start.3) | collective-permute-done | bytes 262176 | tf_op jit(solution)/shard_map/ppermute | solution.py:81
  41.4 2.9 %collective-permute-start.10 = (bf16[4,128,256]{2,1,0:T(8,128)(2,1)S(1)}, bf16[4,128,256]{2,1,0:T(8,128)(2,1)}, u32[]{:S(2)}, u32[]{:S(2)}) collective-permute-start(bf16[4,128,256]{2,1,0:T(8,128)(2,1)S(1)} %get-tuple-element.282), channel_id=1, source_target_pairs={{0,3},{1,0},{2,1},{3,2},{4,7},{5,4},{6,5},{7,6},{8,11},{9,8},{10,9... | collective-permute-start | bytes 786440 | tf_op jit(solution)/shard_map/ppermute | solution.py:81
  45.6 3.3 %collective-permute-done.5 = bf16[4,128,256]{2,1,0:T(8,128)(2,1)S(1)} collective-permute-done((bf16[4,128,256]{2,1,0:T(8,128)(2,1)S(1)}, bf16[4,128,256]{2,1,0:T(8,128)(2,1)S(1)}, u32[]{:S(2)}, u32[]{:S(2)}) %collective-permute-start.5) | collective-permute-done | bytes 262176 | tf_op jit(solution)/shard_map/ppermute | solution.py:81
  49.8 3.5 %collective-permute-done.11 = bf16[4,128,256]{2,1,0:T(8,128)(2,1)} collective-permute-done((bf16[4,128,256]{2,1,0:T(8,128)(2,1)S(1)}, bf16[4,128,256]{2,1,0:T(8,128)(2,1)}, u32[]{:S(2)}, u32[]{:S(2)}) %collective-permute-start.11) | collective-permute-done | bytes 262176 | tf_op jit(solution)/shard_map/ppermute | solution.py:81
  53.3 1.2 pad_maximum_fusion.2
  54.6 2.1 gather_fusion
  56.7 39.0 %while.28 = (s32[]{:T(128)}, f32[1024]{0:T(1024)S(1)}, f32[1024]{0:T(1024)S(1)}, f32[1024,128]{1,0:T(8,128)}, s32[8,512]{1,0:T(8,128)S(1)}, /*index=5*/s32[8,512...) while((s32[]{:T(128)}, f32[1024]{0:T(1024)S(1)}, ...), condition=%wide.region_7.8_spmd.clone, body=%wide.region_4.7_spmd.clone.sunk | while | flops 278795264 | bytes 12720321 | solution.py:295
  56.8 1.0 dynamic-slice_bitcast_fusion.4
  61.7 1.0 dynamic-slice_bitcast_fusion.4
  66.5 1.0 dynamic-slice_bitcast_fusion.4
  71.4 1.0 dynamic-slice_bitcast_fusion.4
  76.3 1.0 dynamic-slice_bitcast_fusion.4
  81.2 1.0 dynamic-slice_bitcast_fusion.4
  86.0 1.0 dynamic-slice_bitcast_fusion.4
  90.9 1.0 dynamic-slice_bitcast_fusion.4
  95.7 3.4 %collective-permute-start.22 = (bf16[256,8192]{1,0:T(8,128)(2,1)}, bf16[256,8192]{1,0:T(8,128)(2,1)}, u32[]{:S(2)}, u32[]{:S(2)}) collective-permute-start(bf16[256,8192]{1,0:T(8,128)(2,1)} %bitcast.196), channel_id=1, source_target_pairs={{16,0},{32,16},{48,32},{64,48},{80,64},{96,80},{112,96},{17,1},{33... | collective-permute-start | bytes 12582920 | tf_op jit(solution)/shard_map/ppermute | solution.py:25
  99.2 7.7 %fusion.35 = bf16[256,512]{1,0:T(8,128)(2,1)S(1)} fusion(bf16[1,8192,512]{2,1,0:T(8,128)(2,1)} %all-gather.6.cloned.1.call-done, bf16[1,256,8192]{2,1,0:T(8,128)(2,1)} %param.13), kind=kOutput, calls=%fused_computation.55 | convolution fusion | flops 2147614720 | bytes 12845056 | tf_op jit(solution)/shard_map/dot_general | solution.py:225
  107.5 42.3 %while.29 = (s32[]{:T(128)}, f32[1024,128]{1,0:T(8,128)S(1)}, f32[8,512,256]{2,1,0:T(8,128)}, s32[8,512]{1,0:T(8,128)S(1)}, s32[8,512]{1,0:T(8,128)S(1)}, /*inde...) while((s32[]{:T(128)}, f32[1024,128]{1,0:T(8,128)S(1)}, ...), condition=%wide.region_10.11_spmd.clone, body=%wide.region_9.10_spmd.clone.sunk | while | flops 677249024 | bytes 16177815 | solution.py:317
  107.5 1.0 dynamic-slice_bitcast_fusion.5
  112.8 1.0 dynamic-slice_bitcast_fusion.5
  118.1 1.0 dynamic-slice_bitcast_fusion.5
  134.0 1.0 dynamic-slice_bitcast_fusion.5
  139.2 1.0 dynamic-slice_bitcast_fusion.5
  149.8 1.8 copy_bitcast_fusion
  152.2 2.7 %collective-permute-start.14 = (bf16[4,256,128]{2,1,0:T(8,128)(2,1)S(1)}, bf16[4,256,128]{2,1,0:T(8,128)(2,1)S(1)}, u32[]{:S(2)}, u32[]{:S(2)}) collective-permute-start(bf16[4,256,128]{2,1,0:T(8,128)(2,1)S(1)} %get-tuple-element.271), channel_id=1, source_target_pairs={{0,3},{1,0},{2,1},{3,2},{4,7},{5,4},{6,5},{7,6},{8,11},{9,8},{10,9... | collective-permute-start | bytes 786440 | tf_op jit(solution)/shard_map/ppermute | solution.py:81
  154.8 12.5 %collective-permute-done.15 = bf16[4,256,128]{2,1,0:T(8,128)(2,1)S(1)} collective-permute-done((bf16[4,256,128]{2,1,0:T(8,128)(2,1)S(1)}, bf16[4,256,128]{2,1,0:T(8,128)(2,1)S(1)}, u32[]{:S(2)}, u32[]{:S(2)}) %collective-permute-start.15) | collective-permute-done | bytes 262176 | tf_op jit(solution)/shard_map/ppermute | solution.py:81
  168.5 2.5 %convert.15 = bf16[8,512,256]{2,1,0:T(8,128)(2,1)S(1)} convert(f32[8,512,256]{2,1,0:T(8,128)} %get-tuple-element.129) | non-fusion elementwise | flops 1048576 | bytes 6291456 | tf_op jit(solution)/shard_map/convert.2
  171.0 1.0 slice.137
  172.0 6.5 %all-to-all-start = ((bf16[16,256,128]{2,1,0:T(8,128)(2,1)}), bf16[16,256,128]{2,1,0:T(8,128)(2,1)}, u32[]{:S(2)}, u32[]{:S(2)}) async-start(bf16[16,256,128]{2,1,0:T(8,128)(2,1)} %bitcast.173), calls=%async_computation | async-start | bytes 2097152 | tf_op jit(solution)/shard_map/all_to_all | solution.py:36
  178.5 5.1 %collective-permute-done.16 = bf16[4,256,128]{2,1,0:T(8,128)(2,1)S(1)} collective-permute-done((bf16[4,256,128]{2,1,0:T(8,128)(2,1)}, bf16[4,256,128]{2,1,0:T(8,128)(2,1)S(1)}, u32[]{:S(2)}, u32[]{:S(2)}) %collective-permute-start.16) | collective-permute-done | bytes 262176 | tf_op jit(solution)/shard_map/ppermute | solution.py:81
  184.3 2.9 %collective-permute-start.17 = (bf16[256,128]{1,0:T(8,128)(2,1)S(1)}, bf16[256,128]{1,0:T(8,128)(2,1)S(1)}, u32[]{:S(2)}, u32[]{:S(2)}) collective-permute-start(bf16[256,128]{1,0:T(8,128)(2,1)S(1)} %get-tuple-element.275), channel_id=1, source_target_pairs={{0,12},{1,13},{2,14},{3,15},{4,0},{5,1},{6,2},{7,3},{8,4},{9,5},{1... | collective-permute-start | bytes 196616 | tf_op jit(solution)/shard_map/ppermute | solution.py:81
  187.2 2.3 %collective-permute-done.18 = bf16[256,128]{1,0:T(8,128)(2,1)S(1)} collective-permute-done((bf16[256,128]{1,0:T(8,128)(2,1)S(1)}, bf16[256,128]{1,0:T(8,128)(2,1)S(1)}, u32[]{:S(2)}, u32[]{:S(2)}) %collective-permute-start.18) | collective-permute-done | bytes 65568 | tf_op jit(solution)/shard_map/ppermute | solution.py:81
  189.6 2.4 %fusion.44 = bf16[1024,128]{1,0:T(8,128)(2,1)S(1)} fusion(f32[1024,64]{1,0:T(8,128)S(1)} %get-tuple-element.274, f32[1024,64]{1,0:T(8,128)S(1)} %get-tuple-element.273, f32[1024,128]{1,0:T(8,128)S(1)} %get-tuple-element.128, f32[1024,64]{1,0:T(8,128)S(1)} %get-tuple-element.291), kind=kLoop, calls=%fused_computation.70 | loop fusion | flops 786432 | bytes 1572864 | tf_op jit(solution)/shard_map/convert_element_type | solution.py:324
  192.1 9.0 %collective-permute-start.13 = (bf16[256,512]{1,0:T(8,128)(2,1)S(1)}, bf16[256,512]{1,0:T(8,128)(2,1)S(1)}, u32[]{:S(2)}, u32[]{:S(2)}) collective-permute-start(bf16[256,512]{1,0:T(8,128)(2,1)S(1)} %convert_element_type.99), channel_id=1, source_target_pairs={{16,0},{32,16},{48,32},{64,48},{80,64},{96,80},{112,96},{17,1},{33... | collective-permute-start | bytes 786440 | tf_op jit(solution)/shard_map/ppermute | solution.py:25
  201.9 2.7 %all-to-all-done = bf16[16,256,128]{2,1,0:T(8,128)(2,1)} async-done(((bf16[16,256,128]{2,1,0:T(8,128)(2,1)}), bf16[16,256,128]{2,1,0:T(8,128)(2,1)}, u32[]{:S(2)}, u32[]{:S(2)}) %all-to-all-start) | async-done | bytes 1048608 | tf_op jit(solution)/shard_map/all_to_all | solution.py:36
  204.6 1.4 reduce_sum.64
  206.0 2.7 %collective-permute-start.20 = (bf16[256,256]{1,0:T(8,128)(2,1)S(1)}, bf16[256,256]{1,0:T(8,128)(2,1)S(1)}, u32[]{:S(2)}, u32[]{:S(2)}) collective-permute-start(bf16[256,256]{1,0:T(8,128)(2,1)S(1)} %pad_maximum_fusion.10), channel_id=1, source_target_pairs={{16,0},{32,16},{48,32},{64,48},{80,64},{96,80},{112,96},{17,1},{33... | collective-permute-start | bytes 393224 | tf_op jit(solution)/shard_map/ppermute | solution.py:25
  208.8 3.8 %collective-permute-done.20 = bf16[256,256]{1,0:T(8,128)(2,1)S(1)} collective-permute-done((bf16[256,256]{1,0:T(8,128)(2,1)S(1)}, bf16[256,256]{1,0:T(8,128)(2,1)S(1)}, u32[]{:S(2)}, u32[]{:S(2)}) %collective-permute-start.20) | collective-permute-done | bytes 131104 | tf_op jit(solution)/shard_map/ppermute | solution.py:25
  213.4 9.1 %shard_map.91 = bf16[256,8192]{1,0:T(8,128)(2,1)} custom-call(bf16[256,768]{1,0:T(8,128)(2,1)} %pad_maximum_fusion.4.grad_ref, bf16[8192,768]{1,0:T(8,128)(2,1)} %all-gather.4.cloned.1.call-done.weight_ref, bf16[256,8192]{1,0:T(8,128)(2,1)} %collective-permute-done.22.base_ref), custom_call_target="tpu_custom_call" | custom-call | flops 3221225472 | bytes 21364736 | tf_op jit(solution)/shard_map/pallas_call | solution.py:50
  (312 shorter events, 80.0 us)
Async XLA Ops:
  6.5 25.0 %copy-start.3 = (s32[1,32]{1,0:T(1,128)S(1)}, s32[1,32]{1,0:T(1,128)}, u32[]{:S(2)}) copy-start(s32[1,32]{1,0:T(1,128)} %param.19) | copy-start | bytes 388
  6.5 92.7 %all-gather.6.cloned.1.call-start = ((), (), s32[]{:S(2)}) async-start(), calls=%async_computation.2 | async-start | bytes 8912896 | tf_op jit(solution)/shard_map/all_gather | solution.py:227
  7.3 206.2 %all-gather.4.cloned.1.call-start = ((), (), s32[]{:S(2)}) async-start(), calls=%async_computation.1 | async-start | bytes 13369344 | tf_op jit(solution)/shard_map/all_gather | solution.py:224
  8.2 10.8 %collective-permute-start = (bf16[128,256]{1,0:T(8,128)(2,1)S(1)}, bf16[128,256]{1,0:T(8,128)(2,1)S(1)}, u32[]{:S(2)}, u32[]{:S(2)}) collective-permute-start(bf16[128,256]{1,0:T(8,128)(2,1)S(1)} %get-tuple-element.286), channel_id=1, source_target_pairs={{0,1},{1,2},{2,3},{3,0},{4,5},{5,6},{6,7},{7,4},{8,9},{9,10},{10,1... | collective-permute-start | bytes 196616 | tf_op jit(solution)/shard_map/ppermute | solution.py:81
  10.3 8.9 %collective-permute-start.1 = (bf16[128,256]{1,0:T(8,128)(2,1)S(1)}, bf16[128,256]{1,0:T(8,128)(2,1)S(1)}, u32[]{:S(2)}, u32[]{:S(2)}) collective-permute-start(bf16[128,256]{1,0:T(8,128)(2,1)S(1)} %get-tuple-element.286), channel_id=1, source_target_pairs={{0,3},{1,0},{2,1},{3,2},{4,7},{5,4},{6,5},{7,6},{8,11},{9,8},{10,9... | collective-permute-start | bytes 196616 | tf_op jit(solution)/shard_map/ppermute | solution.py:81
  11.7 11.8 %collective-permute-start.6 = (bf16[128,256]{1,0:T(8,128)(2,1)S(1)}, bf16[128,256]{1,0:T(8,128)(2,1)S(1)}, u32[]{:S(2)}, u32[]{:S(2)}) collective-permute-start(bf16[128,256]{1,0:T(8,128)(2,1)S(1)} %get-tuple-element.287), channel_id=1, source_target_pairs={{0,4},{1,5},{2,6},{3,7},{4,8},{5,9},{6,10},{7,11},{8,12},{9,13},{1... | collective-permute-start | bytes 196616 | tf_op jit(solution)/shard_map/ppermute | solution.py:81
  13.1 11.5 %collective-permute-start.7 = (bf16[128,256]{1,0:T(8,128)(2,1)S(1)}, bf16[128,256]{1,0:T(8,128)(2,1)S(1)}, u32[]{:S(2)}, u32[]{:S(2)}) collective-permute-start(bf16[128,256]{1,0:T(8,128)(2,1)S(1)} %get-tuple-element.287), channel_id=1, source_target_pairs={{0,12},{1,13},{2,14},{3,15},{4,0},{5,1},{6,2},{7,3},{8,4},{9,5},{1... | collective-permute-start | bytes 196616 | tf_op jit(solution)/shard_map/ppermute | solution.py:81
  15.5 25.9 %collective-permute-start.12 = (bf16[128,512]{1,0:T(8,128)(2,1)S(1)}, bf16[128,512]{1,0:T(8,128)(2,1)S(1)}, u32[]{:S(2)}, u32[]{:S(2)}) collective-permute-start(bf16[128,512]{1,0:T(8,128)(2,1)S(1)} %get-tuple-element.278), channel_id=1, source_target_pairs={{0,8},{1,9},{2,10},{3,11},{4,12},{5,13},{6,14},{7,15},{8,0},{9,1},... | collective-permute-start | bytes 393224 | tf_op jit(solution)/shard_map/ppermute | solution.py:19
  19.0 4.9 %collective-permute-start.2 = (bf16[128,256]{1,0:T(8,128)(2,1)S(1)}, bf16[128,256]{1,0:T(8,128)(2,1)S(1)}, u32[]{:S(2)}, u32[]{:S(2)}) collective-permute-start(bf16[128,256]{1,0:T(8,128)(2,1)S(1)} %collective-permute-done), channel_id=1, source_target_pairs={{0,1},{1,2},{2,3},{3,0},{4,5},{5,6},{6,7},{7,4},{8,9},{9,10},{10,1... | collective-permute-start | bytes 196616 | tf_op jit(solution)/shard_map/ppermute | solution.py:81
  19.2 37.5 %collective-permute-start.21 = (bf16[512,768]{1,0:T(8,128)(2,1)}, bf16[512,768]{1,0:T(8,128)(2,1)}, u32[]{:S(2)}, u32[]{:S(2)}) collective-permute-start(bf16[512,768]{1,0:T(8,128)(2,1)} %bitcast.197), channel_id=1, source_target_pairs={{16,0},{32,16},{48,32},{64,48},{80,64},{96,80},{112,96},{17,1},{33... | collective-permute-start | bytes 2359304 | tf_op jit(solution)/shard_map/ppermute | solution.py:25
  23.5 6.7 %collective-permute-start.8 = (bf16[128,256]{1,0:T(8,128)(2,1)S(1)}, bf16[128,256]{1,0:T(8,128)(2,1)S(1)}, u32[]{:S(2)}, u32[]{:S(2)}) collective-permute-start(bf16[128,256]{1,0:T(8,128)(2,1)S(1)} %collective-permute-done.6), channel_id=1, source_target_pairs={{0,4},{1,5},{2,6},{3,7},{4,8},{5,9},{6,10},{7,11},{8,12},{9,13},{1... | collective-permute-start | bytes 196616 | tf_op jit(solution)/shard_map/ppermute | solution.py:81
  24.0 17.1 %collective-permute-start.3 = (bf16[4,128,256]{2,1,0:T(8,128)(2,1)S(1)}, bf16[4,128,256]{2,1,0:T(8,128)(2,1)S(1)}, u32[]{:S(2)}, u32[]{:S(2)}) collective-permute-start(bf16[4,128,256]{2,1,0:T(8,128)(2,1)S(1)} %get-tuple-element.280), channel_id=1, source_target_pairs={{0,4},{1,5},{2,6},{3,7},{4,8},{5,9},{6,10},{7,11},{8,12},{9,13},{1... | collective-permute-start | bytes 786440 | tf_op jit(solution)/shard_map/ppermute | solution.py:81
  30.2 14.3 %collective-permute-start.9 = (bf16[4,128,256]{2,1,0:T(8,128)(2,1)S(1)}, bf16[4,128,256]{2,1,0:T(8,128)(2,1)S(1)}, u32[]{:S(2)}, u32[]{:S(2)}) collective-permute-start(bf16[4,128,256]{2,1,0:T(8,128)(2,1)S(1)} %get-tuple-element.282), channel_id=1, source_target_pairs={{0,1},{1,2},{2,3},{3,0},{4,5},{5,6},{6,7},{7,4},{8,9},{9,10},{10,1... | collective-permute-start | bytes 786440 | tf_op jit(solution)/shard_map/ppermute | solution.py:81
  33.5 12.1 %collective-permute-start.4 = (bf16[4,128,256]{2,1,0:T(8,128)(2,1)S(1)}, bf16[4,128,256]{2,1,0:T(8,128)(2,1)S(1)}, u32[]{:S(2)}, u32[]{:S(2)}) collective-permute-start(bf16[4,128,256]{2,1,0:T(8,128)(2,1)S(1)} %get-tuple-element.280), channel_id=1, source_target_pairs={{0,12},{1,13},{2,14},{3,15},{4,0},{5,1},{6,2},{7,3},{8,4},{9,5},{1... | collective-permute-start | bytes 786440 | tf_op jit(solution)/shard_map/ppermute | solution.py:81
  41.1 7.7 %collective-permute-start.5 = (bf16[4,128,256]{2,1,0:T(8,128)(2,1)S(1)}, bf16[4,128,256]{2,1,0:T(8,128)(2,1)S(1)}, u32[]{:S(2)}, u32[]{:S(2)}) collective-permute-start(bf16[4,128,256]{2,1,0:T(8,128)(2,1)S(1)} %collective-permute-done.3), channel_id=1, source_target_pairs={{0,4},{1,5},{2,6},{3,7},{4,8},{5,9},{6,10},{7,11},{8,12},{9,13},{1... | collective-permute-start | bytes 786440 | tf_op jit(solution)/shard_map/ppermute | solution.py:81
  41.4 8.4 %collective-permute-start.10 = (bf16[4,128,256]{2,1,0:T(8,128)(2,1)S(1)}, bf16[4,128,256]{2,1,0:T(8,128)(2,1)}, u32[]{:S(2)}, u32[]{:S(2)}) collective-permute-start(bf16[4,128,256]{2,1,0:T(8,128)(2,1)S(1)} %get-tuple-element.282), channel_id=1, source_target_pairs={{0,3},{1,0},{2,1},{3,2},{4,7},{5,4},{6,5},{7,6},{8,11},{9,8},{10,9... | collective-permute-start | bytes 786440 | tf_op jit(solution)/shard_map/ppermute | solution.py:81
  44.5 8.8 %collective-permute-start.11 = (bf16[4,128,256]{2,1,0:T(8,128)(2,1)S(1)}, bf16[4,128,256]{2,1,0:T(8,128)(2,1)}, u32[]{:S(2)}, u32[]{:S(2)}) collective-permute-start(bf16[4,128,256]{2,1,0:T(8,128)(2,1)S(1)} %collective-permute-done.9), channel_id=1, source_target_pairs={{0,1},{1,2},{2,3},{3,0},{4,5},{5,6},{6,7},{7,4},{8,9},{9,10},{10,1... | collective-permute-start | bytes 786440 | tf_op jit(solution)/shard_map/ppermute | solution.py:81
  58.8 1.1 copy-start
  60.8 0.8 copy-start.1
  63.7 1.1 copy-start
  65.7 0.8 copy-start.1
  68.6 1.0 copy-start
  70.6 0.8 copy-start.1
  73.4 1.0 copy-start
  75.5 0.8 copy-start.1
  78.3 1.1 copy-start
  80.3 0.8 copy-start.1
  83.2 1.0 copy-start
  85.2 0.8 copy-start.1
  88.1 1.0 copy-start
  90.1 0.8 copy-start.1
  92.9 1.0 copy-start
  94.9 0.8 copy-start.1
  95.7 117.7 %collective-permute-start.22 = (bf16[256,8192]{1,0:T(8,128)(2,1)}, bf16[256,8192]{1,0:T(8,128)(2,1)}, u32[]{:S(2)}, u32[]{:S(2)}) collective-permute-start(bf16[256,8192]{1,0:T(8,128)(2,1)} %bitcast.196), channel_id=1, source_target_pairs={{16,0},{32,16},{48,32},{64,48},{80,64},{96,80},{112,96},{17,1},{33... | collective-permute-start | bytes 12582920 | tf_op jit(solution)/shard_map/ppermute | solution.py:25
  99.2 7.9 %copy-start.2 = (f32[1024,128]{1,0:T(8,128)S(1)}, f32[1024,128]{1,0:T(8,128)}, u32[]{:S(2)}) copy-start(f32[1024,128]{1,0:T(8,128)} %get-tuple-element.127) | copy-start | bytes 1572868
  152.1 15.3 %collective-permute-start.15 = (bf16[4,256,128]{2,1,0:T(8,128)(2,1)S(1)}, bf16[4,256,128]{2,1,0:T(8,128)(2,1)S(1)}, u32[]{:S(2)}, u32[]{:S(2)}) collective-permute-start(bf16[4,256,128]{2,1,0:T(8,128)(2,1)S(1)} %get-tuple-element.272), channel_id=1, source_target_pairs={{0,1},{1,2},{2,3},{3,0},{4,5},{5,6},{6,7},{7,4},{8,9},{9,10},{10,1... | collective-permute-start | bytes 786440 | tf_op jit(solution)/shard_map/ppermute | solution.py:81
  152.2 26.3 %collective-permute-start.14 = (bf16[4,256,128]{2,1,0:T(8,128)(2,1)S(1)}, bf16[4,256,128]{2,1,0:T(8,128)(2,1)S(1)}, u32[]{:S(2)}, u32[]{:S(2)}) collective-permute-start(bf16[4,256,128]{2,1,0:T(8,128)(2,1)S(1)} %get-tuple-element.271), channel_id=1, source_target_pairs={{0,3},{1,0},{2,1},{3,2},{4,7},{5,4},{6,5},{7,6},{8,11},{9,8},{10,9... | collective-permute-start | bytes 786440 | tf_op jit(solution)/shard_map/ppermute | solution.py:81
  168.2 15.4 %collective-permute-start.16 = (bf16[4,256,128]{2,1,0:T(8,128)(2,1)}, bf16[4,256,128]{2,1,0:T(8,128)(2,1)S(1)}, u32[]{:S(2)}, u32[]{:S(2)}) collective-permute-start(bf16[4,256,128]{2,1,0:T(8,128)(2,1)} %fusion.40), channel_id=1, source_target_pairs={{0,1},{1,2},{2,3},{3,0},{4,5},{5,6},{6,7},{7,4},{8,9},{9,10},{10,1... | collective-permute-start | bytes 786440 | tf_op jit(solution)/shard_map/ppermute | solution.py:81
  172.0 32.6 %all-to-all-start = ((bf16[16,256,128]{2,1,0:T(8,128)(2,1)}), bf16[16,256,128]{2,1,0:T(8,128)(2,1)}, u32[]{:S(2)}, u32[]{:S(2)}) async-start(bf16[16,256,128]{2,1,0:T(8,128)(2,1)} %bitcast.173), calls=%async_computation | async-start | bytes 2097152 | tf_op jit(solution)/shard_map/all_to_all | solution.py:36
  183.8 5.7 %collective-permute-start.18 = (bf16[256,128]{1,0:T(8,128)(2,1)S(1)}, bf16[256,128]{1,0:T(8,128)(2,1)S(1)}, u32[]{:S(2)}, u32[]{:S(2)}) collective-permute-start(bf16[256,128]{1,0:T(8,128)(2,1)S(1)} %get-tuple-element.276), channel_id=1, source_target_pairs={{0,4},{1,5},{2,6},{3,7},{4,8},{5,9},{6,10},{7,11},{8,12},{9,13},{1... | collective-permute-start | bytes 196616 | tf_op jit(solution)/shard_map/ppermute | solution.py:81
  184.3 16.9 %collective-permute-start.17 = (bf16[256,128]{1,0:T(8,128)(2,1)S(1)}, bf16[256,128]{1,0:T(8,128)(2,1)S(1)}, u32[]{:S(2)}, u32[]{:S(2)}) collective-permute-start(bf16[256,128]{1,0:T(8,128)(2,1)S(1)} %get-tuple-element.275), channel_id=1, source_target_pairs={{0,12},{1,13},{2,14},{3,15},{4,0},{5,1},{6,2},{7,3},{8,4},{9,5},{1... | collective-permute-start | bytes 196616 | tf_op jit(solution)/shard_map/ppermute | solution.py:81
  189.5 11.7 %collective-permute-start.19 = (bf16[256,128]{1,0:T(8,128)(2,1)S(1)}, bf16[256,128]{1,0:T(8,128)(2,1)S(1)}, u32[]{:S(2)}, u32[]{:S(2)}) collective-permute-start(bf16[256,128]{1,0:T(8,128)(2,1)S(1)} %fusion.47), channel_id=1, source_target_pairs={{0,4},{1,5},{2,6},{3,7},{4,8},{5,9},{6,10},{7,11},{8,12},{9,13},{1... | collective-permute-start | bytes 196616 | tf_op jit(solution)/shard_map/ppermute | solution.py:81
  192.1 16.6 %collective-permute-start.13 = (bf16[256,512]{1,0:T(8,128)(2,1)S(1)}, bf16[256,512]{1,0:T(8,128)(2,1)S(1)}, u32[]{:S(2)}, u32[]{:S(2)}) collective-permute-start(bf16[256,512]{1,0:T(8,128)(2,1)S(1)} %convert_element_type.99), channel_id=1, source_target_pairs={{16,0},{32,16},{48,32},{64,48},{80,64},{96,80},{112,96},{17,1},{33... | collective-permute-start | bytes 786440 | tf_op jit(solution)/shard_map/ppermute | solution.py:25
  206.0 6.5 %collective-permute-start.20 = (bf16[256,256]{1,0:T(8,128)(2,1)S(1)}, bf16[256,256]{1,0:T(8,128)(2,1)S(1)}, u32[]{:S(2)}, u32[]{:S(2)}) collective-permute-start(bf16[256,256]{1,0:T(8,128)(2,1)S(1)} %pad_maximum_fusion.10), channel_id=1, source_target_pairs={{16,0},{32,16},{48,32},{64,48},{80,64},{96,80},{112,96},{17,1},{33... | collective-permute-start | bytes 393224 | tf_op jit(solution)/shard_map/ppermute | solution.py:25
Sparse Core Ops, SparseCore 0:
  9.5 79.0 all-gather.5
  90.7 110.5 all-gather.3
